TPU v7x, 128 devices: a whole 4x4x4 slice. The times are simulated.
128 devices in a mesh: ctx: 32 (over x, y, core), head: 4 (over z).
Axes of the slice: x: 4, y: 4, z: 4, core: 2. Of those that a mesh axis runs over, the one named last changes fastest.
Arguments:
- x_in: bfloat16 [16384, 1, 8192], P('ctx', None, 'head'), may hold values from -6 to 6
- z_in: bfloat16 [16384, 1, 8192], P('ctx', None, 'head')
- bc_in: bfloat16 [16384, 1, 256], P('ctx'), may hold values from -6 to 6
- dt_in: float32 [16384, 1, 128], P('ctx', None, 'head'), may hold values from -3 to 3
- dt_bias: float32 [128], P('head')
- a_log: float32 [128], P('head'), may hold values from -1.5 to 0.5
- skip: float32 [128], P('head'), may hold values from 0.5 to 1.5
- conv_x: bfloat16 [4, 8192], P(None, 'head'), may hold values from -3 to 3
- conv_bc: bfloat16 [4, 256], replicated, may hold values from -3 to 3
- norm_gain: float32 [8192], P('head'), may hold values from 0.1 to 1.9
- w_out: bfloat16 [8192, 4096], P('head'), may hold values from -0.0625 to 0.0625
- requests: int32 [256], P('ctx'), may hold values from 0 to 1, as said below
- step_x: bfloat16 [4, 256, 8192], P(None, 'ctx', 'head'), may hold values from -6 to 6
- step_z: bfloat16 [4, 256, 8192], P(None, 'ctx', 'head'), may hold values from -6 to 6
- step_bc: bfloat16 [4, 256, 256], P(None, 'ctx'), may hold values from -6 to 6
- step_dt: float32 [4, 256, 128], P(None, 'ctx', 'head'), may hold values from -3 to 3
Outputs:
- out: bfloat16 [16384, 1, 4096], P(('ctx', 'head'))
- dec_out: bfloat16 [4, 256, 8192], P(None, 'ctx', 'head')
Inputs may be any that keep to these rules, and one draw needn't show every extreme that they name: Slot r is decoded on index r // 8 of ctx. Each index's 8 slots hold its requests first, then empty slots marked 1; every index has one request or more, and some index has all 8 slots in use.
All inputs are finite; a program needn't handle non-finite values.
Results may differ from a plain program's by a relative error of at most 0.007.
Values may be sent and summed in bfloat16 or wider, within the bound.
No kernel may reach another device: no remote copies, remote signals or barrier semaphores. Data moves between devices by JAX's collectives and lax.ppermute only.
A program may use at most 256 MiB of HBM per device.

v0:
```python
import jax
import jax.numpy as jnp
from jax import lax
from jax.sharding import PartitionSpec as P

norm_eps = 1e-05


def passed_along(value, axis, steps):
    count = lax.axis_size(axis)
    leading, last = (max(0, -steps), min(count, count - steps))
    return lax.ppermute(value, axis, [(source, source + steps) for source in range(leading, last)])


def group_shift(value, axis, count, stride, group, shift):
    pairs = []
    for source in range(count):
        member = (source // stride) % group
        target = source + (((member + shift) % group) - member) * stride
        pairs.append((source, target))
    return lax.ppermute(value, axis, pairs)


def conv_silu(window, weight, length):
    running_sum = jnp.zeros((length,) + window.shape[1:], jnp.float32)
    for offset in range(weight.shape[0]):
        running_sum = running_sum + window[offset : offset + length].astype(jnp.float32) * weight[
            offset
        ].astype(jnp.float32)
    return jax.nn.silu(running_sum).astype(jnp.bfloat16)


def chain(earlier, later):
    return (earlier[0] * later[0], later[0][..., None, None] * earlier[1] + later[1])


def pick(flag, first, second):
    return jax.tree.map(lambda a, b: jnp.where(flag, a, b), first, second)


def ring_scan(own, axis, count, stride, group):
    member = (lax.axis_index(axis) // stride) % group
    if group == 4:
        from_prev = group_shift(own, axis, count, stride, group, 1)
        from_next = group_shift(own, axis, count, stride, group, -1)
        split = own[1].shape[2] // 2
        lead = group_shift(
            (from_prev[0], from_prev[1][:, :, :split]), axis, count, stride, group, 1
        )
        rest = group_shift(from_next[1][:, :, split:], axis, count, stride, group, -1)
        far = (lead[0], jnp.concatenate([lead[1], rest], 2))
        received = [None, from_prev, far, from_next]
    else:
        received = [None] + [
            group_shift(own, axis, count, stride, group, shift) for shift in range(1, group)
        ]
    identity = (jnp.ones_like(own[0]), jnp.zeros_like(own[1]))
    before = identity
    for shift in range(group - 1, 0, -1):
        before = pick(shift <= member, chain(before, received[shift]), before)
    total = chain(before, own)
    for shift in range(group - 1, 0, -1):
        total = pick(shift > member, chain(total, received[shift]), total)
    return before, total


def body(
    x_in,
    z_in,
    bc_in,
    dt_in,
    dt_bias,
    a_log,
    skip,
    conv_x,
    conv_bc,
    norm_gain,
    w_out,
    requests,
    step_x,
    step_z,
    step_bc,
    step_dt,
):
    block_len, prompts, inner_loc = x_in.shape
    heads_loc = dt_in.shape[2]
    head_dim = inner_loc // heads_loc
    state_dim = bc_in.shape[2] // 2
    conv_taps = conv_x.shape[0]
    edge_x, edge_bc = passed_along(
        (x_in[block_len - conv_taps + 1 :], bc_in[block_len - conv_taps + 1 :]), "ctx", 1
    )
    x_conv = conv_silu(jnp.concatenate([edge_x, x_in], axis=0), conv_x, block_len)
    bc_conv = conv_silu(jnp.concatenate([edge_bc, bc_in], axis=0), conv_bc, block_len)
    b_rows = bc_conv[..., :state_dim]
    c_rows = bc_conv[..., state_dim:]
    decay_rates = -jnp.exp(a_log)
    dt_full = jax.nn.softplus(dt_in + dt_bias)
    cum_log = jnp.cumsum(dt_full * decay_rates, axis=0)
    cum_heads = jnp.transpose(cum_log, (1, 2, 0))
    dt_heads = jnp.transpose(dt_full, (1, 2, 0))
    x_heads = x_conv.reshape(block_len, prompts, heads_loc, head_dim)
    block_log = cum_heads[..., -1]
    tail_weights = jnp.transpose(jnp.exp(block_log[..., None] - cum_heads) * dt_heads, (2, 0, 1))
    weighted_x = (x_heads * tail_weights[..., None]).astype(jnp.bfloat16)
    s_local = jnp.einsum("jphd,jpn->phdn", weighted_x, b_rows, preferred_element_type=jnp.float32)
    block_decay = jnp.exp(block_log)

    count = lax.axis_size("ctx")
    here = lax.axis_index("ctx")
    core = here % 2
    tails = jax.tree.map(
        lambda part: lax.all_gather(part, "ctx")[count - 1],
        (x_in[block_len - conv_taps + 1 :], bc_in[block_len - conv_taps + 1 :]),
    )
    own = (block_decay, s_local)
    other = group_shift(own, "ctx", count, 1, 2, 1)
    first = pick(core == 0, own, other)
    second = pick(core == 0, other, own)
    chip_total = chain(first, second)
    half = head_dim // 2
    chip_half = (chip_total[0], lax.dynamic_slice_in_dim(chip_total[1], core * half, half, 2))
    row_before, row_total = ring_scan(chip_half, "ctx", count, 2, 4)
    rows = count // 8
    top_before, top_total = ring_scan(row_total, "ctx", count, 8, rows)
    chip_before = chain(top_before, row_before)
    mine = (chip_before[1], top_total[1])
    theirs = group_shift(mine, "ctx", count, 1, 2, 1)
    joined = jax.tree.map(
        lambda a, b: jnp.where(core == 0, jnp.concatenate([a, b], 2), jnp.concatenate([b, a], 2)),
        mine,
        theirs,
    )
    chip_state, final_state = joined
    s_before = jnp.where(
        core == 0, chip_state, first[0][..., None, None] * chip_state + first[1]
    )

    scores = jnp.einsum("ipn,jpn->pij", c_rows, b_rows, preferred_element_type=jnp.float32)
    position = lax.iota(jnp.int32, block_len)
    causal = position[:, None] >= position[None, :]
    gaps = jnp.where(causal, cum_heads[..., :, None] - cum_heads[..., None, :], -jnp.inf)
    mixing = (scores[:, None] * jnp.exp(gaps) * dt_heads[..., None, :]).astype(jnp.bfloat16)
    y_intra = jnp.einsum("phij,jphd->iphd", mixing, x_heads, preferred_element_type=jnp.float32)
    y_inter = (
        jnp.einsum(
            "ipn,phdn->iphd", c_rows.astype(jnp.float32), s_before, precision=lax.Precision.HIGHEST
        )
        * jnp.exp(cum_log)[..., None]
    )
    y_all = y_intra + y_inter + skip[:, None] * x_heads.astype(jnp.float32)
    gated_out = y_all.reshape(block_len, prompts, inner_loc) * jax.nn.silu(z_in.astype(jnp.float32))
    square_local = jnp.sum(gated_out * gated_out, axis=-1)
    head_count = lax.axis_size("head")
    square_sums = square_local
    for shift in range(1, head_count):
        square_sums = square_sums + group_shift(square_local, "head", head_count, 1, head_count, shift)
    inner_total = inner_loc * lax.axis_size("head")
    normed = (
        gated_out * lax.rsqrt(square_sums / inner_total + norm_eps)[..., None] * norm_gain
    ).astype(jnp.bfloat16)
    projected = lax.psum_scatter(
        jnp.einsum("tpi,id->tpd", normed, w_out, preferred_element_type=jnp.float32).astype(
            jnp.bfloat16
        ),
        "head",
        scatter_dimension=0,
        tiled=True,
    )
    out = projected.astype(jnp.bfloat16)

    final_x, final_bc = tails
    slot_count = requests.shape[0]
    steps = step_x.shape[0]
    slot_pick = (requests[:, None] == lax.iota(jnp.int32, prompts)[None, :]).astype(jnp.float32)
    live_slots = requests < prompts
    hist_x = jnp.einsum(
        "rp,kpi->kri", slot_pick, final_x.astype(jnp.float32), precision=lax.Precision.HIGHEST
    ).astype(jnp.bfloat16)
    hist_bc = jnp.einsum(
        "rp,kpi->kri", slot_pick, final_bc.astype(jnp.float32), precision=lax.Precision.HIGHEST
    ).astype(jnp.bfloat16)
    window_x = jnp.concatenate([hist_x, step_x], axis=0)
    window_bc = jnp.concatenate([hist_bc, step_bc], axis=0)
    new_x = conv_silu(window_x, conv_x, steps)
    new_bc = conv_silu(window_bc, conv_bc, steps)
    dt_step = jax.nn.softplus(step_dt + dt_bias)
    x_step = new_x.reshape(steps, slot_count, heads_loc, head_dim).astype(jnp.float32)
    b_step = new_bc[..., :state_dim].astype(jnp.float32)
    c_step = new_bc[..., state_dim:].astype(jnp.float32)
    step_decay = jnp.exp(dt_step * decay_rates)
    pushed = dt_step[..., None] * x_step
    from_final = jnp.einsum(
        "phdn,srn->psrhd", final_state.reshape(prompts, heads_loc, head_dim, state_dim), c_step,
        precision=lax.Precision.HIGHEST,
    )
    from_final = jnp.einsum("rp,psrhd->srhd", slot_pick, from_final, precision=lax.Precision.HIGHEST)
    overlap = jnp.einsum("trn,srn->tsr", b_step, c_step, precision=lax.Precision.HIGHEST)
    outputs = []
    carried = jnp.ones_like(step_decay[0])
    for step_index in range(steps):
        carried = carried * step_decay[step_index]
        y_step = carried[..., None] * from_final[step_index]
        for earlier in range(step_index + 1):
            weight = jnp.ones_like(step_decay[0])
            for later in range(earlier + 1, step_index + 1):
                weight = weight * step_decay[later]
            y_step = y_step + (weight * overlap[earlier, step_index][:, None])[..., None] * pushed[
                earlier
            ]
        y_step = y_step + skip[:, None] * x_step[step_index]
        gated_step = y_step.reshape(slot_count, inner_loc) * jax.nn.silu(
            step_z[step_index].astype(jnp.float32)
        )
        outputs.append(jnp.where(live_slots[:, None], gated_step, 0.0).astype(jnp.bfloat16))
    return (out, jnp.stack(outputs))

def solution(mesh):
    placed = (
        P("ctx", None, "head"),
        P("ctx", None, "head"),
        P("ctx", None, None),
        P("ctx", None, "head"),
        P("head"),
        P("head"),
        P("head"),
        P(None, "head"),
        P(),
        P("head"),
        P("head", None),
        P("ctx"),
        P(None, "ctx", "head"),
        P(None, "ctx", "head"),
        P(None, "ctx", None),
        P(None, "ctx", "head"),
    )
    return jax.shard_map(
        body,
        mesh=mesh,
        in_specs=placed,
        out_specs=(P(("ctx", "head"), None, None), P(None, "ctx", "head")),
        check_vma=False,
    )
```

profile of v0, /device:TPU:0, one launch (start us, length us, event | category | flops | bytes accessed | tf_op | source)
XLA Modules:
  0.0 201.9 jit_solution(16781352256027657491)
XLA Ops:
  7.2 2.9 %copy.62 = bf16[512,1,2048]{0,2,1:T(8,128)(2,1)S(1)} copy(bf16[512,1,2048]{2,0,1:T(8,128)(2,1)} %param.16) | data formatting | bytes 4194304 | tf_op args[0]
  10.3 1.3 collective-permute-start
  11.7 1.3 slice.233
  12.9 4.9 %collective-permute-start.1 = (bf16[3,1,256]{2,0,1:T(4,128)(2,1)}, bf16[3,1,256]{2,0,1:T(4,128)(2,1)}, u32[]{:S(2)}, u32[]{:S(2)}) collective-permute-start(bf16[3,1,256]{2,0,1:T(4,128)(2,1)} %slice.233), channel_id=1, source_target_pairs={{0,4},{4,8},{8,12},{12,16},{16,20},{20,24},{24,28},{28,32},{32,36}... | collective-permute-start | bytes 4616 | tf_op jit(solution)/shard_map/ppermute | solution.py:12
  18.6 1.2 reduce-window.6
  21.1 0.9 slice_convert_fusion.4
  22.0 0.8 slice_convert_fusion.9
  22.9 2.0 multiply_convert_fusion.4
  25.4 5.6 %fusion.9 = (bf16[512,1,2048]{0,2,1:T(8,128)(2,1)S(1)}, bf16[512,1,2048]{0,2,1:T(8,128)(2,1)}) fusion(f32[2048]{0:T(1024)S(1)} %bitcast.220, bf16[512,1,2048]{0,2,1:T(8,128)(2,1)S(1)} %copy.62, f32[2048]{0:T(1024)S(1)} %bitcast.222, bf16[3,1,2048]{0,2,1:T(8,128)(2,1)S(1)} %collective-permute-done, f32[2048]{0:T(1024)S(1)} %bitcast.218, ...), kind=kLoop, calls=%fused_computation.15 | loop fusion | flops 29360128 | bytes 10530816 | tf_op jit(solution)/shard_map/convert_element_type | solution.py:105
  32.4 2.1 %collective-permute-done.2 = f32[1,32]{1,0:T(1,128)S(1)} collective-permute-done((f32[1,32]{1,0:T(1,128)}, f32[1,32]{1,0:T(1,128)S(1)}, u32[]{:S(2)}, u32[]{:S(2)}) %collective-permute-start.2) | collective-permute-done | bytes 160 | tf_op jit(solution)/shard_map/ppermute | solution.py:21
  34.5 1.3 fusion.91
  36.0 0.9 fusion.27
  36.9 1.0 collective-permute-start.11
  37.9 2.2 %collective-permute-start.10 = (f32[1,32,32,128]{3,2,1,0:T(8,128)}, f32[1,32,32,128]{3,2,1,0:T(8,128)S(1)}, u32[]{:S(2)}, u32[]{:S(2)}) collective-permute-start(f32[1,32,32,128]{3,2,1,0:T(8,128)} %fusion.27), channel_id=1, source_target_pairs={{0,24},{4,28},{8,0},{12,4},{16,8},{20,12},{24,16},{28,20},{32,56},... | collective-permute-start | bytes 1572872 | tf_op jit(solution)/shard_map/ppermute | solution.py:21
  40.1 12.1 %collective-permute-done.11 = f32[1,32,32,128]{3,2,1,0:T(8,128)S(1)} collective-permute-done((f32[1,32,32,128]{3,2,1,0:T(8,128)}, f32[1,32,32,128]{3,2,1,0:T(8,128)S(1)}, u32[]{:S(2)}, u32[]{:S(2)}) %collective-permute-start.11) | collective-permute-done | bytes 524320 | tf_op jit(solution)/shard_map/ppermute | solution.py:21
  52.4 1.0 exponential_bitcast_fusion
  53.5 1.1 collective-permute-start.4
  54.6 2.2 %collective-permute-start.3 = (f32[1,32]{1,0:T(1,128)}, f32[1,32]{1,0:T(1,128)S(1)}, u32[]{:S(2)}, u32[]{:S(2)}) collective-permute-start(f32[1,32]{1,0:T(1,128)} %get-tuple-element.59), channel_id=1, source_target_pairs={{0,24},{4,28},{8,0},{12,4},{16,8},{20,12},{24,16},{28,20},{32,56},... | collective-permute-start | bytes 392 | tf_op jit(solution)/shard_map/ppermute | solution.py:21
  56.8 4.3 %collective-permute-done.4 = f32[1,32]{1,0:T(1,128)S(1)} collective-permute-done((f32[1,32]{1,0:T(1,128)}, f32[1,32]{1,0:T(1,128)S(1)}, u32[]{:S(2)}, u32[]{:S(2)}) %collective-permute-start.4) | collective-permute-done | bytes 160 | tf_op jit(solution)/shard_map/ppermute | solution.py:21
  61.2 3.3 %collective-permute-start.13 = (f32[1,32,16,128]{3,2,1,0:T(8,128)S(1)}, f32[1,32,16,128]{3,2,1,0:T(8,128)S(1)}, u32[]{:S(2)}, u32[]{:S(2)}) collective-permute-start(f32[1,32,16,128]{3,2,1,0:T(8,128)S(1)} %slice.306), channel_id=1, source_target_pairs={{0,24},{4,28},{8,0},{12,4},{16,8},{20,12},{24,16},{28,20},{32,56},... | collective-permute-start | bytes 786440 | tf_op jit(solution)/shard_map/ppermute | solution.py:21
  64.5 3.8 %collective-permute-done.13 = f32[1,32,16,128]{3,2,1,0:T(8,128)S(1)} collective-permute-done((f32[1,32,16,128]{3,2,1,0:T(8,128)S(1)}, f32[1,32,16,128]{3,2,1,0:T(8,128)S(1)}, u32[]{:S(2)}, u32[]{:S(2)}) %collective-permute-start.13) | collective-permute-done | bytes 262176 | tf_op jit(solution)/shard_map/ppermute | solution.py:21
  68.4 2.5 %add_select_fusion.2 = f32[1,32,32,128]{3,2,1,0:T(8,128)} fusion(f32[1,32,32,128]{3,2,1,0:T(8,128)S(1)} %collective-permute-done.11, f32[1,32,32,128]{3,2,1,0:T(8,128)S(1)} %constant_dynamic-update-slice_fusion, f32[1,32,32,128]{3,2,1,0:T(8,128)S(1)} %collective-permute-done.10, f32[1,32,32,128]{3,2,1,0:T(8,128)} %fusion.27, ...), kind=kLoop, calls=%fused_computation.52 | loop fusion | flops 2490368 | bytes 2622086 | tf_op jit(solution)/shard_map/jit(_where)/select_n | solution.py:38
  70.9 1.8 collective-permute-start.15
  73.3 1.5 collective-permute-start.14
  74.8 0.8 iota_compare_fusion
  75.6 1.3 broadcast_select_fusion.3
  77.5 2.9 %copy.71 = bf16[512,1,2048]{0,2,1:T(8,128)(2,1)S(1)} copy(bf16[512,1,2048]{2,0,1:T(8,128)(2,1)} %param.17) | data formatting | bytes 4194304 | tf_op args[1]
  80.4 2.7 %collective-permute-start.8 = (f32[1,32]{1,0:T(1,128)}, f32[1,32]{1,0:T(1,128)S(1)}, u32[]{:S(2)}, u32[]{:S(2)}) collective-permute-start(f32[1,32]{1,0:T(1,128)} %get-tuple-element.21), channel_id=1, source_target_pairs={{0,96},{4,100},{8,104},{12,108},{16,112},{20,116},{24,120},{28,124... | collective-permute-start | bytes 392 | tf_op jit(solution)/shard_map/ppermute | solution.py:21
  84.2 1.0 slice.307
  85.1 1.6 collective-permute-start.16
  87.2 1.0 slice.308
  88.2 2.0 collective-permute-start.17
  90.5 2.3 %collective-permute-done.16 = f32[1,32,16,128]{3,2,1,0:T(8,128)S(1)} collective-permute-done((f32[1,32,16,128]{3,2,1,0:T(8,128)S(1)}, f32[1,32,16,128]{3,2,1,0:T(8,128)S(1)}, u32[]{:S(2)}, u32[]{:S(2)}) %collective-permute-start.16) | collective-permute-done | bytes 262176 | tf_op jit(solution)/shard_map/ppermute | solution.py:21
  92.8 2.0 collective-permute-done.17
  94.9 2.5 %multiply_add_fusion = f32[1,32,32,128]{3,2,1,0:T(8,128)S(1)} fusion(f32[1,32,32,128]{3,2,1,0:T(8,128)} %collective-permute-done.15, f32[1,32,32,128]{3,2,1,0:T(8,128)S(1)} %constant_dynamic-update-slice_fusion.2, f32[1,32,32,128]{3,2,1,0:T(8,128)} %collective-permute-done.14, f32[1,32,32,128]{3,2,1,0:T(8,128)} %copy-done.1, ...), kind=kLoop, calls=%fused_computation.50 | loop fusion | flops 2359296 | bytes 3670918 | tf_op jit(solution)/shard_map/add | solution.py:34
  97.5 9.5 %fusion = f32[32,64,512]{2,1,0:T(8,128)S(1)} fusion(bf16[512,32,64]{0,2,1:T(8,128)(2,1)S(1)} %bitcast.205, f32[32,512]{1,0:T(8,128)S(1)} %copy-done.17, f32[32,512]{1,0:T(8,128)S(1)} %copy-done.18, f32[512,512]{1,0:T(8,128)S(1)} %fusion.37, pred[512,512]{1,0:T(8,128)(4,1)S(1)} %copy-done.10), kind=kOutput, calls=%fused_computation.1 | convolution fusion | flops 1115684864 | bytes 7733248 | tf_op jit(solution)/shard_map/phij,jphd->iphd/dot_general | solution.py:144
  107.1 2.3 %fusion.8 = f32[512,1,32,64]{0,3,2,1:T(8,128)S(1)} fusion(f32[32,64,512]{2,1,0:T(8,128)S(1)} %fusion, f32[32]{0:T(128)S(1)} %copy-done.40, f32[512,32]{0,1:T(8,128)S(1)} %bitcast.214, f32[1,32,64,128]{3,2,1,0:T(8,128)S(1)} %broadcast_select_fusion, f32[1,32,32,128]{3,2,1,0:T(8,128)S(1)} %collective-permute-done.18, ...), kind=kOutput, calls=%fused_computation.13 | convolution fusion | flops 1617428480 | bytes 12780545 | tf_op jit(solution)/shard_map/ipn,phdn->iphd/dot_general | solution.py:146
  109.4 1.4 multiply_reduce_fusion
  110.8 2.0 collective-permute-start.19
  112.8 3.6 %collective-permute-start.20 = (f32[512,1]{0,1:T(1,128)S(1)}, f32[512,1]{0,1:T(1,128)S(1)}, u32[]{:S(2)}, u32[]{:S(2)}) collective-permute-start(f32[512,1]{0,1:T(1,128)S(1)} %bitcast.235), channel_id=1, source_target_pairs={{0,2},{1,3},{2,0},{3,1},{4,6},{5,7},{6,4},{7,5},{8,10},{9,11},{10,... | collective-permute-start | bytes 6152 | tf_op jit(solution)/shard_map/ppermute | solution.py:21
  116.4 1.0 collective-permute-start.21
  118.0 2.0 collective-permute-done.21
  120.0 14.6 %fusion.2 = bf16[512,1,4096]{2,0,1:T(8,128)(2,1)} fusion(bf16[2048,4096]{1,0:T(8,128)(2,1)} %param.26, f32[512,1,2048]{0,2,1:T(8,128)S(1)} %get-tuple-element.20, f32[2048]{0:T(1024)S(1)} %copy-done.45, f32[512]{0:T(512)S(1)} %bitcast.244), kind=kOutput, calls=%fused_computation.4 | convolution fusion | flops 8595177472 | bytes 25176064 | tf_op jit(solution)/shard_map/tpi,id->tpd/dot_general | solution.py:163
  134.8 0.8 copy.72
  136.0 24.9 %all-gather = bf16[96,1,256]{2,1,0:T(2,128)(2,1)S(1)} all-gather(bf16[3,1,256]{2,1,0:T(2,128)(2,1)S(1)} %copy.72), channel_id=2, replica_groups=mesh['ctx'=32,'head'=4] {'ctx'}, dimensions={0}, use_global_device_ids=true | all-gather | bytes 50688 | tf_op jit(solution)/shard_map/all_gather | solution.py:113
  161.0 24.7 %all-gather.1 = bf16[96,1,2048]{2,1,0:T(2,128)(2,1)S(1)} all-gather(bf16[3,1,2048]{2,1,0:T(2,128)(2,1)S(1)} %copy.76), channel_id=3, replica_groups=mesh['ctx'=32,'head'=4] {'ctx'}, dimensions={0}, use_global_device_ids=true | all-gather | bytes 405504 | tf_op jit(solution)/shard_map/all_gather | solution.py:113
  187.1 1.8 add_select_fusion
  192.0 1.6 convolution_multiply_fusion
  (211 shorter events, 14.5 us)
Async XLA Ops:
  7.2 187.8 %reduce-scatter.2.cloned.1.call-start = ((), (), s32[]{:S(2)}) async-start(), calls=%async_computation.1 | async-start | bytes 5242880 | tf_op jit(solution)/shard_map/reduce_scatter | solution.py:162
  10.3 20.7 %copy-start.6 = (bf16[3,1,2048]{0,2,1:T(8,128)(2,1)}, bf16[3,1,2048]{0,2,1:T(8,128)(2,1)S(1)}, u32[]{:S(2)}) copy-start(bf16[3,1,2048]{0,2,1:T(8,128)(2,1)S(1)} %slice.292) | copy-start | bytes 36868
  10.3 14.6 %collective-permute-start = (bf16[3,1,2048]{0,2,1:T(8,128)(2,1)S(1)}, bf16[3,1,2048]{0,2,1:T(8,128)(2,1)S(1)}, u32[]{:S(2)}, u32[]{:S(2)}) collective-permute-start(bf16[3,1,2048]{0,2,1:T(8,128)(2,1)S(1)} %slice.292), channel_id=1, source_target_pairs={{0,4},{4,8},{8,12},{12,16},{16,20},{20,24},{24,28},{28,32},{32,36}... | collective-permute-start | bytes 36872 | tf_op jit(solution)/shard_map/ppermute | solution.py:12
  12.9 9.9 %collective-permute-start.1 = (bf16[3,1,256]{2,0,1:T(4,128)(2,1)}, bf16[3,1,256]{2,0,1:T(4,128)(2,1)}, u32[]{:S(2)}, u32[]{:S(2)}) collective-permute-start(bf16[3,1,256]{2,0,1:T(4,128)(2,1)} %slice.233), channel_id=1, source_target_pairs={{0,4},{4,8},{8,12},{12,16},{16,20},{20,24},{24,28},{28,32},{32,36}... | collective-permute-start | bytes 4616 | tf_op jit(solution)/shard_map/ppermute | solution.py:12
  31.8 4.0 %collective-permute-start.9 = (f32[1,32,64,128]{3,2,1,0:T(8,128)S(1)}, f32[1,32,64,128]{3,2,1,0:T(8,128)S(1)}, u32[]{:S(2)}, u32[]{:S(2)}) collective-permute-start(f32[1,32,64,128]{3,2,1,0:T(8,128)S(1)} %convolution_bitcast_fusion), channel_id=1, source_target_pairs={{0,4},{4,0},{8,12},{12,8},{16,20},{20,16},{24,28},{28,24},{32,36},... | collective-permute-start | bytes 3145736 | tf_op jit(solution)/shard_map/ppermute | solution.py:21
  31.9 2.6 %collective-permute-start.2 = (f32[1,32]{1,0:T(1,128)}, f32[1,32]{1,0:T(1,128)S(1)}, u32[]{:S(2)}, u32[]{:S(2)}) collective-permute-start(f32[1,32]{1,0:T(1,128)} %bitcast.70), channel_id=1, source_target_pairs={{0,4},{4,0},{8,12},{12,8},{16,20},{20,16},{24,28},{28,24},{32,36},... | collective-permute-start | bytes 392 | tf_op jit(solution)/shard_map/ppermute | solution.py:21
  36.9 15.4 %collective-permute-start.11 = (f32[1,32,32,128]{3,2,1,0:T(8,128)}, f32[1,32,32,128]{3,2,1,0:T(8,128)S(1)}, u32[]{:S(2)}, u32[]{:S(2)}) collective-permute-start(f32[1,32,32,128]{3,2,1,0:T(8,128)} %fusion.27), channel_id=1, source_target_pairs={{0,8},{4,12},{8,16},{12,20},{16,24},{20,28},{24,0},{28,4},{32,40},... | collective-permute-start | bytes 1572872 | tf_op jit(solution)/shard_map/ppermute | solution.py:21
  37.9 23.2 %collective-permute-start.10 = (f32[1,32,32,128]{3,2,1,0:T(8,128)}, f32[1,32,32,128]{3,2,1,0:T(8,128)S(1)}, u32[]{:S(2)}, u32[]{:S(2)}) collective-permute-start(f32[1,32,32,128]{3,2,1,0:T(8,128)} %fusion.27), channel_id=1, source_target_pairs={{0,24},{4,28},{8,0},{12,4},{16,8},{20,12},{24,16},{28,20},{32,56},... | collective-permute-start | bytes 1572872 | tf_op jit(solution)/shard_map/ppermute | solution.py:21
  52.3 24.6 %copy-start.1 = (f32[1,32,32,128]{3,2,1,0:T(8,128)}, f32[1,32,32,128]{3,2,1,0:T(8,128)S(1)}, u32[]{:S(2)}) copy-start(f32[1,32,32,128]{3,2,1,0:T(8,128)S(1)} %collective-permute-done.11) | copy-start | bytes 1572868
  52.3 12.2 %collective-permute-start.12 = (f32[1,32,16,128]{3,2,1,0:T(8,128)S(1)}, f32[1,32,16,128]{3,2,1,0:T(8,128)S(1)}, u32[]{:S(2)}, u32[]{:S(2)}) collective-permute-start(f32[1,32,16,128]{3,2,1,0:T(8,128)S(1)} %slice.305), channel_id=1, source_target_pairs={{0,8},{4,12},{8,16},{12,20},{16,24},{20,28},{24,0},{28,4},{32,40},... | collective-permute-start | bytes 786440 | tf_op jit(solution)/shard_map/ppermute | solution.py:21
  53.5 7.6 %collective-permute-start.4 = (f32[1,32]{1,0:T(1,128)}, f32[1,32]{1,0:T(1,128)S(1)}, u32[]{:S(2)}, u32[]{:S(2)}) collective-permute-start(f32[1,32]{1,0:T(1,128)} %get-tuple-element.59), channel_id=1, source_target_pairs={{0,8},{4,12},{8,16},{12,20},{16,24},{20,28},{24,0},{28,4},{32,40},... | collective-permute-start | bytes 392 | tf_op jit(solution)/shard_map/ppermute | solution.py:21
  54.6 9.9 %collective-permute-start.3 = (f32[1,32]{1,0:T(1,128)}, f32[1,32]{1,0:T(1,128)S(1)}, u32[]{:S(2)}, u32[]{:S(2)}) collective-permute-start(f32[1,32]{1,0:T(1,128)} %get-tuple-element.59), channel_id=1, source_target_pairs={{0,24},{4,28},{8,0},{12,4},{16,8},{20,12},{24,16},{28,20},{32,56},... | collective-permute-start | bytes 392 | tf_op jit(solution)/shard_map/ppermute | solution.py:21
  61.2 15.7 %copy-start.31 = (f32[1,32]{1,0:T(1,128)}, f32[1,32]{1,0:T(1,128)S(1)}, u32[]{:S(2)}) copy-start(f32[1,32]{1,0:T(1,128)S(1)} %collective-permute-done.4) | copy-start | bytes 388
  61.2 7.3 %collective-permute-start.5 = (f32[1,32]{1,0:T(1,128)S(1)}, f32[1,32]{1,0:T(1,128)S(1)}, u32[]{:S(2)}, u32[]{:S(2)}) collective-permute-start(f32[1,32]{1,0:T(1,128)S(1)} %collective-permute-done.4), channel_id=1, source_target_pairs={{0,8},{4,12},{8,16},{12,20},{16,24},{20,28},{24,0},{28,4},{32,40},... | collective-permute-start | bytes 392 | tf_op jit(solution)/shard_map/ppermute | solution.py:21
  61.2 7.2 %collective-permute-start.13 = (f32[1,32,16,128]{3,2,1,0:T(8,128)S(1)}, f32[1,32,16,128]{3,2,1,0:T(8,128)S(1)}, u32[]{:S(2)}, u32[]{:S(2)}) collective-permute-start(f32[1,32,16,128]{3,2,1,0:T(8,128)S(1)} %slice.306), channel_id=1, source_target_pairs={{0,24},{4,28},{8,0},{12,4},{16,8},{20,12},{24,16},{28,20},{32,56},... | collective-permute-start | bytes 786440 | tf_op jit(solution)/shard_map/ppermute | solution.py:21
  70.9 13.2 %collective-permute-start.15 = (f32[1,32,32,128]{3,2,1,0:T(8,128)}, f32[1,32,32,128]{3,2,1,0:T(8,128)}, u32[]{:S(2)}, u32[]{:S(2)}) collective-permute-start(f32[1,32,32,128]{3,2,1,0:T(8,128)} %add_select_fusion.2), channel_id=1, source_target_pairs={{0,32},{4,36},{8,40},{12,44},{16,48},{20,52},{24,56},{28,60},{32,6... | collective-permute-start | bytes 1572872 | tf_op jit(solution)/shard_map/ppermute | solution.py:21
  73.3 13.4 %collective-permute-start.14 = (f32[1,32,32,128]{3,2,1,0:T(8,128)}, f32[1,32,32,128]{3,2,1,0:T(8,128)}, u32[]{:S(2)}, u32[]{:S(2)}) collective-permute-start(f32[1,32,32,128]{3,2,1,0:T(8,128)} %add_select_fusion.2), channel_id=1, source_target_pairs={{0,96},{4,100},{8,104},{12,108},{16,112},{20,116},{24,120},{28,124... | collective-permute-start | bytes 1572872 | tf_op jit(solution)/shard_map/ppermute | solution.py:21
  76.9 6.8 %collective-permute-start.6 = (f32[1,32]{1,0:T(1,128)}, f32[1,32]{1,0:T(1,128)}, u32[]{:S(2)}, u32[]{:S(2)}) collective-permute-start(f32[1,32]{1,0:T(1,128)} %get-tuple-element.21), channel_id=1, source_target_pairs={{0,32},{4,36},{8,40},{12,44},{16,48},{20,52},{24,56},{28,60},{32,6... | collective-permute-start | bytes 392 | tf_op jit(solution)/shard_map/ppermute | solution.py:21
  80.4 17.1 %copy-start = (bf16[512,1,2048]{0,2,1:T(8,128)(2,1)S(1)}, bf16[512,1,2048]{0,2,1:T(8,128)(2,1)}, u32[]{:S(2)}) copy-start(bf16[512,1,2048]{0,2,1:T(8,128)(2,1)} %get-tuple-element.24) | copy-start | bytes 6291460
  80.4 17.1 %copy-start.10 = (pred[512,512]{1,0:T(8,128)(4,1)S(1)}, pred[512,512]{1,0:T(8,128)(4,1)}, u32[]{:S(2)}) copy-start(pred[512,512]{1,0:T(8,128)(4,1)} %iota_compare_fusion) | copy-start | bytes 786436
  80.4 17.1 %copy-start.17 = (f32[32,512]{1,0:T(8,128)S(1)}, f32[32,512]{1,0:T(8,128)}, u32[]{:S(2)}) copy-start(f32[32,512]{1,0:T(8,128)} %get-tuple-element.37) | copy-start | bytes 196612
  80.4 17.1 %copy-start.18 = (f32[32,512]{1,0:T(8,128)S(1)}, f32[32,512]{1,0:T(8,128)}, u32[]{:S(2)}) copy-start(f32[32,512]{1,0:T(8,128)} %bitcast_add_fusion) | copy-start | bytes 196612
  80.4 6.3 %collective-permute-start.8 = (f32[1,32]{1,0:T(1,128)}, f32[1,32]{1,0:T(1,128)S(1)}, u32[]{:S(2)}, u32[]{:S(2)}) collective-permute-start(f32[1,32]{1,0:T(1,128)} %get-tuple-element.21), channel_id=1, source_target_pairs={{0,96},{4,100},{8,104},{12,108},{16,112},{20,116},{24,120},{28,124... | collective-permute-start | bytes 392 | tf_op jit(solution)/shard_map/ppermute | solution.py:21
  83.7 11.2 %collective-permute-start.7 = (f32[1,32]{1,0:T(1,128)}, f32[1,32]{1,0:T(1,128)S(1)}, u32[]{:S(2)}, u32[]{:S(2)}) collective-permute-start(f32[1,32]{1,0:T(1,128)} %collective-permute-done.6), channel_id=1, source_target_pairs={{0,32},{4,36},{8,40},{12,44},{16,48},{20,52},{24,56},{28,60},{32,6... | collective-permute-start | bytes 392 | tf_op jit(solution)/shard_map/ppermute | solution.py:21
  85.1 7.7 %collective-permute-start.16 = (f32[1,32,16,128]{3,2,1,0:T(8,128)S(1)}, f32[1,32,16,128]{3,2,1,0:T(8,128)S(1)}, u32[]{:S(2)}, u32[]{:S(2)}) collective-permute-start(f32[1,32,16,128]{3,2,1,0:T(8,128)S(1)} %slice.307), channel_id=1, source_target_pairs={{0,32},{4,36},{8,40},{12,44},{16,48},{20,52},{24,56},{28,60},{32,6... | collective-permute-start | bytes 786440 | tf_op jit(solution)/shard_map/ppermute | solution.py:21
  86.7 20.3 %copy-start.37 = (f32[32]{0:T(128)}, f32[32]{0:T(128)S(1)}, u32[]{:S(2)}) copy-start(f32[32]{0:T(128)S(1)} %multiply_bitcast_fusion.1) | copy-start | bytes 388
  88.2 6.6 %collective-permute-start.17 = (f32[1,32,16,128]{3,2,1,0:T(8,128)S(1)}, f32[1,32,16,128]{3,2,1,0:T(8,128)S(1)}, u32[]{:S(2)}, u32[]{:S(2)}) collective-permute-start(f32[1,32,16,128]{3,2,1,0:T(8,128)S(1)} %slice.308), channel_id=1, source_target_pairs={{0,96},{4,100},{8,104},{12,108},{16,112},{20,116},{24,120},{28,124... | collective-permute-start | bytes 786440 | tf_op jit(solution)/shard_map/ppermute | solution.py:21
  97.4 9.6 %collective-permute-start.18 = (f32[1,32,32,128]{3,2,1,0:T(8,128)S(1)}, f32[1,32,32,128]{3,2,1,0:T(8,128)S(1)}, u32[]{:S(2)}, u32[]{:S(2)}) collective-permute-start(f32[1,32,32,128]{3,2,1,0:T(8,128)S(1)} %multiply_add_fusion), channel_id=1, source_target_pairs={{0,4},{4,0},{8,12},{12,8},{16,20},{20,16},{24,28},{28,24},{32,36},... | collective-permute-start | bytes 1572872 | tf_op jit(solution)/shard_map/ppermute | solution.py:21
  110.8 6.6 %collective-permute-start.19 = (f32[512,1]{0,1:T(1,128)S(1)}, f32[512,1]{0,1:T(1,128)S(1)}, u32[]{:S(2)}, u32[]{:S(2)}) collective-permute-start(f32[512,1]{0,1:T(1,128)S(1)} %bitcast.234), channel_id=1, source_target_pairs={{0,1},{1,2},{2,3},{3,0},{4,5},{5,6},{6,7},{7,4},{8,9},{9,10},{10,1... | collective-permute-start | bytes 6152 | tf_op jit(solution)/shard_map/ppermute | solution.py:21
  112.8 5.2 %collective-permute-start.20 = (f32[512,1]{0,1:T(1,128)S(1)}, f32[512,1]{0,1:T(1,128)S(1)}, u32[]{:S(2)}, u32[]{:S(2)}) collective-permute-start(f32[512,1]{0,1:T(1,128)S(1)} %bitcast.235), channel_id=1, source_target_pairs={{0,2},{1,3},{2,0},{3,1},{4,6},{5,7},{6,4},{7,5},{8,10},{9,11},{10,... | collective-permute-start | bytes 6152 | tf_op jit(solution)/shard_map/ppermute | solution.py:21
  116.4 3.6 %collective-permute-start.21 = (f32[512,1]{0,1:T(1,128)S(1)}, f32[512,1]{0,1:T(1,128)S(1)}, u32[]{:S(2)}, u32[]{:S(2)}) collective-permute-start(f32[512,1]{0,1:T(1,128)S(1)} %bitcast.236), channel_id=1, source_target_pairs={{0,3},{1,0},{2,1},{3,2},{4,7},{5,4},{6,5},{7,6},{8,11},{9,8},{10,9... | collective-permute-start | bytes 6152 | tf_op jit(solution)/shard_map/ppermute | solution.py:21
  134.6 51.1 %copy-start.47 = (s32[8]{0:T(128)S(1)}, s32[8]{0:T(128)}, u32[]{:S(2)}) copy-start(s32[8]{0:T(128)} %param.27) | copy-start | bytes 100
  134.6 51.2 %copy-start.12 = (bf16[4,8,2048]{2,1,0:T(8,128)(2,1)S(1)}, bf16[4,8,2048]{2,1,0:T(8,128)(2,1)}, u32[]{:S(2)}) copy-start(bf16[4,8,2048]{2,1,0:T(8,128)(2,1)} %param.28) | copy-start | bytes 393220
  134.6 51.2 %copy-start.14 = (f32[1,2048]{1,0:T(1,128)S(1)}, f32[1,2048]{1,0:T(1,128)}, u32[]{:S(2)}) copy-start(f32[1,2048]{1,0:T(1,128)} %copy-done.13) | copy-start | bytes 24580
  134.6 51.2 %copy-start.16 = (f32[1,2048]{1,0:T(1,128)S(1)}, f32[1,2048]{1,0:T(1,128)}, u32[]{:S(2)}) copy-start(f32[1,2048]{1,0:T(1,128)} %copy-done.15) | copy-start | bytes 24580
  134.6 51.7 %copy-start.19 = (bf16[4,8,256]{2,1,0:T(8,128)(2,1)S(1)}, bf16[4,8,256]{2,1,0:T(8,128)(2,1)}, u32[]{:S(2)}) copy-start(bf16[4,8,256]{2,1,0:T(8,128)(2,1)} %param.30) | copy-start | bytes 49156
  134.6 51.6 %copy-start.22 = (f32[1,256]{1,0:T(1,128)S(1)}, f32[1,256]{1,0:T(1,128)}, u32[]{:S(2)}) copy-start(f32[1,256]{1,0:T(1,128)} %copy-done.21) | copy-start | bytes 3076
  134.6 51.6 %copy-start.24 = (f32[1,256]{1,0:T(1,128)S(1)}, f32[1,256]{1,0:T(1,128)}, u32[]{:S(2)}) copy-start(f32[1,256]{1,0:T(1,128)} %copy-done.23) | copy-start | bytes 3076
  134.7 51.6 %copy-start.26 = (f32[1,256]{1,0:T(1,128)S(1)}, f32[1,256]{1,0:T(1,128)}, u32[]{:S(2)}) copy-start(f32[1,256]{1,0:T(1,128)} %copy-done.25) | copy-start | bytes 3076
  134.7 51.6 %copy-start.28 = (f32[1,256]{1,0:T(1,128)S(1)}, f32[1,256]{1,0:T(1,128)}, u32[]{:S(2)}) copy-start(f32[1,256]{1,0:T(1,128)} %copy-done.27) | copy-start | bytes 3076
  134.7 52.1 %copy-start.20 = (f32[4,8,32]{2,1,0:T(8,128)S(1)}, f32[4,8,32]{2,1,0:T(8,128)}, u32[]{:S(2)}) copy-start(f32[4,8,32]{2,1,0:T(8,128)} %param.31) | copy-start | bytes 12292
  134.7 52.1 %copy-start.30 = (f32[32]{0:T(128)S(1)}, f32[32]{0:T(128)}, u32[]{:S(2)}) copy-start(f32[32]{0:T(128)} %param.20) | copy-start | bytes 388
  134.7 52.1 %copy-start.34 = (f32[32]{0:T(128)S(1)}, f32[32]{0:T(128)}, u32[]{:S(2)}) copy-start(f32[32]{0:T(128)} %copy-done.33) | copy-start | bytes 388
  134.7 52.4 %copy-start.5 = (f32[1,32,32,128]{3,2,1,0:T(8,128)S(1)}, f32[1,32,32,128]{3,2,1,0:T(8,128)}, u32[]{:S(2)}) copy-start(f32[1,32,32,128]{3,2,1,0:T(8,128)} %copy-done.4) | copy-start | bytes 1572868
  134.7 52.4 %copy-start.36 = (f32[1,32]{1,0:T(1,128)S(1)}, f32[1,32]{1,0:T(1,128)}, u32[]{:S(2)}) copy-start(f32[1,32]{1,0:T(1,128)} %copy-done.35) | copy-start | bytes 388
  134.7 52.4 %copy-start.38 = (f32[32]{0:T(128)S(1)}, f32[32]{0:T(128)}, u32[]{:S(2)}) copy-start(f32[32]{0:T(128)} %copy-done.37) | copy-start | bytes 388
  134.7 52.4 %copy-start.44 = (f32[1,32]{1,0:T(1,128)S(1)}, f32[1,32]{1,0:T(1,128)}, u32[]{:S(2)}) copy-start(f32[1,32]{1,0:T(1,128)} %copy-done.43) | copy-start | bytes 388
  188.9 3.1 %collective-permute-start.22 = (f32[1,32,32,128]{3,2,1,0:T(8,128)S(1)}, f32[1,32,32,128]{3,2,1,0:T(8,128)S(1)}, u32[]{:S(2)}, u32[]{:S(2)}) collective-permute-start(f32[1,32,32,128]{3,2,1,0:T(8,128)S(1)} %add_select_fusion), channel_id=1, source_target_pairs={{0,4},{4,0},{8,12},{12,8},{16,20},{20,16},{24,28},{28,24},{32,36},... | collective-permute-start | bytes 1572872 | tf_op jit(solution)/shard_map/ppermute | solution.py:21
  (24 other events, 161.7 us)
Sparse Core Ops, SparseCore 0:
  134.9 47.7 reduce-scatter.1
where the time goes:
time: 204 us; the launch traced here: 202 us
  blocking collectives  49.6 us (24%)
  starting transfers between devices  34.5 us (17%)
  waiting for transfers between devices  29.9 us (15%)
  matrix products  29 us (14%)
  other arithmetic  27.2 us (13%)
  local copies, waits for them, and re-layouts  16.4 us (8%)
  between operations  15.2 us (7%)
    all_gather x2, blocking collectives, body(): lax.all_gather(part, 'ctx')[count - 1]  49.6 us
    ppermute x21, waiting for transfers between devices, group_shift(): return lax.ppermute(value, axis, pairs)  29.9 us
    ppermute x21, starting transfers between devices, group_shift(): return lax.ppermute(value, axis, pairs)  28.2 us
    dot_general x1, matrix products, body(): jnp.einsum('tpi,id->tpd', normed, w_out, preferred_element_type=jnp.float32)  14.6 us
    dot_general x1, matrix products, body(): jnp.einsum('phij,jphd->iphd', mixing, x_heads, preferred_element_type=jnp...  9.45 us
    unnamed x103, local copies, waits for them, and re-layouts  6.52 us
    ppermute x2, starting transfers between devices, passed_along(): lax.ppermute(value, axis, [(source, source + steps) for source in range(l...  6.18 us
    select_n x4, other arithmetic, pick(): return jax.tree.map(lambda a, b: jnp.where(flag, a, b), first, second)  5.7 us
  transfers between devices with their start and end apart: 24, of which 9 were waited for; matrix products, arithmetic and copies ran while one was open for 19% of the time, Pallas kernels for 0%

commit v1 on v0

--- a/solution.py
+++ b/solution.py
@@ -148,7 +148,8 @@
         )
         * jnp.exp(cum_log)[..., None]
     )
-    y_all = y_intra + y_inter + skip[:, None] * x_heads.astype(jnp.float32)
+    y_local = lax.optimization_barrier(y_intra + skip[:, None] * x_heads.astype(jnp.float32))
+    y_all = y_local + y_inter
     gated_out = y_all.reshape(block_len, prompts, inner_loc) * jax.nn.silu(z_in.astype(jnp.float32))
     square_local = jnp.sum(gated_out * gated_out, axis=-1)
     head_count = lax.axis_size("head")
@@ -159,15 +160,26 @@
     normed = (
         gated_out * lax.rsqrt(square_sums / inner_total + norm_eps)[..., None] * norm_gain
     ).astype(jnp.bfloat16)
-    projected = lax.psum_scatter(
-        jnp.einsum("tpi,id->tpd", normed, w_out, preferred_element_type=jnp.float32).astype(
-            jnp.bfloat16
-        ),
-        "head",
-        scatter_dimension=0,
-        tiled=True,
-    )
-    out = projected.astype(jnp.bfloat16)
+    head_count = lax.axis_size("head")
+    share = block_len // head_count
+    halves = normed.reshape(head_count, 2, share // 2, prompts, inner_loc)
+    out = jnp.concatenate(
+        [
+            lax.psum_scatter(
+                jnp.einsum(
+                    "tpi,id->tpd",
+                    halves[:, part].reshape(block_len // 2, prompts, inner_loc),
+                    w_out,
+                    preferred_element_type=jnp.float32,
+                ).astype(jnp.bfloat16),
+                "head",
+                scatter_dimension=0,
+                tiled=True,
+            )
+            for part in range(2)
+        ],
+        axis=0,
+    )
 
     final_x, final_bc = tails
     slot_count = requests.shape[0]
@@ -188,7 +200,7 @@
     x_step = new_x.reshape(steps, slot_count, heads_loc, head_dim).astype(jnp.float32)
     b_step = new_bc[..., :state_dim].astype(jnp.float32)
     c_step = new_bc[..., state_dim:].astype(jnp.float32)
-    step_decay = jnp.exp(dt_step * decay_rates)
+    step_log = jnp.cumsum(dt_step * decay_rates, axis=0)
     pushed = dt_step[..., None] * x_step
     from_final = jnp.einsum(
         "phdn,srn->psrhd", final_state.reshape(prompts, heads_loc, head_dim, state_dim), c_step,
@@ -196,24 +208,20 @@
     )
     from_final = jnp.einsum("rp,psrhd->srhd", slot_pick, from_final, precision=lax.Precision.HIGHEST)
     overlap = jnp.einsum("trn,srn->tsr", b_step, c_step, precision=lax.Precision.HIGHEST)
-    outputs = []
-    carried = jnp.ones_like(step_decay[0])
-    for step_index in range(steps):
-        carried = carried * step_decay[step_index]
-        y_step = carried[..., None] * from_final[step_index]
-        for earlier in range(step_index + 1):
-            weight = jnp.ones_like(step_decay[0])
-            for later in range(earlier + 1, step_index + 1):
-                weight = weight * step_decay[later]
-            y_step = y_step + (weight * overlap[earlier, step_index][:, None])[..., None] * pushed[
-                earlier
-            ]
-        y_step = y_step + skip[:, None] * x_step[step_index]
-        gated_step = y_step.reshape(slot_count, inner_loc) * jax.nn.silu(
-            step_z[step_index].astype(jnp.float32)
-        )
-        outputs.append(jnp.where(live_slots[:, None], gated_step, 0.0).astype(jnp.bfloat16))
-    return (out, jnp.stack(outputs))
+    order = lax.iota(jnp.int32, steps)
+    reach = (order[:, None] <= order[None, :])[..., None, None]
+    gaps = jnp.where(reach, step_log[None, :] - step_log[:, None], -jnp.inf)
+    weights = jnp.exp(gaps) * overlap[..., None]
+    y_steps = (
+        jnp.exp(step_log)[..., None] * from_final
+        + jnp.einsum("tsrh,trhd->srhd", weights, pushed, precision=lax.Precision.HIGHEST)
+        + skip[:, None] * x_step
+    )
+    gated_steps = y_steps.reshape(steps, slot_count, inner_loc) * jax.nn.silu(
+        step_z.astype(jnp.float32)
+    )
+    dec_out = jnp.where(live_slots[None, :, None], gated_steps, 0.0).astype(jnp.bfloat16)
+    return (out, dec_out)
 
 def solution(mesh):
     placed = (

time: 204 us -> 239 us (1.17)
  waiting for transfers between devices: 29.9 us -> 49.5 us
  matrix products: 29 us -> 40 us
  other arithmetic: 27.2 us -> 30.9 us
  starting transfers between devices: 34.5 us -> 36.9 us
    reduce_scatter x1 -> x2, waiting for transfers between devices: 0.01 us -> 18.9 us  [body(): lax.psum_scatter(jnp.einsum('tpi,id->tpd', halves[:, part].reshape(block_...]
    dot_general x1 -> x3, matrix products: 14.6 us -> 25.3 us  [the longest x2 23.1 us: body(): jnp.einsum('tpi,id->tpd', halves[:, part].reshape(block_len // 2, prompts...]
    convert_element_type x2, other arithmetic: 0.2 us -> 3.5 us  [the longest x1 2.74 us: body(): normed = (gated_out * lax.rsqrt(square_sums / inner_total + norm_eps)[......]
    convert_element_type x0 -> x1, local copies, waits for them, and re-layouts: none -> 2.93 us  [body(): normed = (gated_out * lax.rsqrt(square_sums / inner_total + norm_eps)[......]
    ppermute x21, starting transfers between devices: 28.2 us -> 30.9 us  [group_shift(): return lax.ppermute(value, axis, pairs)]
    unnamed x103 -> x115, local copies, waits for them, and re-layouts: 6.52 us -> 7.21 us
  transfers between devices with their start and end apart: 24 -> 25, of which waited for: 9 -> 10; matrix products, arithmetic and copies ran while one was open for 19% -> 19% of each run, Pallas kernels for 0% -> 0%
where the time goes in v1:
time: 239 us; the launch traced here: 237 us
  blocking collectives  49.6 us (21%)
  waiting for transfers between devices  49.5 us (21%)
  matrix products  40 us (17%)
  starting transfers between devices  36.9 us (15%)
  other arithmetic  30.9 us (13%)
  local copies, waits for them, and re-layouts  15.4 us (6%)
  between operations  15.3 us (6%)
    all_gather x2, blocking collectives, body(): lax.all_gather(part, 'ctx')[count - 1]  49.6 us
    ppermute x21, starting transfers between devices, group_shift(): return lax.ppermute(value, axis, pairs)  30.9 us
    ppermute x21, waiting for transfers between devices, group_shift(): return lax.ppermute(value, axis, pairs)  30.5 us
    dot_general x2, matrix products, body(): jnp.einsum('tpi,id->tpd', halves[:, part].reshape(block_len // 2, prompts...  23.1 us
    reduce_scatter x2, waiting for transfers between devices, body(): lax.psum_scatter(jnp.einsum('tpi,id->tpd', halves[:, part].reshape(block_...  18.9 us
    dot_general x1, matrix products, body(): jnp.einsum('phij,jphd->iphd', mixing, x_heads, preferred_element_type=jnp...  9.73 us
    convert_element_type x1, other arithmetic, body(): weighted_x = (x_heads * tail_weights[..., None]).astype(jnp.bfloat16)  7.37 us
    unnamed x115, local copies, waits for them, and re-layouts  7.21 us
  transfers between devices with their start and end apart: 25, of which 10 were waited for; matrix products, arithmetic and copies ran while one was open for 19% of the time, Pallas kernels for 0%

profile of v1, /device:TPU:0, one launch (start us, length us, event | category | flops | bytes accessed | tf_op | source)
XLA Modules:
  0.0 237.5 jit_solution(10546269485039885160)
XLA Ops:
  7.3 2.9 %copy.92 = bf16[512,1,2048]{0,2,1:T(8,128)(2,1)S(1)} copy(bf16[512,1,2048]{2,0,1:T(8,128)(2,1)} %param.16) | data formatting | bytes 4194304 | tf_op args[0]
  10.4 2.1 collective-permute-start
  12.5 3.6 %collective-permute-start.1 = (bf16[3,1,256]{2,0,1:T(4,128)(2,1)S(1)}, bf16[3,1,256]{2,0,1:T(4,128)(2,1)S(1)}, u32[]{:S(2)}, u32[]{:S(2)}) collective-permute-start(bf16[3,1,256]{2,0,1:T(4,128)(2,1)S(1)} %slice.129), channel_id=1, source_target_pairs={{0,4},{4,8},{8,12},{12,16},{16,20},{20,24},{24,28},{28,32},{32,36}... | collective-permute-start | bytes 4616 | tf_op jit(solution)/shard_map/ppermute | solution.py:12
  16.9 1.2 reduce-window.6
  20.2 1.1 multiply_convert_fusion.6
  21.9 7.4 %fusion.9 = (bf16[512,1,2048]{0,2,1:T(8,128)(2,1)S(1)}, bf16[512,1,2048]{0,2,1:T(8,128)(2,1)}) fusion(f32[2048]{0:T(1024)S(1)} %bitcast.174, bf16[512,1,2048]{0,2,1:T(8,128)(2,1)S(1)} %copy.92, f32[2048]{0:T(1024)S(1)} %bitcast.176, bf16[3,1,2048]{0,2,1:T(8,128)(2,1)} %collective-permute-done, f32[2048]{0:T(1024)S(1)} %bitcast.172, f32[2048]{0:T(1024)S(1)} %bitcast.170, ...), kind=kLoop, calls=%fused_computation.17 | loop fusion | flops 29360128 | bytes 10530816 | tf_op jit(solution)/shard_map/convert_element_type | solution.py:105
  30.8 2.2 collective-permute-done.2
  33.0 1.2 fusion.76
  35.4 2.8 %collective-permute-start.11 = (f32[1,32,32,128]{3,2,1,0:T(8,128)}, f32[1,32,32,128]{3,2,1,0:T(8,128)S(1)}, u32[]{:S(2)}, u32[]{:S(2)}) collective-permute-start(f32[1,32,32,128]{3,2,1,0:T(8,128)} %fusion.26), channel_id=1, source_target_pairs={{0,8},{4,12},{8,16},{12,20},{16,24},{20,28},{24,0},{28,4},{32,40},... | collective-permute-start | bytes 1572872 | tf_op jit(solution)/shard_map/ppermute | solution.py:21
  38.2 1.4 collective-permute-start.10
  39.6 12.4 %collective-permute-done.11 = f32[1,32,32,128]{3,2,1,0:T(8,128)S(1)} collective-permute-done((f32[1,32,32,128]{3,2,1,0:T(8,128)}, f32[1,32,32,128]{3,2,1,0:T(8,128)S(1)}, u32[]{:S(2)}, u32[]{:S(2)}) %collective-permute-start.11) | collective-permute-done | bytes 524320 | tf_op jit(solution)/shard_map/ppermute | solution.py:21
  52.5 0.9 exponential_bitcast_fusion
  53.5 1.6 collective-permute-start.4
  55.2 1.7 collective-permute-start.3
  56.8 4.4 %collective-permute-done.4 = f32[1,32]{1,0:T(1,128)S(1)} collective-permute-done((f32[1,32]{1,0:T(1,128)}, f32[1,32]{1,0:T(1,128)S(1)}, u32[]{:S(2)}, u32[]{:S(2)}) %collective-permute-start.4) | collective-permute-done | bytes 160 | tf_op jit(solution)/shard_map/ppermute | solution.py:21
  61.3 3.3 %collective-permute-start.13 = (f32[1,32,16,128]{3,2,1,0:T(8,128)S(1)}, f32[1,32,16,128]{3,2,1,0:T(8,128)S(1)}, u32[]{:S(2)}, u32[]{:S(2)}) collective-permute-start(f32[1,32,16,128]{3,2,1,0:T(8,128)S(1)} %slice.174), channel_id=1, source_target_pairs={{0,24},{4,28},{8,0},{12,4},{16,8},{20,12},{24,16},{28,20},{32,56},... | collective-permute-start | bytes 786440 | tf_op jit(solution)/shard_map/ppermute | solution.py:21
  64.6 4.0 %collective-permute-done.13 = f32[1,32,16,128]{3,2,1,0:T(8,128)S(1)} collective-permute-done((f32[1,32,16,128]{3,2,1,0:T(8,128)S(1)}, f32[1,32,16,128]{3,2,1,0:T(8,128)S(1)}, u32[]{:S(2)}, u32[]{:S(2)}) %collective-permute-start.13) | collective-permute-done | bytes 262176 | tf_op jit(solution)/shard_map/ppermute | solution.py:21
  68.7 2.4 %add_select_fusion.2 = f32[1,32,32,128]{3,2,1,0:T(8,128)} fusion(f32[1,32,32,128]{3,2,1,0:T(8,128)S(1)} %collective-permute-done.11, f32[1,32,32,128]{3,2,1,0:T(8,128)S(1)} %constant_dynamic-update-slice_fusion, f32[1,32,32,128]{3,2,1,0:T(8,128)S(1)} %collective-permute-done.10, f32[1,32,32,128]{3,2,1,0:T(8,128)} %fusion.26, ...), kind=kLoop, calls=%fused_computation.62 | loop fusion | flops 2490368 | bytes 2622086 | tf_op jit(solution)/shard_map/jit(_where)/select_n | solution.py:38
  71.2 3.1 %collective-permute-start.15 = (f32[1,32,32,128]{3,2,1,0:T(8,128)}, f32[1,32,32,128]{3,2,1,0:T(8,128)}, u32[]{:S(2)}, u32[]{:S(2)}) collective-permute-start(f32[1,32,32,128]{3,2,1,0:T(8,128)} %add_select_fusion.2), channel_id=1, source_target_pairs={{0,32},{4,36},{8,40},{12,44},{16,48},{20,52},{24,56},{28,60},{32,6... | collective-permute-start | bytes 1572872 | tf_op jit(solution)/shard_map/ppermute | solution.py:21
  74.9 1.3 collective-permute-start.14
  76.9 1.3 broadcast_select_fusion.3
  79.0 2.9 %copy.101 = bf16[512,1,2048]{0,2,1:T(8,128)(2,1)S(1)} copy(bf16[512,1,2048]{2,0,1:T(8,128)(2,1)} %param.17) | data formatting | bytes 4194304 | tf_op args[1]
  82.0 2.5 %collective-permute-start.8 = (f32[1,32]{1,0:T(1,128)}, f32[1,32]{1,0:T(1,128)S(1)}, u32[]{:S(2)}, u32[]{:S(2)}) collective-permute-start(f32[1,32]{1,0:T(1,128)} %get-tuple-element.4), channel_id=1, source_target_pairs={{0,96},{4,100},{8,104},{12,108},{16,112},{20,116},{24,120},{28,124... | collective-permute-start | bytes 392 | tf_op jit(solution)/shard_map/ppermute | solution.py:21
  85.6 1.0 slice.175
  86.6 1.6 collective-permute-start.16
  88.2 1.0 slice.176
  89.1 2.0 collective-permute-start.17
  91.4 2.8 %collective-permute-done.16 = f32[1,32,16,128]{3,2,1,0:T(8,128)S(1)} collective-permute-done((f32[1,32,16,128]{3,2,1,0:T(8,128)S(1)}, f32[1,32,16,128]{3,2,1,0:T(8,128)S(1)}, u32[]{:S(2)}, u32[]{:S(2)}) %collective-permute-start.16) | collective-permute-done | bytes 262176 | tf_op jit(solution)/shard_map/ppermute | solution.py:21
  94.3 1.5 collective-permute-done.17
  96.4 2.3 multiply_add_fusion
  98.9 9.7 %bitcast_add_fusion = f32[512,1,32,64]{0,3,2,1:T(8,128)S(1)} fusion(bf16[512,32,64]{0,2,1:T(8,128)(2,1)S(1)} %bitcast.157, f32[32,512]{1,0:T(8,128)S(1)} %copy-done.18, f32[32,512]{1,0:T(8,128)S(1)} %copy-done.19, f32[512,512]{1,0:T(8,128)S(1)} %fusion.53, pred[512,512]{1,0:T(8,128)(4,1)S(1)} %copy-done.11, f32[32]{0:T(128)S(1)} %copy-done.52, ...), kind=kOutput, calls=%fused_computation.15 | convolution fusion | flops 1118830592 | bytes 9830528 | tf_op jit(solution)/shard_map/phij,jphd->iphd/dot_general | solution.py:144
  108.7 2.0 fusion.8
  110.7 1.4 multiply_reduce_fusion
  112.0 2.0 collective-permute-start.19
  114.0 3.6 %collective-permute-start.20 = (f32[512,1]{0,1:T(1,128)S(1)}, f32[512,1]{0,1:T(1,128)S(1)}, u32[]{:S(2)}, u32[]{:S(2)}) collective-permute-start(f32[512,1]{0,1:T(1,128)S(1)} %bitcast.188), channel_id=1, source_target_pairs={{0,2},{1,3},{2,0},{3,1},{4,6},{5,7},{6,4},{7,5},{8,10},{9,11},{10,... | collective-permute-start | bytes 6152 | tf_op jit(solution)/shard_map/ppermute | solution.py:21
  117.6 1.0 collective-permute-start.21
  119.2 2.0 collective-permute-done.21
  121.2 2.7 %multiply_convert_fusion.2 = bf16[512,1,2048]{0,2,1:T(8,128)(2,1)} fusion(f32[2048]{0:T(1024)S(1)} %copy-done.34, f32[512]{0:T(512)S(1)} %bitcast.192, bf16[512,1,2048]{0,2,1:T(8,128)(2,1)S(1)} %copy.101, f32[512,1,32,64]{0,3,2,1:T(8,128)S(1)} %fusion.8), kind=kLoop, calls=%fused_computation.18 | loop fusion | flops 9437184 | bytes 8398848 | tf_op jit(solution)/shard_map/convert_element_type | solution.py:162
  124.0 2.9 %copy.102 = bf16[512,1,2048]{2,0,1:T(8,128)(2,1)S(1)} copy(bf16[512,1,2048]{0,2,1:T(8,128)(2,1)} %multiply_convert_fusion.2) | data formatting | bytes 4194304 | tf_op jit(solution)/shard_map/convert_element_type | solution.py:162
  127.1 11.5 %fusion.2 = bf16[256,1,4096]{2,0,1:T(8,128)(2,1)} fusion(bf16[256,2048]{1,0:T(8,128)(2,1)S(1)} %bitcast.162, bf16[2048,4096]{1,0:T(8,128)(2,1)} %param.26), kind=kOutput, calls=%fused_computation.7 | convolution fusion | flops 4296015872 | bytes 19922944 | tf_op jit(solution)/shard_map/tpi,id->tpd/dot_general | solution.py:169
  139.4 24.9 %all-gather = bf16[96,1,256]{2,1,0:T(2,128)(2,1)S(1)} all-gather(bf16[3,1,256]{2,1,0:T(2,128)(2,1)S(1)} %copy.104), channel_id=2, replica_groups=mesh['ctx'=32,'head'=4] {'ctx'}, dimensions={0}, use_global_device_ids=true | all-gather | bytes 50688 | tf_op jit(solution)/shard_map/all_gather | solution.py:113
  164.3 24.7 %all-gather.1 = bf16[96,1,2048]{2,1,0:T(2,128)(2,1)S(1)} all-gather(bf16[3,1,2048]{2,1,0:T(2,128)(2,1)S(1)} %copy.105), channel_id=3, replica_groups=mesh['ctx'=32,'head'=4] {'ctx'}, dimensions={0}, use_global_device_ids=true | all-gather | bytes 405504 | tf_op jit(solution)/shard_map/all_gather | solution.py:113
  189.2 11.6 %fusion.3 = bf16[256,1,4096]{2,0,1:T(8,128)(2,1)} fusion(bf16[256,2048]{1,0:T(8,128)(2,1)S(1)} %bitcast.161, bf16[2048,4096]{1,0:T(8,128)(2,1)} %param.26), kind=kOutput, calls=%fused_computation.8 | convolution fusion | flops 4296015872 | bytes 19922944 | tf_op jit(solution)/shard_map/tpi,id->tpd/dot_general | solution.py:169
  201.5 1.8 add_select_fusion
  204.4 2.2 fusion.27
  206.6 1.9 fusion.14
  209.5 18.9 %reduce-scatter.5.cloned.1.call-done = bf16[64,1,4096]{2,0,1:T(8,128)(2,1)} async-done(((bf16[256,1,4096]{2,0,1:T(8,128)(2,1)}), bf16[64,1,4096]{2,0,1:T(8,128)(2,1)}) %reduce-scatter.5.cloned.1.call-update) | async-done | bytes 524304 | tf_op jit(solution)/shard_map/reduce_scatter | solution.py:168
  228.4 2.3 pad_maximum_fusion.1
  (196 shorter events, 15.3 us)
Async XLA Ops:
  7.2 12.3 %copy-start.20 = (bf16[4,2048]{1,0:T(4,128)(2,1)S(1)}, bf16[4,2048]{1,0:T(4,128)(2,1)}, u32[]{:S(2)}) copy-start(bf16[4,2048]{1,0:T(4,128)(2,1)} %param.23) | copy-start | bytes 49156
  7.2 12.3 %copy-start.31 = (bf16[4,256]{1,0:T(4,128)(2,1)S(1)}, bf16[4,256]{1,0:T(4,128)(2,1)}, u32[]{:S(2)}) copy-start(bf16[4,256]{1,0:T(4,128)(2,1)} %param.24) | copy-start | bytes 6148
  7.2 202.3 %reduce-scatter.3.cloned.1.call-start = ((), (), s32[]{:S(2)}) async-start(), calls=%async_computation.2 | async-start | bytes 2621440 | tf_op jit(solution)/shard_map/reduce_scatter | solution.py:168
  10.4 18.8 %copy-start.5 = (bf16[3,1,2048]{0,2,1:T(8,128)(2,1)}, bf16[3,1,2048]{0,2,1:T(8,128)(2,1)S(1)}, u32[]{:S(2)}) copy-start(bf16[3,1,2048]{0,2,1:T(8,128)(2,1)S(1)} %slice.160) | copy-start | bytes 36868
  10.4 10.9 %collective-permute-start = (bf16[3,1,2048]{0,2,1:T(8,128)(2,1)S(1)}, bf16[3,1,2048]{0,2,1:T(8,128)(2,1)}, u32[]{:S(2)}, u32[]{:S(2)}) collective-permute-start(bf16[3,1,2048]{0,2,1:T(8,128)(2,1)S(1)} %slice.160), channel_id=1, source_target_pairs={{0,4},{4,8},{8,12},{12,16},{16,20},{20,24},{24,28},{28,32},{32,36}... | collective-permute-start | bytes 36872 | tf_op jit(solution)/shard_map/ppermute | solution.py:12
  12.5 7.1 %collective-permute-start.1 = (bf16[3,1,256]{2,0,1:T(4,128)(2,1)S(1)}, bf16[3,1,256]{2,0,1:T(4,128)(2,1)S(1)}, u32[]{:S(2)}, u32[]{:S(2)}) collective-permute-start(bf16[3,1,256]{2,0,1:T(4,128)(2,1)S(1)} %slice.129), channel_id=1, source_target_pairs={{0,4},{4,8},{8,12},{12,16},{16,20},{20,24},{24,28},{28,32},{32,36}... | collective-permute-start | bytes 4616 | tf_op jit(solution)/shard_map/ppermute | solution.py:12
  30.0 4.3 %collective-permute-start.9 = (f32[1,32,64,128]{3,2,1,0:T(8,128)S(1)}, f32[1,32,64,128]{3,2,1,0:T(8,128)S(1)}, u32[]{:S(2)}, u32[]{:S(2)}) collective-permute-start(f32[1,32,64,128]{3,2,1,0:T(8,128)S(1)} %convolution_bitcast_fusion), channel_id=1, source_target_pairs={{0,4},{4,0},{8,12},{12,8},{16,20},{20,16},{24,28},{28,24},{32,36},... | collective-permute-start | bytes 3145736 | tf_op jit(solution)/shard_map/ppermute | solution.py:21
  30.7 2.3 collective-permute-start.2
  35.4 16.7 %collective-permute-start.11 = (f32[1,32,32,128]{3,2,1,0:T(8,128)}, f32[1,32,32,128]{3,2,1,0:T(8,128)S(1)}, u32[]{:S(2)}, u32[]{:S(2)}) collective-permute-start(f32[1,32,32,128]{3,2,1,0:T(8,128)} %fusion.26), channel_id=1, source_target_pairs={{0,8},{4,12},{8,16},{12,20},{16,24},{20,28},{24,0},{28,4},{32,40},... | collective-permute-start | bytes 1572872 | tf_op jit(solution)/shard_map/ppermute | solution.py:21
  38.2 23.1 %collective-permute-start.10 = (f32[1,32,32,128]{3,2,1,0:T(8,128)}, f32[1,32,32,128]{3,2,1,0:T(8,128)S(1)}, u32[]{:S(2)}, u32[]{:S(2)}) collective-permute-start(f32[1,32,32,128]{3,2,1,0:T(8,128)} %fusion.26), channel_id=1, source_target_pairs={{0,24},{4,28},{8,0},{12,4},{16,8},{20,12},{24,16},{28,20},{32,56},... | collective-permute-start | bytes 1572872 | tf_op jit(solution)/shard_map/ppermute | solution.py:21
  52.1 26.1 %copy-start = (f32[1,32,32,128]{3,2,1,0:T(8,128)}, f32[1,32,32,128]{3,2,1,0:T(8,128)S(1)}, u32[]{:S(2)}) copy-start(f32[1,32,32,128]{3,2,1,0:T(8,128)S(1)} %collective-permute-done.11) | copy-start | bytes 1572868
  52.1 12.5 %collective-permute-start.12 = (f32[1,32,16,128]{3,2,1,0:T(8,128)S(1)}, f32[1,32,16,128]{3,2,1,0:T(8,128)S(1)}, u32[]{:S(2)}, u32[]{:S(2)}) collective-permute-start(f32[1,32,16,128]{3,2,1,0:T(8,128)S(1)} %slice.173), channel_id=1, source_target_pairs={{0,8},{4,12},{8,16},{12,20},{16,24},{20,28},{24,0},{28,4},{32,40},... | collective-permute-start | bytes 786440 | tf_op jit(solution)/shard_map/ppermute | solution.py:21
  53.5 7.7 %collective-permute-start.4 = (f32[1,32]{1,0:T(1,128)}, f32[1,32]{1,0:T(1,128)S(1)}, u32[]{:S(2)}, u32[]{:S(2)}) collective-permute-start(f32[1,32]{1,0:T(1,128)} %get-tuple-element.24), channel_id=1, source_target_pairs={{0,8},{4,12},{8,16},{12,20},{16,24},{20,28},{24,0},{28,4},{32,40},... | collective-permute-start | bytes 392 | tf_op jit(solution)/shard_map/ppermute | solution.py:21
  55.2 9.4 %collective-permute-start.3 = (f32[1,32]{1,0:T(1,128)}, f32[1,32]{1,0:T(1,128)S(1)}, u32[]{:S(2)}, u32[]{:S(2)}) collective-permute-start(f32[1,32]{1,0:T(1,128)} %get-tuple-element.24), channel_id=1, source_target_pairs={{0,24},{4,28},{8,0},{12,4},{16,8},{20,12},{24,16},{28,20},{32,56},... | collective-permute-start | bytes 392 | tf_op jit(solution)/shard_map/ppermute | solution.py:21
  61.2 16.9 %copy-start.37 = (f32[1,32]{1,0:T(1,128)}, f32[1,32]{1,0:T(1,128)S(1)}, u32[]{:S(2)}) copy-start(f32[1,32]{1,0:T(1,128)S(1)} %collective-permute-done.4) | copy-start | bytes 388
  61.2 7.4 %collective-permute-start.5 = (f32[1,32]{1,0:T(1,128)S(1)}, f32[1,32]{1,0:T(1,128)S(1)}, u32[]{:S(2)}, u32[]{:S(2)}) collective-permute-start(f32[1,32]{1,0:T(1,128)S(1)} %collective-permute-done.4), channel_id=1, source_target_pairs={{0,8},{4,12},{8,16},{12,20},{16,24},{20,28},{24,0},{28,4},{32,40},... | collective-permute-start | bytes 392 | tf_op jit(solution)/shard_map/ppermute | solution.py:21
  61.3 16.9 %copy-start.1 = (f32[1,32,32,128]{3,2,1,0:T(8,128)}, f32[1,32,32,128]{3,2,1,0:T(8,128)S(1)}, u32[]{:S(2)}) copy-start(f32[1,32,32,128]{3,2,1,0:T(8,128)S(1)} %collective-permute-done.10) | copy-start | bytes 1572868
  61.3 7.4 %collective-permute-start.13 = (f32[1,32,16,128]{3,2,1,0:T(8,128)S(1)}, f32[1,32,16,128]{3,2,1,0:T(8,128)S(1)}, u32[]{:S(2)}, u32[]{:S(2)}) collective-permute-start(f32[1,32,16,128]{3,2,1,0:T(8,128)S(1)} %slice.174), channel_id=1, source_target_pairs={{0,24},{4,28},{8,0},{12,4},{16,8},{20,12},{24,16},{28,20},{32,56},... | collective-permute-start | bytes 786440 | tf_op jit(solution)/shard_map/ppermute | solution.py:21
  64.6 13.6 %copy-start.47 = (f32[32]{0:T(128)}, f32[32]{0:T(128)S(1)}, u32[]{:S(2)}) copy-start(f32[32]{0:T(128)S(1)} %broadcast_multiply_fusion.1) | copy-start | bytes 388
  71.2 14.4 %collective-permute-start.15 = (f32[1,32,32,128]{3,2,1,0:T(8,128)}, f32[1,32,32,128]{3,2,1,0:T(8,128)}, u32[]{:S(2)}, u32[]{:S(2)}) collective-permute-start(f32[1,32,32,128]{3,2,1,0:T(8,128)} %add_select_fusion.2), channel_id=1, source_target_pairs={{0,32},{4,36},{8,40},{12,44},{16,48},{20,52},{24,56},{28,60},{32,6... | collective-permute-start | bytes 1572872 | tf_op jit(solution)/shard_map/ppermute | solution.py:21
  74.9 13.3 %collective-permute-start.14 = (f32[1,32,32,128]{3,2,1,0:T(8,128)}, f32[1,32,32,128]{3,2,1,0:T(8,128)}, u32[]{:S(2)}, u32[]{:S(2)}) collective-permute-start(f32[1,32,32,128]{3,2,1,0:T(8,128)} %add_select_fusion.2), channel_id=1, source_target_pairs={{0,96},{4,100},{8,104},{12,108},{16,112},{20,116},{24,120},{28,124... | collective-permute-start | bytes 1572872 | tf_op jit(solution)/shard_map/ppermute | solution.py:21
  78.2 6.9 %collective-permute-start.6 = (f32[1,32]{1,0:T(1,128)}, f32[1,32]{1,0:T(1,128)}, u32[]{:S(2)}, u32[]{:S(2)}) collective-permute-start(f32[1,32]{1,0:T(1,128)} %get-tuple-element.4), channel_id=1, source_target_pairs={{0,32},{4,36},{8,40},{12,44},{16,48},{20,52},{24,56},{28,60},{32,6... | collective-permute-start | bytes 392 | tf_op jit(solution)/shard_map/ppermute | solution.py:21
  81.9 16.9 %copy-start.7 = (bf16[512,1,2048]{0,2,1:T(8,128)(2,1)S(1)}, bf16[512,1,2048]{0,2,1:T(8,128)(2,1)}, u32[]{:S(2)}) copy-start(bf16[512,1,2048]{0,2,1:T(8,128)(2,1)} %get-tuple-element.7) | copy-start | bytes 6291460
  81.9 16.9 %copy-start.11 = (pred[512,512]{1,0:T(8,128)(4,1)S(1)}, pred[512,512]{1,0:T(8,128)(4,1)}, u32[]{:S(2)}) copy-start(pred[512,512]{1,0:T(8,128)(4,1)} %iota_compare_fusion) | copy-start | bytes 786436
  81.9 16.9 %copy-start.18 = (f32[32,512]{1,0:T(8,128)S(1)}, f32[32,512]{1,0:T(8,128)}, u32[]{:S(2)}) copy-start(f32[32,512]{1,0:T(8,128)} %get-tuple-element.10) | copy-start | bytes 196612
  81.9 16.9 %copy-start.19 = (f32[32,512]{1,0:T(8,128)S(1)}, f32[32,512]{1,0:T(8,128)}, u32[]{:S(2)}) copy-start(f32[32,512]{1,0:T(8,128)} %bitcast_add_fusion.1) | copy-start | bytes 196612
  82.0 16.9 %copy-start.52 = (f32[32]{0:T(128)S(1)}, f32[32]{0:T(128)}, u32[]{:S(2)}) copy-start(f32[32]{0:T(128)} %param.22) | copy-start | bytes 388
  82.0 6.2 %collective-permute-start.8 = (f32[1,32]{1,0:T(1,128)}, f32[1,32]{1,0:T(1,128)S(1)}, u32[]{:S(2)}, u32[]{:S(2)}) collective-permute-start(f32[1,32]{1,0:T(1,128)} %get-tuple-element.4), channel_id=1, source_target_pairs={{0,96},{4,100},{8,104},{12,108},{16,112},{20,116},{24,120},{28,124... | collective-permute-start | bytes 392 | tf_op jit(solution)/shard_map/ppermute | solution.py:21
  85.1 10.7 %collective-permute-start.7 = (f32[1,32]{1,0:T(1,128)}, f32[1,32]{1,0:T(1,128)S(1)}, u32[]{:S(2)}, u32[]{:S(2)}) collective-permute-start(f32[1,32]{1,0:T(1,128)} %collective-permute-done.6), channel_id=1, source_target_pairs={{0,32},{4,36},{8,40},{12,44},{16,48},{20,52},{24,56},{28,60},{32,6... | collective-permute-start | bytes 392 | tf_op jit(solution)/shard_map/ppermute | solution.py:21
  86.6 7.7 %collective-permute-start.16 = (f32[1,32,16,128]{3,2,1,0:T(8,128)S(1)}, f32[1,32,16,128]{3,2,1,0:T(8,128)S(1)}, u32[]{:S(2)}, u32[]{:S(2)}) collective-permute-start(f32[1,32,16,128]{3,2,1,0:T(8,128)S(1)} %slice.175), channel_id=1, source_target_pairs={{0,32},{4,36},{8,40},{12,44},{16,48},{20,52},{24,56},{28,60},{32,6... | collective-permute-start | bytes 786440 | tf_op jit(solution)/shard_map/ppermute | solution.py:21
  89.1 6.6 %collective-permute-start.17 = (f32[1,32,16,128]{3,2,1,0:T(8,128)S(1)}, f32[1,32,16,128]{3,2,1,0:T(8,128)S(1)}, u32[]{:S(2)}, u32[]{:S(2)}) collective-permute-start(f32[1,32,16,128]{3,2,1,0:T(8,128)S(1)} %slice.176), channel_id=1, source_target_pairs={{0,96},{4,100},{8,104},{12,108},{16,112},{20,116},{24,120},{28,124... | collective-permute-start | bytes 786440 | tf_op jit(solution)/shard_map/ppermute | solution.py:21
  98.7 9.9 %collective-permute-start.18 = (f32[1,32,32,128]{3,2,1,0:T(8,128)S(1)}, f32[1,32,32,128]{3,2,1,0:T(8,128)S(1)}, u32[]{:S(2)}, u32[]{:S(2)}) collective-permute-start(f32[1,32,32,128]{3,2,1,0:T(8,128)S(1)} %multiply_add_fusion), channel_id=1, source_target_pairs={{0,4},{4,0},{8,12},{12,8},{16,20},{20,16},{24,28},{28,24},{32,36},... | collective-permute-start | bytes 1572872 | tf_op jit(solution)/shard_map/ppermute | solution.py:21
  112.0 6.6 %collective-permute-start.19 = (f32[512,1]{0,1:T(1,128)S(1)}, f32[512,1]{0,1:T(1,128)S(1)}, u32[]{:S(2)}, u32[]{:S(2)}) collective-permute-start(f32[512,1]{0,1:T(1,128)S(1)} %bitcast.187), channel_id=1, source_target_pairs={{0,1},{1,2},{2,3},{3,0},{4,5},{5,6},{6,7},{7,4},{8,9},{9,10},{10,1... | collective-permute-start | bytes 6152 | tf_op jit(solution)/shard_map/ppermute | solution.py:21
  114.0 5.2 %collective-permute-start.20 = (f32[512,1]{0,1:T(1,128)S(1)}, f32[512,1]{0,1:T(1,128)S(1)}, u32[]{:S(2)}, u32[]{:S(2)}) collective-permute-start(f32[512,1]{0,1:T(1,128)S(1)} %bitcast.188), channel_id=1, source_target_pairs={{0,2},{1,3},{2,0},{3,1},{4,6},{5,7},{6,4},{7,5},{8,10},{9,11},{10,... | collective-permute-start | bytes 6152 | tf_op jit(solution)/shard_map/ppermute | solution.py:21
  117.6 3.6 %collective-permute-start.21 = (f32[512,1]{0,1:T(1,128)S(1)}, f32[512,1]{0,1:T(1,128)S(1)}, u32[]{:S(2)}, u32[]{:S(2)}) collective-permute-start(f32[512,1]{0,1:T(1,128)S(1)} %bitcast.189), channel_id=1, source_target_pairs={{0,3},{1,0},{2,1},{3,2},{4,7},{5,4},{6,5},{7,6},{8,11},{9,8},{10,9... | collective-permute-start | bytes 6152 | tf_op jit(solution)/shard_map/ppermute | solution.py:21
  138.7 89.7 %reduce-scatter.5.cloned.1.call-start = ((), (), s32[]{:S(2)}) async-start(), calls=%async_computation.3 | async-start | bytes 2621440 | tf_op jit(solution)/shard_map/reduce_scatter | solution.py:168
  189.0 11.9 %copy-start.21 = (bf16[4,8,256]{2,1,0:T(8,128)(2,1)S(1)}, bf16[4,8,256]{2,1,0:T(8,128)(2,1)}, u32[]{:S(2)}) copy-start(bf16[4,8,256]{2,1,0:T(8,128)(2,1)} %param.30) | copy-start | bytes 49156
  189.0 11.9 %copy-start.22 = (f32[4,8,32]{2,1,0:T(8,128)S(1)}, f32[4,8,32]{2,1,0:T(8,128)}, u32[]{:S(2)}) copy-start(f32[4,8,32]{2,1,0:T(8,128)} %param.31) | copy-start | bytes 12292
  189.1 11.9 %copy-start.36 = (f32[32]{0:T(128)S(1)}, f32[32]{0:T(128)}, u32[]{:S(2)}) copy-start(f32[32]{0:T(128)} %param.20) | copy-start | bytes 388
  189.1 12.0 %copy-start.41 = (f32[32]{0:T(128)S(1)}, f32[32]{0:T(128)}, u32[]{:S(2)}) copy-start(f32[32]{0:T(128)} %copy-done.40) | copy-start | bytes 388
  189.1 12.2 %copy-start.13 = (bf16[4,8,2048]{2,1,0:T(8,128)(2,1)S(1)}, bf16[4,8,2048]{2,1,0:T(8,128)(2,1)}, u32[]{:S(2)}) copy-start(bf16[4,8,2048]{2,1,0:T(8,128)(2,1)} %param.28) | copy-start | bytes 393220
  189.1 12.2 %copy-start.15 = (f32[1,2048]{1,0:T(1,128)S(1)}, f32[1,2048]{1,0:T(1,128)}, u32[]{:S(2)}) copy-start(f32[1,2048]{1,0:T(1,128)} %copy-done.14) | copy-start | bytes 24580
  189.1 12.2 %copy-start.17 = (f32[1,2048]{1,0:T(1,128)S(1)}, f32[1,2048]{1,0:T(1,128)}, u32[]{:S(2)}) copy-start(f32[1,2048]{1,0:T(1,128)} %copy-done.16) | copy-start | bytes 24580
  189.1 12.3 %copy-start.4 = (f32[1,32,32,128]{3,2,1,0:T(8,128)S(1)}, f32[1,32,32,128]{3,2,1,0:T(8,128)}, u32[]{:S(2)}) copy-start(f32[1,32,32,128]{3,2,1,0:T(8,128)} %copy-done.3) | copy-start | bytes 1572868
  189.1 12.3 %copy-start.44 = (f32[1,32]{1,0:T(1,128)S(1)}, f32[1,32]{1,0:T(1,128)}, u32[]{:S(2)}) copy-start(f32[1,32]{1,0:T(1,128)} %copy-done.43) | copy-start | bytes 388
  189.1 12.3 %copy-start.46 = (f32[32]{0:T(128)S(1)}, f32[32]{0:T(128)}, u32[]{:S(2)}) copy-start(f32[32]{0:T(128)} %copy-done.45) | copy-start | bytes 388
  189.1 12.3 %copy-start.49 = (f32[1,32]{1,0:T(1,128)S(1)}, f32[1,32]{1,0:T(1,128)}, u32[]{:S(2)}) copy-start(f32[1,32]{1,0:T(1,128)} %copy-done.48) | copy-start | bytes 388
  203.3 3.3 %collective-permute-start.22 = (f32[1,32,32,128]{3,2,1,0:T(8,128)S(1)}, f32[1,32,32,128]{3,2,1,0:T(8,128)S(1)}, u32[]{:S(2)}, u32[]{:S(2)}) collective-permute-start(f32[1,32,32,128]{3,2,1,0:T(8,128)S(1)} %add_select_fusion), channel_id=1, source_target_pairs={{0,4},{4,0},{8,12},{12,8},{16,20},{20,16},{24,28},{28,24},{32,36},... | collective-permute-start | bytes 1572872 | tf_op jit(solution)/shard_map/ppermute | solution.py:21
  (31 other events, 261.7 us)
Sparse Core Ops, SparseCore 0:
  138.8 30.6 reduce-scatter.2
  200.9 27.4 reduce-scatter.4

commit v2 on v0

--- a/solution.py
+++ b/solution.py
@@ -109,10 +109,17 @@
     count = lax.axis_size("ctx")
     here = lax.axis_index("ctx")
     core = here % 2
-    tails = jax.tree.map(
-        lambda part: lax.all_gather(part, "ctx")[count - 1],
-        (x_in[block_len - conv_taps + 1 :], bc_in[block_len - conv_taps + 1 :]),
-    )
+    tails = (x_in[block_len - conv_taps + 1 :], bc_in[block_len - conv_taps + 1 :])
+    reach = count // 2
+    while reach >= 1:
+        sent = lax.ppermute(
+            tails,
+            "ctx",
+            [(source, source - reach) for source in range(count) if source % (2 * reach) == 2 * reach - 1],
+        )
+        taking = here % (2 * reach) == reach - 1
+        tails = pick(taking, sent, tails)
+        reach //= 2
     own = (block_decay, s_local)
     other = group_shift(own, "ctx", count, 1, 2, 1)
     first = pick(core == 0, own, other)

time: 204 us -> 205 us (level)
  blocking collectives: 49.6 us -> 0 us
  waiting for transfers between devices: 29.9 us -> 57.3 us
  starting transfers between devices: 34.5 us -> 47.5 us
  other arithmetic: 27.2 us -> 33 us
  local copies, waits for them, and re-layouts: 16.4 us -> 20.9 us
    all_gather x2 -> x0, blocking collectives: 49.6 us -> none  [body(): lax.all_gather(part, 'ctx')[count - 1]]
    ppermute x0 -> x10, waiting for transfers between devices: none -> 26.7 us  [body(): lax.ppermute(tails, 'ctx', [(source, source - reach) for source in range(...]
    ppermute x0 -> x10, starting transfers between devices: none -> 9.69 us  [body(): lax.ppermute(tails, 'ctx', [(source, source - reach) for source in range(...]
    ppermute x21, starting transfers between devices: 28.2 us -> 31.6 us  [group_shift(): return lax.ppermute(value, axis, pairs)]
    mul x12, local copies, waits for them, and re-layouts: 1.12 us -> 4.33 us  [body(): (weight * overlap[earlier, step_index][:, None])[..., None]]
    unnamed x103 -> x121, local copies, waits for them, and re-layouts: 6.52 us -> 9.29 us
    select_n x4 -> x12, other arithmetic: 5.7 us -> 5.83 us  [pick(): return jax.tree.map(lambda a, b: jnp.where(flag, a, b), first, second)]
  transfers between devices with their start and end apart: 24 -> 34, of which waited for: 9 -> 10; matrix products, arithmetic and copies ran while one was open for 19% -> 34% of each run, Pallas kernels for 0% -> 0%
where the time goes in v2:
time: 205 us; the launch traced here: 203 us
  waiting for transfers between devices  57.3 us (28%)
  starting transfers between devices  47.5 us (23%)
  other arithmetic  33 us (16%)
  matrix products  29 us (14%)
  local copies, waits for them, and re-layouts  20.9 us (10%)
  between operations  15.4 us (8%)
    ppermute x21, starting transfers between devices, group_shift(): return lax.ppermute(value, axis, pairs)  31.6 us
    ppermute x21, waiting for transfers between devices, group_shift(): return lax.ppermute(value, axis, pairs)  30.6 us
    ppermute x10, waiting for transfers between devices, body(): lax.ppermute(tails, 'ctx', [(source, source - reach) for source in range(...  26.7 us
    dot_general x1, matrix products, body(): jnp.einsum('tpi,id->tpd', normed, w_out, preferred_element_type=jnp.float32)  14.6 us
    ppermute x10, starting transfers between devices, body(): lax.ppermute(tails, 'ctx', [(source, source - reach) for source in range(...  9.69 us
    dot_general x1, matrix products, body(): jnp.einsum('phij,jphd->iphd', mixing, x_heads, preferred_element_type=jnp...  9.45 us
    unnamed x121, local copies, waits for them, and re-layouts  9.29 us
    ppermute x2, starting transfers between devices, passed_along(): lax.ppermute(value, axis, [(source, source + steps) for source in range(l...  6.16 us
  transfers between devices with their start and end apart: 34, of which 10 were waited for; matrix products, arithmetic and copies ran while one was open for 34% of the time, Pallas kernels for 0%

profile of v2, /device:TPU:0, one launch (start us, length us, event | category | flops | bytes accessed | tf_op | source)
XLA Modules:
  0.0 203.1 jit_solution(15321176660090320654)
XLA Ops:
  7.2 2.9 %copy.44 = bf16[512,1,2048]{0,2,1:T(8,128)(2,1)S(1)} copy(bf16[512,1,2048]{2,0,1:T(8,128)(2,1)} %param.16) | data formatting | bytes 4194304 | tf_op args[0]
  10.3 1.3 collective-permute-start
  11.7 1.3 slice.227
  12.9 4.8 %collective-permute-start.1 = (bf16[3,1,256]{2,0,1:T(4,128)(2,1)}, bf16[3,1,256]{2,0,1:T(4,128)(2,1)}, u32[]{:S(2)}, u32[]{:S(2)}) collective-permute-start(bf16[3,1,256]{2,0,1:T(4,128)(2,1)} %slice.227), channel_id=1, source_target_pairs={{0,4},{4,8},{8,12},{12,16},{16,20},{20,24},{24,28},{28,32},{32,36}... | collective-permute-start | bytes 4616 | tf_op jit(solution)/shard_map/ppermute | solution.py:12
  18.6 1.2 reduce-window.6
  22.9 2.0 multiply_convert_fusion.4
  25.4 5.6 %fusion.9 = (bf16[512,1,2048]{0,2,1:T(8,128)(2,1)S(1)}, bf16[512,1,2048]{0,2,1:T(8,128)(2,1)}) fusion(f32[2048]{0:T(1024)S(1)} %bitcast.219, bf16[512,1,2048]{0,2,1:T(8,128)(2,1)S(1)} %copy.44, f32[2048]{0:T(1024)S(1)} %bitcast.221, bf16[3,1,2048]{0,2,1:T(8,128)(2,1)S(1)} %collective-permute-done, f32[2048]{0:T(1024)S(1)} %bitcast.217, ...), kind=kLoop, calls=%fused_computation.15 | loop fusion | flops 29360128 | bytes 10530816 | tf_op jit(solution)/shard_map/convert_element_type | solution.py:105
  32.4 2.3 %collective-permute-done.2 = f32[1,32]{1,0:T(1,128)} collective-permute-done((f32[1,32]{1,0:T(1,128)}, f32[1,32]{1,0:T(1,128)}, u32[]{:S(2)}, u32[]{:S(2)}) %collective-permute-start.2) | collective-permute-done | bytes 160 | tf_op jit(solution)/shard_map/ppermute | solution.py:21
  34.7 1.2 fusion.91
  36.1 2.4 %fusion.27 = f32[1,32,32,128]{3,2,1,0:T(8,128)} fusion(f32[1,32,64,128]{3,2,1,0:T(8,128)S(1)} %convolution_bitcast_fusion, s32[]{:T(128)S(6)} %select_n.336, f32[1,32,64,128]{3,2,1,0:T(8,128)} %collective-permute-done.9, f32[1,32,64,128]{3,2,1,0:T(8,128)S(1)} %broadcast_select_fusion.4, f32[32]{0:T(128)S(1)} %get-tuple-element.58, pred[]{:T(512)S(6)} %eq.33), kind=kLoop, calls=%fused_computation.46 | loop fusion | flops 393216 | bytes 2097285 | tf_op jit(solution)/shard_map/add | solution.py:34
  38.5 1.0 collective-permute-start.11
  39.5 2.2 %collective-permute-start.10 = (f32[1,32,32,128]{3,2,1,0:T(8,128)}, f32[1,32,32,128]{3,2,1,0:T(8,128)S(1)}, u32[]{:S(2)}, u32[]{:S(2)}) collective-permute-start(f32[1,32,32,128]{3,2,1,0:T(8,128)} %fusion.27), channel_id=1, source_target_pairs={{0,24},{4,28},{8,0},{12,4},{16,8},{20,12},{24,16},{28,20},{32,56},... | collective-permute-start | bytes 1572872 | tf_op jit(solution)/shard_map/ppermute | solution.py:21
  41.7 1.2 collective-permute-start.22
  43.6 10.7 %collective-permute-done.11 = f32[1,32,32,128]{3,2,1,0:T(8,128)S(1)} collective-permute-done((f32[1,32,32,128]{3,2,1,0:T(8,128)}, f32[1,32,32,128]{3,2,1,0:T(8,128)S(1)}, u32[]{:S(2)}, u32[]{:S(2)}) %collective-permute-start.11) | collective-permute-done | bytes 524320 | tf_op jit(solution)/shard_map/ppermute | solution.py:21
  55.3 1.2 collective-permute-start.4
  56.5 2.2 %collective-permute-start.3 = (f32[1,32]{1,0:T(1,128)S(1)}, f32[1,32]{1,0:T(1,128)S(1)}, u32[]{:S(2)}, u32[]{:S(2)}) collective-permute-start(f32[1,32]{1,0:T(1,128)S(1)} %get-tuple-element.59), channel_id=1, source_target_pairs={{0,24},{4,28},{8,0},{12,4},{16,8},{20,12},{24,16},{28,20},{32,56},... | collective-permute-start | bytes 392 | tf_op jit(solution)/shard_map/ppermute | solution.py:21
  58.7 6.4 %collective-permute-done.4 = f32[1,32]{1,0:T(1,128)S(1)} collective-permute-done((f32[1,32]{1,0:T(1,128)S(1)}, f32[1,32]{1,0:T(1,128)S(1)}, u32[]{:S(2)}, u32[]{:S(2)}) %collective-permute-start.4) | collective-permute-done | bytes 160 | tf_op jit(solution)/shard_map/ppermute | solution.py:21
  65.1 3.3 %collective-permute-start.13 = (f32[1,32,16,128]{3,2,1,0:T(8,128)S(1)}, f32[1,32,16,128]{3,2,1,0:T(8,128)S(1)}, u32[]{:S(2)}, u32[]{:S(2)}) collective-permute-start(f32[1,32,16,128]{3,2,1,0:T(8,128)S(1)} %slice.296), channel_id=1, source_target_pairs={{0,24},{4,28},{8,0},{12,4},{16,8},{20,12},{24,16},{28,20},{32,56},... | collective-permute-start | bytes 786440 | tf_op jit(solution)/shard_map/ppermute | solution.py:21
  69.3 3.8 %collective-permute-done.13 = f32[1,32,16,128]{3,2,1,0:T(8,128)S(1)} collective-permute-done((f32[1,32,16,128]{3,2,1,0:T(8,128)S(1)}, f32[1,32,16,128]{3,2,1,0:T(8,128)S(1)}, u32[]{:S(2)}, u32[]{:S(2)}) %collective-permute-start.13) | collective-permute-done | bytes 262176 | tf_op jit(solution)/shard_map/ppermute | solution.py:21
  73.2 2.5 %add_select_fusion.2 = f32[1,32,32,128]{3,2,1,0:T(8,128)} fusion(f32[1,32,32,128]{3,2,1,0:T(8,128)S(1)} %collective-permute-done.11, f32[1,32,32,128]{3,2,1,0:T(8,128)S(1)} %constant_dynamic-update-slice_fusion, f32[1,32,32,128]{3,2,1,0:T(8,128)S(1)} %collective-permute-done.10, f32[1,32,32,128]{3,2,1,0:T(8,128)} %fusion.27, ...), kind=kLoop, calls=%fused_computation.53 | loop fusion | flops 2490368 | bytes 2622086 | tf_op jit(solution)/shard_map/jit(_where)/select_n | solution.py:38
  75.7 1.8 collective-permute-start.15
  78.3 1.4 collective-permute-start.14
  81.0 3.9 %copy.53 = bf16[512,1,2048]{0,2,1:T(8,128)(2,1)} copy(bf16[512,1,2048]{2,0,1:T(8,128)(2,1)} %param.17) | data formatting | bytes 4194304 | tf_op args[1]
  84.9 2.7 %collective-permute-start.8 = (f32[1,32]{1,0:T(1,128)}, f32[1,32]{1,0:T(1,128)S(1)}, u32[]{:S(2)}, u32[]{:S(2)}) collective-permute-start(f32[1,32]{1,0:T(1,128)} %get-tuple-element.21), channel_id=1, source_target_pairs={{0,96},{4,100},{8,104},{12,108},{16,112},{20,116},{24,120},{28,124... | collective-permute-start | bytes 392 | tf_op jit(solution)/shard_map/ppermute | solution.py:21
  87.6 1.8 collective-permute-done.6
  89.4 1.5 collective-permute-start.28
  90.9 1.0 collective-permute-start.7
  91.9 1.3 collective-permute-start.16
  94.6 2.3 %collective-permute-start.17 = (f32[1,32,16,128]{3,2,1,0:T(8,128)S(1)}, f32[1,32,16,128]{3,2,1,0:T(8,128)S(1)}, u32[]{:S(2)}, u32[]{:S(2)}) collective-permute-start(f32[1,32,16,128]{3,2,1,0:T(8,128)S(1)} %slice.298), channel_id=1, source_target_pairs={{0,96},{4,100},{8,104},{12,108},{16,112},{20,116},{24,120},{28,124... | collective-permute-start | bytes 786440 | tf_op jit(solution)/shard_map/ppermute | solution.py:21
  97.2 2.4 %collective-permute-done.16 = f32[1,32,16,128]{3,2,1,0:T(8,128)S(1)} collective-permute-done((f32[1,32,16,128]{3,2,1,0:T(8,128)S(1)}, f32[1,32,16,128]{3,2,1,0:T(8,128)S(1)}, u32[]{:S(2)}, u32[]{:S(2)}) %collective-permute-start.16) | collective-permute-done | bytes 262176 | tf_op jit(solution)/shard_map/ppermute | solution.py:21
  99.6 1.6 collective-permute-done.17
  101.9 2.0 multiply_add_fusion
  104.1 9.5 %fusion = f32[32,64,512]{2,1,0:T(8,128)S(1)} fusion(bf16[512,32,64]{0,2,1:T(8,128)(2,1)S(1)} %bitcast.205, f32[32,512]{1,0:T(8,128)S(1)} %copy-done.22, f32[32,512]{1,0:T(8,128)S(1)} %copy-done.23, f32[512,512]{1,0:T(8,128)S(1)} %fusion.37, pred[512,512]{1,0:T(8,128)(4,1)S(1)} %copy-done.17), kind=kOutput, calls=%fused_computation.1 | convolution fusion | flops 1115684864 | bytes 7733248 | tf_op jit(solution)/shard_map/phij,jphd->iphd/dot_general | solution.py:151
  113.6 2.3 %fusion.8 = f32[512,1,32,64]{0,3,2,1:T(8,128)S(1)} fusion(f32[32,64,512]{2,1,0:T(8,128)S(1)} %fusion, f32[32]{0:T(128)S(1)} %copy-done.51, f32[512,32]{0,1:T(8,128)S(1)} %bitcast.214, f32[1,32,64,128]{3,2,1,0:T(8,128)S(1)} %copy-done.3, f32[1,32,32,128]{3,2,1,0:T(8,128)S(1)} %collective-permute-done.18, f32[1,32,32,128]{3,2,1,0:T(8,128)S(1)} %multiply_add_fusion, ...), kind=kOutput, calls=%fused_computation.13 | convolution fusion | flops 1617428480 | bytes 12780545 | tf_op jit(solution)/shard_map/ipn,phdn->iphd/dot_general | solution.py:153
  115.9 1.4 multiply_reduce_fusion
  117.4 2.0 collective-permute-start.19
  119.4 3.6 %collective-permute-start.20 = (f32[512,1]{0,1:T(1,128)S(1)}, f32[512,1]{0,1:T(1,128)S(1)}, u32[]{:S(2)}, u32[]{:S(2)}) collective-permute-start(f32[512,1]{0,1:T(1,128)S(1)} %bitcast.233), channel_id=1, source_target_pairs={{0,2},{1,3},{2,0},{3,1},{4,6},{5,7},{6,4},{7,5},{8,10},{9,11},{10,... | collective-permute-start | bytes 6152 | tf_op jit(solution)/shard_map/ppermute | solution.py:21
  124.9 1.6 collective-permute-done.21
  126.6 14.6 %fusion.2 = bf16[512,1,4096]{2,0,1:T(8,128)(2,1)} fusion(bf16[2048,4096]{1,0:T(8,128)(2,1)} %param.26, f32[512,1,2048]{0,2,1:T(8,128)S(1)} %get-tuple-element.20, f32[2048]{0:T(1024)S(1)} %copy-done.55, f32[512]{0:T(512)S(1)} %bitcast.242), kind=kOutput, calls=%fused_computation.4 | convolution fusion | flops 8595177472 | bytes 25176064 | tf_op jit(solution)/shard_map/tpi,id->tpd/dot_general | solution.py:170
  143.2 1.3 collective-permute-start.26
  145.5 2.1 %collective-permute-done.26 = bf16[3,1,256]{2,0,1:T(4,128)(2,1)S(1)} collective-permute-done((bf16[3,1,256]{2,0,1:T(4,128)(2,1)S(1)}, bf16[3,1,256]{2,0,1:T(4,128)(2,1)S(1)}, u32[]{:S(2)}, u32[]{:S(2)}) %collective-permute-start.26) | collective-permute-done | bytes 1568 | tf_op jit(solution)/shard_map/ppermute | solution.py:115
  152.0 1.3 collective-permute-start.32
  158.4 24.6 %collective-permute-done.32 = bf16[3,1,2048]{0,2,1:T(8,128)(2,1)} collective-permute-done((bf16[3,1,2048]{0,2,1:T(8,128)(2,1)S(1)}, bf16[3,1,2048]{0,2,1:T(8,128)(2,1)}, u32[]{:S(2)}, u32[]{:S(2)}) %collective-permute-start.32) | collective-permute-done | bytes 12320 | tf_op jit(solution)/shard_map/ppermute | solution.py:115
  183.0 1.1 bitcast_convert_fusion
  185.3 1.5 add_select_fusion
  186.8 3.3 %collective-permute-start.27 = (f32[1,32,32,128]{3,2,1,0:T(8,128)S(1)}, f32[1,32,32,128]{3,2,1,0:T(8,128)S(1)}, u32[]{:S(2)}, u32[]{:S(2)}) collective-permute-start(f32[1,32,32,128]{3,2,1,0:T(8,128)S(1)} %add_select_fusion), channel_id=1, source_target_pairs={{0,4},{4,0},{8,12},{12,8},{16,20},{20,16},{24,28},{28,24},{32,36},... | collective-permute-start | bytes 1572872 | tf_op jit(solution)/shard_map/ppermute | solution.py:21
  190.1 1.2 fusion.40
  193.1 1.6 convolution_multiply_fusion
  (254 shorter events, 31.5 us)
Async XLA Ops:
  7.2 10.6 %copy-start.56 = (f32[32]{0:T(128)S(1)}, f32[32]{0:T(128)}, u32[]{:S(2)}) copy-start(f32[32]{0:T(128)} %param.21) | copy-start | bytes 388
  7.2 10.6 %copy-start.12 = (f32[512,1,32]{0,2,1:T(8,128)S(1)}, f32[512,1,32]{0,2,1:T(8,128)}, u32[]{:S(2)}) copy-start(f32[512,1,32]{0,2,1:T(8,128)} %param.19) | copy-start | bytes 196612
  7.2 10.6 %copy-start.36 = (f32[32]{0:T(128)S(1)}, f32[32]{0:T(128)}, u32[]{:S(2)}) copy-start(f32[32]{0:T(128)} %param.20) | copy-start | bytes 388
  7.2 189.0 %reduce-scatter.2.cloned.1.call-start = ((), (), s32[]{:S(2)}) async-start(), calls=%async_computation.1 | async-start | bytes 5242880 | tf_op jit(solution)/shard_map/reduce_scatter | solution.py:169
  10.3 20.7 %copy-start.11 = (bf16[3,1,2048]{0,2,1:T(8,128)(2,1)}, bf16[3,1,2048]{0,2,1:T(8,128)(2,1)S(1)}, u32[]{:S(2)}) copy-start(bf16[3,1,2048]{0,2,1:T(8,128)(2,1)S(1)} %slice.282) | copy-start | bytes 36868
  10.3 14.5 %collective-permute-start = (bf16[3,1,2048]{0,2,1:T(8,128)(2,1)S(1)}, bf16[3,1,2048]{0,2,1:T(8,128)(2,1)S(1)}, u32[]{:S(2)}, u32[]{:S(2)}) collective-permute-start(bf16[3,1,2048]{0,2,1:T(8,128)(2,1)S(1)} %slice.282), channel_id=1, source_target_pairs={{0,4},{4,8},{8,12},{12,16},{16,20},{20,24},{24,28},{28,32},{32,36}... | collective-permute-start | bytes 36872 | tf_op jit(solution)/shard_map/ppermute | solution.py:12
  12.9 9.9 %collective-permute-start.1 = (bf16[3,1,256]{2,0,1:T(4,128)(2,1)}, bf16[3,1,256]{2,0,1:T(4,128)(2,1)}, u32[]{:S(2)}, u32[]{:S(2)}) collective-permute-start(bf16[3,1,256]{2,0,1:T(4,128)(2,1)} %slice.227), channel_id=1, source_target_pairs={{0,4},{4,8},{8,12},{12,16},{16,20},{20,24},{24,28},{28,32},{32,36}... | collective-permute-start | bytes 4616 | tf_op jit(solution)/shard_map/ppermute | solution.py:12
  31.8 4.1 %collective-permute-start.9 = (f32[1,32,64,128]{3,2,1,0:T(8,128)S(1)}, f32[1,32,64,128]{3,2,1,0:T(8,128)}, u32[]{:S(2)}, u32[]{:S(2)}) collective-permute-start(f32[1,32,64,128]{3,2,1,0:T(8,128)S(1)} %convolution_bitcast_fusion), channel_id=1, source_target_pairs={{0,4},{4,0},{8,12},{12,8},{16,20},{20,16},{24,28},{28,24},{32,36},... | collective-permute-start | bytes 3145736 | tf_op jit(solution)/shard_map/ppermute | solution.py:21
  31.9 2.8 %collective-permute-start.2 = (f32[1,32]{1,0:T(1,128)}, f32[1,32]{1,0:T(1,128)}, u32[]{:S(2)}, u32[]{:S(2)}) collective-permute-start(f32[1,32]{1,0:T(1,128)} %bitcast.72), channel_id=1, source_target_pairs={{0,4},{4,0},{8,12},{12,8},{16,20},{20,16},{24,28},{28,24},{32,36},... | collective-permute-start | bytes 392 | tf_op jit(solution)/shard_map/ppermute | solution.py:21
  32.4 22.7 %copy-start.10 = (f32[32,1,4,128]{3,2,1,0:T(4,128)S(1)}, f32[32,1,4,128]{3,2,1,0:T(4,128)}, u32[]{:S(2)}) copy-start(f32[32,1,4,128]{3,2,1,0:T(4,128)} %copy-done.9) | copy-start | bytes 196612
  38.5 15.8 %collective-permute-start.11 = (f32[1,32,32,128]{3,2,1,0:T(8,128)}, f32[1,32,32,128]{3,2,1,0:T(8,128)S(1)}, u32[]{:S(2)}, u32[]{:S(2)}) collective-permute-start(f32[1,32,32,128]{3,2,1,0:T(8,128)} %fusion.27), channel_id=1, source_target_pairs={{0,8},{4,12},{8,16},{12,20},{16,24},{20,28},{24,0},{28,4},{32,40},... | collective-permute-start | bytes 1572872 | tf_op jit(solution)/shard_map/ppermute | solution.py:21
  39.5 25.5 %collective-permute-start.10 = (f32[1,32,32,128]{3,2,1,0:T(8,128)}, f32[1,32,32,128]{3,2,1,0:T(8,128)S(1)}, u32[]{:S(2)}, u32[]{:S(2)}) collective-permute-start(f32[1,32,32,128]{3,2,1,0:T(8,128)} %fusion.27), channel_id=1, source_target_pairs={{0,24},{4,28},{8,0},{12,4},{16,8},{20,12},{24,16},{28,20},{32,56},... | collective-permute-start | bytes 1572872 | tf_op jit(solution)/shard_map/ppermute | solution.py:21
  41.7 51.5 %collective-permute-start.22 = (bf16[3,1,256]{2,0,1:T(4,128)(2,1)}, bf16[3,1,256]{2,0,1:T(4,128)(2,1)}, u32[]{:S(2)}, u32[]{:S(2)}) collective-permute-start(bf16[3,1,256]{2,0,1:T(4,128)(2,1)} %slice.227), channel_id=1, source_target_pairs={{124,60},{125,61},{126,62},{127,63}} | collective-permute-start | bytes 4616 | tf_op jit(solution)/shard_map/ppermute | solution.py:115
  54.3 18.9 %copy-start.4 = (f32[1,32,32,128]{3,2,1,0:T(8,128)}, f32[1,32,32,128]{3,2,1,0:T(8,128)S(1)}, u32[]{:S(2)}) copy-start(f32[1,32,32,128]{3,2,1,0:T(8,128)S(1)} %collective-permute-done.11) | copy-start | bytes 1572868
  55.1 13.3 %collective-permute-start.12 = (f32[1,32,16,128]{3,2,1,0:T(8,128)}, f32[1,32,16,128]{3,2,1,0:T(8,128)}, u32[]{:S(2)}, u32[]{:S(2)}) collective-permute-start(f32[1,32,16,128]{3,2,1,0:T(8,128)} %slice.295), channel_id=1, source_target_pairs={{0,8},{4,12},{8,16},{12,20},{16,24},{20,28},{24,0},{28,4},{32,40},... | collective-permute-start | bytes 786440 | tf_op jit(solution)/shard_map/ppermute | solution.py:21
  55.3 9.8 %collective-permute-start.4 = (f32[1,32]{1,0:T(1,128)S(1)}, f32[1,32]{1,0:T(1,128)S(1)}, u32[]{:S(2)}, u32[]{:S(2)}) collective-permute-start(f32[1,32]{1,0:T(1,128)S(1)} %get-tuple-element.59), channel_id=1, source_target_pairs={{0,8},{4,12},{8,16},{12,20},{16,24},{20,28},{24,0},{28,4},{32,40},... | collective-permute-start | bytes 392 | tf_op jit(solution)/shard_map/ppermute | solution.py:21
  56.5 11.9 %collective-permute-start.3 = (f32[1,32]{1,0:T(1,128)S(1)}, f32[1,32]{1,0:T(1,128)S(1)}, u32[]{:S(2)}, u32[]{:S(2)}) collective-permute-start(f32[1,32]{1,0:T(1,128)S(1)} %get-tuple-element.59), channel_id=1, source_target_pairs={{0,24},{4,28},{8,0},{12,4},{16,8},{20,12},{24,16},{28,20},{32,56},... | collective-permute-start | bytes 392 | tf_op jit(solution)/shard_map/ppermute | solution.py:21
  65.0 8.2 %collective-permute-start.5 = (f32[1,32]{1,0:T(1,128)S(1)}, f32[1,32]{1,0:T(1,128)S(1)}, u32[]{:S(2)}, u32[]{:S(2)}) collective-permute-start(f32[1,32]{1,0:T(1,128)S(1)} %collective-permute-done.4), channel_id=1, source_target_pairs={{0,8},{4,12},{8,16},{12,20},{16,24},{20,28},{24,0},{28,4},{32,40},... | collective-permute-start | bytes 392 | tf_op jit(solution)/shard_map/ppermute | solution.py:21
  65.0 12.5 %copy-start.5 = (f32[1,32,32,128]{3,2,1,0:T(8,128)}, f32[1,32,32,128]{3,2,1,0:T(8,128)S(1)}, u32[]{:S(2)}) copy-start(f32[1,32,32,128]{3,2,1,0:T(8,128)S(1)} %collective-permute-done.10) | copy-start | bytes 1572868
  65.1 8.1 %collective-permute-start.13 = (f32[1,32,16,128]{3,2,1,0:T(8,128)S(1)}, f32[1,32,16,128]{3,2,1,0:T(8,128)S(1)}, u32[]{:S(2)}, u32[]{:S(2)}) collective-permute-start(f32[1,32,16,128]{3,2,1,0:T(8,128)S(1)} %slice.296), channel_id=1, source_target_pairs={{0,24},{4,28},{8,0},{12,4},{16,8},{20,12},{24,16},{28,20},{32,56},... | collective-permute-start | bytes 786440 | tf_op jit(solution)/shard_map/ppermute | solution.py:21
  68.4 12.6 %copy-start.50 = (f32[32]{0:T(128)}, f32[32]{0:T(128)S(1)}, u32[]{:S(2)}) copy-start(f32[32]{0:T(128)S(1)} %broadcast_multiply_fusion.2) | copy-start | bytes 388
  75.7 16.2 %collective-permute-start.15 = (f32[1,32,32,128]{3,2,1,0:T(8,128)}, f32[1,32,32,128]{3,2,1,0:T(8,128)S(1)}, u32[]{:S(2)}, u32[]{:S(2)}) collective-permute-start(f32[1,32,32,128]{3,2,1,0:T(8,128)} %add_select_fusion.2), channel_id=1, source_target_pairs={{0,32},{4,36},{8,40},{12,44},{16,48},{20,52},{24,56},{28,60},{32,6... | collective-permute-start | bytes 1572872 | tf_op jit(solution)/shard_map/ppermute | solution.py:21
  78.3 16.2 %collective-permute-start.14 = (f32[1,32,32,128]{3,2,1,0:T(8,128)}, f32[1,32,32,128]{3,2,1,0:T(8,128)S(1)}, u32[]{:S(2)}, u32[]{:S(2)}) collective-permute-start(f32[1,32,32,128]{3,2,1,0:T(8,128)} %add_select_fusion.2), channel_id=1, source_target_pairs={{0,96},{4,100},{8,104},{12,108},{16,112},{20,116},{24,120},{28,124... | collective-permute-start | bytes 1572872 | tf_op jit(solution)/shard_map/ppermute | solution.py:21
  80.4 9.0 %collective-permute-start.6 = (f32[1,32]{1,0:T(1,128)}, f32[1,32]{1,0:T(1,128)}, u32[]{:S(2)}, u32[]{:S(2)}) collective-permute-start(f32[1,32]{1,0:T(1,128)} %get-tuple-element.21), channel_id=1, source_target_pairs={{0,32},{4,36},{8,40},{12,44},{16,48},{20,52},{24,56},{28,60},{32,6... | collective-permute-start | bytes 392 | tf_op jit(solution)/shard_map/ppermute | solution.py:21
  84.9 19.1 %copy-start.1 = (bf16[512,1,2048]{0,2,1:T(8,128)(2,1)S(1)}, bf16[512,1,2048]{0,2,1:T(8,128)(2,1)}, u32[]{:S(2)}) copy-start(bf16[512,1,2048]{0,2,1:T(8,128)(2,1)} %get-tuple-element.24) | copy-start | bytes 6291460
  84.9 19.1 %copy-start.17 = (pred[512,512]{1,0:T(8,128)(4,1)S(1)}, pred[512,512]{1,0:T(8,128)(4,1)}, u32[]{:S(2)}) copy-start(pred[512,512]{1,0:T(8,128)(4,1)} %iota_compare_fusion) | copy-start | bytes 786436
  84.9 19.2 %copy-start.22 = (f32[32,512]{1,0:T(8,128)S(1)}, f32[32,512]{1,0:T(8,128)}, u32[]{:S(2)}) copy-start(f32[32,512]{1,0:T(8,128)} %get-tuple-element.37) | copy-start | bytes 196612
  84.9 19.2 %copy-start.23 = (f32[32,512]{1,0:T(8,128)S(1)}, f32[32,512]{1,0:T(8,128)}, u32[]{:S(2)}) copy-start(f32[32,512]{1,0:T(8,128)} %bitcast_add_fusion) | copy-start | bytes 196612
  84.9 6.0 %collective-permute-start.8 = (f32[1,32]{1,0:T(1,128)}, f32[1,32]{1,0:T(1,128)S(1)}, u32[]{:S(2)}, u32[]{:S(2)}) collective-permute-start(f32[1,32]{1,0:T(1,128)} %get-tuple-element.21), channel_id=1, source_target_pairs={{0,96},{4,100},{8,104},{12,108},{16,112},{20,116},{24,120},{28,124... | collective-permute-start | bytes 392 | tf_op jit(solution)/shard_map/ppermute | solution.py:21
  89.4 58.3 %collective-permute-start.28 = (bf16[3,1,2048]{0,2,1:T(8,128)(2,1)}, bf16[3,1,2048]{0,2,1:T(8,128)(2,1)}, u32[]{:S(2)}, u32[]{:S(2)}) collective-permute-start(bf16[3,1,2048]{0,2,1:T(8,128)(2,1)} %copy-done.11), channel_id=1, source_target_pairs={{124,60},{125,61},{126,62},{127,63}} | collective-permute-start | bytes 36872 | tf_op jit(solution)/shard_map/ppermute | solution.py:115
  90.9 10.4 %collective-permute-start.7 = (f32[1,32]{1,0:T(1,128)}, f32[1,32]{1,0:T(1,128)S(1)}, u32[]{:S(2)}, u32[]{:S(2)}) collective-permute-start(f32[1,32]{1,0:T(1,128)} %collective-permute-done.6), channel_id=1, source_target_pairs={{0,32},{4,36},{8,40},{12,44},{16,48},{20,52},{24,56},{28,60},{32,6... | collective-permute-start | bytes 392 | tf_op jit(solution)/shard_map/ppermute | solution.py:21
  91.9 7.7 %collective-permute-start.16 = (f32[1,32,16,128]{3,2,1,0:T(8,128)S(1)}, f32[1,32,16,128]{3,2,1,0:T(8,128)S(1)}, u32[]{:S(2)}, u32[]{:S(2)}) collective-permute-start(f32[1,32,16,128]{3,2,1,0:T(8,128)S(1)} %slice.297), channel_id=1, source_target_pairs={{0,32},{4,36},{8,40},{12,44},{16,48},{20,52},{24,56},{28,60},{32,6... | collective-permute-start | bytes 786440 | tf_op jit(solution)/shard_map/ppermute | solution.py:21
  93.9 30.1 %collective-permute-start.23 = (bf16[3,1,256]{2,0,1:T(4,128)(2,1)S(1)}, bf16[3,1,256]{2,0,1:T(4,128)(2,1)S(1)}, u32[]{:S(2)}, u32[]{:S(2)}) collective-permute-start(bf16[3,1,256]{2,0,1:T(4,128)(2,1)S(1)} %broadcast_select_fusion.5), channel_id=1, source_target_pairs={{60,28},{124,92},{61,29},{125,93},{62,30},{126,94},{63,31},{127,95}} | collective-permute-start | bytes 4616 | tf_op jit(solution)/shard_map/ppermute | solution.py:115
  94.6 6.6 %collective-permute-start.17 = (f32[1,32,16,128]{3,2,1,0:T(8,128)S(1)}, f32[1,32,16,128]{3,2,1,0:T(8,128)S(1)}, u32[]{:S(2)}, u32[]{:S(2)}) collective-permute-start(f32[1,32,16,128]{3,2,1,0:T(8,128)S(1)} %slice.298), channel_id=1, source_target_pairs={{0,96},{4,100},{8,104},{12,108},{16,112},{20,116},{24,120},{28,124... | collective-permute-start | bytes 786440 | tf_op jit(solution)/shard_map/ppermute | solution.py:21
  103.9 9.6 %collective-permute-start.18 = (f32[1,32,32,128]{3,2,1,0:T(8,128)S(1)}, f32[1,32,32,128]{3,2,1,0:T(8,128)S(1)}, u32[]{:S(2)}, u32[]{:S(2)}) collective-permute-start(f32[1,32,32,128]{3,2,1,0:T(8,128)S(1)} %multiply_add_fusion), channel_id=1, source_target_pairs={{0,4},{4,0},{8,12},{12,8},{16,20},{20,16},{24,28},{28,24},{32,36},... | collective-permute-start | bytes 1572872 | tf_op jit(solution)/shard_map/ppermute | solution.py:21
  115.9 10.6 %copy-start.55 = (f32[2048]{0:T(1024)S(1)}, f32[2048]{0:T(1024)}, u32[]{:S(2)}) copy-start(f32[2048]{0:T(1024)} %param.25) | copy-start | bytes 24580
  117.4 7.5 %collective-permute-start.19 = (f32[512,1]{0,1:T(1,128)S(1)}, f32[512,1]{0,1:T(1,128)S(1)}, u32[]{:S(2)}, u32[]{:S(2)}) collective-permute-start(f32[512,1]{0,1:T(1,128)S(1)} %bitcast.232), channel_id=1, source_target_pairs={{0,1},{1,2},{2,3},{3,0},{4,5},{5,6},{6,7},{7,4},{8,9},{9,10},{10,1... | collective-permute-start | bytes 6152 | tf_op jit(solution)/shard_map/ppermute | solution.py:21
  119.4 5.5 %collective-permute-start.20 = (f32[512,1]{0,1:T(1,128)S(1)}, f32[512,1]{0,1:T(1,128)S(1)}, u32[]{:S(2)}, u32[]{:S(2)}) collective-permute-start(f32[512,1]{0,1:T(1,128)S(1)} %bitcast.233), channel_id=1, source_target_pairs={{0,2},{1,3},{2,0},{3,1},{4,6},{5,7},{6,4},{7,5},{8,10},{9,11},{10,... | collective-permute-start | bytes 6152 | tf_op jit(solution)/shard_map/ppermute | solution.py:21
  123.0 3.6 %collective-permute-start.21 = (f32[512,1]{0,1:T(1,128)S(1)}, f32[512,1]{0,1:T(1,128)S(1)}, u32[]{:S(2)}, u32[]{:S(2)}) collective-permute-start(f32[512,1]{0,1:T(1,128)S(1)} %bitcast.234), channel_id=1, source_target_pairs={{0,3},{1,0},{2,1},{3,2},{4,7},{5,4},{6,5},{7,6},{8,11},{9,8},{10,9... | collective-permute-start | bytes 6152 | tf_op jit(solution)/shard_map/ppermute | solution.py:21
  124.0 18.5 %collective-permute-start.24 = (bf16[3,1,256]{2,0,1:T(4,128)(2,1)S(1)}, bf16[3,1,256]{2,0,1:T(4,128)(2,1)S(1)}, u32[]{:S(2)}, u32[]{:S(2)}) collective-permute-start(bf16[3,1,256]{2,0,1:T(4,128)(2,1)S(1)} %broadcast_select_fusion.6), channel_id=1, source_target_pairs={{28,12},{60,44},{92,76},{124,108},{29,13},{61,45},{93,77},{125,109... | collective-permute-start | bytes 4616 | tf_op jit(solution)/shard_map/ppermute | solution.py:115
  142.5 0.7 collective-permute-start.25
  143.2 4.3 %collective-permute-start.26 = (bf16[3,1,256]{2,0,1:T(4,128)(2,1)S(1)}, bf16[3,1,256]{2,0,1:T(4,128)(2,1)S(1)}, u32[]{:S(2)}, u32[]{:S(2)}) collective-permute-start(bf16[3,1,256]{2,0,1:T(4,128)(2,1)S(1)} %broadcast_select_fusion.8), channel_id=1, source_target_pairs={{4,0},{12,8},{20,16},{28,24},{36,32},{44,40},{52,48},{60,56},{68,6... | collective-permute-start | bytes 4616 | tf_op jit(solution)/shard_map/ppermute | solution.py:115
  147.9 0.8 collective-permute-start.29
  148.8 1.6 collective-permute-start.30
  150.5 34.8 %copy-start.8 = (f32[1,32,32,128]{3,2,1,0:T(8,128)S(1)}, f32[1,32,32,128]{3,2,1,0:T(8,128)}, u32[]{:S(2)}) copy-start(f32[1,32,32,128]{3,2,1,0:T(8,128)} %copy-done.7) | copy-start | bytes 1572868
  150.5 1.5 collective-permute-start.31
  152.0 30.9 %collective-permute-start.32 = (bf16[3,1,2048]{0,2,1:T(8,128)(2,1)S(1)}, bf16[3,1,2048]{0,2,1:T(8,128)(2,1)}, u32[]{:S(2)}, u32[]{:S(2)}) collective-permute-start(bf16[3,1,2048]{0,2,1:T(8,128)(2,1)S(1)} %broadcast_select_fusion.3), channel_id=1, source_target_pairs={{4,0},{12,8},{20,16},{28,24},{36,32},{44,40},{52,48},{60,56},{68,6... | collective-permute-start | bytes 36872 | tf_op jit(solution)/shard_map/ppermute | solution.py:115
  186.8 6.3 %collective-permute-start.27 = (f32[1,32,32,128]{3,2,1,0:T(8,128)S(1)}, f32[1,32,32,128]{3,2,1,0:T(8,128)S(1)}, u32[]{:S(2)}, u32[]{:S(2)}) collective-permute-start(f32[1,32,32,128]{3,2,1,0:T(8,128)S(1)} %add_select_fusion), channel_id=1, source_target_pairs={{0,4},{4,0},{8,12},{12,8},{16,20},{20,16},{24,28},{28,24},{32,36},... | collective-permute-start | bytes 1572872 | tf_op jit(solution)/shard_map/ppermute | solution.py:21
  (44 other events, 208.1 us)
Sparse Core Ops, SparseCore 0:
  141.4 50.0 reduce-scatter.1

commit v3 on v2

--- a/solution.py
+++ b/solution.py
@@ -62,6 +62,31 @@
     for shift in range(group - 1, 0, -1):
         total = pick(shift > member, chain(total, received[shift]), total)
     return before, total
+
+
+def ring_reduce_scatter(part, axis):
+    count = lax.axis_size(axis)
+    here = lax.axis_index(axis)
+    share = part.shape[0] // count
+    split = part.shape[2] // 2
+
+    def chunk(offset):
+        return lax.dynamic_slice_in_dim(part, ((here + offset) % count) * share, share, 0)
+
+    def passed(value, shift):
+        return group_shift(value.astype(jnp.bfloat16), axis, count, 1, count, shift).astype(
+            jnp.float32
+        )
+
+    forward = chunk(-1)[..., :split]
+    backward = chunk(1)[..., split:]
+    for step in range(2, count):
+        forward = passed(forward, 1) + chunk(-step)[..., :split]
+        backward = passed(backward, -1) + chunk(step)[..., split:]
+    own = chunk(0)
+    forward = passed(forward, 1) + own[..., :split]
+    backward = passed(backward, -1) + own[..., split:]
+    return jnp.concatenate([forward, backward], axis=2)
 
 
 def body(
@@ -166,15 +191,8 @@
     normed = (
         gated_out * lax.rsqrt(square_sums / inner_total + norm_eps)[..., None] * norm_gain
     ).astype(jnp.bfloat16)
-    projected = lax.psum_scatter(
-        jnp.einsum("tpi,id->tpd", normed, w_out, preferred_element_type=jnp.float32).astype(
-            jnp.bfloat16
-        ),
-        "head",
-        scatter_dimension=0,
-        tiled=True,
-    )
-    out = projected.astype(jnp.bfloat16)
+    projected = jnp.einsum("tpi,id->tpd", normed, w_out, preferred_element_type=jnp.float32)
+    out = ring_reduce_scatter(projected, "head").astype(jnp.bfloat16)
 
     final_x, final_bc = tails
     slot_count = requests.shape[0]

time: 205 us -> 232 us (1.13)
  local copies, waits for them, and re-layouts: 20.9 us -> 39.1 us
  other arithmetic: 33 us -> 46.7 us
  between operations: 15.4 us -> 2.22 us
  matrix products: 29 us -> 32.8 us
    ppermute x21 -> x27, waiting for transfers between devices: 30.6 us -> 55.3 us  [group_shift(): return lax.ppermute(value, axis, pairs)]
    ppermute x10, waiting for transfers between devices: 26.7 us -> 4.18 us  [body(): lax.ppermute(tails, 'ctx', [(source, source - reach) for source in range(...]
    convert_element_type x0 -> x4, other arithmetic: none -> 6.33 us  [passed(): value.astype(jnp.bfloat16)]
    ppermute x21 -> x27, starting transfers between devices: 31.6 us -> 37.1 us  [group_shift(): return lax.ppermute(value, axis, pairs)]
    squeeze x4, local copies, waits for them, and re-layouts: 0.38 us -> 5.22 us  [body(): pushed[earlier]]
    mul x9, local copies, waits for them, and re-layouts: 0.74 us -> 5.25 us  [body(): y_step = carried[..., None] * from_final[step_index]]
    dynamic_slice x0 -> x2, local copies, waits for them, and re-layouts: none -> 3.25 us  [chunk(): lax.dynamic_slice_in_dim(part, (here + offset) % count * share, share, 0)]
    dot_general x1, matrix products: 2.3 us -> 5.3 us  [body(): jnp.einsum('ipn,phdn->iphd', c_rows.astype(jnp.float32), s_before, precis...]
  transfers between devices with their start and end apart: 34 -> 39, of which waited for: 10 -> 16; matrix products, arithmetic and copies ran while one was open for 34% -> 43% of each run, Pallas kernels for 0% -> 0%
where the time goes in v3:
time: 232 us; the launch traced here: 230 us
  waiting for transfers between devices  59.4 us (26%)
  starting transfers between devices  49.5 us (21%)
  other arithmetic  46.7 us (20%)
  local copies, waits for them, and re-layouts  39.1 us (17%)
  matrix products  32.8 us (14%)
    ppermute x27, waiting for transfers between devices, group_shift(): return lax.ppermute(value, axis, pairs)  55.3 us
    ppermute x27, starting transfers between devices, group_shift(): return lax.ppermute(value, axis, pairs)  37.1 us
    dot_general x1, matrix products, body(): jnp.einsum('tpi,id->tpd', normed, w_out, preferred_element_type=jnp.float32)  13.3 us
    dot_general x1, matrix products, body(): jnp.einsum('phij,jphd->iphd', mixing, x_heads, preferred_element_type=jnp...  10.5 us
    unnamed x145, local copies, waits for them, and re-layouts  9.45 us
    ppermute x10, starting transfers between devices, body(): lax.ppermute(tails, 'ctx', [(source, source - reach) for source in range(...  9.28 us
    select_n x12, other arithmetic, pick(): return jax.tree.map(lambda a, b: jnp.where(flag, a, b), first, second)  6.87 us
    convert_element_type x4, other arithmetic, passed(): value.astype(jnp.bfloat16)  6.33 us
  transfers between devices with their start and end apart: 39, of which 16 were waited for; matrix products, arithmetic and copies ran while one was open for 43% of the time, Pallas kernels for 0%

profile of v3, /device:TPU:0, one launch (start us, length us, event | category | flops | bytes accessed | tf_op | source)
XLA Modules:
  0.0 229.8 jit_solution(17712761144837487838)
XLA Ops:
  3.1 1.9 collective-permute-start.1
  5.6 1.6 fusion.103
  9.7 1.9 collective-permute-start.2
  11.5 2.9 %copy.44 = bf16[512,1,2048]{0,2,1:T(8,128)(2,1)S(1)} copy(bf16[512,1,2048]{2,0,1:T(8,128)(2,1)} %param.16) | data formatting | bytes 4194304 | tf_op args[0]
  22.7 3.9 %copy.53 = bf16[512,1,2048]{0,2,1:T(8,128)(2,1)} copy(bf16[512,1,2048]{2,0,1:T(8,128)(2,1)} %param.17) | data formatting | bytes 4194304 | tf_op args[1]
  28.5 1.6 collective-permute-start.4
  30.1 1.7 collective-permute-start.3
  31.7 1.5 collective-permute-done.4
  33.3 1.3 collective-permute-start
  37.6 1.9 collective-permute-done.5
  40.0 4.3 %collective-permute-start.8 = (f32[1,32]{1,0:T(1,128)S(1)}, f32[1,32]{1,0:T(1,128)S(1)}, u32[]{:S(2)}, u32[]{:S(2)}) collective-permute-start(f32[1,32]{1,0:T(1,128)S(1)} %get-tuple-element.21), channel_id=1, source_target_pairs={{0,96},{4,100},{8,104},{12,108},{16,112},{20,116},{24,120},{28,124... | collective-permute-start | bytes 392 | tf_op jit(solution)/shard_map/ppermute | solution.py:21
  46.7 2.5 %collective-permute-done.6 = f32[1,32]{1,0:T(1,128)} collective-permute-done((f32[1,32]{1,0:T(1,128)S(1)}, f32[1,32]{1,0:T(1,128)}, u32[]{:S(2)}, u32[]{:S(2)}) %collective-permute-start.6) | collective-permute-done | bytes 160 | tf_op jit(solution)/shard_map/ppermute | solution.py:21
  49.9 1.7 multiply_convert_fusion.4
  54.2 3.9 %collective-permute-done.32 = bf16[3,1,256]{2,0,1:T(4,128)(2,1)S(1)} collective-permute-done((bf16[3,1,256]{2,0,1:T(4,128)(2,1)S(1)}, bf16[3,1,256]{2,0,1:T(4,128)(2,1)S(1)}, u32[]{:S(2)}, u32[]{:S(2)}) %collective-permute-start.32) | collective-permute-done | bytes 1568 | tf_op jit(solution)/shard_map/ppermute | solution.py:140
  62.3 5.6 %fusion.8 = (bf16[512,1,2048]{0,2,1:T(8,128)(2,1)S(1)}, bf16[512,1,2048]{0,2,1:T(8,128)(2,1)}) fusion(f32[2048]{0:T(1024)S(1)} %bitcast.232, bf16[512,1,2048]{0,2,1:T(8,128)(2,1)S(1)} %copy.44, f32[2048]{0:T(1024)S(1)} %bitcast.234, bf16[3,1,2048]{0,2,1:T(8,128)(2,1)S(1)} %collective-permute-done, f32[2048]{0:T(1024)S(1)} %bitcast.229, ...), kind=kLoop, calls=%fused_computation.13 | loop fusion | flops 29360128 | bytes 10530816 | tf_op jit(solution)/shard_map/convert_element_type | solution.py:130
  70.2 1.5 collective-permute-start.36
  83.9 1.6 fusion.35
  86.7 2.1 collective-permute-start.10
  88.8 10.5 %fusion = f32[32,64,512]{2,1,0:T(8,128)} fusion(bf16[512,32,64]{0,2,1:T(8,128)(2,1)S(1)} %bitcast.217, f32[32,512]{1,0:T(8,128)S(1)} %copy-done.33, f32[32,512]{1,0:T(8,128)S(1)} %copy-done.34, f32[512,512]{1,0:T(8,128)S(1)} %copy-done.10, pred[512,512]{1,0:T(8,128)(4,1)S(1)} %copy-done.21), kind=kOutput, calls=%fused_computation.1 | convolution fusion | flops 1115684864 | bytes 7733248 | tf_op jit(solution)/shard_map/phij,jphd->iphd/dot_general | solution.py:176
  99.5 2.0 collective-permute-done.10
  101.5 1.3 collective-permute-start.13
  104.2 3.2 %collective-permute-done.12 = f32[1,32,16,128]{3,2,1,0:T(8,128)S(1)} collective-permute-done((f32[1,32,16,128]{3,2,1,0:T(8,128)S(1)}, f32[1,32,16,128]{3,2,1,0:T(8,128)S(1)}, u32[]{:S(2)}, u32[]{:S(2)}) %collective-permute-start.12) | collective-permute-done | bytes 262176 | tf_op jit(solution)/shard_map/ppermute | solution.py:21
  111.0 2.7 %collective-permute-start.14 = (f32[1,32,32,128]{3,2,1,0:T(8,128)}, f32[1,32,32,128]{3,2,1,0:T(8,128)S(1)}, u32[]{:S(2)}, u32[]{:S(2)}) collective-permute-start(f32[1,32,32,128]{3,2,1,0:T(8,128)} %add_select_fusion.2), channel_id=1, source_target_pairs={{0,96},{4,100},{8,104},{12,108},{16,112},{20,116},{24,120},{28,124... | collective-permute-start | bytes 1572872 | tf_op jit(solution)/shard_map/ppermute | solution.py:21
  113.8 11.1 %collective-permute-done.15 = f32[1,32,32,128]{3,2,1,0:T(8,128)} collective-permute-done((f32[1,32,32,128]{3,2,1,0:T(8,128)}, f32[1,32,32,128]{3,2,1,0:T(8,128)}, u32[]{:S(2)}, u32[]{:S(2)}) %collective-permute-start.15) | collective-permute-done | bytes 524320 | tf_op jit(solution)/shard_map/ppermute | solution.py:21
  124.9 1.7 slice.331
  127.7 3.3 %collective-permute-start.17 = (f32[1,32,16,128]{3,2,1,0:T(8,128)S(1)}, f32[1,32,16,128]{3,2,1,0:T(8,128)S(1)}, u32[]{:S(2)}, u32[]{:S(2)}) collective-permute-start(f32[1,32,16,128]{3,2,1,0:T(8,128)S(1)} %slice.332), channel_id=1, source_target_pairs={{0,96},{4,100},{8,104},{12,108},{16,112},{20,116},{24,120},{28,124... | collective-permute-start | bytes 786440 | tf_op jit(solution)/shard_map/ppermute | solution.py:21
  131.9 5.0 %collective-permute-done.16 = f32[1,32,16,128]{3,2,1,0:T(8,128)} collective-permute-done((f32[1,32,16,128]{3,2,1,0:T(8,128)}, f32[1,32,16,128]{3,2,1,0:T(8,128)}, u32[]{:S(2)}, u32[]{:S(2)}) %collective-permute-start.16) | collective-permute-done | bytes 262176 | tf_op jit(solution)/shard_map/ppermute | solution.py:21
  138.8 3.2 %multiply_add_fusion = f32[1,32,32,128]{3,2,1,0:T(8,128)} fusion(f32[1,32,32,128]{3,2,1,0:T(8,128)} %collective-permute-done.15, f32[1,32,32,128]{3,2,1,0:T(8,128)S(1)} %constant_dynamic-update-slice_fusion.2, f32[1,32,32,128]{3,2,1,0:T(8,128)} %copy-done.6, f32[1,32,32,128]{3,2,1,0:T(8,128)} %copy-done.4, f32[1,32,32,128]{3,2,1,0:T(8,128)} %copy-done.7, ...), kind=kLoop, calls=%fused_computation.72 | loop fusion | flops 2359296 | bytes 3670918 | tf_op jit(solution)/shard_map/add | solution.py:34
  144.9 1.6 squeeze.26
  146.5 1.6 squeeze.32
  148.1 1.9 add_select_fusion
  150.5 5.3 %fusion.7 = f32[512,1,32,64]{0,3,2,1:T(8,128)S(1)} fusion(f32[32,64,512]{2,1,0:T(8,128)} %fusion, f32[32]{0:T(128)S(1)} %copy-done.65, f32[512,32]{0,1:T(8,128)} %bitcast.226, f32[1,32,64,128]{3,2,1,0:T(8,128)S(1)} %copy-done.3, f32[1,32,32,128]{3,2,1,0:T(8,128)} %collective-permute-done.18, f32[1,32,32,128]{3,2,1,0:T(8,128)} %multiply_add_fusion, ...), kind=kOutput, calls=%fused_computation.11 | convolution fusion | flops 1617428480 | bytes 12779777 | tf_op jit(solution)/shard_map/ipn,phdn->iphd/dot_general | solution.py:178
  155.9 3.4 %multiply_reduce_fusion = (f32[512]{0:T(512)S(1)}, f32[512,1,2048]{0,2,1:T(8,128)}) fusion(bf16[512,1,2048]{0,2,1:T(8,128)(2,1)S(1)} %copy-done, f32[512,1,32,64]{0,3,2,1:T(8,128)S(1)} %fusion.7), kind=kLoop, calls=%fused_computation.15 | loop fusion | flops 8388096 | bytes 10487808 | tf_op jit(solution)/shard_map/reduce_sum | solution.py:185
  159.3 4.0 %collective-permute-start.21 = (f32[512,1]{0,1:T(1,128)S(1)}, f32[512,1]{0,1:T(1,128)S(1)}, u32[]{:S(2)}, u32[]{:S(2)}) collective-permute-start(f32[512,1]{0,1:T(1,128)S(1)} %bitcast.244), channel_id=1, source_target_pairs={{0,3},{1,0},{2,1},{3,2},{4,7},{5,4},{6,5},{7,6},{8,11},{9,8},{10,9... | collective-permute-start | bytes 6152 | tf_op jit(solution)/shard_map/ppermute | solution.py:21
  163.3 1.3 collective-permute-start.19
  164.6 1.6 convolution_multiply_fusion
  168.4 13.3 %fusion.12 = f32[512,4096]{1,0:T(8,128)S(1)} fusion(bf16[2048,4096]{1,0:T(8,128)(2,1)} %param.26, f32[512,1,2048]{0,2,1:T(8,128)} %get-tuple-element.20, f32[2048]{0:T(1024)S(1)} %copy-done.68, f32[512]{0:T(512)S(1)} %bitcast.254), kind=kOutput, calls=%fused_computation.24 | convolution fusion | flops 8593080320 | bytes 29370368 | tf_op jit(solution)/shard_map/tpi,id->tpd/dot_general | solution.py:194
  182.1 1.3 collective-permute-start.25
  184.2 3.0 %dynamic-slice_bitcast_fusion.4 = (f32[128,1,4096]{2,0,1:T(8,128)}, f32[128,1,4096]{2,0,1:T(8,128)}, f32[128,1,4096]{2,0,1:T(8,128)S(1)}, f32[128,1,4096]{2,0,1:T(8,128)S(1)}, f32[128,1,4096]{2,0,1:T(8,128)}) fusion(f32[512,4096]{1,0:T(8,128)S(1)} %fusion.12, s32[]{:T(128)S(6)} %select_n.400, s32[]{:T(128)S(6)} %select_n.410, s32[]{:T(128)S(6)} %select_n.408, ...), kind=kLoop, calls=%fused_computation.31 | loop fusion | bytes 20971540 | tf_op jit(solution)/shard_map/dynamic_slice | solution.py:74
  187.3 10.6 %collective-permute-done.22 = bf16[128,1,2048]{2,0,1:T(8,128)(2,1)} collective-permute-done((bf16[128,1,2048]{2,0,1:T(8,128)(2,1)S(1)}, bf16[128,1,2048]{2,0,1:T(8,128)(2,1)}, u32[]{:S(2)}, u32[]{:S(2)}) %collective-permute-start.22) | collective-permute-done | bytes 524320 | tf_op jit(solution)/shard_map/ppermute | solution.py:21
  197.9 1.5 fusion.23
  199.5 1.9 fusion.20
  201.5 3.2 %collective-permute-start.26 = (bf16[128,1,2048]{2,0,1:T(8,128)(2,1)}, bf16[128,1,2048]{2,0,1:T(8,128)(2,1)}, u32[]{:S(2)}, u32[]{:S(2)}) collective-permute-start(bf16[128,1,2048]{2,0,1:T(8,128)(2,1)} %fusion.20), channel_id=1, source_target_pairs={{0,3},{1,0},{2,1},{3,2},{4,7},{5,4},{6,5},{7,6},{8,11},{9,8},{10,9... | collective-permute-start | bytes 1572872 | tf_op jit(solution)/shard_map/ppermute | solution.py:21
  205.8 7.3 %collective-permute-done.23 = bf16[128,1,2048]{2,0,1:T(8,128)(2,1)} collective-permute-done((bf16[128,1,2048]{2,0,1:T(8,128)(2,1)S(1)}, bf16[128,1,2048]{2,0,1:T(8,128)(2,1)}, u32[]{:S(2)}, u32[]{:S(2)}) %collective-permute-start.23) | collective-permute-done | bytes 524320 | tf_op jit(solution)/shard_map/ppermute | solution.py:21
  213.1 1.5 fusion.22
  214.7 1.5 fusion.19
  216.1 3.6 %collective-permute-start.27 = (bf16[128,1,2048]{2,0,1:T(8,128)(2,1)S(1)}, bf16[128,1,2048]{2,0,1:T(8,128)(2,1)S(1)}, u32[]{:S(2)}, u32[]{:S(2)}) collective-permute-start(bf16[128,1,2048]{2,0,1:T(8,128)(2,1)S(1)} %fusion.19), channel_id=1, source_target_pairs={{0,3},{1,0},{2,1},{3,2},{4,7},{5,4},{6,5},{7,6},{8,11},{9,8},{10,9... | collective-permute-start | bytes 1572872 | tf_op jit(solution)/shard_map/ppermute | solution.py:21
  221.5 5.7 %collective-permute-done.24 = bf16[128,1,2048]{2,0,1:T(8,128)(2,1)S(1)} collective-permute-done((bf16[128,1,2048]{2,0,1:T(8,128)(2,1)S(1)}, bf16[128,1,2048]{2,0,1:T(8,128)(2,1)S(1)}, u32[]{:S(2)}, u32[]{:S(2)}) %collective-permute-start.24) | collective-permute-done | bytes 524320 | tf_op jit(solution)/shard_map/ppermute | solution.py:21
  (297 shorter events, 65.2 us)
Async XLA Ops:
  1.9 34.3 %collective-permute-start.28 = (bf16[3,1,256]{2,0,1:T(4,128)(2,1)}, bf16[3,1,256]{2,0,1:T(4,128)(2,1)}, u32[]{:S(2)}, u32[]{:S(2)}) collective-permute-start(bf16[3,1,256]{2,0,1:T(4,128)(2,1)} %slice.253), channel_id=1, source_target_pairs={{124,60},{125,61},{126,62},{127,63}} | collective-permute-start | bytes 4616 | tf_op jit(solution)/shard_map/ppermute | solution.py:140
  3.1 46.7 %collective-permute-start.1 = (bf16[3,1,256]{2,0,1:T(4,128)(2,1)}, bf16[3,1,256]{2,0,1:T(4,128)(2,1)}, u32[]{:S(2)}, u32[]{:S(2)}) collective-permute-start(bf16[3,1,256]{2,0,1:T(4,128)(2,1)} %slice.253), channel_id=1, source_target_pairs={{0,4},{4,8},{8,12},{12,16},{16,20},{20,24},{24,28},{28,32},{32,36}... | collective-permute-start | bytes 4616 | tf_op jit(solution)/shard_map/ppermute | solution.py:12
  9.7 17.7 %collective-permute-start.2 = (f32[1,32]{1,0:T(1,128)}, f32[1,32]{1,0:T(1,128)}, u32[]{:S(2)}, u32[]{:S(2)}) collective-permute-start(f32[1,32]{1,0:T(1,128)} %bitcast.78), channel_id=1, source_target_pairs={{0,4},{4,0},{8,12},{12,8},{16,20},{20,16},{24,28},{28,24},{32,36},... | collective-permute-start | bytes 392 | tf_op jit(solution)/shard_map/ppermute | solution.py:21
  14.6 46.2 %collective-permute-start.34 = (bf16[3,1,2048]{0,2,1:T(8,128)(2,1)S(1)}, bf16[3,1,2048]{0,2,1:T(8,128)(2,1)S(1)}, u32[]{:S(2)}, u32[]{:S(2)}) collective-permute-start(bf16[3,1,2048]{0,2,1:T(8,128)(2,1)S(1)} %slice.316), channel_id=1, source_target_pairs={{124,60},{125,61},{126,62},{127,63}} | collective-permute-start | bytes 36872 | tf_op jit(solution)/shard_map/ppermute | solution.py:140
  21.0 28.9 %copy-start.40 = (f32[1,256]{1,0:T(1,128)S(1)}, f32[1,256]{1,0:T(1,128)}, u32[]{:S(2)}) copy-start(f32[1,256]{1,0:T(1,128)} %get-tuple-element.63) | copy-start | bytes 3076
  21.0 28.9 %copy-start.41 = (f32[1,256]{1,0:T(1,128)S(1)}, f32[1,256]{1,0:T(1,128)}, u32[]{:S(2)}) copy-start(f32[1,256]{1,0:T(1,128)} %get-tuple-element.64) | copy-start | bytes 3076
  21.0 28.9 %copy-start.42 = (f32[1,256]{1,0:T(1,128)S(1)}, f32[1,256]{1,0:T(1,128)}, u32[]{:S(2)}) copy-start(f32[1,256]{1,0:T(1,128)} %get-tuple-element.65) | copy-start | bytes 3076
  21.0 37.1 %copy-start.55 = (f32[8]{0:T(128)S(1)}, f32[8]{0:T(128)}, u32[]{:S(2)}) copy-start(f32[8]{0:T(128)} %get-tuple-element.70) | copy-start | bytes 100
  26.6 35.6 %copy-start.27 = (f32[1,2048]{1,0:T(1,128)S(1)}, f32[1,2048]{1,0:T(1,128)}, u32[]{:S(2)}) copy-start(f32[1,2048]{1,0:T(1,128)} %get-tuple-element.58) | copy-start | bytes 24580
  26.6 35.6 %copy-start.29 = (f32[1,2048]{1,0:T(1,128)S(1)}, f32[1,2048]{1,0:T(1,128)}, u32[]{:S(2)}) copy-start(f32[1,2048]{1,0:T(1,128)} %get-tuple-element.59) | copy-start | bytes 24580
  26.6 35.6 %copy-start.31 = (f32[1,2048]{1,0:T(1,128)S(1)}, f32[1,2048]{1,0:T(1,128)}, u32[]{:S(2)}) copy-start(f32[1,2048]{1,0:T(1,128)} %get-tuple-element.60) | copy-start | bytes 24580
  26.6 35.6 %copy-start.32 = (f32[1,2048]{1,0:T(1,128)S(1)}, f32[1,2048]{1,0:T(1,128)}, u32[]{:S(2)}) copy-start(f32[1,2048]{1,0:T(1,128)} %get-tuple-element.61) | copy-start | bytes 24580
  28.5 29.6 %copy-start.49 = (f32[1,32]{1,0:T(1,128)}, f32[1,32]{1,0:T(1,128)S(1)}, u32[]{:S(2)}) copy-start(f32[1,32]{1,0:T(1,128)S(1)} %get-tuple-element.68) | copy-start | bytes 388
  28.5 4.8 %collective-permute-start.4 = (f32[1,32]{1,0:T(1,128)S(1)}, f32[1,32]{1,0:T(1,128)S(1)}, u32[]{:S(2)}, u32[]{:S(2)}) collective-permute-start(f32[1,32]{1,0:T(1,128)S(1)} %get-tuple-element.68), channel_id=1, source_target_pairs={{0,8},{4,12},{8,16},{12,20},{16,24},{20,28},{24,0},{28,4},{32,40},... | collective-permute-start | bytes 392 | tf_op jit(solution)/shard_map/ppermute | solution.py:21
  30.1 4.5 %collective-permute-start.3 = (f32[1,32]{1,0:T(1,128)S(1)}, f32[1,32]{1,0:T(1,128)S(1)}, u32[]{:S(2)}, u32[]{:S(2)}) collective-permute-start(f32[1,32]{1,0:T(1,128)S(1)} %get-tuple-element.68), channel_id=1, source_target_pairs={{0,24},{4,28},{8,0},{12,4},{16,8},{20,12},{24,16},{28,20},{32,56},... | collective-permute-start | bytes 392 | tf_op jit(solution)/shard_map/ppermute | solution.py:21
  33.3 28.4 %collective-permute-start = (bf16[3,1,2048]{0,2,1:T(8,128)(2,1)S(1)}, bf16[3,1,2048]{0,2,1:T(8,128)(2,1)S(1)}, u32[]{:S(2)}, u32[]{:S(2)}) collective-permute-start(bf16[3,1,2048]{0,2,1:T(8,128)(2,1)S(1)} %slice.316), channel_id=1, source_target_pairs={{0,4},{4,8},{8,12},{12,16},{16,20},{20,24},{24,28},{28,32},{32,36}... | collective-permute-start | bytes 36872 | tf_op jit(solution)/shard_map/ppermute | solution.py:12
  34.6 4.8 %collective-permute-start.5 = (f32[1,32]{1,0:T(1,128)S(1)}, f32[1,32]{1,0:T(1,128)S(1)}, u32[]{:S(2)}, u32[]{:S(2)}) collective-permute-start(f32[1,32]{1,0:T(1,128)S(1)} %collective-permute-done.4), channel_id=1, source_target_pairs={{0,8},{4,12},{8,16},{12,20},{16,24},{20,28},{24,0},{28,4},{32,40},... | collective-permute-start | bytes 392 | tf_op jit(solution)/shard_map/ppermute | solution.py:21
  36.9 7.4 %collective-permute-start.29 = (bf16[3,1,256]{2,0,1:T(4,128)(2,1)S(1)}, bf16[3,1,256]{2,0,1:T(4,128)(2,1)S(1)}, u32[]{:S(2)}, u32[]{:S(2)}) collective-permute-start(bf16[3,1,256]{2,0,1:T(4,128)(2,1)S(1)} %broadcast_select_fusion.5), channel_id=1, source_target_pairs={{60,28},{124,92},{61,29},{125,93},{62,30},{126,94},{63,31},{127,95}} | collective-permute-start | bytes 4616 | tf_op jit(solution)/shard_map/ppermute | solution.py:140
  40.0 5.6 %collective-permute-start.8 = (f32[1,32]{1,0:T(1,128)S(1)}, f32[1,32]{1,0:T(1,128)S(1)}, u32[]{:S(2)}, u32[]{:S(2)}) collective-permute-start(f32[1,32]{1,0:T(1,128)S(1)} %get-tuple-element.21), channel_id=1, source_target_pairs={{0,96},{4,100},{8,104},{12,108},{16,112},{20,116},{24,120},{28,124... | collective-permute-start | bytes 392 | tf_op jit(solution)/shard_map/ppermute | solution.py:21
  44.3 4.9 %collective-permute-start.6 = (f32[1,32]{1,0:T(1,128)S(1)}, f32[1,32]{1,0:T(1,128)}, u32[]{:S(2)}, u32[]{:S(2)}) collective-permute-start(f32[1,32]{1,0:T(1,128)S(1)} %get-tuple-element.21), channel_id=1, source_target_pairs={{0,32},{4,36},{8,40},{12,44},{16,48},{20,52},{24,56},{28,60},{32,6... | collective-permute-start | bytes 392 | tf_op jit(solution)/shard_map/ppermute | solution.py:21
  45.6 3.6 %collective-permute-start.30 = (bf16[3,1,256]{2,0,1:T(4,128)(2,1)S(1)}, bf16[3,1,256]{2,0,1:T(4,128)(2,1)S(1)}, u32[]{:S(2)}, u32[]{:S(2)}) collective-permute-start(bf16[3,1,256]{2,0,1:T(4,128)(2,1)S(1)} %broadcast_select_fusion.6), channel_id=1, source_target_pairs={{28,12},{60,44},{92,76},{124,108},{29,13},{61,45},{93,77},{125,109... | collective-permute-start | bytes 4616 | tf_op jit(solution)/shard_map/ppermute | solution.py:140
  49.1 88.8 %collective-permute-start.7 = (f32[1,32]{1,0:T(1,128)}, f32[1,32]{1,0:T(1,128)}, u32[]{:S(2)}, u32[]{:S(2)}) collective-permute-start(f32[1,32]{1,0:T(1,128)} %collective-permute-done.6), channel_id=1, source_target_pairs={{0,32},{4,36},{8,40},{12,44},{16,48},{20,52},{24,56},{28,60},{32,6... | collective-permute-start | bytes 392 | tf_op jit(solution)/shard_map/ppermute | solution.py:21
  49.2 2.4 %collective-permute-start.31 = (bf16[3,1,256]{2,0,1:T(4,128)(2,1)S(1)}, bf16[3,1,256]{2,0,1:T(4,128)(2,1)S(1)}, u32[]{:S(2)}, u32[]{:S(2)}) collective-permute-start(bf16[3,1,256]{2,0,1:T(4,128)(2,1)S(1)} %broadcast_select_fusion.7), channel_id=1, source_target_pairs={{12,4},{28,20},{44,36},{60,52},{76,68},{92,84},{108,100},{124,116}... | collective-permute-start | bytes 4616 | tf_op jit(solution)/shard_map/ppermute | solution.py:140
  51.6 6.5 %collective-permute-start.32 = (bf16[3,1,256]{2,0,1:T(4,128)(2,1)S(1)}, bf16[3,1,256]{2,0,1:T(4,128)(2,1)S(1)}, u32[]{:S(2)}, u32[]{:S(2)}) collective-permute-start(bf16[3,1,256]{2,0,1:T(4,128)(2,1)S(1)} %broadcast_select_fusion.8), channel_id=1, source_target_pairs={{4,0},{12,8},{20,16},{28,24},{36,32},{44,40},{52,48},{60,56},{68,6... | collective-permute-start | bytes 4616 | tf_op jit(solution)/shard_map/ppermute | solution.py:140
  61.0 8.4 %collective-permute-start.35 = (bf16[3,1,2048]{0,2,1:T(8,128)(2,1)S(1)}, bf16[3,1,2048]{0,2,1:T(8,128)(2,1)S(1)}, u32[]{:S(2)}, u32[]{:S(2)}) collective-permute-start(bf16[3,1,2048]{0,2,1:T(8,128)(2,1)S(1)} %broadcast_select_fusion), channel_id=1, source_target_pairs={{60,28},{124,92},{61,29},{125,93},{62,30},{126,94},{63,31},{127,95}} | collective-permute-start | bytes 36872 | tf_op jit(solution)/shard_map/ppermute | solution.py:140
  68.6 15.1 %collective-permute-start.9 = (f32[1,32,64,128]{3,2,1,0:T(8,128)S(1)}, f32[1,32,64,128]{3,2,1,0:T(8,128)}, u32[]{:S(2)}, u32[]{:S(2)}) collective-permute-start(f32[1,32,64,128]{3,2,1,0:T(8,128)S(1)} %convolution_bitcast_fusion), channel_id=1, source_target_pairs={{0,4},{4,0},{8,12},{12,8},{16,20},{20,16},{24,28},{28,24},{32,36},... | collective-permute-start | bytes 3145736 | tf_op jit(solution)/shard_map/ppermute | solution.py:21
  70.2 11.6 %collective-permute-start.36 = (bf16[3,1,2048]{0,2,1:T(8,128)(2,1)}, bf16[3,1,2048]{0,2,1:T(8,128)(2,1)}, u32[]{:S(2)}, u32[]{:S(2)}) collective-permute-start(bf16[3,1,2048]{0,2,1:T(8,128)(2,1)} %broadcast_select_fusion.1), channel_id=1, source_target_pairs={{28,12},{60,44},{92,76},{124,108},{29,13},{61,45},{93,77},{125,109... | collective-permute-start | bytes 36872 | tf_op jit(solution)/shard_map/ppermute | solution.py:140
  83.0 19.8 %collective-permute-start.37 = (bf16[3,1,2048]{0,2,1:T(8,128)(2,1)S(1)}, bf16[3,1,2048]{0,2,1:T(8,128)(2,1)S(1)}, u32[]{:S(2)}, u32[]{:S(2)}) collective-permute-start(bf16[3,1,2048]{0,2,1:T(8,128)(2,1)S(1)} %broadcast_select_fusion.2), channel_id=1, source_target_pairs={{12,4},{28,20},{44,36},{60,52},{76,68},{92,84},{108,100},{124,116}... | collective-permute-start | bytes 36872 | tf_op jit(solution)/shard_map/ppermute | solution.py:140
  85.5 13.9 %collective-permute-start.11 = (f32[1,32,32,128]{3,2,1,0:T(8,128)S(1)}, f32[1,32,32,128]{3,2,1,0:T(8,128)S(1)}, u32[]{:S(2)}, u32[]{:S(2)}) collective-permute-start(f32[1,32,32,128]{3,2,1,0:T(8,128)S(1)} %fusion.35), channel_id=1, source_target_pairs={{0,8},{4,12},{8,16},{12,20},{16,24},{20,28},{24,0},{28,4},{32,40},... | collective-permute-start | bytes 1572872 | tf_op jit(solution)/shard_map/ppermute | solution.py:21
  86.7 14.8 %collective-permute-start.10 = (f32[1,32,32,128]{3,2,1,0:T(8,128)S(1)}, f32[1,32,32,128]{3,2,1,0:T(8,128)S(1)}, u32[]{:S(2)}, u32[]{:S(2)}) collective-permute-start(f32[1,32,32,128]{3,2,1,0:T(8,128)S(1)} %fusion.35), channel_id=1, source_target_pairs={{0,24},{4,28},{8,0},{12,4},{16,8},{20,12},{24,16},{28,20},{32,56},... | collective-permute-start | bytes 1572872 | tf_op jit(solution)/shard_map/ppermute | solution.py:21
  99.4 8.1 %collective-permute-start.12 = (f32[1,32,16,128]{3,2,1,0:T(8,128)S(1)}, f32[1,32,16,128]{3,2,1,0:T(8,128)S(1)}, u32[]{:S(2)}, u32[]{:S(2)}) collective-permute-start(f32[1,32,16,128]{3,2,1,0:T(8,128)S(1)} %slice.329), channel_id=1, source_target_pairs={{0,8},{4,12},{8,16},{12,20},{16,24},{20,28},{24,0},{28,4},{32,40},... | collective-permute-start | bytes 786440 | tf_op jit(solution)/shard_map/ppermute | solution.py:21
  101.5 7.2 %collective-permute-start.13 = (f32[1,32,16,128]{3,2,1,0:T(8,128)S(1)}, f32[1,32,16,128]{3,2,1,0:T(8,128)S(1)}, u32[]{:S(2)}, u32[]{:S(2)}) collective-permute-start(f32[1,32,16,128]{3,2,1,0:T(8,128)S(1)} %slice.330), channel_id=1, source_target_pairs={{0,24},{4,28},{8,0},{12,4},{16,8},{20,12},{24,16},{28,20},{32,56},... | collective-permute-start | bytes 786440 | tf_op jit(solution)/shard_map/ppermute | solution.py:21
  102.9 7.7 %collective-permute-start.38 = (bf16[3,1,2048]{0,2,1:T(8,128)(2,1)S(1)}, bf16[3,1,2048]{0,2,1:T(8,128)(2,1)S(1)}, u32[]{:S(2)}, u32[]{:S(2)}) collective-permute-start(bf16[3,1,2048]{0,2,1:T(8,128)(2,1)S(1)} %broadcast_select_fusion.3), channel_id=1, source_target_pairs={{4,0},{12,8},{20,16},{28,24},{36,32},{44,40},{52,48},{60,56},{68,6... | collective-permute-start | bytes 36872 | tf_op jit(solution)/shard_map/ppermute | solution.py:140
  110.0 14.8 %collective-permute-start.15 = (f32[1,32,32,128]{3,2,1,0:T(8,128)}, f32[1,32,32,128]{3,2,1,0:T(8,128)}, u32[]{:S(2)}, u32[]{:S(2)}) collective-permute-start(f32[1,32,32,128]{3,2,1,0:T(8,128)} %add_select_fusion.2), channel_id=1, source_target_pairs={{0,32},{4,36},{8,40},{12,44},{16,48},{20,52},{24,56},{28,60},{32,6... | collective-permute-start | bytes 1572872 | tf_op jit(solution)/shard_map/ppermute | solution.py:21
  111.0 16.7 %collective-permute-start.14 = (f32[1,32,32,128]{3,2,1,0:T(8,128)}, f32[1,32,32,128]{3,2,1,0:T(8,128)S(1)}, u32[]{:S(2)}, u32[]{:S(2)}) collective-permute-start(f32[1,32,32,128]{3,2,1,0:T(8,128)} %add_select_fusion.2), channel_id=1, source_target_pairs={{0,96},{4,100},{8,104},{12,108},{16,112},{20,116},{24,120},{28,124... | collective-permute-start | bytes 1572872 | tf_op jit(solution)/shard_map/ppermute | solution.py:21
  126.5 10.4 %collective-permute-start.16 = (f32[1,32,16,128]{3,2,1,0:T(8,128)}, f32[1,32,16,128]{3,2,1,0:T(8,128)}, u32[]{:S(2)}, u32[]{:S(2)}) collective-permute-start(f32[1,32,16,128]{3,2,1,0:T(8,128)} %slice.331), channel_id=1, source_target_pairs={{0,32},{4,36},{8,40},{12,44},{16,48},{20,52},{24,56},{28,60},{32,6... | collective-permute-start | bytes 786440 | tf_op jit(solution)/shard_map/ppermute | solution.py:21
  127.7 10.2 %collective-permute-start.17 = (f32[1,32,16,128]{3,2,1,0:T(8,128)S(1)}, f32[1,32,16,128]{3,2,1,0:T(8,128)S(1)}, u32[]{:S(2)}, u32[]{:S(2)}) collective-permute-start(f32[1,32,16,128]{3,2,1,0:T(8,128)S(1)} %slice.332), channel_id=1, source_target_pairs={{0,96},{4,100},{8,104},{12,108},{16,112},{20,116},{24,120},{28,124... | collective-permute-start | bytes 786440 | tf_op jit(solution)/shard_map/ppermute | solution.py:21
  141.9 8.6 %collective-permute-start.18 = (f32[1,32,32,128]{3,2,1,0:T(8,128)}, f32[1,32,32,128]{3,2,1,0:T(8,128)}, u32[]{:S(2)}, u32[]{:S(2)}) collective-permute-start(f32[1,32,32,128]{3,2,1,0:T(8,128)} %multiply_add_fusion), channel_id=1, source_target_pairs={{0,4},{4,0},{8,12},{12,8},{16,20},{20,16},{24,28},{28,24},{32,36},... | collective-permute-start | bytes 1572872 | tf_op jit(solution)/shard_map/ppermute | solution.py:21
  150.0 14.5 %collective-permute-start.33 = (f32[1,32,32,128]{3,2,1,0:T(8,128)S(1)}, f32[1,32,32,128]{3,2,1,0:T(8,128)S(1)}, u32[]{:S(2)}, u32[]{:S(2)}) collective-permute-start(f32[1,32,32,128]{3,2,1,0:T(8,128)S(1)} %add_select_fusion), channel_id=1, source_target_pairs={{0,4},{4,0},{8,12},{12,8},{16,20},{20,16},{24,28},{28,24},{32,36},... | collective-permute-start | bytes 1572872 | tf_op jit(solution)/shard_map/ppermute | solution.py:21
  159.3 8.4 %collective-permute-start.21 = (f32[512,1]{0,1:T(1,128)S(1)}, f32[512,1]{0,1:T(1,128)S(1)}, u32[]{:S(2)}, u32[]{:S(2)}) collective-permute-start(f32[512,1]{0,1:T(1,128)S(1)} %bitcast.244), channel_id=1, source_target_pairs={{0,3},{1,0},{2,1},{3,2},{4,7},{5,4},{6,5},{7,6},{8,11},{9,8},{10,9... | collective-permute-start | bytes 6152 | tf_op jit(solution)/shard_map/ppermute | solution.py:21
  163.3 5.1 %collective-permute-start.20 = (f32[512,1]{0,1:T(1,128)S(1)}, f32[512,1]{0,1:T(1,128)S(1)}, u32[]{:S(2)}, u32[]{:S(2)}) collective-permute-start(f32[512,1]{0,1:T(1,128)S(1)} %bitcast.245), channel_id=1, source_target_pairs={{0,2},{1,3},{2,0},{3,1},{4,6},{5,7},{6,4},{7,5},{8,10},{9,11},{10,... | collective-permute-start | bytes 6152 | tf_op jit(solution)/shard_map/ppermute | solution.py:21
  163.3 5.1 %collective-permute-start.19 = (f32[512,1]{0,1:T(1,128)S(1)}, f32[512,1]{0,1:T(1,128)S(1)}, u32[]{:S(2)}, u32[]{:S(2)}) collective-permute-start(f32[512,1]{0,1:T(1,128)S(1)} %bitcast.246), channel_id=1, source_target_pairs={{0,1},{1,2},{2,3},{3,0},{4,5},{5,6},{6,7},{7,4},{8,9},{9,10},{10,1... | collective-permute-start | bytes 6152 | tf_op jit(solution)/shard_map/ppermute | solution.py:21
  182.1 17.4 %collective-permute-start.25 = (bf16[128,1,2048]{2,0,1:T(8,128)(2,1)S(1)}, bf16[128,1,2048]{2,0,1:T(8,128)(2,1)}, u32[]{:S(2)}, u32[]{:S(2)}) collective-permute-start(bf16[128,1,2048]{2,0,1:T(8,128)(2,1)S(1)} %slice.337), channel_id=1, source_target_pairs={{0,3},{1,0},{2,1},{3,2},{4,7},{5,4},{6,5},{7,6},{8,11},{9,8},{10,9... | collective-permute-start | bytes 1572872 | tf_op jit(solution)/shard_map/ppermute | solution.py:21
  183.5 14.5 %collective-permute-start.22 = (bf16[128,1,2048]{2,0,1:T(8,128)(2,1)S(1)}, bf16[128,1,2048]{2,0,1:T(8,128)(2,1)}, u32[]{:S(2)}, u32[]{:S(2)}) collective-permute-start(bf16[128,1,2048]{2,0,1:T(8,128)(2,1)S(1)} %slice.333), channel_id=1, source_target_pairs={{0,1},{1,2},{2,3},{3,0},{4,5},{5,6},{6,7},{7,4},{8,9},{9,10},{10,1... | collective-permute-start | bytes 1572872 | tf_op jit(solution)/shard_map/ppermute | solution.py:21
  199.4 13.7 %collective-permute-start.23 = (bf16[128,1,2048]{2,0,1:T(8,128)(2,1)S(1)}, bf16[128,1,2048]{2,0,1:T(8,128)(2,1)}, u32[]{:S(2)}, u32[]{:S(2)}) collective-permute-start(bf16[128,1,2048]{2,0,1:T(8,128)(2,1)S(1)} %fusion.23), channel_id=1, source_target_pairs={{0,1},{1,2},{2,3},{3,0},{4,5},{5,6},{6,7},{7,4},{8,9},{9,10},{10,1... | collective-permute-start | bytes 1572872 | tf_op jit(solution)/shard_map/ppermute | solution.py:21
  201.5 13.2 %collective-permute-start.26 = (bf16[128,1,2048]{2,0,1:T(8,128)(2,1)}, bf16[128,1,2048]{2,0,1:T(8,128)(2,1)}, u32[]{:S(2)}, u32[]{:S(2)}) collective-permute-start(bf16[128,1,2048]{2,0,1:T(8,128)(2,1)} %fusion.20), channel_id=1, source_target_pairs={{0,3},{1,0},{2,1},{3,2},{4,7},{5,4},{6,5},{7,6},{8,11},{9,8},{10,9... | collective-permute-start | bytes 1572872 | tf_op jit(solution)/shard_map/ppermute | solution.py:21
  214.6 12.7 %collective-permute-start.24 = (bf16[128,1,2048]{2,0,1:T(8,128)(2,1)S(1)}, bf16[128,1,2048]{2,0,1:T(8,128)(2,1)S(1)}, u32[]{:S(2)}, u32[]{:S(2)}) collective-permute-start(bf16[128,1,2048]{2,0,1:T(8,128)(2,1)S(1)} %fusion.22), channel_id=1, source_target_pairs={{0,1},{1,2},{2,3},{3,0},{4,5},{5,6},{6,7},{7,4},{8,9},{9,10},{10,1... | collective-permute-start | bytes 1572872 | tf_op jit(solution)/shard_map/ppermute | solution.py:21
  216.1 12.3 %collective-permute-start.27 = (bf16[128,1,2048]{2,0,1:T(8,128)(2,1)S(1)}, bf16[128,1,2048]{2,0,1:T(8,128)(2,1)S(1)}, u32[]{:S(2)}, u32[]{:S(2)}) collective-permute-start(bf16[128,1,2048]{2,0,1:T(8,128)(2,1)S(1)} %fusion.19), channel_id=1, source_target_pairs={{0,3},{1,0},{2,1},{3,2},{4,7},{5,4},{6,5},{7,6},{8,11},{9,8},{10,9... | collective-permute-start | bytes 1572872 | tf_op jit(solution)/shard_map/ppermute | solution.py:21
  (61 other events, 917.0 us)

commit v4 on v3

--- a/solution.py
+++ b/solution.py
@@ -135,16 +135,19 @@
     here = lax.axis_index("ctx")
     core = here % 2
     tails = (x_in[block_len - conv_taps + 1 :], bc_in[block_len - conv_taps + 1 :])
-    reach = count // 2
-    while reach >= 1:
+    sent = lax.ppermute(tails, "ctx", [(count - 1, count - 2)])
+    tails = pick(here == count - 2, sent, tails)
+    for shift in range(1, 4):
         sent = lax.ppermute(
-            tails,
-            "ctx",
-            [(source, source - reach) for source in range(count) if source % (2 * reach) == 2 * reach - 1],
-        )
-        taking = here % (2 * reach) == reach - 1
-        tails = pick(taking, sent, tails)
-        reach //= 2
+            tails, "ctx", [(count - 2 + c, count - 2 + c - 2 * shift) for c in range(2)]
+        )
+        tails = pick((here >= count - 8) & ((here % 8) // 2 == 3 - shift), sent, tails)
+    rows = count // 8
+    for shift in range(1, rows):
+        sent = lax.ppermute(
+            tails, "ctx", [(count - 8 + j, count - 8 + j - 8 * shift) for j in range(8)]
+        )
+        tails = pick(here // 8 == rows - 1 - shift, sent, tails)
     own = (block_decay, s_local)
     other = group_shift(own, "ctx", count, 1, 2, 1)
     first = pick(core == 0, own, other)

time: 232 us -> 261 us (1.12)
  waiting for transfers between devices: 59.4 us -> 79.1 us
  starting transfers between devices: 49.5 us -> 54.8 us
    ppermute x10 -> x14, waiting for transfers between devices: 4.18 us -> 26.1 us  [the longest x6 26.1 us: body(): lax.ppermute(tails, 'ctx', [(count - 8 + j, count - 8 + j - 8 * shift) fo...]
    ppermute x2, starting transfers between devices: 3.16 us -> 6.42 us  [passed_along(): lax.ppermute(value, axis, [(source, source + steps) for source in range(l...]
    ppermute x10 -> x14, starting transfers between devices: 9.28 us -> 12.1 us  [the longest x6 6.18 us: body(): lax.ppermute(tails, 'ctx', [(count - 8 + j, count - 8 + j - 8 * shift) fo...]
    unnamed x145 -> x141, local copies, waits for them, and re-layouts: 9.45 us -> 10 us
    select_n x12 -> x16, other arithmetic: 6.87 us -> 6.97 us  [pick(): return jax.tree.map(lambda a, b: jnp.where(flag, a, b), first, second)]
  transfers between devices with their start and end apart: 39 -> 43, of which waited for: 16 -> 15; matrix products, arithmetic and copies ran while one was open for 43% -> 39% of each run, Pallas kernels for 0% -> 0%
where the time goes in v4:
time: 261 us; the launch traced here: 259 us
  waiting for transfers between devices  79.1 us (30%)
  starting transfers between devices  54.8 us (21%)
  other arithmetic  49.1 us (19%)
  local copies, waits for them, and re-layouts  40.9 us (16%)
  matrix products  32.8 us (13%)
    ppermute x27, waiting for transfers between devices, group_shift(): return lax.ppermute(value, axis, pairs)  53 us
    ppermute x27, starting transfers between devices, group_shift(): return lax.ppermute(value, axis, pairs)  36.3 us
    ppermute x6, waiting for transfers between devices, body(): lax.ppermute(tails, 'ctx', [(count - 8 + j, count - 8 + j - 8 * shift) fo...  26.1 us
    dot_general x1, matrix products, body(): jnp.einsum('tpi,id->tpd', normed, w_out, preferred_element_type=jnp.float32)  13.3 us
    dot_general x1, matrix products, body(): jnp.einsum('phij,jphd->iphd', mixing, x_heads, preferred_element_type=jnp...  10.5 us
    unnamed x141, local copies, waits for them, and re-layouts  10 us
    convert_element_type x1, other arithmetic, body(): weighted_x = (x_heads * tail_weights[..., None]).astype(jnp.bfloat16)  7.34 us
    select_n x16, other arithmetic, pick(): return jax.tree.map(lambda a, b: jnp.where(flag, a, b), first, second)  6.97 us
  transfers between devices with their start and end apart: 43, of which 15 were waited for; matrix products, arithmetic and copies ran while one was open for 39% of the time, Pallas kernels for 0%

profile of v4, /device:TPU:0, one launch (start us, length us, event | category | flops | bytes accessed | tf_op | source)
XLA Modules:
  0.0 259.0 jit_solution(8590620378708348432)
XLA Ops:
  0.7 1.3 slice.253
  3.2 1.9 collective-permute-start.1
  5.1 2.9 %copy.44 = bf16[512,1,2048]{0,2,1:T(8,128)(2,1)S(1)} copy(bf16[512,1,2048]{2,0,1:T(8,128)(2,1)} %param.16) | data formatting | bytes 4194304 | tf_op args[0]
  8.9 4.6 %collective-permute-start = (bf16[3,1,2048]{0,2,1:T(8,128)(2,1)S(1)}, bf16[3,1,2048]{0,2,1:T(8,128)(2,1)}, u32[]{:S(2)}, u32[]{:S(2)}) collective-permute-start(bf16[3,1,2048]{0,2,1:T(8,128)(2,1)S(1)} %slice.316), channel_id=1, source_target_pairs={{0,4},{4,8},{8,12},{12,16},{16,20},{20,24},{24,28},{28,32},{32,36}... | collective-permute-start | bytes 36872 | tf_op jit(solution)/shard_map/ppermute | solution.py:12
  18.7 1.4 slice_convert_fusion.7
  20.7 1.3 multiply_exponential_fusion
  27.8 3.9 %copy.53 = bf16[512,1,2048]{0,2,1:T(8,128)(2,1)} copy(bf16[512,1,2048]{2,0,1:T(8,128)(2,1)} %param.17) | data formatting | bytes 4194304 | tf_op args[1]
  35.2 4.0 %collective-permute-done.4 = f32[1,32]{1,0:T(1,128)S(1)} collective-permute-done((f32[1,32]{1,0:T(1,128)S(1)}, f32[1,32]{1,0:T(1,128)S(1)}, u32[]{:S(2)}, u32[]{:S(2)}) %collective-permute-start.4) | collective-permute-done | bytes 160 | tf_op jit(solution)/shard_map/ppermute | solution.py:21
  39.7 1.4 collective-permute-start.5
  41.2 1.5 collective-permute-done.3
  45.1 7.2 %collective-permute-start.8 = (f32[1,32]{1,0:T(1,128)S(1)}, f32[1,32]{1,0:T(1,128)S(1)}, u32[]{:S(2)}, u32[]{:S(2)}) collective-permute-start(f32[1,32]{1,0:T(1,128)S(1)} %get-tuple-element.21), channel_id=1, source_target_pairs={{0,96},{4,100},{8,104},{12,108},{16,112},{20,116},{24,120},{28,124... | collective-permute-start | bytes 392 | tf_op jit(solution)/shard_map/ppermute | solution.py:21
  54.7 4.1 %collective-permute-done.6 = f32[1,32]{1,0:T(1,128)} collective-permute-done((f32[1,32]{1,0:T(1,128)S(1)}, f32[1,32]{1,0:T(1,128)}, u32[]{:S(2)}, u32[]{:S(2)}) %collective-permute-start.6) | collective-permute-done | bytes 160 | tf_op jit(solution)/shard_map/ppermute | solution.py:21
  59.5 1.7 multiply_convert_fusion.4
  61.3 1.4 collective-permute-start.34
  64.0 5.8 %collective-permute-done.34 = bf16[3,1,256]{2,0,1:T(4,128)(2,1)S(1)} collective-permute-done((bf16[3,1,256]{2,0,1:T(4,128)(2,1)S(1)}, bf16[3,1,256]{2,0,1:T(4,128)(2,1)S(1)}, u32[]{:S(2)}, u32[]{:S(2)}) %collective-permute-start.34) | collective-permute-done | bytes 1568 | tf_op jit(solution)/shard_map/ppermute | solution.py:147
  75.4 7.3 %fusion.8 = (bf16[512,1,2048]{0,2,1:T(8,128)(2,1)S(1)}, bf16[512,1,2048]{0,2,1:T(8,128)(2,1)}) fusion(f32[2048]{0:T(1024)S(1)} %bitcast.232, bf16[512,1,2048]{0,2,1:T(8,128)(2,1)S(1)} %copy.44, f32[2048]{0:T(1024)S(1)} %bitcast.234, bf16[3,1,2048]{0,2,1:T(8,128)(2,1)} %collective-permute-done, f32[2048]{0:T(1024)S(1)} %bitcast.229, f32[2048]{0:T(1024)S(1)} %bitcast.227, ...), kind=kLoop, calls=%fused_computation.13 | loop fusion | flops 29360128 | bytes 10530816 | tf_op jit(solution)/shard_map/convert_element_type | solution.py:130
  85.2 1.5 collective-permute-start.40
  98.9 1.6 fusion.35
  101.5 2.2 collective-permute-start.10
  103.8 10.5 %fusion = f32[32,64,512]{2,1,0:T(8,128)} fusion(bf16[512,32,64]{0,2,1:T(8,128)(2,1)S(1)} %bitcast.217, f32[32,512]{1,0:T(8,128)S(1)} %copy-done.33, f32[32,512]{1,0:T(8,128)S(1)} %copy-done.34, f32[512,512]{1,0:T(8,128)S(1)} %copy-done.10, pred[512,512]{1,0:T(8,128)(4,1)S(1)} %copy-done.21), kind=kOutput, calls=%fused_computation.1 | convolution fusion | flops 1115684864 | bytes 7733248 | tf_op jit(solution)/shard_map/phij,jphd->iphd/dot_general | solution.py:179
  114.3 1.5 collective-permute-done.11
  116.0 3.5 %collective-permute-start.13 = (f32[1,32,16,128]{3,2,1,0:T(8,128)S(1)}, f32[1,32,16,128]{3,2,1,0:T(8,128)S(1)}, u32[]{:S(2)}, u32[]{:S(2)}) collective-permute-start(f32[1,32,16,128]{3,2,1,0:T(8,128)S(1)} %slice.330), channel_id=1, source_target_pairs={{0,24},{4,28},{8,0},{12,4},{16,8},{20,12},{24,16},{28,20},{32,56},... | collective-permute-start | bytes 786440 | tf_op jit(solution)/shard_map/ppermute | solution.py:21
  120.8 5.1 %collective-permute-done.12 = f32[1,32,16,128]{3,2,1,0:T(8,128)S(1)} collective-permute-done((f32[1,32,16,128]{3,2,1,0:T(8,128)S(1)}, f32[1,32,16,128]{3,2,1,0:T(8,128)S(1)}, u32[]{:S(2)}, u32[]{:S(2)}) %collective-permute-start.12) | collective-permute-done | bytes 262176 | tf_op jit(solution)/shard_map/ppermute | solution.py:21
  128.2 20.3 %collective-permute-done.42 = bf16[3,1,2048]{0,2,1:T(8,128)(2,1)S(1)} collective-permute-done((bf16[3,1,2048]{0,2,1:T(8,128)(2,1)S(1)}, bf16[3,1,2048]{0,2,1:T(8,128)(2,1)S(1)}, u32[]{:S(2)}, u32[]{:S(2)}) %collective-permute-start.42) | collective-permute-done | bytes 12320 | tf_op jit(solution)/shard_map/ppermute | solution.py:147
  149.1 7.8 %collective-permute-done.15 = f32[1,32,32,128]{3,2,1,0:T(8,128)} collective-permute-done((f32[1,32,32,128]{3,2,1,0:T(8,128)}, f32[1,32,32,128]{3,2,1,0:T(8,128)}, u32[]{:S(2)}, u32[]{:S(2)}) %collective-permute-start.15) | collective-permute-done | bytes 524320 | tf_op jit(solution)/shard_map/ppermute | solution.py:21
  156.9 1.7 slice.331
  159.7 3.3 %collective-permute-start.17 = (f32[1,32,16,128]{3,2,1,0:T(8,128)S(1)}, f32[1,32,16,128]{3,2,1,0:T(8,128)S(1)}, u32[]{:S(2)}, u32[]{:S(2)}) collective-permute-start(f32[1,32,16,128]{3,2,1,0:T(8,128)S(1)} %slice.332), channel_id=1, source_target_pairs={{0,96},{4,100},{8,104},{12,108},{16,112},{20,116},{24,120},{28,124... | collective-permute-start | bytes 786440 | tf_op jit(solution)/shard_map/ppermute | solution.py:21
  163.9 2.5 collective-permute-done.16
  168.3 3.2 %multiply_add_fusion = f32[1,32,32,128]{3,2,1,0:T(8,128)} fusion(f32[1,32,32,128]{3,2,1,0:T(8,128)} %collective-permute-done.15, f32[1,32,32,128]{3,2,1,0:T(8,128)S(1)} %constant_dynamic-update-slice_fusion.2, f32[1,32,32,128]{3,2,1,0:T(8,128)} %copy-done.6, f32[1,32,32,128]{3,2,1,0:T(8,128)} %copy-done.4, f32[1,32,32,128]{3,2,1,0:T(8,128)} %copy-done.7, ...), kind=kLoop, calls=%fused_computation.72 | loop fusion | flops 2359296 | bytes 3670918 | tf_op jit(solution)/shard_map/add | solution.py:34
  174.3 1.6 squeeze.26
  175.9 1.6 squeeze.32
  177.5 1.9 add_select_fusion
  180.1 5.3 %fusion.7 = f32[512,1,32,64]{0,3,2,1:T(8,128)S(1)} fusion(f32[32,64,512]{2,1,0:T(8,128)} %fusion, f32[32]{0:T(128)S(1)} %copy-done.63, f32[512,32]{0,1:T(8,128)} %bitcast.226, f32[1,32,64,128]{3,2,1,0:T(8,128)S(1)} %copy-done.3, f32[1,32,32,128]{3,2,1,0:T(8,128)} %collective-permute-done.18, f32[1,32,32,128]{3,2,1,0:T(8,128)} %multiply_add_fusion, ...), kind=kOutput, calls=%fused_computation.11 | convolution fusion | flops 1617428480 | bytes 12779777 | tf_op jit(solution)/shard_map/ipn,phdn->iphd/dot_general | solution.py:181
  185.4 3.4 %multiply_reduce_fusion = (f32[512]{0:T(512)S(1)}, f32[512,1,2048]{0,2,1:T(8,128)}) fusion(bf16[512,1,2048]{0,2,1:T(8,128)(2,1)S(1)} %copy-done, f32[512,1,32,64]{0,3,2,1:T(8,128)S(1)} %fusion.7), kind=kLoop, calls=%fused_computation.15 | loop fusion | flops 8388096 | bytes 10487808 | tf_op jit(solution)/shard_map/reduce_sum | solution.py:188
  188.8 4.0 %collective-permute-start.21 = (f32[512,1]{0,1:T(1,128)S(1)}, f32[512,1]{0,1:T(1,128)S(1)}, u32[]{:S(2)}, u32[]{:S(2)}) collective-permute-start(f32[512,1]{0,1:T(1,128)S(1)} %bitcast.244), channel_id=1, source_target_pairs={{0,3},{1,0},{2,1},{3,2},{4,7},{5,4},{6,5},{7,6},{8,11},{9,8},{10,9... | collective-permute-start | bytes 6152 | tf_op jit(solution)/shard_map/ppermute | solution.py:21
  194.1 1.6 convolution_multiply_fusion
  198.0 13.3 %fusion.12 = f32[512,4096]{1,0:T(8,128)S(1)} fusion(bf16[2048,4096]{1,0:T(8,128)(2,1)} %param.26, f32[512,1,2048]{0,2,1:T(8,128)} %get-tuple-element.20, f32[2048]{0:T(1024)S(1)} %copy-done.66, f32[512]{0:T(512)S(1)} %bitcast.254), kind=kOutput, calls=%fused_computation.24 | convolution fusion | flops 8593080320 | bytes 29370368 | tf_op jit(solution)/shard_map/tpi,id->tpd/dot_general | solution.py:197
  211.7 1.4 collective-permute-start.25
  213.8 2.9 %dynamic-slice_bitcast_fusion.4 = (f32[128,1,4096]{2,0,1:T(8,128)}, f32[128,1,4096]{2,0,1:T(8,128)}, f32[128,1,4096]{2,0,1:T(8,128)S(1)}, f32[128,1,4096]{2,0,1:T(8,128)S(1)}, f32[128,1,4096]{2,0,1:T(8,128)}) fusion(f32[512,4096]{1,0:T(8,128)S(1)} %fusion.12, s32[]{:T(128)S(6)} %select_n.422, s32[]{:T(128)S(6)} %select_n.432, s32[]{:T(128)S(6)} %select_n.430, ...), kind=kLoop, calls=%fused_computation.31 | loop fusion | bytes 20971540 | tf_op jit(solution)/shard_map/dynamic_slice | solution.py:74
  216.8 10.6 %collective-permute-done.22 = bf16[128,1,2048]{2,0,1:T(8,128)(2,1)} collective-permute-done((bf16[128,1,2048]{2,0,1:T(8,128)(2,1)S(1)}, bf16[128,1,2048]{2,0,1:T(8,128)(2,1)}, u32[]{:S(2)}, u32[]{:S(2)}) %collective-permute-start.22) | collective-permute-done | bytes 524320 | tf_op jit(solution)/shard_map/ppermute | solution.py:21
  227.4 1.5 fusion.23
  229.0 1.9 fusion.20
  230.9 3.2 %collective-permute-start.26 = (bf16[128,1,2048]{2,0,1:T(8,128)(2,1)}, bf16[128,1,2048]{2,0,1:T(8,128)(2,1)}, u32[]{:S(2)}, u32[]{:S(2)}) collective-permute-start(bf16[128,1,2048]{2,0,1:T(8,128)(2,1)} %fusion.20), channel_id=1, source_target_pairs={{0,3},{1,0},{2,1},{3,2},{4,7},{5,4},{6,5},{7,6},{8,11},{9,8},{10,9... | collective-permute-start | bytes 1572872 | tf_op jit(solution)/shard_map/ppermute | solution.py:21
  235.2 7.2 %collective-permute-done.23 = bf16[128,1,2048]{2,0,1:T(8,128)(2,1)} collective-permute-done((bf16[128,1,2048]{2,0,1:T(8,128)(2,1)S(1)}, bf16[128,1,2048]{2,0,1:T(8,128)(2,1)}, u32[]{:S(2)}, u32[]{:S(2)}) %collective-permute-start.23) | collective-permute-done | bytes 524320 | tf_op jit(solution)/shard_map/ppermute | solution.py:21
  242.4 1.5 fusion.22
  244.0 1.5 fusion.19
  245.5 3.6 %collective-permute-start.27 = (bf16[128,1,2048]{2,0,1:T(8,128)(2,1)S(1)}, bf16[128,1,2048]{2,0,1:T(8,128)(2,1)S(1)}, u32[]{:S(2)}, u32[]{:S(2)}) collective-permute-start(bf16[128,1,2048]{2,0,1:T(8,128)(2,1)S(1)} %fusion.19), channel_id=1, source_target_pairs={{0,3},{1,0},{2,1},{3,2},{4,7},{5,4},{6,5},{7,6},{8,11},{9,8},{10,9... | collective-permute-start | bytes 1572872 | tf_op jit(solution)/shard_map/ppermute | solution.py:21
  250.9 5.6 %collective-permute-done.24 = bf16[128,1,2048]{2,0,1:T(8,128)(2,1)S(1)} collective-permute-done((bf16[128,1,2048]{2,0,1:T(8,128)(2,1)S(1)}, bf16[128,1,2048]{2,0,1:T(8,128)(2,1)S(1)}, u32[]{:S(2)}, u32[]{:S(2)}) %collective-permute-start.24) | collective-permute-done | bytes 524320 | tf_op jit(solution)/shard_map/ppermute | solution.py:21
  (305 shorter events, 67.0 us)
Async XLA Ops:
  2.0 29.7 %collective-permute-start.28 = (bf16[3,1,256]{2,0,1:T(4,128)(2,1)}, bf16[3,1,256]{2,0,1:T(4,128)(2,1)}, u32[]{:S(2)}, u32[]{:S(2)}) collective-permute-start(bf16[3,1,256]{2,0,1:T(4,128)(2,1)} %slice.253), channel_id=1, source_target_pairs={{124,120},{125,121},{126,122},{127,123}} | collective-permute-start | bytes 4616 | tf_op jit(solution)/shard_map/ppermute | solution.py:138
  3.2 56.3 %collective-permute-start.1 = (bf16[3,1,256]{2,0,1:T(4,128)(2,1)}, bf16[3,1,256]{2,0,1:T(4,128)(2,1)}, u32[]{:S(2)}, u32[]{:S(2)}) collective-permute-start(bf16[3,1,256]{2,0,1:T(4,128)(2,1)} %slice.253), channel_id=1, source_target_pairs={{0,4},{4,8},{8,12},{12,16},{16,20},{20,24},{24,28},{28,32},{32,36}... | collective-permute-start | bytes 4616 | tf_op jit(solution)/shard_map/ppermute | solution.py:12
  8.2 64.2 %collective-permute-start.36 = (bf16[3,1,2048]{0,2,1:T(8,128)(2,1)S(1)}, bf16[3,1,2048]{0,2,1:T(8,128)(2,1)S(1)}, u32[]{:S(2)}, u32[]{:S(2)}) collective-permute-start(bf16[3,1,2048]{0,2,1:T(8,128)(2,1)S(1)} %slice.316), channel_id=1, source_target_pairs={{124,120},{125,121},{126,122},{127,123}} | collective-permute-start | bytes 36872 | tf_op jit(solution)/shard_map/ppermute | solution.py:138
  8.9 65.9 %collective-permute-start = (bf16[3,1,2048]{0,2,1:T(8,128)(2,1)S(1)}, bf16[3,1,2048]{0,2,1:T(8,128)(2,1)}, u32[]{:S(2)}, u32[]{:S(2)}) collective-permute-start(bf16[3,1,2048]{0,2,1:T(8,128)(2,1)S(1)} %slice.316), channel_id=1, source_target_pairs={{0,4},{4,8},{8,12},{12,16},{16,20},{20,24},{24,28},{28,32},{32,36}... | collective-permute-start | bytes 36872 | tf_op jit(solution)/shard_map/ppermute | solution.py:12
  16.6 16.5 %collective-permute-start.2 = (f32[1,32]{1,0:T(1,128)}, f32[1,32]{1,0:T(1,128)}, u32[]{:S(2)}, u32[]{:S(2)}) collective-permute-start(f32[1,32]{1,0:T(1,128)} %bitcast.78), channel_id=1, source_target_pairs={{0,4},{4,0},{8,12},{12,8},{16,20},{20,16},{24,28},{28,24},{32,36},... | collective-permute-start | bytes 392 | tf_op jit(solution)/shard_map/ppermute | solution.py:21
  23.5 46.3 %copy-start.54 = (f32[8]{0:T(128)S(1)}, f32[8]{0:T(128)}, u32[]{:S(2)}) copy-start(f32[8]{0:T(128)} %get-tuple-element.70) | copy-start | bytes 100
  32.4 7.3 %collective-permute-start.29 = (bf16[3,1,256]{2,0,1:T(4,128)(2,1)S(1)}, bf16[3,1,256]{2,0,1:T(4,128)(2,1)S(1)}, u32[]{:S(2)}, u32[]{:S(2)}) collective-permute-start(bf16[3,1,256]{2,0,1:T(4,128)(2,1)S(1)} %broadcast_select_fusion.7), channel_id=1, source_target_pairs={{120,112},{124,116},{121,113},{125,117},{122,114},{126,118},{123,1... | collective-permute-start | bytes 4616 | tf_op jit(solution)/shard_map/ppermute | solution.py:141
  34.3 40.9 %copy-start.47 = (f32[1,32]{1,0:T(1,128)}, f32[1,32]{1,0:T(1,128)S(1)}, u32[]{:S(2)}) copy-start(f32[1,32]{1,0:T(1,128)S(1)} %get-tuple-element.68) | copy-start | bytes 388
  34.3 4.8 %collective-permute-start.4 = (f32[1,32]{1,0:T(1,128)S(1)}, f32[1,32]{1,0:T(1,128)S(1)}, u32[]{:S(2)}, u32[]{:S(2)}) collective-permute-start(f32[1,32]{1,0:T(1,128)S(1)} %get-tuple-element.68), channel_id=1, source_target_pairs={{0,8},{4,12},{8,16},{12,20},{16,24},{20,28},{24,0},{28,4},{32,40},... | collective-permute-start | bytes 392 | tf_op jit(solution)/shard_map/ppermute | solution.py:21
  39.1 3.6 %collective-permute-start.3 = (f32[1,32]{1,0:T(1,128)S(1)}, f32[1,32]{1,0:T(1,128)S(1)}, u32[]{:S(2)}, u32[]{:S(2)}) collective-permute-start(f32[1,32]{1,0:T(1,128)S(1)} %get-tuple-element.68), channel_id=1, source_target_pairs={{0,24},{4,28},{8,0},{12,4},{16,8},{20,12},{24,16},{28,20},{32,56},... | collective-permute-start | bytes 392 | tf_op jit(solution)/shard_map/ppermute | solution.py:21
  39.7 4.8 %collective-permute-start.5 = (f32[1,32]{1,0:T(1,128)S(1)}, f32[1,32]{1,0:T(1,128)S(1)}, u32[]{:S(2)}, u32[]{:S(2)}) collective-permute-start(f32[1,32]{1,0:T(1,128)S(1)} %collective-permute-done.4), channel_id=1, source_target_pairs={{0,8},{4,12},{8,16},{12,20},{16,24},{20,28},{24,0},{28,4},{32,40},... | collective-permute-start | bytes 392 | tf_op jit(solution)/shard_map/ppermute | solution.py:21
  42.7 1.2 collective-permute-start.30
  43.9 8.4 %collective-permute-start.31 = (bf16[3,1,256]{2,0,1:T(4,128)(2,1)S(1)}, bf16[3,1,256]{2,0,1:T(4,128)(2,1)S(1)}, u32[]{:S(2)}, u32[]{:S(2)}) collective-permute-start(bf16[3,1,256]{2,0,1:T(4,128)(2,1)S(1)} %broadcast_select_fusion.9), channel_id=1, source_target_pairs={{120,96},{124,100},{121,97},{125,101},{122,98},{126,102},{123,99},... | collective-permute-start | bytes 4616 | tf_op jit(solution)/shard_map/ppermute | solution.py:141
  45.1 8.5 %collective-permute-start.8 = (f32[1,32]{1,0:T(1,128)S(1)}, f32[1,32]{1,0:T(1,128)S(1)}, u32[]{:S(2)}, u32[]{:S(2)}) collective-permute-start(f32[1,32]{1,0:T(1,128)S(1)} %get-tuple-element.21), channel_id=1, source_target_pairs={{0,96},{4,100},{8,104},{12,108},{16,112},{20,116},{24,120},{28,124... | collective-permute-start | bytes 392 | tf_op jit(solution)/shard_map/ppermute | solution.py:21
  52.2 6.6 %collective-permute-start.6 = (f32[1,32]{1,0:T(1,128)S(1)}, f32[1,32]{1,0:T(1,128)}, u32[]{:S(2)}, u32[]{:S(2)}) collective-permute-start(f32[1,32]{1,0:T(1,128)S(1)} %get-tuple-element.21), channel_id=1, source_target_pairs={{0,32},{4,36},{8,40},{12,44},{16,48},{20,52},{24,56},{28,60},{32,6... | collective-permute-start | bytes 392 | tf_op jit(solution)/shard_map/ppermute | solution.py:21
  53.5 5.3 %collective-permute-start.32 = (bf16[3,1,256]{2,0,1:T(4,128)(2,1)S(1)}, bf16[3,1,256]{2,0,1:T(4,128)(2,1)S(1)}, u32[]{:S(2)}, u32[]{:S(2)}) collective-permute-start(bf16[3,1,256]{2,0,1:T(4,128)(2,1)S(1)} %broadcast_select_fusion.10), channel_id=1, source_target_pairs={{96,64},{100,68},{104,72},{108,76},{112,80},{116,84},{120,88},{124... | collective-permute-start | bytes 4616 | tf_op jit(solution)/shard_map/ppermute | solution.py:147
  58.8 108.7 %collective-permute-start.7 = (f32[1,32]{1,0:T(1,128)}, f32[1,32]{1,0:T(1,128)}, u32[]{:S(2)}, u32[]{:S(2)}) collective-permute-start(f32[1,32]{1,0:T(1,128)} %collective-permute-done.6), channel_id=1, source_target_pairs={{0,32},{4,36},{8,40},{12,44},{16,48},{20,52},{24,56},{28,60},{32,6... | collective-permute-start | bytes 392 | tf_op jit(solution)/shard_map/ppermute | solution.py:21
  58.8 2.4 collective-permute-start.33
  61.3 8.5 %collective-permute-start.34 = (bf16[3,1,256]{2,0,1:T(4,128)(2,1)S(1)}, bf16[3,1,256]{2,0,1:T(4,128)(2,1)S(1)}, u32[]{:S(2)}, u32[]{:S(2)}) collective-permute-start(bf16[3,1,256]{2,0,1:T(4,128)(2,1)S(1)} %broadcast_select_fusion.12), channel_id=1, source_target_pairs={{96,0},{100,4},{104,8},{108,12},{112,16},{116,20},{120,24},{124,28... | collective-permute-start | bytes 4616 | tf_op jit(solution)/shard_map/ppermute | solution.py:147
  72.6 1.4 collective-permute-start.37
  74.0 8.7 %collective-permute-start.38 = (bf16[3,1,2048]{0,2,1:T(8,128)(2,1)S(1)}, bf16[3,1,2048]{0,2,1:T(8,128)(2,1)S(1)}, u32[]{:S(2)}, u32[]{:S(2)}) collective-permute-start(bf16[3,1,2048]{0,2,1:T(8,128)(2,1)S(1)} %broadcast_select_fusion.1), channel_id=1, source_target_pairs={{120,104},{124,108},{121,105},{125,109},{122,106},{126,110},{123,1... | collective-permute-start | bytes 36872 | tf_op jit(solution)/shard_map/ppermute | solution.py:141
  82.8 1.5 collective-permute-start.39
  84.2 14.5 %collective-permute-start.9 = (f32[1,32,64,128]{3,2,1,0:T(8,128)S(1)}, f32[1,32,64,128]{3,2,1,0:T(8,128)}, u32[]{:S(2)}, u32[]{:S(2)}) collective-permute-start(f32[1,32,64,128]{3,2,1,0:T(8,128)S(1)} %convolution_bitcast_fusion), channel_id=1, source_target_pairs={{0,4},{4,0},{8,12},{12,8},{16,20},{20,16},{24,28},{28,24},{32,36},... | collective-permute-start | bytes 3145736 | tf_op jit(solution)/shard_map/ppermute | solution.py:21
  85.2 11.6 %collective-permute-start.40 = (bf16[3,1,2048]{0,2,1:T(8,128)(2,1)}, bf16[3,1,2048]{0,2,1:T(8,128)(2,1)}, u32[]{:S(2)}, u32[]{:S(2)}) collective-permute-start(bf16[3,1,2048]{0,2,1:T(8,128)(2,1)} %broadcast_select_fusion.3), channel_id=1, source_target_pairs={{96,64},{100,68},{104,72},{108,76},{112,80},{116,84},{120,88},{124... | collective-permute-start | bytes 36872 | tf_op jit(solution)/shard_map/ppermute | solution.py:147
  98.0 21.4 %collective-permute-start.41 = (bf16[3,1,2048]{0,2,1:T(8,128)(2,1)S(1)}, bf16[3,1,2048]{0,2,1:T(8,128)(2,1)S(1)}, u32[]{:S(2)}, u32[]{:S(2)}) collective-permute-start(bf16[3,1,2048]{0,2,1:T(8,128)(2,1)S(1)} %broadcast_select_fusion.4), channel_id=1, source_target_pairs={{96,32},{100,36},{104,40},{108,44},{112,48},{116,52},{120,56},{124... | collective-permute-start | bytes 36872 | tf_op jit(solution)/shard_map/ppermute | solution.py:147
  100.4 15.3 %collective-permute-start.11 = (f32[1,32,32,128]{3,2,1,0:T(8,128)S(1)}, f32[1,32,32,128]{3,2,1,0:T(8,128)S(1)}, u32[]{:S(2)}, u32[]{:S(2)}) collective-permute-start(f32[1,32,32,128]{3,2,1,0:T(8,128)S(1)} %fusion.35), channel_id=1, source_target_pairs={{0,8},{4,12},{8,16},{12,20},{16,24},{20,28},{24,0},{28,4},{32,40},... | collective-permute-start | bytes 1572872 | tf_op jit(solution)/shard_map/ppermute | solution.py:21
  101.5 14.4 %collective-permute-start.10 = (f32[1,32,32,128]{3,2,1,0:T(8,128)S(1)}, f32[1,32,32,128]{3,2,1,0:T(8,128)S(1)}, u32[]{:S(2)}, u32[]{:S(2)}) collective-permute-start(f32[1,32,32,128]{3,2,1,0:T(8,128)S(1)} %fusion.35), channel_id=1, source_target_pairs={{0,24},{4,28},{8,0},{12,4},{16,8},{20,12},{24,16},{28,20},{32,56},... | collective-permute-start | bytes 1572872 | tf_op jit(solution)/shard_map/ppermute | solution.py:21
  115.8 10.0 %collective-permute-start.12 = (f32[1,32,16,128]{3,2,1,0:T(8,128)S(1)}, f32[1,32,16,128]{3,2,1,0:T(8,128)S(1)}, u32[]{:S(2)}, u32[]{:S(2)}) collective-permute-start(f32[1,32,16,128]{3,2,1,0:T(8,128)S(1)} %slice.329), channel_id=1, source_target_pairs={{0,8},{4,12},{8,16},{12,20},{16,24},{20,28},{24,0},{28,4},{32,40},... | collective-permute-start | bytes 786440 | tf_op jit(solution)/shard_map/ppermute | solution.py:21
  115.9 42.6 %copy-start.23 = (bf16[4,8,2048]{2,1,0:T(8,128)(2,1)S(1)}, bf16[4,8,2048]{2,1,0:T(8,128)(2,1)}, u32[]{:S(2)}) copy-start(bf16[4,8,2048]{2,1,0:T(8,128)(2,1)} %param.28) | copy-start | bytes 393220
  115.9 42.6 %copy-start.28 = (f32[1,2048]{1,0:T(1,128)S(1)}, f32[1,2048]{1,0:T(1,128)}, u32[]{:S(2)}) copy-start(f32[1,2048]{1,0:T(1,128)} %get-tuple-element.58) | copy-start | bytes 24580
  116.0 42.6 %copy-start.30 = (f32[1,2048]{1,0:T(1,128)S(1)}, f32[1,2048]{1,0:T(1,128)}, u32[]{:S(2)}) copy-start(f32[1,2048]{1,0:T(1,128)} %get-tuple-element.59) | copy-start | bytes 24580
  116.0 9.9 %collective-permute-start.13 = (f32[1,32,16,128]{3,2,1,0:T(8,128)S(1)}, f32[1,32,16,128]{3,2,1,0:T(8,128)S(1)}, u32[]{:S(2)}, u32[]{:S(2)}) collective-permute-start(f32[1,32,16,128]{3,2,1,0:T(8,128)S(1)} %slice.330), channel_id=1, source_target_pairs={{0,24},{4,28},{8,0},{12,4},{16,8},{20,12},{24,16},{28,20},{32,56},... | collective-permute-start | bytes 786440 | tf_op jit(solution)/shard_map/ppermute | solution.py:21
  119.5 29.0 %collective-permute-start.42 = (bf16[3,1,2048]{0,2,1:T(8,128)(2,1)S(1)}, bf16[3,1,2048]{0,2,1:T(8,128)(2,1)S(1)}, u32[]{:S(2)}, u32[]{:S(2)}) collective-permute-start(bf16[3,1,2048]{0,2,1:T(8,128)(2,1)S(1)} %broadcast_select_fusion.5), channel_id=1, source_target_pairs={{96,0},{100,4},{104,8},{108,12},{112,16},{116,20},{120,24},{124,28... | collective-permute-start | bytes 36872 | tf_op jit(solution)/shard_map/ppermute | solution.py:147
  127.2 29.7 %collective-permute-start.15 = (f32[1,32,32,128]{3,2,1,0:T(8,128)}, f32[1,32,32,128]{3,2,1,0:T(8,128)}, u32[]{:S(2)}, u32[]{:S(2)}) collective-permute-start(f32[1,32,32,128]{3,2,1,0:T(8,128)} %add_select_fusion.2), channel_id=1, source_target_pairs={{0,32},{4,36},{8,40},{12,44},{16,48},{20,52},{24,56},{28,60},{32,6... | collective-permute-start | bytes 1572872 | tf_op jit(solution)/shard_map/ppermute | solution.py:21
  148.9 10.8 %collective-permute-start.14 = (f32[1,32,32,128]{3,2,1,0:T(8,128)}, f32[1,32,32,128]{3,2,1,0:T(8,128)S(1)}, u32[]{:S(2)}, u32[]{:S(2)}) collective-permute-start(f32[1,32,32,128]{3,2,1,0:T(8,128)} %add_select_fusion.2), channel_id=1, source_target_pairs={{0,96},{4,100},{8,104},{12,108},{16,112},{20,116},{24,120},{28,124... | collective-permute-start | bytes 1572872 | tf_op jit(solution)/shard_map/ppermute | solution.py:21
  158.6 7.9 %collective-permute-start.16 = (f32[1,32,16,128]{3,2,1,0:T(8,128)}, f32[1,32,16,128]{3,2,1,0:T(8,128)}, u32[]{:S(2)}, u32[]{:S(2)}) collective-permute-start(f32[1,32,16,128]{3,2,1,0:T(8,128)} %slice.331), channel_id=1, source_target_pairs={{0,32},{4,36},{8,40},{12,44},{16,48},{20,52},{24,56},{28,60},{32,6... | collective-permute-start | bytes 786440 | tf_op jit(solution)/shard_map/ppermute | solution.py:21
  159.7 7.7 %collective-permute-start.17 = (f32[1,32,16,128]{3,2,1,0:T(8,128)S(1)}, f32[1,32,16,128]{3,2,1,0:T(8,128)S(1)}, u32[]{:S(2)}, u32[]{:S(2)}) collective-permute-start(f32[1,32,16,128]{3,2,1,0:T(8,128)S(1)} %slice.332), channel_id=1, source_target_pairs={{0,96},{4,100},{8,104},{12,108},{16,112},{20,116},{24,120},{28,124... | collective-permute-start | bytes 786440 | tf_op jit(solution)/shard_map/ppermute | solution.py:21
  171.5 8.6 %collective-permute-start.18 = (f32[1,32,32,128]{3,2,1,0:T(8,128)}, f32[1,32,32,128]{3,2,1,0:T(8,128)}, u32[]{:S(2)}, u32[]{:S(2)}) collective-permute-start(f32[1,32,32,128]{3,2,1,0:T(8,128)} %multiply_add_fusion), channel_id=1, source_target_pairs={{0,4},{4,0},{8,12},{12,8},{16,20},{20,16},{24,28},{28,24},{32,36},... | collective-permute-start | bytes 1572872 | tf_op jit(solution)/shard_map/ppermute | solution.py:21
  179.4 14.7 %collective-permute-start.35 = (f32[1,32,32,128]{3,2,1,0:T(8,128)S(1)}, f32[1,32,32,128]{3,2,1,0:T(8,128)S(1)}, u32[]{:S(2)}, u32[]{:S(2)}) collective-permute-start(f32[1,32,32,128]{3,2,1,0:T(8,128)S(1)} %add_select_fusion), channel_id=1, source_target_pairs={{0,4},{4,0},{8,12},{12,8},{16,20},{20,16},{24,28},{28,24},{32,36},... | collective-permute-start | bytes 1572872 | tf_op jit(solution)/shard_map/ppermute | solution.py:21
  188.8 8.4 %collective-permute-start.21 = (f32[512,1]{0,1:T(1,128)S(1)}, f32[512,1]{0,1:T(1,128)S(1)}, u32[]{:S(2)}, u32[]{:S(2)}) collective-permute-start(f32[512,1]{0,1:T(1,128)S(1)} %bitcast.244), channel_id=1, source_target_pairs={{0,3},{1,0},{2,1},{3,2},{4,7},{5,4},{6,5},{7,6},{8,11},{9,8},{10,9... | collective-permute-start | bytes 6152 | tf_op jit(solution)/shard_map/ppermute | solution.py:21
  192.9 5.1 %collective-permute-start.20 = (f32[512,1]{0,1:T(1,128)S(1)}, f32[512,1]{0,1:T(1,128)S(1)}, u32[]{:S(2)}, u32[]{:S(2)}) collective-permute-start(f32[512,1]{0,1:T(1,128)S(1)} %bitcast.245), channel_id=1, source_target_pairs={{0,2},{1,3},{2,0},{3,1},{4,6},{5,7},{6,4},{7,5},{8,10},{9,11},{10,... | collective-permute-start | bytes 6152 | tf_op jit(solution)/shard_map/ppermute | solution.py:21
  192.9 5.1 %collective-permute-start.19 = (f32[512,1]{0,1:T(1,128)S(1)}, f32[512,1]{0,1:T(1,128)S(1)}, u32[]{:S(2)}, u32[]{:S(2)}) collective-permute-start(f32[512,1]{0,1:T(1,128)S(1)} %bitcast.246), channel_id=1, source_target_pairs={{0,1},{1,2},{2,3},{3,0},{4,5},{5,6},{6,7},{7,4},{8,9},{9,10},{10,1... | collective-permute-start | bytes 6152 | tf_op jit(solution)/shard_map/ppermute | solution.py:21
  211.7 17.3 %collective-permute-start.25 = (bf16[128,1,2048]{2,0,1:T(8,128)(2,1)S(1)}, bf16[128,1,2048]{2,0,1:T(8,128)(2,1)}, u32[]{:S(2)}, u32[]{:S(2)}) collective-permute-start(bf16[128,1,2048]{2,0,1:T(8,128)(2,1)S(1)} %slice.337), channel_id=1, source_target_pairs={{0,3},{1,0},{2,1},{3,2},{4,7},{5,4},{6,5},{7,6},{8,11},{9,8},{10,9... | collective-permute-start | bytes 1572872 | tf_op jit(solution)/shard_map/ppermute | solution.py:21
  213.1 14.3 %collective-permute-start.22 = (bf16[128,1,2048]{2,0,1:T(8,128)(2,1)S(1)}, bf16[128,1,2048]{2,0,1:T(8,128)(2,1)}, u32[]{:S(2)}, u32[]{:S(2)}) collective-permute-start(bf16[128,1,2048]{2,0,1:T(8,128)(2,1)S(1)} %slice.333), channel_id=1, source_target_pairs={{0,1},{1,2},{2,3},{3,0},{4,5},{5,6},{6,7},{7,4},{8,9},{9,10},{10,1... | collective-permute-start | bytes 1572872 | tf_op jit(solution)/shard_map/ppermute | solution.py:21
  228.9 13.6 %collective-permute-start.23 = (bf16[128,1,2048]{2,0,1:T(8,128)(2,1)S(1)}, bf16[128,1,2048]{2,0,1:T(8,128)(2,1)}, u32[]{:S(2)}, u32[]{:S(2)}) collective-permute-start(bf16[128,1,2048]{2,0,1:T(8,128)(2,1)S(1)} %fusion.23), channel_id=1, source_target_pairs={{0,1},{1,2},{2,3},{3,0},{4,5},{5,6},{6,7},{7,4},{8,9},{9,10},{10,1... | collective-permute-start | bytes 1572872 | tf_op jit(solution)/shard_map/ppermute | solution.py:21
  230.9 13.1 %collective-permute-start.26 = (bf16[128,1,2048]{2,0,1:T(8,128)(2,1)}, bf16[128,1,2048]{2,0,1:T(8,128)(2,1)}, u32[]{:S(2)}, u32[]{:S(2)}) collective-permute-start(bf16[128,1,2048]{2,0,1:T(8,128)(2,1)} %fusion.20), channel_id=1, source_target_pairs={{0,3},{1,0},{2,1},{3,2},{4,7},{5,4},{6,5},{7,6},{8,11},{9,8},{10,9... | collective-permute-start | bytes 1572872 | tf_op jit(solution)/shard_map/ppermute | solution.py:21
  243.9 12.6 %collective-permute-start.24 = (bf16[128,1,2048]{2,0,1:T(8,128)(2,1)S(1)}, bf16[128,1,2048]{2,0,1:T(8,128)(2,1)S(1)}, u32[]{:S(2)}, u32[]{:S(2)}) collective-permute-start(bf16[128,1,2048]{2,0,1:T(8,128)(2,1)S(1)} %fusion.22), channel_id=1, source_target_pairs={{0,1},{1,2},{2,3},{3,0},{4,5},{5,6},{6,7},{7,4},{8,9},{9,10},{10,1... | collective-permute-start | bytes 1572872 | tf_op jit(solution)/shard_map/ppermute | solution.py:21
  245.5 12.2 %collective-permute-start.27 = (bf16[128,1,2048]{2,0,1:T(8,128)(2,1)S(1)}, bf16[128,1,2048]{2,0,1:T(8,128)(2,1)S(1)}, u32[]{:S(2)}, u32[]{:S(2)}) collective-permute-start(bf16[128,1,2048]{2,0,1:T(8,128)(2,1)S(1)} %fusion.19), channel_id=1, source_target_pairs={{0,3},{1,0},{2,1},{3,2},{4,7},{5,4},{6,5},{7,6},{8,11},{9,8},{10,9... | collective-permute-start | bytes 1572872 | tf_op jit(solution)/shard_map/ppermute | solution.py:21
  (63 other events, 1108.1 us)

commit v5 on v3

--- a/solution.py
+++ b/solution.py
@@ -135,16 +135,6 @@
     here = lax.axis_index("ctx")
     core = here % 2
     tails = (x_in[block_len - conv_taps + 1 :], bc_in[block_len - conv_taps + 1 :])
-    reach = count // 2
-    while reach >= 1:
-        sent = lax.ppermute(
-            tails,
-            "ctx",
-            [(source, source - reach) for source in range(count) if source % (2 * reach) == 2 * reach - 1],
-        )
-        taking = here % (2 * reach) == reach - 1
-        tails = pick(taking, sent, tails)
-        reach //= 2
     own = (block_decay, s_local)
     other = group_shift(own, "ctx", count, 1, 2, 1)
     first = pick(core == 0, own, other)
@@ -167,6 +157,21 @@
     s_before = jnp.where(
         core == 0, chip_state, first[0][..., None, None] * chip_state + first[1]
     )
+
+    tails, s_before = lax.optimization_barrier((tails, s_before))
+    sent = lax.ppermute(tails, "ctx", [(count - 1, count - 2)])
+    tails = pick(here == count - 2, sent, tails)
+    for shift in range(1, 4):
+        sent = lax.ppermute(
+            tails, "ctx", [(count - 2 + c, count - 2 + c - 2 * shift) for c in range(2)]
+        )
+        tails = pick((here >= count - 8) & ((here % 8) // 2 == 3 - shift), sent, tails)
+    rows = count // 8
+    for shift in range(1, rows):
+        sent = lax.ppermute(
+            tails, "ctx", [(count - 8 + j, count - 8 + j - 8 * shift) for j in range(8)]
+        )
+        tails = pick(here // 8 == rows - 1 - shift, sent, tails)
 
     scores = jnp.einsum("ipn,jpn->pij", c_rows, b_rows, preferred_element_type=jnp.float32)
     position = lax.iota(jnp.int32, block_len)

time: 232 us -> 275 us (1.19)
  waiting for transfers between devices: 59.4 us -> 115 us
  other arithmetic: 46.7 us -> 38.6 us
  starting transfers between devices: 49.5 us -> 55 us
  matrix products: 32.8 us -> 27.6 us
  local copies, waits for them, and re-layouts: 39.1 us -> 35 us
    ppermute x10 -> x14, waiting for transfers between devices: 4.18 us -> 68.1 us  [the longest x6 68.1 us: body(): lax.ppermute(tails, 'ctx', [(count - 8 + j, count - 8 + j - 8 * shift) fo...]
    ppermute x27, waiting for transfers between devices: 55.3 us -> 46.8 us  [group_shift(): return lax.ppermute(value, axis, pairs)]
    squeeze x4, local copies, waits for them, and re-layouts: 5.22 us -> 0.38 us  [body(): pushed[earlier]]
    mul x9, local copies, waits for them, and re-layouts: 5.25 us -> 1.36 us  [body(): y_step = carried[..., None] * from_final[step_index]]
    dot_general x1, matrix products: 5.3 us -> 1.87 us  [body(): jnp.einsum('ipn,phdn->iphd', c_rows.astype(jnp.float32), s_before, precis...]
    ppermute x2, starting transfers between devices: 3.16 us -> 6.4 us  [passed_along(): lax.ppermute(value, axis, [(source, source + steps) for source in range(l...]
    convert_element_type x4, other arithmetic: 6.33 us -> 3.29 us  [passed(): value.astype(jnp.bfloat16)]
    ppermute x10 -> x14, starting transfers between devices: 9.28 us -> 11 us  [the longest x6 5.3 us: body(): lax.ppermute(tails, 'ctx', [(count - 8 + j, count - 8 + j - 8 * shift) fo...]
  transfers between devices with their start and end apart: 39 -> 43, of which waited for: 16 -> 14; matrix products, arithmetic and copies ran while one was open for 43% -> 30% of each run, Pallas kernels for 0% -> 0%
where the time goes in v5:
time: 275 us; the launch traced here: 273 us
  waiting for transfers between devices  115 us (42%)
  starting transfers between devices  55 us (20%)
  other arithmetic  38.6 us (14%)
  local copies, waits for them, and re-layouts  35 us (13%)
  matrix products  27.6 us (10%)
    ppermute x6, waiting for transfers between devices, body(): lax.ppermute(tails, 'ctx', [(count - 8 + j, count - 8 + j - 8 * shift) fo...  68.1 us
    ppermute x27, waiting for transfers between devices, group_shift(): return lax.ppermute(value, axis, pairs)  46.8 us
    ppermute x27, starting transfers between devices, group_shift(): return lax.ppermute(value, axis, pairs)  37.6 us
    dot_general x1, matrix products, body(): jnp.einsum('tpi,id->tpd', normed, w_out, preferred_element_type=jnp.float32)  12.3 us
    dot_general x1, matrix products, body(): jnp.einsum('phij,jphd->iphd', mixing, x_heads, preferred_element_type=jnp...  10.8 us
    unnamed x119, local copies, waits for them, and re-layouts  10.7 us
    convert_element_type x1, other arithmetic, body(): weighted_x = (x_heads * tail_weights[..., None]).astype(jnp.bfloat16)  7.33 us
    ppermute x2, starting transfers between devices, passed_along(): lax.ppermute(value, axis, [(source, source + steps) for source in range(l...  6.4 us
  transfers between devices with their start and end apart: 43, of which 14 were waited for; matrix products, arithmetic and copies ran while one was open for 30% of the time, Pallas kernels for 0%

profile of v5, /device:TPU:0, one launch (start us, length us, event | category | flops | bytes accessed | tf_op | source)
XLA Modules:
  0.0 273.1 jit_solution(17412590408928991663)
XLA Ops:
  1.5 1.3 collective-permute-start.1
  2.8 2.9 %copy.44 = bf16[512,1,2048]{0,2,1:T(8,128)(2,1)S(1)} copy(bf16[512,1,2048]{2,0,1:T(8,128)(2,1)} %param.16) | data formatting | bytes 4194304 | tf_op args[0]
  5.9 5.1 %collective-permute-start = (bf16[3,1,2048]{0,2,1:T(8,128)(2,1)S(1)}, bf16[3,1,2048]{0,2,1:T(8,128)(2,1)}, u32[]{:S(2)}, u32[]{:S(2)}) collective-permute-start(bf16[3,1,2048]{0,2,1:T(8,128)(2,1)S(1)} %slice.316), channel_id=1, source_target_pairs={{0,4},{4,8},{8,12},{12,16},{16,20},{20,24},{24,28},{28,32},{32,36}... | collective-permute-start | bytes 36872 | tf_op jit(solution)/shard_map/ppermute | solution.py:12
  17.3 7.3 %fusion.8 = (bf16[512,1,2048]{0,2,1:T(8,128)(2,1)S(1)}, bf16[512,1,2048]{0,2,1:T(8,128)(2,1)}) fusion(f32[2048]{0:T(1024)S(1)} %bitcast.231, bf16[512,1,2048]{0,2,1:T(8,128)(2,1)S(1)} %copy.44, f32[2048]{0:T(1024)S(1)} %bitcast.233, bf16[3,1,2048]{0,2,1:T(8,128)(2,1)} %collective-permute-done, f32[2048]{0:T(1024)S(1)} %bitcast.228, f32[2048]{0:T(1024)S(1)} %bitcast.226, ...), kind=kLoop, calls=%fused_computation.13 | loop fusion | flops 29360128 | bytes 10530816 | tf_op jit(solution)/shard_map/convert_element_type | solution.py:130
  26.0 2.1 collective-permute-done.2
  30.5 2.0 collective-permute-start.11
  32.5 1.4 collective-permute-start.10
  33.9 1.3 multiply_exponential_fusion
  36.2 10.2 %collective-permute-done.11 = f32[1,32,32,128]{3,2,1,0:T(8,128)S(1)} collective-permute-done((f32[1,32,32,128]{3,2,1,0:T(8,128)}, f32[1,32,32,128]{3,2,1,0:T(8,128)S(1)}, u32[]{:S(2)}, u32[]{:S(2)}) %collective-permute-start.11) | collective-permute-done | bytes 524320 | tf_op jit(solution)/shard_map/ppermute | solution.py:21
  51.1 2.9 %copy.53 = bf16[512,1,2048]{0,2,1:T(8,128)(2,1)S(1)} copy(bf16[512,1,2048]{2,0,1:T(8,128)(2,1)} %param.17) | data formatting | bytes 4194304 | tf_op args[1]
  54.0 1.6 collective-permute-start.4
  55.6 1.7 collective-permute-start.3
  57.3 1.5 collective-permute-done.4
  60.2 2.9 %collective-permute-start.13 = (f32[1,32,16,128]{3,2,1,0:T(8,128)S(1)}, f32[1,32,16,128]{3,2,1,0:T(8,128)S(1)}, u32[]{:S(2)}, u32[]{:S(2)}) collective-permute-start(f32[1,32,16,128]{3,2,1,0:T(8,128)S(1)} %slice.330), channel_id=1, source_target_pairs={{0,24},{4,28},{8,0},{12,4},{16,8},{20,12},{24,16},{28,20},{32,56},... | collective-permute-start | bytes 786440 | tf_op jit(solution)/shard_map/ppermute | solution.py:21
  64.1 2.9 %collective-permute-done.13 = f32[1,32,16,128]{3,2,1,0:T(8,128)S(1)} collective-permute-done((f32[1,32,16,128]{3,2,1,0:T(8,128)S(1)}, f32[1,32,16,128]{3,2,1,0:T(8,128)S(1)}, u32[]{:S(2)}, u32[]{:S(2)}) %collective-permute-start.13) | collective-permute-done | bytes 262176 | tf_op jit(solution)/shard_map/ppermute | solution.py:21
  67.1 2.8 %add_select_fusion.3 = f32[1,32,32,128]{3,2,1,0:T(8,128)} fusion(f32[1,32,32,128]{3,2,1,0:T(8,128)} %copy-done.2, f32[1,32,32,128]{3,2,1,0:T(8,128)S(1)} %constant_dynamic-update-slice_fusion, f32[1,32,32,128]{3,2,1,0:T(8,128)} %collective-permute-done.10, f32[1,32,32,128]{3,2,1,0:T(8,128)} %fusion.33, f32[32]{0:T(128)S(1)} %broadcast_multiply_fusion.2, ...), kind=kLoop, calls=%fused_computation.72 | loop fusion | flops 2490368 | bytes 2622086 | tf_op jit(solution)/shard_map/jit(_where)/select_n | solution.py:38
  69.8 3.3 %collective-permute-start.15 = (f32[1,32,32,128]{3,2,1,0:T(8,128)}, f32[1,32,32,128]{3,2,1,0:T(8,128)S(1)}, u32[]{:S(2)}, u32[]{:S(2)}) collective-permute-start(f32[1,32,32,128]{3,2,1,0:T(8,128)} %add_select_fusion.3), channel_id=1, source_target_pairs={{0,32},{4,36},{8,40},{12,44},{16,48},{20,52},{24,56},{28,60},{32,6... | collective-permute-start | bytes 1572872 | tf_op jit(solution)/shard_map/ppermute | solution.py:21
  73.6 1.3 collective-permute-start.14
  76.3 7.7 %collective-permute-done.15 = f32[1,32,32,128]{3,2,1,0:T(8,128)S(1)} collective-permute-done((f32[1,32,32,128]{3,2,1,0:T(8,128)}, f32[1,32,32,128]{3,2,1,0:T(8,128)S(1)}, u32[]{:S(2)}, u32[]{:S(2)}) %collective-permute-start.15) | collective-permute-done | bytes 524320 | tf_op jit(solution)/shard_map/ppermute | solution.py:21
  86.6 1.6 collective-permute-start.6
  88.2 1.7 collective-permute-start.8
  89.9 3.4 %collective-permute-done.6 = f32[1,32]{1,0:T(1,128)S(1)} collective-permute-done((f32[1,32]{1,0:T(1,128)S(1)}, f32[1,32]{1,0:T(1,128)S(1)}, u32[]{:S(2)}, u32[]{:S(2)}) %collective-permute-start.6) | collective-permute-done | bytes 160 | tf_op jit(solution)/shard_map/ppermute | solution.py:21
  94.4 3.5 %collective-permute-start.17 = (f32[1,32,16,128]{3,2,1,0:T(8,128)S(1)}, f32[1,32,16,128]{3,2,1,0:T(8,128)S(1)}, u32[]{:S(2)}, u32[]{:S(2)}) collective-permute-start(f32[1,32,16,128]{3,2,1,0:T(8,128)S(1)} %slice.332), channel_id=1, source_target_pairs={{0,96},{4,100},{8,104},{12,108},{16,112},{20,116},{24,120},{28,124... | collective-permute-start | bytes 786440 | tf_op jit(solution)/shard_map/ppermute | solution.py:21
  98.8 2.9 %collective-permute-done.17 = f32[1,32,16,128]{3,2,1,0:T(8,128)S(1)} collective-permute-done((f32[1,32,16,128]{3,2,1,0:T(8,128)S(1)}, f32[1,32,16,128]{3,2,1,0:T(8,128)S(1)}, u32[]{:S(2)}, u32[]{:S(2)}) %collective-permute-start.17) | collective-permute-done | bytes 262176 | tf_op jit(solution)/shard_map/ppermute | solution.py:21
  101.8 2.3 multiply_add_fusion
  104.5 1.6 add_select_fusion.1
  107.8 1.9 fusion.31
  110.5 10.8 %fusion.7 = f32[512,1,32,64]{0,3,2,1:T(8,128)S(1)} fusion(f32[32,64,512]{2,1,0:T(8,128)S(1)} %fusion.31, bf16[512,32,64]{0,2,1:T(8,128)(2,1)S(1)} %bitcast.217, f32[32,512]{1,0:T(8,128)S(1)} %copy-done.25, f32[32,512]{1,0:T(8,128)S(1)} %copy-done.26, f32[512,512]{1,0:T(8,128)S(1)} %fusion.41, pred[512,512]{1,0:T(8,128)(4,1)S(1)} %copy-done.18, ...), kind=kOutput, calls=%fused_computation.11 | convolution fusion | flops 1120927744 | bytes 14090368 | tf_op jit(solution)/shard_map/phij,jphd->iphd/dot_general | solution.py:181
  122.1 1.5 multiply_reduce_fusion
  123.6 4.1 %collective-permute-start.21 = (f32[512,1]{0,1:T(1,128)S(1)}, f32[512,1]{0,1:T(1,128)S(1)}, u32[]{:S(2)}, u32[]{:S(2)}) collective-permute-start(f32[512,1]{0,1:T(1,128)S(1)} %bitcast.244), channel_id=1, source_target_pairs={{0,3},{1,0},{2,1},{3,2},{4,7},{5,4},{6,5},{7,6},{8,11},{9,8},{10,9... | collective-permute-start | bytes 6152 | tf_op jit(solution)/shard_map/ppermute | solution.py:21
  127.7 1.3 collective-permute-start.19
  130.3 2.4 collective-permute-done.20
  133.5 12.3 %fusion.12 = f32[512,4096]{1,0:T(8,128)S(1)} fusion(bf16[2048,4096]{1,0:T(8,128)(2,1)} %param.26, f32[512,1,2048]{0,2,1:T(8,128)S(1)} %get-tuple-element.26, f32[2048]{0:T(1024)S(1)} %copy-done.54, f32[512]{0:T(512)S(1)} %bitcast.252), kind=kOutput, calls=%fused_computation.24 | convolution fusion | flops 8593080320 | bytes 29370368 | tf_op jit(solution)/shard_map/tpi,id->tpd/dot_general | solution.py:199
  149.0 1.4 collective-permute-start.22
  150.5 1.3 collective-permute-start.34
  151.8 3.6 %dynamic-slice_bitcast_fusion.4 = (f32[128,1,4096]{2,0,1:T(8,128)}, f32[128,1,4096]{2,0,1:T(8,128)}, f32[128,1,4096]{2,0,1:T(8,128)}, f32[128,1,4096]{2,0,1:T(8,128)S(1)}, f32[128,1,4096]{2,0,1:T(8,128)}) fusion(f32[512,4096]{1,0:T(8,128)S(1)} %fusion.12, s32[]{:T(128)S(6)} %select_n.422, s32[]{:T(128)S(6)} %select_n.432, s32[]{:T(128)S(6)} %select_n.430, ...), kind=kLoop, calls=%fused_computation.31 | loop fusion | bytes 20971540 | tf_op jit(solution)/shard_map/dynamic_slice | solution.py:74
  155.4 9.0 %collective-permute-done.34 = bf16[3,1,256]{2,0,1:T(4,128)(2,1)S(1)} collective-permute-done((bf16[3,1,256]{2,0,1:T(4,128)(2,1)S(1)}, bf16[3,1,256]{2,0,1:T(4,128)(2,1)S(1)}, u32[]{:S(2)}, u32[]{:S(2)}) %collective-permute-start.34) | collective-permute-done | bytes 1568 | tf_op jit(solution)/shard_map/ppermute | solution.py:171
  164.6 1.6 convolution_multiply_fusion
  171.8 1.3 collective-permute-start.42
  181.2 59.1 %collective-permute-done.42 = bf16[3,1,2048]{0,2,1:T(8,128)(2,1)} collective-permute-done((bf16[3,1,2048]{0,2,1:T(8,128)(2,1)S(1)}, bf16[3,1,2048]{0,2,1:T(8,128)(2,1)}, u32[]{:S(2)}, u32[]{:S(2)}) %collective-permute-start.42) | collective-permute-done | bytes 12320 | tf_op jit(solution)/shard_map/ppermute | solution.py:171
  243.2 1.2 fusion.44
  246.1 1.6 fusion.23
  248.4 1.5 fusion.20
  249.9 2.7 collective-permute-start.26
  253.7 6.0 %collective-permute-done.23 = bf16[128,1,2048]{2,0,1:T(8,128)(2,1)S(1)} collective-permute-done((bf16[128,1,2048]{2,0,1:T(8,128)(2,1)S(1)}, bf16[128,1,2048]{2,0,1:T(8,128)(2,1)S(1)}, u32[]{:S(2)}, u32[]{:S(2)}) %collective-permute-start.23) | collective-permute-done | bytes 524320 | tf_op jit(solution)/shard_map/ppermute | solution.py:21
  259.9 1.3 collective-permute-done.26
  261.3 3.4 %collective-permute-start.27 = (bf16[128,1,2048]{2,0,1:T(8,128)(2,1)S(1)}, bf16[128,1,2048]{2,0,1:T(8,128)(2,1)S(1)}, u32[]{:S(2)}, u32[]{:S(2)}) collective-permute-start(bf16[128,1,2048]{2,0,1:T(8,128)(2,1)S(1)} %fusion.19), channel_id=1, source_target_pairs={{0,3},{1,0},{2,1},{3,2},{4,7},{5,4},{6,5},{7,6},{8,11},{9,8},{10,9... | collective-permute-start | bytes 1572872 | tf_op jit(solution)/shard_map/ppermute | solution.py:21
  265.5 5.5 %collective-permute-done.24 = bf16[128,1,2048]{2,0,1:T(8,128)(2,1)S(1)} collective-permute-done((bf16[128,1,2048]{2,0,1:T(8,128)(2,1)S(1)}, bf16[128,1,2048]{2,0,1:T(8,128)(2,1)S(1)}, u32[]{:S(2)}, u32[]{:S(2)}) %collective-permute-start.24) | collective-permute-done | bytes 524320 | tf_op jit(solution)/shard_map/ppermute | solution.py:21
  (284 shorter events, 57.2 us)
Async XLA Ops:
  1.5 13.6 %collective-permute-start.1 = (bf16[3,1,256]{2,0,1:T(4,128)(2,1)S(1)}, bf16[3,1,256]{2,0,1:T(4,128)(2,1)S(1)}, u32[]{:S(2)}, u32[]{:S(2)}) collective-permute-start(bf16[3,1,256]{2,0,1:T(4,128)(2,1)S(1)} %slice.253), channel_id=1, source_target_pairs={{0,4},{4,8},{8,12},{12,16},{16,20},{20,24},{24,28},{28,32},{32,36}... | collective-permute-start | bytes 4616 | tf_op jit(solution)/shard_map/ppermute | solution.py:12
  5.8 18.8 %copy-start.7 = (bf16[3,1,2048]{0,2,1:T(8,128)(2,1)}, bf16[3,1,2048]{0,2,1:T(8,128)(2,1)S(1)}, u32[]{:S(2)}) copy-start(bf16[3,1,2048]{0,2,1:T(8,128)(2,1)S(1)} %slice.316) | copy-start | bytes 36868
  5.9 10.9 %collective-permute-start = (bf16[3,1,2048]{0,2,1:T(8,128)(2,1)S(1)}, bf16[3,1,2048]{0,2,1:T(8,128)(2,1)}, u32[]{:S(2)}, u32[]{:S(2)}) collective-permute-start(bf16[3,1,2048]{0,2,1:T(8,128)(2,1)S(1)} %slice.316), channel_id=1, source_target_pairs={{0,4},{4,8},{8,12},{12,16},{16,20},{20,24},{24,28},{28,32},{32,36}... | collective-permute-start | bytes 36872 | tf_op jit(solution)/shard_map/ppermute | solution.py:12
  25.4 3.9 %collective-permute-start.9 = (f32[1,32,64,128]{3,2,1,0:T(8,128)S(1)}, f32[1,32,64,128]{3,2,1,0:T(8,128)S(1)}, u32[]{:S(2)}, u32[]{:S(2)}) collective-permute-start(f32[1,32,64,128]{3,2,1,0:T(8,128)S(1)} %convolution_bitcast_fusion), channel_id=1, source_target_pairs={{0,4},{4,0},{8,12},{12,8},{16,20},{20,16},{24,28},{28,24},{32,36},... | collective-permute-start | bytes 3145736 | tf_op jit(solution)/shard_map/ppermute | solution.py:21
  25.5 2.6 collective-permute-start.2
  30.5 15.9 %collective-permute-start.11 = (f32[1,32,32,128]{3,2,1,0:T(8,128)}, f32[1,32,32,128]{3,2,1,0:T(8,128)S(1)}, u32[]{:S(2)}, u32[]{:S(2)}) collective-permute-start(f32[1,32,32,128]{3,2,1,0:T(8,128)} %fusion.33), channel_id=1, source_target_pairs={{0,8},{4,12},{8,16},{12,20},{16,24},{20,28},{24,0},{28,4},{32,40},... | collective-permute-start | bytes 1572872 | tf_op jit(solution)/shard_map/ppermute | solution.py:21
  32.5 26.7 %collective-permute-start.10 = (f32[1,32,32,128]{3,2,1,0:T(8,128)}, f32[1,32,32,128]{3,2,1,0:T(8,128)}, u32[]{:S(2)}, u32[]{:S(2)}) collective-permute-start(f32[1,32,32,128]{3,2,1,0:T(8,128)} %fusion.33), channel_id=1, source_target_pairs={{0,24},{4,28},{8,0},{12,4},{16,8},{20,12},{24,16},{28,20},{32,56},... | collective-permute-start | bytes 1572872 | tf_op jit(solution)/shard_map/ppermute | solution.py:21
  47.9 15.2 %collective-permute-start.12 = (f32[1,32,16,128]{3,2,1,0:T(8,128)}, f32[1,32,16,128]{3,2,1,0:T(8,128)}, u32[]{:S(2)}, u32[]{:S(2)}) collective-permute-start(f32[1,32,16,128]{3,2,1,0:T(8,128)} %slice.329), channel_id=1, source_target_pairs={{0,8},{4,12},{8,16},{12,20},{16,24},{20,28},{24,0},{28,4},{32,40},... | collective-permute-start | bytes 786440 | tf_op jit(solution)/shard_map/ppermute | solution.py:21
  54.0 4.9 %collective-permute-start.4 = (f32[1,32]{1,0:T(1,128)}, f32[1,32]{1,0:T(1,128)}, u32[]{:S(2)}, u32[]{:S(2)}) collective-permute-start(f32[1,32]{1,0:T(1,128)} %get-tuple-element.74), channel_id=1, source_target_pairs={{0,8},{4,12},{8,16},{12,20},{16,24},{20,28},{24,0},{28,4},{32,40},... | collective-permute-start | bytes 392 | tf_op jit(solution)/shard_map/ppermute | solution.py:21
  55.6 20.1 %copy-start.17 = (f32[32,1,4,128]{3,2,0,1:T(4,128)S(1)}, f32[32,1,4,128]{3,2,0,1:T(4,128)}, u32[]{:S(2)}) copy-start(f32[32,1,4,128]{3,2,0,1:T(4,128)} %copy.48) | copy-start | bytes 196612
  55.6 30.3 %copy-start.43 = (f32[1,32]{1,0:T(1,128)S(1)}, f32[1,32]{1,0:T(1,128)}, u32[]{:S(2)}) copy-start(f32[1,32]{1,0:T(1,128)} %get-tuple-element.74) | copy-start | bytes 388
  55.6 7.5 %collective-permute-start.3 = (f32[1,32]{1,0:T(1,128)}, f32[1,32]{1,0:T(1,128)S(1)}, u32[]{:S(2)}, u32[]{:S(2)}) collective-permute-start(f32[1,32]{1,0:T(1,128)} %get-tuple-element.74), channel_id=1, source_target_pairs={{0,24},{4,28},{8,0},{12,4},{16,8},{20,12},{24,16},{28,20},{32,56},... | collective-permute-start | bytes 392 | tf_op jit(solution)/shard_map/ppermute | solution.py:21
  58.8 8.2 %collective-permute-start.5 = (f32[1,32]{1,0:T(1,128)}, f32[1,32]{1,0:T(1,128)S(1)}, u32[]{:S(2)}, u32[]{:S(2)}) collective-permute-start(f32[1,32]{1,0:T(1,128)} %collective-permute-done.4), channel_id=1, source_target_pairs={{0,8},{4,12},{8,16},{12,20},{16,24},{20,28},{24,0},{28,4},{32,40},... | collective-permute-start | bytes 392 | tf_op jit(solution)/shard_map/ppermute | solution.py:21
  60.2 6.9 %collective-permute-start.13 = (f32[1,32,16,128]{3,2,1,0:T(8,128)S(1)}, f32[1,32,16,128]{3,2,1,0:T(8,128)S(1)}, u32[]{:S(2)}, u32[]{:S(2)}) collective-permute-start(f32[1,32,16,128]{3,2,1,0:T(8,128)S(1)} %slice.330), channel_id=1, source_target_pairs={{0,24},{4,28},{8,0},{12,4},{16,8},{20,12},{24,16},{28,20},{32,56},... | collective-permute-start | bytes 786440 | tf_op jit(solution)/shard_map/ppermute | solution.py:21
  63.1 23.5 %copy-start.52 = (f32[32]{0:T(128)}, f32[32]{0:T(128)S(1)}, u32[]{:S(2)}) copy-start(f32[32]{0:T(128)S(1)} %broadcast_multiply_fusion.2) | copy-start | bytes 388
  67.1 18.9 %copy-start.42 = (f32[1,32]{1,0:T(1,128)}, f32[1,32]{1,0:T(1,128)S(1)}, u32[]{:S(2)}) copy-start(f32[1,32]{1,0:T(1,128)S(1)} %collective-permute-done.5) | copy-start | bytes 388
  69.8 14.1 %collective-permute-start.15 = (f32[1,32,32,128]{3,2,1,0:T(8,128)}, f32[1,32,32,128]{3,2,1,0:T(8,128)S(1)}, u32[]{:S(2)}, u32[]{:S(2)}) collective-permute-start(f32[1,32,32,128]{3,2,1,0:T(8,128)} %add_select_fusion.3), channel_id=1, source_target_pairs={{0,32},{4,36},{8,40},{12,44},{16,48},{20,52},{24,56},{28,60},{32,6... | collective-permute-start | bytes 1572872 | tf_op jit(solution)/shard_map/ppermute | solution.py:21
  73.6 19.8 %collective-permute-start.14 = (f32[1,32,32,128]{3,2,1,0:T(8,128)}, f32[1,32,32,128]{3,2,1,0:T(8,128)}, u32[]{:S(2)}, u32[]{:S(2)}) collective-permute-start(f32[1,32,32,128]{3,2,1,0:T(8,128)} %add_select_fusion.3), channel_id=1, source_target_pairs={{0,96},{4,100},{8,104},{12,108},{16,112},{20,116},{24,120},{28,124... | collective-permute-start | bytes 1572872 | tf_op jit(solution)/shard_map/ppermute | solution.py:21
  85.5 12.4 %collective-permute-start.16 = (f32[1,32,16,128]{3,2,1,0:T(8,128)}, f32[1,32,16,128]{3,2,1,0:T(8,128)}, u32[]{:S(2)}, u32[]{:S(2)}) collective-permute-start(f32[1,32,16,128]{3,2,1,0:T(8,128)} %slice.331), channel_id=1, source_target_pairs={{0,32},{4,36},{8,40},{12,44},{16,48},{20,52},{24,56},{28,60},{32,6... | collective-permute-start | bytes 786440 | tf_op jit(solution)/shard_map/ppermute | solution.py:21
  86.6 6.7 %collective-permute-start.6 = (f32[1,32]{1,0:T(1,128)S(1)}, f32[1,32]{1,0:T(1,128)S(1)}, u32[]{:S(2)}, u32[]{:S(2)}) collective-permute-start(f32[1,32]{1,0:T(1,128)S(1)} %get-tuple-element.27), channel_id=1, source_target_pairs={{0,32},{4,36},{8,40},{12,44},{16,48},{20,52},{24,56},{28,60},{32,6... | collective-permute-start | bytes 392 | tf_op jit(solution)/shard_map/ppermute | solution.py:21
  88.2 9.6 %collective-permute-start.8 = (f32[1,32]{1,0:T(1,128)S(1)}, f32[1,32]{1,0:T(1,128)S(1)}, u32[]{:S(2)}, u32[]{:S(2)}) collective-permute-start(f32[1,32]{1,0:T(1,128)S(1)} %get-tuple-element.27), channel_id=1, source_target_pairs={{0,96},{4,100},{8,104},{12,108},{16,112},{20,116},{24,120},{28,124... | collective-permute-start | bytes 392 | tf_op jit(solution)/shard_map/ppermute | solution.py:21
  93.4 8.4 %collective-permute-start.7 = (f32[1,32]{1,0:T(1,128)S(1)}, f32[1,32]{1,0:T(1,128)S(1)}, u32[]{:S(2)}, u32[]{:S(2)}) collective-permute-start(f32[1,32]{1,0:T(1,128)S(1)} %collective-permute-done.6), channel_id=1, source_target_pairs={{0,32},{4,36},{8,40},{12,44},{16,48},{20,52},{24,56},{28,60},{32,6... | collective-permute-start | bytes 392 | tf_op jit(solution)/shard_map/ppermute | solution.py:21
  94.4 7.4 %collective-permute-start.17 = (f32[1,32,16,128]{3,2,1,0:T(8,128)S(1)}, f32[1,32,16,128]{3,2,1,0:T(8,128)S(1)}, u32[]{:S(2)}, u32[]{:S(2)}) collective-permute-start(f32[1,32,16,128]{3,2,1,0:T(8,128)S(1)} %slice.332), channel_id=1, source_target_pairs={{0,96},{4,100},{8,104},{12,108},{16,112},{20,116},{24,120},{28,124... | collective-permute-start | bytes 786440 | tf_op jit(solution)/shard_map/ppermute | solution.py:21
  104.1 2.6 collective-permute-start.18
  106.2 58.4 %collective-permute-start.35 = (f32[1,32,32,128]{3,2,1,0:T(8,128)S(1)}, f32[1,32,32,128]{3,2,1,0:T(8,128)S(1)}, u32[]{:S(2)}, u32[]{:S(2)}) collective-permute-start(f32[1,32,32,128]{3,2,1,0:T(8,128)S(1)} %add_select_fusion.1), channel_id=1, source_target_pairs={{0,4},{4,0},{8,12},{12,8},{16,20},{20,16},{24,28},{28,24},{32,36},... | collective-permute-start | bytes 1572872 | tf_op jit(solution)/shard_map/ppermute | solution.py:21
  107.0 2.7 collective-permute-start.28
  109.7 11.5 %collective-permute-start.29 = (bf16[3,1,256]{2,0,1:T(4,128)(2,1)S(1)}, bf16[3,1,256]{2,0,1:T(4,128)(2,1)S(1)}, u32[]{:S(2)}, u32[]{:S(2)}) collective-permute-start(bf16[3,1,256]{2,0,1:T(4,128)(2,1)S(1)} %broadcast_select_fusion.7), channel_id=1, source_target_pairs={{120,112},{124,116},{121,113},{125,117},{122,114},{126,118},{123,1... | collective-permute-start | bytes 4616 | tf_op jit(solution)/shard_map/ppermute | solution.py:165
  121.3 7.6 %collective-permute-start.30 = (bf16[3,1,256]{2,0,1:T(4,128)(2,1)S(1)}, bf16[3,1,256]{2,0,1:T(4,128)(2,1)S(1)}, u32[]{:S(2)}, u32[]{:S(2)}) collective-permute-start(bf16[3,1,256]{2,0,1:T(4,128)(2,1)S(1)} %broadcast_select_fusion.8), channel_id=1, source_target_pairs={{120,104},{124,108},{121,105},{125,109},{122,106},{126,110},{123,1... | collective-permute-start | bytes 4616 | tf_op jit(solution)/shard_map/ppermute | solution.py:165
  123.6 6.1 %collective-permute-start.21 = (f32[512,1]{0,1:T(1,128)S(1)}, f32[512,1]{0,1:T(1,128)S(1)}, u32[]{:S(2)}, u32[]{:S(2)}) collective-permute-start(f32[512,1]{0,1:T(1,128)S(1)} %bitcast.244), channel_id=1, source_target_pairs={{0,3},{1,0},{2,1},{3,2},{4,7},{5,4},{6,5},{7,6},{8,11},{9,8},{10,9... | collective-permute-start | bytes 6152 | tf_op jit(solution)/shard_map/ppermute | solution.py:21
  127.7 5.1 %collective-permute-start.20 = (f32[512,1]{0,1:T(1,128)S(1)}, f32[512,1]{0,1:T(1,128)S(1)}, u32[]{:S(2)}, u32[]{:S(2)}) collective-permute-start(f32[512,1]{0,1:T(1,128)S(1)} %bitcast.245), channel_id=1, source_target_pairs={{0,2},{1,3},{2,0},{3,1},{4,6},{5,7},{6,4},{7,5},{8,10},{9,11},{10,... | collective-permute-start | bytes 6152 | tf_op jit(solution)/shard_map/ppermute | solution.py:21
  127.7 5.1 %collective-permute-start.19 = (f32[512,1]{0,1:T(1,128)S(1)}, f32[512,1]{0,1:T(1,128)S(1)}, u32[]{:S(2)}, u32[]{:S(2)}) collective-permute-start(f32[512,1]{0,1:T(1,128)S(1)} %bitcast.246), channel_id=1, source_target_pairs={{0,1},{1,2},{2,3},{3,0},{4,5},{5,6},{6,7},{7,4},{8,9},{9,10},{10,1... | collective-permute-start | bytes 6152 | tf_op jit(solution)/shard_map/ppermute | solution.py:21
  128.9 37.2 %collective-permute-start.36 = (bf16[3,1,2048]{0,2,1:T(8,128)(2,1)S(1)}, bf16[3,1,2048]{0,2,1:T(8,128)(2,1)S(1)}, u32[]{:S(2)}, u32[]{:S(2)}) collective-permute-start(bf16[3,1,2048]{0,2,1:T(8,128)(2,1)S(1)} %copy-done.8), channel_id=1, source_target_pairs={{124,120},{125,121},{126,122},{127,123}} | collective-permute-start | bytes 36872 | tf_op jit(solution)/shard_map/ppermute | solution.py:162
  129.7 3.1 %collective-permute-start.31 = (bf16[3,1,256]{2,0,1:T(4,128)(2,1)S(1)}, bf16[3,1,256]{2,0,1:T(4,128)(2,1)S(1)}, u32[]{:S(2)}, u32[]{:S(2)}) collective-permute-start(bf16[3,1,256]{2,0,1:T(4,128)(2,1)S(1)} %broadcast_select_fusion.9), channel_id=1, source_target_pairs={{120,96},{124,100},{121,97},{125,101},{122,98},{126,102},{123,99},... | collective-permute-start | bytes 4616 | tf_op jit(solution)/shard_map/ppermute | solution.py:165
  132.8 13.0 %collective-permute-start.32 = (bf16[3,1,256]{2,0,1:T(4,128)(2,1)S(1)}, bf16[3,1,256]{2,0,1:T(4,128)(2,1)S(1)}, u32[]{:S(2)}, u32[]{:S(2)}) collective-permute-start(bf16[3,1,256]{2,0,1:T(4,128)(2,1)S(1)} %broadcast_select_fusion.10), channel_id=1, source_target_pairs={{96,64},{100,68},{104,72},{108,76},{112,80},{116,84},{120,88},{124... | collective-permute-start | bytes 4616 | tf_op jit(solution)/shard_map/ppermute | solution.py:171
  145.8 4.7 %collective-permute-start.33 = (bf16[3,1,256]{2,0,1:T(4,128)(2,1)S(1)}, bf16[3,1,256]{2,0,1:T(4,128)(2,1)S(1)}, u32[]{:S(2)}, u32[]{:S(2)}) collective-permute-start(bf16[3,1,256]{2,0,1:T(4,128)(2,1)S(1)} %broadcast_select_fusion.11), channel_id=1, source_target_pairs={{96,32},{100,36},{104,40},{108,44},{112,48},{116,52},{120,56},{124... | collective-permute-start | bytes 4616 | tf_op jit(solution)/shard_map/ppermute | solution.py:171
  148.4 100.0 %collective-permute-start.25 = (bf16[128,1,2048]{2,0,1:T(8,128)(2,1)}, bf16[128,1,2048]{2,0,1:T(8,128)(2,1)}, u32[]{:S(2)}, u32[]{:S(2)}) collective-permute-start(bf16[128,1,2048]{2,0,1:T(8,128)(2,1)} %slice.337), channel_id=1, source_target_pairs={{0,3},{1,0},{2,1},{3,2},{4,7},{5,4},{6,5},{7,6},{8,11},{9,8},{10,9... | collective-permute-start | bytes 1572872 | tf_op jit(solution)/shard_map/ppermute | solution.py:21
  149.0 97.1 %collective-permute-start.22 = (bf16[128,1,2048]{2,0,1:T(8,128)(2,1)}, bf16[128,1,2048]{2,0,1:T(8,128)(2,1)}, u32[]{:S(2)}, u32[]{:S(2)}) collective-permute-start(bf16[128,1,2048]{2,0,1:T(8,128)(2,1)} %slice.333), channel_id=1, source_target_pairs={{0,1},{1,2},{2,3},{3,0},{4,5},{5,6},{6,7},{7,4},{8,9},{9,10},{10,1... | collective-permute-start | bytes 1572872 | tf_op jit(solution)/shard_map/ppermute | solution.py:21
  150.5 13.9 %collective-permute-start.34 = (bf16[3,1,256]{2,0,1:T(4,128)(2,1)S(1)}, bf16[3,1,256]{2,0,1:T(4,128)(2,1)S(1)}, u32[]{:S(2)}, u32[]{:S(2)}) collective-permute-start(bf16[3,1,256]{2,0,1:T(4,128)(2,1)S(1)} %broadcast_select_fusion.12), channel_id=1, source_target_pairs={{96,0},{100,4},{104,8},{108,12},{112,16},{116,20},{120,24},{124,28... | collective-permute-start | bytes 4616 | tf_op jit(solution)/shard_map/ppermute | solution.py:171
  166.2 0.7 collective-permute-start.37
  167.1 0.7 collective-permute-start.38
  167.8 0.8 collective-permute-start.39
  168.7 1.6 collective-permute-start.40
  170.4 1.4 collective-permute-start.41
  171.8 68.5 %collective-permute-start.42 = (bf16[3,1,2048]{0,2,1:T(8,128)(2,1)S(1)}, bf16[3,1,2048]{0,2,1:T(8,128)(2,1)}, u32[]{:S(2)}, u32[]{:S(2)}) collective-permute-start(bf16[3,1,2048]{0,2,1:T(8,128)(2,1)S(1)} %broadcast_select_fusion.5), channel_id=1, source_target_pairs={{96,0},{100,4},{104,8},{108,12},{112,16},{116,20},{120,24},{124,28... | collective-permute-start | bytes 36872 | tf_op jit(solution)/shard_map/ppermute | solution.py:171
  247.7 12.0 %collective-permute-start.23 = (bf16[128,1,2048]{2,0,1:T(8,128)(2,1)S(1)}, bf16[128,1,2048]{2,0,1:T(8,128)(2,1)S(1)}, u32[]{:S(2)}, u32[]{:S(2)}) collective-permute-start(bf16[128,1,2048]{2,0,1:T(8,128)(2,1)S(1)} %fusion.23), channel_id=1, source_target_pairs={{0,1},{1,2},{2,3},{3,0},{4,5},{5,6},{6,7},{7,4},{8,9},{9,10},{10,1... | collective-permute-start | bytes 1572872 | tf_op jit(solution)/shard_map/ppermute | solution.py:21
  249.9 11.3 %collective-permute-start.26 = (bf16[128,1,2048]{2,0,1:T(8,128)(2,1)S(1)}, bf16[128,1,2048]{2,0,1:T(8,128)(2,1)S(1)}, u32[]{:S(2)}, u32[]{:S(2)}) collective-permute-start(bf16[128,1,2048]{2,0,1:T(8,128)(2,1)S(1)} %fusion.20), channel_id=1, source_target_pairs={{0,3},{1,0},{2,1},{3,2},{4,7},{5,4},{6,5},{7,6},{8,11},{9,8},{10,9... | collective-permute-start | bytes 1572872 | tf_op jit(solution)/shard_map/ppermute | solution.py:21
  259.8 11.1 %collective-permute-start.24 = (bf16[128,1,2048]{2,0,1:T(8,128)(2,1)S(1)}, bf16[128,1,2048]{2,0,1:T(8,128)(2,1)S(1)}, u32[]{:S(2)}, u32[]{:S(2)}) collective-permute-start(bf16[128,1,2048]{2,0,1:T(8,128)(2,1)S(1)} %fusion.22), channel_id=1, source_target_pairs={{0,1},{1,2},{2,3},{3,0},{4,5},{5,6},{6,7},{7,4},{8,9},{9,10},{10,1... | collective-permute-start | bytes 1572872 | tf_op jit(solution)/shard_map/ppermute | solution.py:21
  261.3 10.4 %collective-permute-start.27 = (bf16[128,1,2048]{2,0,1:T(8,128)(2,1)S(1)}, bf16[128,1,2048]{2,0,1:T(8,128)(2,1)S(1)}, u32[]{:S(2)}, u32[]{:S(2)}) collective-permute-start(bf16[128,1,2048]{2,0,1:T(8,128)(2,1)S(1)} %fusion.19), channel_id=1, source_target_pairs={{0,3},{1,0},{2,1},{3,2},{4,7},{5,4},{6,5},{7,6},{8,11},{9,8},{10,9... | collective-permute-start | bytes 1572872 | tf_op jit(solution)/shard_map/ppermute | solution.py:21
  (52 other events, 522.9 us)

commit v6 on v2

--- a/solution.py
+++ b/solution.py
@@ -121,7 +121,15 @@
         tails = pick(taking, sent, tails)
         reach //= 2
     own = (block_decay, s_local)
+    scores = jnp.einsum("ipn,jpn->pij", c_rows, b_rows, preferred_element_type=jnp.float32)
+    position = lax.iota(jnp.int32, block_len)
+    causal = position[:, None] >= position[None, :]
+    gaps = jnp.where(causal, cum_heads[..., :, None] - cum_heads[..., None, :], -jnp.inf)
+    mixing = (scores[:, None] * jnp.exp(gaps) * dt_heads[..., None, :]).astype(jnp.bfloat16)
+    y_intra = jnp.einsum("phij,jphd->iphd", mixing, x_heads, preferred_element_type=jnp.float32)
+    y_local = y_intra + skip[:, None] * x_heads.astype(jnp.float32)
     other = group_shift(own, "ctx", count, 1, 2, 1)
+    other, y_local = lax.optimization_barrier((other, y_local))
     first = pick(core == 0, own, other)
     second = pick(core == 0, other, own)
     chip_total = chain(first, second)
@@ -143,19 +151,13 @@
         core == 0, chip_state, first[0][..., None, None] * chip_state + first[1]
     )
 
-    scores = jnp.einsum("ipn,jpn->pij", c_rows, b_rows, preferred_element_type=jnp.float32)
-    position = lax.iota(jnp.int32, block_len)
-    causal = position[:, None] >= position[None, :]
-    gaps = jnp.where(causal, cum_heads[..., :, None] - cum_heads[..., None, :], -jnp.inf)
-    mixing = (scores[:, None] * jnp.exp(gaps) * dt_heads[..., None, :]).astype(jnp.bfloat16)
-    y_intra = jnp.einsum("phij,jphd->iphd", mixing, x_heads, preferred_element_type=jnp.float32)
     y_inter = (
         jnp.einsum(
             "ipn,phdn->iphd", c_rows.astype(jnp.float32), s_before, precision=lax.Precision.HIGHEST
         )
         * jnp.exp(cum_log)[..., None]
     )
-    y_all = y_intra + y_inter + skip[:, None] * x_heads.astype(jnp.float32)
+    y_all = y_local + y_inter
     gated_out = y_all.reshape(block_len, prompts, inner_loc) * jax.nn.silu(z_in.astype(jnp.float32))
     square_local = jnp.sum(gated_out * gated_out, axis=-1)
     head_count = lax.axis_size("head")

time: 205 us -> 215 us (1.049)
  waiting for transfers between devices: 57.3 us -> 71.2 us
  other arithmetic: 33 us -> 24.2 us
  matrix products: 29 us -> 33.2 us
  local copies, waits for them, and re-layouts: 20.9 us -> 24.1 us
    ppermute x21, waiting for transfers between devices: 30.6 us -> 40.4 us  [group_shift(): return lax.ppermute(value, axis, pairs)]
    unnamed x121 -> x95, local copies, waits for them, and re-layouts: 9.29 us -> 13.3 us
    mul x12, local copies, waits for them, and re-layouts: 4.33 us -> 1.12 us  [body(): (weight * overlap[earlier, step_index][:, None])[..., None]]
    ppermute x10, waiting for transfers between devices: 26.7 us -> 29.9 us  [body(): lax.ppermute(tails, 'ctx', [(source, source - reach) for source in range(...]
  transfers between devices with their start and end apart: 34 -> 34, of which waited for: 10 -> 11; matrix products, arithmetic and copies ran while one was open for 34% -> 31% of each run, Pallas kernels for 0% -> 0%
where the time goes in v6:
time: 215 us; the launch traced here: 213 us
  waiting for transfers between devices  71.2 us (33%)
  starting transfers between devices  45.4 us (21%)
  matrix products  33.2 us (15%)
  other arithmetic  24.2 us (11%)
  local copies, waits for them, and re-layouts  24.1 us (11%)
  between operations  15.2 us (7%)
    ppermute x21, waiting for transfers between devices, group_shift(): return lax.ppermute(value, axis, pairs)  40.4 us
    ppermute x21, starting transfers between devices, group_shift(): return lax.ppermute(value, axis, pairs)  30 us
    ppermute x10, waiting for transfers between devices, body(): lax.ppermute(tails, 'ctx', [(source, source - reach) for source in range(...  29.9 us
    dot_general x1, matrix products, body(): jnp.einsum('tpi,id->tpd', normed, w_out, preferred_element_type=jnp.float32)  14.6 us
    unnamed x95, local copies, waits for them, and re-layouts  13.3 us
    dot_general x1, matrix products, body(): jnp.einsum('phij,jphd->iphd', mixing, x_heads, preferred_element_type=jnp...  11.4 us
    ppermute x10, starting transfers between devices, body(): lax.ppermute(tails, 'ctx', [(source, source - reach) for source in range(...  9.81 us
    select_n x12, other arithmetic, pick(): return jax.tree.map(lambda a, b: jnp.where(flag, a, b), first, second)  7.09 us
  transfers between devices with their start and end apart: 34, of which 11 were waited for; matrix products, arithmetic and copies ran while one was open for 31% of the time, Pallas kernels for 0%

profile of v6, /device:TPU:0, one launch (start us, length us, event | category | flops | bytes accessed | tf_op | source)
XLA Modules:
  0.0 213.5 jit_solution(7363820493308265342)
XLA Ops:
  7.3 2.9 %copy.48 = bf16[512,1,2048]{0,2,1:T(8,128)(2,1)S(1)} copy(bf16[512,1,2048]{2,0,1:T(8,128)(2,1)} %param.16) | data formatting | bytes 4194304 | tf_op args[0]
  10.2 1.0 slice.284
  11.2 1.3 collective-permute-start.1
  13.1 4.3 %collective-permute-start.2 = (bf16[3,1,256]{2,0,1:T(4,128)(2,1)}, bf16[3,1,256]{2,0,1:T(4,128)(2,1)S(1)}, u32[]{:S(2)}, u32[]{:S(2)}) collective-permute-start(bf16[3,1,256]{2,0,1:T(4,128)(2,1)} %slice.230), channel_id=1, source_target_pairs={{0,4},{4,8},{8,12},{12,16},{16,20},{20,24},{24,28},{28,32},{32,36}... | collective-permute-start | bytes 4616 | tf_op jit(solution)/shard_map/ppermute | solution.py:12
  17.5 1.2 reduce-window.6
  21.8 4.9 %fusion.8 = (bf16[512,1,2048]{0,2,1:T(8,128)(2,1)S(1)}, bf16[512,1,2048]{0,2,1:T(8,128)(2,1)S(1)}) fusion(f32[2048]{0:T(1024)S(1)} %bitcast.217, bf16[512,1,2048]{0,2,1:T(8,128)(2,1)S(1)} %copy.48, f32[2048]{0:T(1024)S(1)} %bitcast.219, bf16[3,1,2048]{0,2,1:T(8,128)(2,1)S(1)} %collective-permute-done.1, f32[2048]{0:T(1024)S(1)} %bitcast.215, ...), kind=kLoop, calls=%fused_computation.15 | loop fusion | flops 29360128 | bytes 10530816 | tf_op jit(solution)/shard_map/convert_element_type | solution.py:105
  28.3 11.4 %bitcast_add_fusion = f32[512,1,32,64]{0,3,2,1:T(8,128)} fusion(bf16[512,32,64]{0,2,1:T(8,128)(2,1)S(1)} %bitcast.203, f32[32,512]{1,0:T(8,128)S(1)} %get-tuple-element.43, f32[32,512]{1,0:T(8,128)S(1)} %bitcast_add_fusion.1, f32[512,512]{1,0:T(8,128)S(1)} %fusion.36, pred[512,512]{1,0:T(8,128)(4,1)S(1)} %copy-done.8, f32[32]{0:T(128)S(1)} %copy-done.38, ...), kind=kOutput, calls=%fused_computation.13 | convolution fusion | flops 1118830592 | bytes 9830528 | tf_op jit(solution)/shard_map/phij,jphd->iphd/dot_general | solution.py:129
  41.4 2.3 %collective-permute-start.11 = (f32[1,32,32,128]{3,2,1,0:T(8,128)}, f32[1,32,32,128]{3,2,1,0:T(8,128)S(1)}, u32[]{:S(2)}, u32[]{:S(2)}) collective-permute-start(f32[1,32,32,128]{3,2,1,0:T(8,128)} %fusion.27), channel_id=1, source_target_pairs={{0,8},{4,12},{8,16},{12,20},{16,24},{20,28},{24,0},{28,4},{32,40},... | collective-permute-start | bytes 1572872 | tf_op jit(solution)/shard_map/ppermute | solution.py:21
  43.7 1.4 collective-permute-start.10
  45.1 12.8 %collective-permute-done.11 = f32[1,32,32,128]{3,2,1,0:T(8,128)S(1)} collective-permute-done((f32[1,32,32,128]{3,2,1,0:T(8,128)}, f32[1,32,32,128]{3,2,1,0:T(8,128)S(1)}, u32[]{:S(2)}, u32[]{:S(2)}) %collective-permute-start.11) | collective-permute-done | bytes 524320 | tf_op jit(solution)/shard_map/ppermute | solution.py:21
  59.7 1.6 collective-permute-start.5
  61.3 1.7 collective-permute-start.4
  63.0 6.1 %collective-permute-done.5 = f32[1,32]{1,0:T(1,128)} collective-permute-done((f32[1,32]{1,0:T(1,128)}, f32[1,32]{1,0:T(1,128)}, u32[]{:S(2)}, u32[]{:S(2)}) %collective-permute-start.5) | collective-permute-done | bytes 160 | tf_op jit(solution)/shard_map/ppermute | solution.py:21
  69.1 1.0 slice.296
  70.0 3.3 %collective-permute-start.13 = (f32[1,32,16,128]{3,2,1,0:T(8,128)S(1)}, f32[1,32,16,128]{3,2,1,0:T(8,128)S(1)}, u32[]{:S(2)}, u32[]{:S(2)}) collective-permute-start(f32[1,32,16,128]{3,2,1,0:T(8,128)S(1)} %slice.296), channel_id=1, source_target_pairs={{0,24},{4,28},{8,0},{12,4},{16,8},{20,12},{24,16},{28,20},{32,56},... | collective-permute-start | bytes 786440 | tf_op jit(solution)/shard_map/ppermute | solution.py:21
  73.4 1.0 constant_dynamic-update-slice_fusion.1
  74.3 3.5 %collective-permute-done.13 = f32[1,32,16,128]{3,2,1,0:T(8,128)S(1)} collective-permute-done((f32[1,32,16,128]{3,2,1,0:T(8,128)S(1)}, f32[1,32,16,128]{3,2,1,0:T(8,128)S(1)}, u32[]{:S(2)}, u32[]{:S(2)}) %collective-permute-start.13) | collective-permute-done | bytes 262176 | tf_op jit(solution)/shard_map/ppermute | solution.py:21
  78.7 2.6 %add_select_fusion.2 = f32[1,32,32,128]{3,2,1,0:T(8,128)} fusion(f32[1,32,32,128]{3,2,1,0:T(8,128)} %copy-done.2, f32[1,32,32,128]{3,2,1,0:T(8,128)S(1)} %constant_dynamic-update-slice_fusion, f32[1,32,32,128]{3,2,1,0:T(8,128)} %collective-permute-done.10, f32[1,32,32,128]{3,2,1,0:T(8,128)} %fusion.27, f32[32]{0:T(128)S(1)} %broadcast_multiply_fusion.2, ...), kind=kLoop, calls=%fused_computation.54 | loop fusion | flops 2490368 | bytes 2622086 | tf_op jit(solution)/shard_map/jit(_where)/select_n | solution.py:38
  81.3 3.0 %collective-permute-start.15 = (f32[1,32,32,128]{3,2,1,0:T(8,128)}, f32[1,32,32,128]{3,2,1,0:T(8,128)}, u32[]{:S(2)}, u32[]{:S(2)}) collective-permute-start(f32[1,32,32,128]{3,2,1,0:T(8,128)} %add_select_fusion.2), channel_id=1, source_target_pairs={{0,32},{4,36},{8,40},{12,44},{16,48},{20,52},{24,56},{28,60},{32,6... | collective-permute-start | bytes 1572872 | tf_op jit(solution)/shard_map/ppermute | solution.py:21
  84.2 1.4 collective-permute-start.14
  85.6 9.9 %collective-permute-done.15 = f32[1,32,32,128]{3,2,1,0:T(8,128)} collective-permute-done((f32[1,32,32,128]{3,2,1,0:T(8,128)}, f32[1,32,32,128]{3,2,1,0:T(8,128)}, u32[]{:S(2)}, u32[]{:S(2)}) %collective-permute-start.15) | collective-permute-done | bytes 524320 | tf_op jit(solution)/shard_map/ppermute | solution.py:21
  95.5 1.7 slice.297
  97.7 1.2 broadcast_select_fusion.11
  98.9 1.5 collective-permute-start.7
  100.4 1.7 collective-permute-start.9
  102.1 3.0 %collective-permute-done.7 = f32[1,32]{1,0:T(1,128)} collective-permute-done((f32[1,32]{1,0:T(1,128)}, f32[1,32]{1,0:T(1,128)}, u32[]{:S(2)}, u32[]{:S(2)}) %collective-permute-start.7) | collective-permute-done | bytes 160 | tf_op jit(solution)/shard_map/ppermute | solution.py:21
  105.1 1.0 slice.298
  106.1 3.3 %collective-permute-start.17 = (f32[1,32,16,128]{3,2,1,0:T(8,128)S(1)}, f32[1,32,16,128]{3,2,1,0:T(8,128)S(1)}, u32[]{:S(2)}, u32[]{:S(2)}) collective-permute-start(f32[1,32,16,128]{3,2,1,0:T(8,128)S(1)} %slice.298), channel_id=1, source_target_pairs={{0,96},{4,100},{8,104},{12,108},{16,112},{20,116},{24,120},{28,124... | collective-permute-start | bytes 786440 | tf_op jit(solution)/shard_map/ppermute | solution.py:21
  109.4 1.0 constant_dynamic-update-slice_fusion.3
  110.4 2.9 %collective-permute-done.17 = f32[1,32,16,128]{3,2,1,0:T(8,128)S(1)} collective-permute-done((f32[1,32,16,128]{3,2,1,0:T(8,128)S(1)}, f32[1,32,16,128]{3,2,1,0:T(8,128)S(1)}, u32[]{:S(2)}, u32[]{:S(2)}) %collective-permute-start.17) | collective-permute-done | bytes 262176 | tf_op jit(solution)/shard_map/ppermute | solution.py:21
  114.1 3.1 %multiply_add_fusion = f32[1,32,32,128]{3,2,1,0:T(8,128)} fusion(f32[1,32,32,128]{3,2,1,0:T(8,128)} %collective-permute-done.15, f32[1,32,32,128]{3,2,1,0:T(8,128)S(1)} %constant_dynamic-update-slice_fusion.2, f32[1,32,32,128]{3,2,1,0:T(8,128)} %collective-permute-done.14, f32[1,32,32,128]{3,2,1,0:T(8,128)} %copy-done.2, f32[1,32,32,128]{3,2,1,0:T(8,128)} %copy-done.3, ...), kind=kLoop, calls=%fused_computation.52 | loop fusion | flops 2359296 | bytes 3670918 | tf_op jit(solution)/shard_map/add | solution.py:34
  117.3 1.2 collective-permute-start.22
  118.5 1.5 collective-permute-start.28
  121.5 3.9 %copy.53 = bf16[512,1,2048]{0,2,1:T(8,128)(2,1)} copy(bf16[512,1,2048]{2,0,1:T(8,128)(2,1)} %param.17) | data formatting | bytes 4194304 | tf_op args[1]
  127.1 3.4 %fusion.22 = f32[32,64,512]{2,1,0:T(8,128)S(1)} fusion(f32[1,32,64,128]{3,2,1,0:T(8,128)S(1)} %broadcast_select_fusion.4, f32[1,32,32,128]{3,2,1,0:T(8,128)} %collective-permute-done.18, f32[1,32,32,128]{3,2,1,0:T(8,128)} %multiply_add_fusion, f32[32]{0:T(128)} %get-tuple-element.63, pred[]{:T(512)S(6)} %eq.33, ...), kind=kOutput, calls=%fused_computation.40 | convolution fusion | flops 1612185600 | bytes 6422657 | tf_op jit(solution)/shard_map/ipn,phdn->iphd/dot_general | solution.py:155
  130.5 1.1 fusion.7
  132.1 1.4 multiply_reduce_fusion
  133.6 2.0 collective-permute-start.19
  135.5 3.6 %collective-permute-start.20 = (f32[512,1]{0,1:T(1,128)S(1)}, f32[512,1]{0,1:T(1,128)S(1)}, u32[]{:S(2)}, u32[]{:S(2)}) collective-permute-start(f32[512,1]{0,1:T(1,128)S(1)} %bitcast.231), channel_id=1, source_target_pairs={{0,2},{1,3},{2,0},{3,1},{4,6},{5,7},{6,4},{7,5},{8,10},{9,11},{10,... | collective-permute-start | bytes 6152 | tf_op jit(solution)/shard_map/ppermute | solution.py:21
  139.1 1.0 collective-permute-start.21
  141.0 1.7 collective-permute-done.21
  142.7 14.6 %fusion.2 = bf16[512,1,4096]{2,0,1:T(8,128)(2,1)} fusion(bf16[2048,4096]{1,0:T(8,128)(2,1)} %param.26, f32[512,1,2048]{0,2,1:T(8,128)S(1)} %get-tuple-element.26, f32[2048]{0:T(1024)S(1)} %copy-done.42, f32[512]{0:T(512)S(1)} %bitcast.238), kind=kOutput, calls=%fused_computation.4 | convolution fusion | flops 8595177472 | bytes 25176064 | tf_op jit(solution)/shard_map/tpi,id->tpd/dot_general | solution.py:172
  158.8 1.3 collective-permute-start.26
  160.5 2.6 %collective-permute-done.26 = bf16[3,1,256]{2,0,1:T(4,128)(2,1)S(1)} collective-permute-done((bf16[3,1,256]{2,0,1:T(4,128)(2,1)S(1)}, bf16[3,1,256]{2,0,1:T(4,128)(2,1)S(1)}, u32[]{:S(2)}, u32[]{:S(2)}) %collective-permute-start.26) | collective-permute-done | bytes 1568 | tf_op jit(solution)/shard_map/ppermute | solution.py:115
  166.5 1.3 collective-permute-start.32
  169.6 27.2 %collective-permute-done.32 = bf16[3,1,2048]{0,2,1:T(8,128)(2,1)S(1)} collective-permute-done((bf16[3,1,2048]{0,2,1:T(8,128)(2,1)S(1)}, bf16[3,1,2048]{0,2,1:T(8,128)(2,1)S(1)}, u32[]{:S(2)}, u32[]{:S(2)}) %collective-permute-start.32) | collective-permute-done | bytes 12320 | tf_op jit(solution)/shard_map/ppermute | solution.py:115
  197.4 1.8 add_select_fusion
  201.5 2.7 %convolution_multiply_fusion = f32[4,8,32,64]{3,1,2,0:T(8,128)S(1)} fusion(f32[32,32,128]{2,1,0:T(8,128)} %bitcast.55, f32[32,32,128]{2,1,0:T(8,128)S(1)} %bitcast.209, pred[]{:T(512)S(6)} %eq.33, f32[8]{0:T(128)S(1)} %get-tuple-element.67, bf16[4,8,256]{2,1,0:T(8,128)(2,1)S(1)} %multiply_convert_fusion.9), kind=kOutput, calls=%fused_computation.30 | convolution fusion | flops 101515264 | bytes 1319425 | tf_op jit(solution)/shard_map/phdn,srn->psrhd/dot_general | solution.py:202
  (229 shorter events, 27.1 us)
Async XLA Ops:
  7.2 10.2 %copy-start.7 = (f32[512,1,32]{0,2,1:T(8,128)S(1)}, f32[512,1,32]{0,2,1:T(8,128)}, u32[]{:S(2)}) copy-start(f32[512,1,32]{0,2,1:T(8,128)} %param.19) | copy-start | bytes 196612
  7.2 10.2 %copy-start.27 = (f32[32]{0:T(128)S(1)}, f32[32]{0:T(128)}, u32[]{:S(2)}) copy-start(f32[32]{0:T(128)} %param.20) | copy-start | bytes 388
  7.2 12.5 %copy-start.15 = (bf16[4,2048]{1,0:T(4,128)(2,1)S(1)}, bf16[4,2048]{1,0:T(4,128)(2,1)}, u32[]{:S(2)}) copy-start(bf16[4,2048]{1,0:T(4,128)(2,1)} %param.23) | copy-start | bytes 49156
  7.2 12.5 %copy-start.26 = (bf16[4,256]{1,0:T(4,128)(2,1)S(1)}, bf16[4,256]{1,0:T(4,128)(2,1)}, u32[]{:S(2)}) copy-start(bf16[4,256]{1,0:T(4,128)(2,1)} %param.24) | copy-start | bytes 6148
  7.2 199.4 %reduce-scatter.2.cloned.1.call-start = ((), (), s32[]{:S(2)}) async-start(), calls=%async_computation.1 | async-start | bytes 5242880 | tf_op jit(solution)/shard_map/reduce_scatter | solution.py:171
  11.2 10.1 %collective-permute-start.1 = (bf16[3,1,2048]{0,2,1:T(8,128)(2,1)}, bf16[3,1,2048]{0,2,1:T(8,128)(2,1)S(1)}, u32[]{:S(2)}, u32[]{:S(2)}) collective-permute-start(bf16[3,1,2048]{0,2,1:T(8,128)(2,1)} %slice.284), channel_id=1, source_target_pairs={{0,4},{4,8},{8,12},{12,16},{16,20},{20,24},{24,28},{28,32},{32,36}... | collective-permute-start | bytes 36872 | tf_op jit(solution)/shard_map/ppermute | solution.py:12
  13.1 7.5 %collective-permute-start.2 = (bf16[3,1,256]{2,0,1:T(4,128)(2,1)}, bf16[3,1,256]{2,0,1:T(4,128)(2,1)S(1)}, u32[]{:S(2)}, u32[]{:S(2)}) collective-permute-start(bf16[3,1,256]{2,0,1:T(4,128)(2,1)} %slice.230), channel_id=1, source_target_pairs={{0,4},{4,8},{8,12},{12,16},{16,20},{20,24},{24,28},{28,32},{32,36}... | collective-permute-start | bytes 4616 | tf_op jit(solution)/shard_map/ppermute | solution.py:12
  19.4 20.3 %collective-permute-start = (f32[1,32]{1,0:T(1,128)S(1)}, f32[1,32]{1,0:T(1,128)S(1)}, u32[]{:S(2)}, u32[]{:S(2)}) collective-permute-start(f32[1,32]{1,0:T(1,128)S(1)} %bitcast.239), channel_id=1, source_target_pairs={{0,4},{4,0},{8,12},{12,8},{16,20},{20,16},{24,28},{28,24},{32,36},... | collective-permute-start | bytes 392 | tf_op jit(solution)/shard_map/ppermute | solution.py:21
  27.5 12.2 %collective-permute-start.3 = (f32[1,32,64,128]{3,2,1,0:T(8,128)S(1)}, f32[1,32,64,128]{3,2,1,0:T(8,128)S(1)}, u32[]{:S(2)}, u32[]{:S(2)}) collective-permute-start(f32[1,32,64,128]{3,2,1,0:T(8,128)S(1)} %convolution_bitcast_fusion), channel_id=1, source_target_pairs={{0,4},{4,0},{8,12},{12,8},{16,20},{20,16},{24,28},{28,24},{32,36},... | collective-permute-start | bytes 3145736 | tf_op jit(solution)/shard_map/ppermute | solution.py:21
  41.4 16.5 %collective-permute-start.11 = (f32[1,32,32,128]{3,2,1,0:T(8,128)}, f32[1,32,32,128]{3,2,1,0:T(8,128)S(1)}, u32[]{:S(2)}, u32[]{:S(2)}) collective-permute-start(f32[1,32,32,128]{3,2,1,0:T(8,128)} %fusion.27), channel_id=1, source_target_pairs={{0,8},{4,12},{8,16},{12,20},{16,24},{20,28},{24,0},{28,4},{32,40},... | collective-permute-start | bytes 1572872 | tf_op jit(solution)/shard_map/ppermute | solution.py:21
  43.7 25.4 %collective-permute-start.10 = (f32[1,32,32,128]{3,2,1,0:T(8,128)}, f32[1,32,32,128]{3,2,1,0:T(8,128)}, u32[]{:S(2)}, u32[]{:S(2)}) collective-permute-start(f32[1,32,32,128]{3,2,1,0:T(8,128)} %fusion.27), channel_id=1, source_target_pairs={{0,24},{4,28},{8,0},{12,4},{16,8},{20,12},{24,16},{28,20},{32,56},... | collective-permute-start | bytes 1572872 | tf_op jit(solution)/shard_map/ppermute | solution.py:21
  59.4 13.9 %collective-permute-start.12 = (f32[1,32,16,128]{3,2,1,0:T(8,128)}, f32[1,32,16,128]{3,2,1,0:T(8,128)}, u32[]{:S(2)}, u32[]{:S(2)}) collective-permute-start(f32[1,32,16,128]{3,2,1,0:T(8,128)} %slice.295), channel_id=1, source_target_pairs={{0,8},{4,12},{8,16},{12,20},{16,24},{20,28},{24,0},{28,4},{32,40},... | collective-permute-start | bytes 786440 | tf_op jit(solution)/shard_map/ppermute | solution.py:21
  59.7 9.3 %collective-permute-start.5 = (f32[1,32]{1,0:T(1,128)}, f32[1,32]{1,0:T(1,128)}, u32[]{:S(2)}, u32[]{:S(2)}) collective-permute-start(f32[1,32]{1,0:T(1,128)} %get-tuple-element.65), channel_id=1, source_target_pairs={{0,8},{4,12},{8,16},{12,20},{16,24},{20,28},{24,0},{28,4},{32,40},... | collective-permute-start | bytes 392 | tf_op jit(solution)/shard_map/ppermute | solution.py:21
  61.3 12.0 %collective-permute-start.4 = (f32[1,32]{1,0:T(1,128)}, f32[1,32]{1,0:T(1,128)S(1)}, u32[]{:S(2)}, u32[]{:S(2)}) collective-permute-start(f32[1,32]{1,0:T(1,128)} %get-tuple-element.65), channel_id=1, source_target_pairs={{0,24},{4,28},{8,0},{12,4},{16,8},{20,12},{24,16},{28,20},{32,56},... | collective-permute-start | bytes 392 | tf_op jit(solution)/shard_map/ppermute | solution.py:21
  69.1 8.8 %collective-permute-start.6 = (f32[1,32]{1,0:T(1,128)}, f32[1,32]{1,0:T(1,128)S(1)}, u32[]{:S(2)}, u32[]{:S(2)}) collective-permute-start(f32[1,32]{1,0:T(1,128)} %collective-permute-done.5), channel_id=1, source_target_pairs={{0,8},{4,12},{8,16},{12,20},{16,24},{20,28},{24,0},{28,4},{32,40},... | collective-permute-start | bytes 392 | tf_op jit(solution)/shard_map/ppermute | solution.py:21
  70.0 7.8 %collective-permute-start.13 = (f32[1,32,16,128]{3,2,1,0:T(8,128)S(1)}, f32[1,32,16,128]{3,2,1,0:T(8,128)S(1)}, u32[]{:S(2)}, u32[]{:S(2)}) collective-permute-start(f32[1,32,16,128]{3,2,1,0:T(8,128)S(1)} %slice.296), channel_id=1, source_target_pairs={{0,24},{4,28},{8,0},{12,4},{16,8},{20,12},{24,16},{28,20},{32,56},... | collective-permute-start | bytes 786440 | tf_op jit(solution)/shard_map/ppermute | solution.py:21
  73.3 10.9 %copy-start.37 = (f32[1,32]{1,0:T(1,128)}, f32[1,32]{1,0:T(1,128)S(1)}, u32[]{:S(2)}) copy-start(f32[1,32]{1,0:T(1,128)S(1)} %collective-permute-done.4) | copy-start | bytes 388
  73.3 10.9 %copy-start.36 = (f32[32]{0:T(128)}, f32[32]{0:T(128)S(1)}, u32[]{:S(2)}) copy-start(f32[32]{0:T(128)S(1)} %broadcast_multiply_fusion.2) | copy-start | bytes 388
  81.3 14.3 %collective-permute-start.15 = (f32[1,32,32,128]{3,2,1,0:T(8,128)}, f32[1,32,32,128]{3,2,1,0:T(8,128)}, u32[]{:S(2)}, u32[]{:S(2)}) collective-permute-start(f32[1,32,32,128]{3,2,1,0:T(8,128)} %add_select_fusion.2), channel_id=1, source_target_pairs={{0,32},{4,36},{8,40},{12,44},{16,48},{20,52},{24,56},{28,60},{32,6... | collective-permute-start | bytes 1572872 | tf_op jit(solution)/shard_map/ppermute | solution.py:21
  84.2 20.9 %collective-permute-start.14 = (f32[1,32,32,128]{3,2,1,0:T(8,128)}, f32[1,32,32,128]{3,2,1,0:T(8,128)}, u32[]{:S(2)}, u32[]{:S(2)}) collective-permute-start(f32[1,32,32,128]{3,2,1,0:T(8,128)} %add_select_fusion.2), channel_id=1, source_target_pairs={{0,96},{4,100},{8,104},{12,108},{16,112},{20,116},{24,120},{28,124... | collective-permute-start | bytes 1572872 | tf_op jit(solution)/shard_map/ppermute | solution.py:21
  97.2 12.2 %collective-permute-start.16 = (f32[1,32,16,128]{3,2,1,0:T(8,128)}, f32[1,32,16,128]{3,2,1,0:T(8,128)}, u32[]{:S(2)}, u32[]{:S(2)}) collective-permute-start(f32[1,32,16,128]{3,2,1,0:T(8,128)} %slice.297), channel_id=1, source_target_pairs={{0,32},{4,36},{8,40},{12,44},{16,48},{20,52},{24,56},{28,60},{32,6... | collective-permute-start | bytes 786440 | tf_op jit(solution)/shard_map/ppermute | solution.py:21
  98.9 6.2 %collective-permute-start.7 = (f32[1,32]{1,0:T(1,128)}, f32[1,32]{1,0:T(1,128)}, u32[]{:S(2)}, u32[]{:S(2)}) collective-permute-start(f32[1,32]{1,0:T(1,128)} %get-tuple-element.27), channel_id=1, source_target_pairs={{0,32},{4,36},{8,40},{12,44},{16,48},{20,52},{24,56},{28,60},{32,6... | collective-permute-start | bytes 392 | tf_op jit(solution)/shard_map/ppermute | solution.py:21
  100.4 9.0 %collective-permute-start.9 = (f32[1,32]{1,0:T(1,128)}, f32[1,32]{1,0:T(1,128)S(1)}, u32[]{:S(2)}, u32[]{:S(2)}) collective-permute-start(f32[1,32]{1,0:T(1,128)} %get-tuple-element.27), channel_id=1, source_target_pairs={{0,96},{4,100},{8,104},{12,108},{16,112},{20,116},{24,120},{28,124... | collective-permute-start | bytes 392 | tf_op jit(solution)/shard_map/ppermute | solution.py:21
  105.1 8.2 %collective-permute-start.8 = (f32[1,32]{1,0:T(1,128)}, f32[1,32]{1,0:T(1,128)S(1)}, u32[]{:S(2)}, u32[]{:S(2)}) collective-permute-start(f32[1,32]{1,0:T(1,128)} %collective-permute-done.7), channel_id=1, source_target_pairs={{0,32},{4,36},{8,40},{12,44},{16,48},{20,52},{24,56},{28,60},{32,6... | collective-permute-start | bytes 392 | tf_op jit(solution)/shard_map/ppermute | solution.py:21
  106.1 7.2 %collective-permute-start.17 = (f32[1,32,16,128]{3,2,1,0:T(8,128)S(1)}, f32[1,32,16,128]{3,2,1,0:T(8,128)S(1)}, u32[]{:S(2)}, u32[]{:S(2)}) collective-permute-start(f32[1,32,16,128]{3,2,1,0:T(8,128)S(1)} %slice.298), channel_id=1, source_target_pairs={{0,96},{4,100},{8,104},{12,108},{16,112},{20,116},{24,120},{28,124... | collective-permute-start | bytes 786440 | tf_op jit(solution)/shard_map/ppermute | solution.py:21
  117.3 9.8 %collective-permute-start.18 = (f32[1,32,32,128]{3,2,1,0:T(8,128)}, f32[1,32,32,128]{3,2,1,0:T(8,128)}, u32[]{:S(2)}, u32[]{:S(2)}) collective-permute-start(f32[1,32,32,128]{3,2,1,0:T(8,128)} %multiply_add_fusion), channel_id=1, source_target_pairs={{0,4},{4,0},{8,12},{12,8},{16,20},{20,16},{24,28},{28,24},{32,36},... | collective-permute-start | bytes 1572872 | tf_op jit(solution)/shard_map/ppermute | solution.py:21
  117.3 8.2 %collective-permute-start.22 = (bf16[3,1,256]{2,0,1:T(4,128)(2,1)}, bf16[3,1,256]{2,0,1:T(4,128)(2,1)}, u32[]{:S(2)}, u32[]{:S(2)}) collective-permute-start(bf16[3,1,256]{2,0,1:T(4,128)(2,1)} %slice.230), channel_id=1, source_target_pairs={{124,60},{125,61},{126,62},{127,63}} | collective-permute-start | bytes 4616 | tf_op jit(solution)/shard_map/ppermute | solution.py:115
  118.5 44.8 %collective-permute-start.28 = (bf16[3,1,2048]{0,2,1:T(8,128)(2,1)}, bf16[3,1,2048]{0,2,1:T(8,128)(2,1)}, u32[]{:S(2)}, u32[]{:S(2)}) collective-permute-start(bf16[3,1,2048]{0,2,1:T(8,128)(2,1)} %slice.284), channel_id=1, source_target_pairs={{124,60},{125,61},{126,62},{127,63}} | collective-permute-start | bytes 36872 | tf_op jit(solution)/shard_map/ppermute | solution.py:115
  126.3 13.8 %collective-permute-start.23 = (bf16[3,1,256]{2,0,1:T(4,128)(2,1)S(1)}, bf16[3,1,256]{2,0,1:T(4,128)(2,1)S(1)}, u32[]{:S(2)}, u32[]{:S(2)}) collective-permute-start(bf16[3,1,256]{2,0,1:T(4,128)(2,1)S(1)} %broadcast_select_fusion.5), channel_id=1, source_target_pairs={{60,28},{124,92},{61,29},{125,93},{62,30},{126,94},{63,31},{127,95}} | collective-permute-start | bytes 4616 | tf_op jit(solution)/shard_map/ppermute | solution.py:115
  132.1 10.6 %copy-start.42 = (f32[2048]{0:T(1024)S(1)}, f32[2048]{0:T(1024)}, u32[]{:S(2)}) copy-start(f32[2048]{0:T(1024)} %param.25) | copy-start | bytes 24580
  133.6 7.5 %collective-permute-start.19 = (f32[512,1]{0,1:T(1,128)S(1)}, f32[512,1]{0,1:T(1,128)S(1)}, u32[]{:S(2)}, u32[]{:S(2)}) collective-permute-start(f32[512,1]{0,1:T(1,128)S(1)} %bitcast.230), channel_id=1, source_target_pairs={{0,1},{1,2},{2,3},{3,0},{4,5},{5,6},{6,7},{7,4},{8,9},{9,10},{10,1... | collective-permute-start | bytes 6152 | tf_op jit(solution)/shard_map/ppermute | solution.py:21
  135.5 5.5 %collective-permute-start.20 = (f32[512,1]{0,1:T(1,128)S(1)}, f32[512,1]{0,1:T(1,128)S(1)}, u32[]{:S(2)}, u32[]{:S(2)}) collective-permute-start(f32[512,1]{0,1:T(1,128)S(1)} %bitcast.231), channel_id=1, source_target_pairs={{0,2},{1,3},{2,0},{3,1},{4,6},{5,7},{6,4},{7,5},{8,10},{9,11},{10,... | collective-permute-start | bytes 6152 | tf_op jit(solution)/shard_map/ppermute | solution.py:21
  139.1 3.6 %collective-permute-start.21 = (f32[512,1]{0,1:T(1,128)S(1)}, f32[512,1]{0,1:T(1,128)S(1)}, u32[]{:S(2)}, u32[]{:S(2)}) collective-permute-start(f32[512,1]{0,1:T(1,128)S(1)} %bitcast.232), channel_id=1, source_target_pairs={{0,3},{1,0},{2,1},{3,2},{4,7},{5,4},{6,5},{7,6},{8,11},{9,8},{10,9... | collective-permute-start | bytes 6152 | tf_op jit(solution)/shard_map/ppermute | solution.py:21
  140.1 17.9 %collective-permute-start.24 = (bf16[3,1,256]{2,0,1:T(4,128)(2,1)S(1)}, bf16[3,1,256]{2,0,1:T(4,128)(2,1)S(1)}, u32[]{:S(2)}, u32[]{:S(2)}) collective-permute-start(bf16[3,1,256]{2,0,1:T(4,128)(2,1)S(1)} %broadcast_select_fusion.6), channel_id=1, source_target_pairs={{28,12},{60,44},{92,76},{124,108},{29,13},{61,45},{93,77},{125,109... | collective-permute-start | bytes 4616 | tf_op jit(solution)/shard_map/ppermute | solution.py:115
  158.1 0.7 collective-permute-start.25
  158.8 4.3 %collective-permute-start.26 = (bf16[3,1,256]{2,0,1:T(4,128)(2,1)S(1)}, bf16[3,1,256]{2,0,1:T(4,128)(2,1)S(1)}, u32[]{:S(2)}, u32[]{:S(2)}) collective-permute-start(bf16[3,1,256]{2,0,1:T(4,128)(2,1)S(1)} %broadcast_select_fusion.8), channel_id=1, source_target_pairs={{4,0},{12,8},{20,16},{28,24},{36,32},{44,40},{52,48},{60,56},{68,6... | collective-permute-start | bytes 4616 | tf_op jit(solution)/shard_map/ppermute | solution.py:115
  163.5 0.8 collective-permute-start.29
  164.4 1.0 collective-permute-start.30
  165.5 31.9 %copy-start.5 = (f32[1,32,32,128]{3,2,1,0:T(8,128)S(1)}, f32[1,32,32,128]{3,2,1,0:T(8,128)}, u32[]{:S(2)}) copy-start(f32[1,32,32,128]{3,2,1,0:T(8,128)} %copy-done.4) | copy-start | bytes 1572868
  165.5 31.9 %copy-start.33 = (f32[1,32]{1,0:T(1,128)S(1)}, f32[1,32]{1,0:T(1,128)}, u32[]{:S(2)}) copy-start(f32[1,32]{1,0:T(1,128)} %copy-done.32) | copy-start | bytes 388
  165.5 31.9 %copy-start.35 = (f32[32]{0:T(128)S(1)}, f32[32]{0:T(128)}, u32[]{:S(2)}) copy-start(f32[32]{0:T(128)} %copy-done.34) | copy-start | bytes 388
  165.5 31.9 %copy-start.41 = (f32[1,32]{1,0:T(1,128)S(1)}, f32[1,32]{1,0:T(1,128)}, u32[]{:S(2)}) copy-start(f32[1,32]{1,0:T(1,128)} %copy-done.40) | copy-start | bytes 388
  165.5 0.9 collective-permute-start.31
  166.5 30.4 %collective-permute-start.32 = (bf16[3,1,2048]{0,2,1:T(8,128)(2,1)S(1)}, bf16[3,1,2048]{0,2,1:T(8,128)(2,1)S(1)}, u32[]{:S(2)}, u32[]{:S(2)}) collective-permute-start(bf16[3,1,2048]{0,2,1:T(8,128)(2,1)S(1)} %broadcast_select_fusion.3), channel_id=1, source_target_pairs={{4,0},{12,8},{20,16},{28,24},{36,32},{44,40},{52,48},{60,56},{68,6... | collective-permute-start | bytes 36872 | tf_op jit(solution)/shard_map/ppermute | solution.py:115
  168.1 31.7 %copy-start.10 = (bf16[4,8,2048]{2,1,0:T(8,128)(2,1)S(1)}, bf16[4,8,2048]{2,1,0:T(8,128)(2,1)}, u32[]{:S(2)}) copy-start(bf16[4,8,2048]{2,1,0:T(8,128)(2,1)} %param.28) | copy-start | bytes 393220
  168.2 31.7 %copy-start.12 = (f32[1,2048]{1,0:T(1,128)S(1)}, f32[1,2048]{1,0:T(1,128)}, u32[]{:S(2)}) copy-start(f32[1,2048]{1,0:T(1,128)} %copy-done.11) | copy-start | bytes 24580
  168.2 31.7 %copy-start.14 = (f32[1,2048]{1,0:T(1,128)S(1)}, f32[1,2048]{1,0:T(1,128)}, u32[]{:S(2)}) copy-start(f32[1,2048]{1,0:T(1,128)} %copy-done.13) | copy-start | bytes 24580
  199.3 2.2 %collective-permute-start.27 = (f32[1,32,32,128]{3,2,1,0:T(8,128)S(1)}, f32[1,32,32,128]{3,2,1,0:T(8,128)}, u32[]{:S(2)}, u32[]{:S(2)}) collective-permute-start(f32[1,32,32,128]{3,2,1,0:T(8,128)S(1)} %add_select_fusion), channel_id=1, source_target_pairs={{0,4},{4,0},{8,12},{12,8},{16,20},{20,16},{24,28},{28,24},{32,36},... | collective-permute-start | bytes 1572872 | tf_op jit(solution)/shard_map/ppermute | solution.py:21
  (31 other events, 142.9 us)
Sparse Core Ops, SparseCore 0:
  157.5 49.0 reduce-scatter.1

commit v7 on v0

--- a/solution.py
+++ b/solution.py
@@ -113,27 +113,38 @@
         lambda part: lax.all_gather(part, "ctx")[count - 1],
         (x_in[block_len - conv_taps + 1 :], bc_in[block_len - conv_taps + 1 :]),
     )
-    own = (block_decay, s_local)
-    other = group_shift(own, "ctx", count, 1, 2, 1)
-    first = pick(core == 0, own, other)
-    second = pick(core == 0, other, own)
-    chip_total = chain(first, second)
     half = head_dim // 2
-    chip_half = (chip_total[0], lax.dynamic_slice_in_dim(chip_total[1], core * half, half, 2))
+    keep = lax.dynamic_slice_in_dim(s_local, core * half, half, 2)
+    give = lax.dynamic_slice_in_dim(s_local, (1 - core) * half, half, 2)
+    other_decay, other_half = group_shift((block_decay, give), "ctx", count, 1, 2, 1)
+    first_decay = jnp.where(core == 0, block_decay, other_decay)
+    second_decay = jnp.where(core == 0, other_decay, block_decay)
+    first_half = jnp.where(core == 0, keep, other_half)
+    second_half = jnp.where(core == 0, other_half, keep)
+    chip_half = (
+        first_decay * second_decay,
+        second_decay[..., None, None] * first_half + second_half,
+    )
     row_before, row_total = ring_scan(chip_half, "ctx", count, 2, 4)
     rows = count // 8
     top_before, top_total = ring_scan(row_total, "ctx", count, 8, rows)
     chip_before = chain(top_before, row_before)
-    mine = (chip_before[1], top_total[1])
-    theirs = group_shift(mine, "ctx", count, 1, 2, 1)
-    joined = jax.tree.map(
-        lambda a, b: jnp.where(core == 0, jnp.concatenate([a, b], 2), jnp.concatenate([b, a], 2)),
-        mine,
-        theirs,
-    )
-    chip_state, final_state = joined
+    finished = jnp.where(
+        core == 0, chip_before[1], first_decay[..., None, None] * chip_before[1] + first_half
+    )
+    sent = jnp.where(
+        core == 0, first_decay[..., None, None] * chip_before[1] + keep, chip_before[1]
+    )
+    theirs = group_shift((sent, top_total[1]), "ctx", count, 1, 2, 1)
     s_before = jnp.where(
-        core == 0, chip_state, first[0][..., None, None] * chip_state + first[1]
+        core == 0,
+        jnp.concatenate([finished, theirs[0]], 2),
+        jnp.concatenate([theirs[0], finished], 2),
+    )
+    final_state = jnp.where(
+        core == 0,
+        jnp.concatenate([top_total[1], theirs[1]], 2),
+        jnp.concatenate([theirs[1], top_total[1]], 2),
     )
 
     scores = jnp.einsum("ipn,jpn->pij", c_rows, b_rows, preferred_element_type=jnp.float32)

time: 204 us -> 201 us (0.985)
  other arithmetic: 27.2 us -> 20.9 us
  starting transfers between devices: 34.5 us -> 37.3 us
    ppermute x21, starting transfers between devices: 28.2 us -> 31.7 us  [group_shift(): return lax.ppermute(value, axis, pairs)]
    add x2 -> x1, other arithmetic: 3.43 us -> 0.13 us  [body(): second_decay[..., None, None] * first_half + second_half]
    concatenate x0 -> x1, other arithmetic: none -> 2.69 us  [body(): jnp.concatenate([finished, theirs[0]], 2)]
    select_n x4 -> x3, other arithmetic: 5.7 us -> 3.59 us  [pick(): return jax.tree.map(lambda a, b: jnp.where(flag, a, b), first, second)]
    slice x2, local copies, waits for them, and re-layouts: 2.12 us -> 0.01 us  [body(): bc_in[block_len - conv_taps + 1:]]
    unnamed x103 -> x75, local copies, waits for them, and re-layouts: 6.52 us -> 7.71 us
  transfers between devices with their start and end apart: 24 -> 24, of which waited for: 9 -> 9; matrix products, arithmetic and copies ran while one was open for 19% -> 15% of each run, Pallas kernels for 0% -> 0%
where the time goes in v7:
time: 201 us; the launch traced here: 199 us
  blocking collectives  49.6 us (25%)
  starting transfers between devices  37.3 us (19%)
  waiting for transfers between devices  31.3 us (16%)
  matrix products  28.9 us (14%)
  other arithmetic  20.9 us (10%)
  local copies, waits for them, and re-layouts  15.8 us (8%)
  between operations  15.1 us (8%)
    all_gather x2, blocking collectives, body(): lax.all_gather(part, 'ctx')[count - 1]  49.6 us
    ppermute x21, starting transfers between devices, group_shift(): return lax.ppermute(value, axis, pairs)  31.7 us
    ppermute x21, waiting for transfers between devices, group_shift(): return lax.ppermute(value, axis, pairs)  31.3 us
    dot_general x1, matrix products, body(): jnp.einsum('tpi,id->tpd', normed, w_out, preferred_element_type=jnp.float32)  14.6 us
    dot_general x1, matrix products, body(): jnp.einsum('phij,jphd->iphd', mixing, x_heads, preferred_element_type=jnp...  9.46 us
    unnamed x75, local copies, waits for them, and re-layouts  7.71 us
    convert_element_type x1, other arithmetic, body(): weighted_x = (x_heads * tail_weights[..., None]).astype(jnp.bfloat16)  7.34 us
    ppermute x2, starting transfers between devices, passed_along(): lax.ppermute(value, axis, [(source, source + steps) for source in range(l...  5.64 us
  transfers between devices with their start and end apart: 24, of which 9 were waited for; matrix products, arithmetic and copies ran while one was open for 15% of the time, Pallas kernels for 0%

profile of v7, /device:TPU:0, one launch (start us, length us, event | category | flops | bytes accessed | tf_op | source)
XLA Modules:
  0.0 198.9 jit_solution(2460611093775803691)
XLA Ops:
  7.3 2.9 %copy.62 = bf16[512,1,2048]{0,2,1:T(8,128)(2,1)S(1)} copy(bf16[512,1,2048]{2,0,1:T(8,128)(2,1)} %param.16) | data formatting | bytes 4194304 | tf_op args[0]
  10.4 2.1 %collective-permute-start = (bf16[3,1,2048]{0,2,1:T(8,128)(2,1)S(1)}, bf16[3,1,2048]{0,2,1:T(8,128)(2,1)}, u32[]{:S(2)}, u32[]{:S(2)}) collective-permute-start(bf16[3,1,2048]{0,2,1:T(8,128)(2,1)S(1)} %slice.292), channel_id=1, source_target_pairs={{0,4},{4,8},{8,12},{12,16},{16,20},{20,24},{24,28},{28,32},{32,36}... | collective-permute-start | bytes 36872 | tf_op jit(solution)/shard_map/ppermute | solution.py:12
  12.5 3.5 %collective-permute-start.1 = (bf16[3,1,256]{2,0,1:T(4,128)(2,1)S(1)}, bf16[3,1,256]{2,0,1:T(4,128)(2,1)S(1)}, u32[]{:S(2)}, u32[]{:S(2)}) collective-permute-start(bf16[3,1,256]{2,0,1:T(4,128)(2,1)S(1)} %slice.233), channel_id=1, source_target_pairs={{0,4},{4,8},{8,12},{12,16},{16,20},{20,24},{24,28},{28,32},{32,36}... | collective-permute-start | bytes 4616 | tf_op jit(solution)/shard_map/ppermute | solution.py:12
  16.1 0.7 fusion.97
  16.9 1.2 reduce-window.6
  19.8 7.3 %fusion.9 = (bf16[512,1,2048]{0,2,1:T(8,128)(2,1)S(1)}, bf16[512,1,2048]{0,2,1:T(8,128)(2,1)}) fusion(f32[2048]{0:T(1024)S(1)} %bitcast.233, bf16[512,1,2048]{0,2,1:T(8,128)(2,1)S(1)} %copy.62, f32[2048]{0:T(1024)S(1)} %bitcast.235, bf16[3,1,2048]{0,2,1:T(8,128)(2,1)} %collective-permute-done, f32[2048]{0:T(1024)S(1)} %bitcast.231, f32[2048]{0:T(1024)S(1)} %bitcast.229, ...), kind=kLoop, calls=%fused_computation.15 | loop fusion | flops 29360128 | bytes 10530816 | tf_op jit(solution)/shard_map/convert_element_type | solution.py:105
  27.2 0.7 fusion.37
  27.9 1.4 collective-permute-start.9
  29.4 1.4 collective-permute-done.2
  30.9 0.8 copy-done.6
  31.8 2.9 %collective-permute-start.11 = (f32[1,32,32,128]{3,2,1,0:T(8,128)S(1)}, f32[1,32,32,128]{3,2,1,0:T(8,128)S(1)}, u32[]{:S(2)}, u32[]{:S(2)}) collective-permute-start(f32[1,32,32,128]{3,2,1,0:T(8,128)S(1)} %fusion.28), channel_id=1, source_target_pairs={{0,8},{4,12},{8,16},{12,20},{16,24},{20,28},{24,0},{28,4},{32,40},... | collective-permute-start | bytes 1572872 | tf_op jit(solution)/shard_map/ppermute | solution.py:21
  34.7 1.5 collective-permute-start.10
  36.2 12.1 %collective-permute-done.11 = f32[1,32,32,128]{3,2,1,0:T(8,128)S(1)} collective-permute-done((f32[1,32,32,128]{3,2,1,0:T(8,128)S(1)}, f32[1,32,32,128]{3,2,1,0:T(8,128)S(1)}, u32[]{:S(2)}, u32[]{:S(2)}) %collective-permute-start.11) | collective-permute-done | bytes 524320 | tf_op jit(solution)/shard_map/ppermute | solution.py:21
  48.4 0.8 slice.305
  49.7 1.6 collective-permute-start.4
  51.3 1.7 collective-permute-start.3
  53.0 5.5 %collective-permute-done.4 = f32[1,32]{1,0:T(1,128)S(1)} collective-permute-done((f32[1,32]{1,0:T(1,128)S(1)}, f32[1,32]{1,0:T(1,128)S(1)}, u32[]{:S(2)}, u32[]{:S(2)}) %collective-permute-start.4) | collective-permute-done | bytes 160 | tf_op jit(solution)/shard_map/ppermute | solution.py:21
  58.5 3.3 %collective-permute-start.13 = (f32[1,32,16,128]{3,2,1,0:T(8,128)S(1)}, f32[1,32,16,128]{3,2,1,0:T(8,128)S(1)}, u32[]{:S(2)}, u32[]{:S(2)}) collective-permute-start(f32[1,32,16,128]{3,2,1,0:T(8,128)S(1)} %slice.306), channel_id=1, source_target_pairs={{0,24},{4,28},{8,0},{12,4},{16,8},{20,12},{24,16},{28,20},{32,56},... | collective-permute-start | bytes 786440 | tf_op jit(solution)/shard_map/ppermute | solution.py:21
  61.8 4.0 %collective-permute-done.13 = f32[1,32,16,128]{3,2,1,0:T(8,128)S(1)} collective-permute-done((f32[1,32,16,128]{3,2,1,0:T(8,128)S(1)}, f32[1,32,16,128]{3,2,1,0:T(8,128)S(1)}, u32[]{:S(2)}, u32[]{:S(2)}) %collective-permute-start.13) | collective-permute-done | bytes 262176 | tf_op jit(solution)/shard_map/ppermute | solution.py:21
  65.9 1.2 add_select_fusion.2
  67.1 3.1 %collective-permute-start.15 = (f32[1,32,32,128]{3,2,1,0:T(8,128)}, f32[1,32,32,128]{3,2,1,0:T(8,128)}, u32[]{:S(2)}, u32[]{:S(2)}) collective-permute-start(f32[1,32,32,128]{3,2,1,0:T(8,128)} %add_select_fusion.2), channel_id=1, source_target_pairs={{0,32},{4,36},{8,40},{12,44},{16,48},{20,52},{24,56},{28,60},{32,6... | collective-permute-start | bytes 1572872 | tf_op jit(solution)/shard_map/ppermute | solution.py:21
  70.8 1.3 collective-permute-start.14
  72.1 0.8 iota_compare_fusion
  73.5 0.8 collective-permute-start.6
  74.3 2.9 %copy.71 = bf16[512,1,2048]{0,2,1:T(8,128)(2,1)S(1)} copy(bf16[512,1,2048]{2,0,1:T(8,128)(2,1)} %param.17) | data formatting | bytes 4194304 | tf_op args[1]
  77.2 2.5 %collective-permute-start.8 = (f32[1,32]{1,0:T(1,128)}, f32[1,32]{1,0:T(1,128)S(1)}, u32[]{:S(2)}, u32[]{:S(2)}) collective-permute-start(f32[1,32]{1,0:T(1,128)} %get-tuple-element.23), channel_id=1, source_target_pairs={{0,96},{4,100},{8,104},{12,108},{16,112},{20,116},{24,120},{28,124... | collective-permute-start | bytes 392 | tf_op jit(solution)/shard_map/ppermute | solution.py:21
  79.7 1.4 collective-permute-done.6
  81.6 1.0 slice.307
  82.6 1.6 collective-permute-start.16
  84.1 1.0 slice.308
  85.1 2.0 %collective-permute-start.17 = (f32[1,32,16,128]{3,2,1,0:T(8,128)S(1)}, f32[1,32,16,128]{3,2,1,0:T(8,128)S(1)}, u32[]{:S(2)}, u32[]{:S(2)}) collective-permute-start(f32[1,32,16,128]{3,2,1,0:T(8,128)S(1)} %slice.308), channel_id=1, source_target_pairs={{0,96},{4,100},{8,104},{12,108},{16,112},{20,116},{24,120},{28,124... | collective-permute-start | bytes 786440 | tf_op jit(solution)/shard_map/ppermute | solution.py:21
  87.5 2.8 %collective-permute-done.16 = f32[1,32,16,128]{3,2,1,0:T(8,128)S(1)} collective-permute-done((f32[1,32,16,128]{3,2,1,0:T(8,128)S(1)}, f32[1,32,16,128]{3,2,1,0:T(8,128)S(1)}, u32[]{:S(2)}, u32[]{:S(2)}) %collective-permute-start.16) | collective-permute-done | bytes 262176 | tf_op jit(solution)/shard_map/ppermute | solution.py:21
  90.2 1.5 collective-permute-done.17
  91.8 2.7 %select_bitcast_fusion = (f32[32,32,128]{2,1,0:T(8,128)S(1)}, f32[1,32,32,128]{3,2,1,0:T(8,128)S(1)}) fusion(f32[1,32,32,128]{3,2,1,0:T(8,128)} %copy-done.6, f32[32,64,128]{2,1,0:T(8,128)S(1)} %fusion.37, s32[]{:T(128)S(6)} %select_n.251, f32[32]{0:T(128)S(1)} %get-tuple-element.60, pred[]{:T(512)S(6)} %eq.9, f32[1,32,32,128]{3,2,1,0:T(8,128)} %copy-done.1, ...), kind=kLoop, calls=%fused_computation.51 | loop fusion | flops 2883584 | bytes 5243915 | tf_op jit(solution)/shard_map/concatenate | solution.py:141
  94.8 9.5 %fusion = f32[32,64,512]{2,1,0:T(8,128)S(1)} fusion(bf16[512,32,64]{0,2,1:T(8,128)(2,1)S(1)} %bitcast.217, f32[32,512]{1,0:T(8,128)S(1)} %copy-done.14, f32[32,512]{1,0:T(8,128)S(1)} %copy-done.15, f32[512,512]{1,0:T(8,128)S(1)} %fusion.39, pred[512,512]{1,0:T(8,128)(4,1)S(1)} %copy-done.11), kind=kOutput, calls=%fused_computation.1 | convolution fusion | flops 1115684864 | bytes 7733248 | tf_op jit(solution)/shard_map/phij,jphd->iphd/dot_general | solution.py:155
  104.3 2.3 %fusion.8 = f32[512,1,32,64]{0,3,2,1:T(8,128)S(1)} fusion(f32[32,64,512]{2,1,0:T(8,128)S(1)} %fusion, f32[32]{0:T(128)S(1)} %copy-done.21, f32[512,32]{0,1:T(8,128)S(1)} %bitcast.225, f32[32,32,128]{2,1,0:T(8,128)S(1)} %bitcast.223, f32[32,32,128]{2,1,0:T(8,128)S(1)} %get-tuple-element.21, pred[]{:T(512)S(6)} %eq.9, ...), kind=kOutput, calls=%fused_computation.13 | convolution fusion | flops 1616642048 | bytes 11731457 | tf_op jit(solution)/shard_map/ipn,phdn->iphd/dot_general | solution.py:157
  106.6 1.4 multiply_reduce_fusion
  108.0 2.0 collective-permute-start.19
  110.0 3.6 %collective-permute-start.20 = (f32[512,1]{0,1:T(1,128)S(1)}, f32[512,1]{0,1:T(1,128)S(1)}, u32[]{:S(2)}, u32[]{:S(2)}) collective-permute-start(f32[512,1]{0,1:T(1,128)S(1)} %bitcast.248), channel_id=1, source_target_pairs={{0,2},{1,3},{2,0},{3,1},{4,6},{5,7},{6,4},{7,5},{8,10},{9,11},{10,... | collective-permute-start | bytes 6152 | tf_op jit(solution)/shard_map/ppermute | solution.py:21
  113.6 1.0 collective-permute-start.21
  115.2 2.0 %collective-permute-done.21 = f32[512,1]{0,1:T(1,128)S(1)} collective-permute-done((f32[512,1]{0,1:T(1,128)S(1)}, f32[512,1]{0,1:T(1,128)S(1)}, u32[]{:S(2)}, u32[]{:S(2)}) %collective-permute-start.21) | collective-permute-done | bytes 2080 | tf_op jit(solution)/shard_map/ppermute | solution.py:21
  117.2 14.6 %fusion.2 = bf16[512,1,4096]{2,0,1:T(8,128)(2,1)} fusion(bf16[2048,4096]{1,0:T(8,128)(2,1)} %param.26, f32[512,1,2048]{0,2,1:T(8,128)S(1)} %get-tuple-element.20, f32[2048]{0:T(1024)S(1)} %copy-done.31, f32[512]{0:T(512)S(1)} %bitcast.257), kind=kOutput, calls=%fused_computation.4 | convolution fusion | flops 8595177472 | bytes 25176064 | tf_op jit(solution)/shard_map/tpi,id->tpd/dot_general | solution.py:174
  131.9 0.9 copy-done.8
  133.2 24.9 %all-gather = bf16[96,1,256]{2,1,0:T(2,128)(2,1)S(1)} all-gather(bf16[3,1,256]{2,1,0:T(2,128)(2,1)S(1)} %copy.72), channel_id=2, replica_groups=mesh['ctx'=32,'head'=4] {'ctx'}, dimensions={0}, use_global_device_ids=true | all-gather | bytes 50688 | tf_op jit(solution)/shard_map/all_gather | solution.py:113
  158.1 24.7 %all-gather.1 = bf16[96,1,2048]{2,1,0:T(2,128)(2,1)S(1)} all-gather(bf16[3,1,2048]{2,1,0:T(2,128)(2,1)S(1)} %copy.76), channel_id=3, replica_groups=mesh['ctx'=32,'head'=4] {'ctx'}, dimensions={0}, use_global_device_ids=true | all-gather | bytes 405504 | tf_op jit(solution)/shard_map/all_gather | solution.py:113
  184.2 1.8 add_select_fusion
  189.1 1.6 convolution_multiply_fusion
  191.4 0.7 pad_maximum_fusion.3
  (184 shorter events, 11.1 us)
Async XLA Ops:
  7.2 8.9 %copy-start.32 = (f32[32]{0:T(128)S(1)}, f32[32]{0:T(128)}, u32[]{:S(2)}) copy-start(f32[32]{0:T(128)} %param.21) | copy-start | bytes 388
  7.2 8.9 %copy-start.10 = (f32[512,1,32]{0,2,1:T(8,128)S(1)}, f32[512,1,32]{0,2,1:T(8,128)}, u32[]{:S(2)}) copy-start(f32[512,1,32]{0,2,1:T(8,128)} %param.19) | copy-start | bytes 196612
  7.2 8.9 %copy-start.20 = (f32[32]{0:T(128)S(1)}, f32[32]{0:T(128)}, u32[]{:S(2)}) copy-start(f32[32]{0:T(128)} %param.20) | copy-start | bytes 388
  7.2 11.6 %copy-start.16 = (bf16[4,2048]{1,0:T(4,128)(2,1)S(1)}, bf16[4,2048]{1,0:T(4,128)(2,1)}, u32[]{:S(2)}) copy-start(bf16[4,2048]{1,0:T(4,128)(2,1)} %param.23) | copy-start | bytes 49156
  7.2 11.7 %copy-start.19 = (bf16[4,256]{1,0:T(4,128)(2,1)S(1)}, bf16[4,256]{1,0:T(4,128)(2,1)}, u32[]{:S(2)}) copy-start(bf16[4,256]{1,0:T(4,128)(2,1)} %param.24) | copy-start | bytes 6148
  7.2 184.9 %reduce-scatter.2.cloned.1.call-start = ((), (), s32[]{:S(2)}) async-start(), calls=%async_computation.1 | async-start | bytes 5242880 | tf_op jit(solution)/shard_map/reduce_scatter | solution.py:173
  10.4 16.8 %copy-start.7 = (bf16[3,1,2048]{0,2,1:T(8,128)(2,1)}, bf16[3,1,2048]{0,2,1:T(8,128)(2,1)S(1)}, u32[]{:S(2)}) copy-start(bf16[3,1,2048]{0,2,1:T(8,128)(2,1)S(1)} %slice.292) | copy-start | bytes 36868
  10.4 8.9 %collective-permute-start = (bf16[3,1,2048]{0,2,1:T(8,128)(2,1)S(1)}, bf16[3,1,2048]{0,2,1:T(8,128)(2,1)}, u32[]{:S(2)}, u32[]{:S(2)}) collective-permute-start(bf16[3,1,2048]{0,2,1:T(8,128)(2,1)S(1)} %slice.292), channel_id=1, source_target_pairs={{0,4},{4,8},{8,12},{12,16},{16,20},{20,24},{24,28},{28,32},{32,36}... | collective-permute-start | bytes 36872 | tf_op jit(solution)/shard_map/ppermute | solution.py:12
  12.5 6.4 %collective-permute-start.1 = (bf16[3,1,256]{2,0,1:T(4,128)(2,1)S(1)}, bf16[3,1,256]{2,0,1:T(4,128)(2,1)S(1)}, u32[]{:S(2)}, u32[]{:S(2)}) collective-permute-start(bf16[3,1,256]{2,0,1:T(4,128)(2,1)S(1)} %slice.233), channel_id=1, source_target_pairs={{0,4},{4,8},{8,12},{12,16},{16,20},{20,24},{24,28},{28,32},{32,36}... | collective-permute-start | bytes 4616 | tf_op jit(solution)/shard_map/ppermute | solution.py:12
  27.9 2.9 %collective-permute-start.9 = (f32[1,32,32,128]{3,2,1,0:T(8,128)S(1)}, f32[1,32,32,128]{3,2,1,0:T(8,128)S(1)}, u32[]{:S(2)}, u32[]{:S(2)}) collective-permute-start(f32[1,32,32,128]{3,2,1,0:T(8,128)S(1)} %dynamic-slice_bitcast_fusion), channel_id=1, source_target_pairs={{0,4},{4,0},{8,12},{12,8},{16,20},{20,16},{24,28},{28,24},{32,36},... | collective-permute-start | bytes 1572872 | tf_op jit(solution)/shard_map/ppermute | solution.py:21
  29.3 1.5 collective-permute-start.2
  31.8 16.6 %collective-permute-start.11 = (f32[1,32,32,128]{3,2,1,0:T(8,128)S(1)}, f32[1,32,32,128]{3,2,1,0:T(8,128)S(1)}, u32[]{:S(2)}, u32[]{:S(2)}) collective-permute-start(f32[1,32,32,128]{3,2,1,0:T(8,128)S(1)} %fusion.28), channel_id=1, source_target_pairs={{0,8},{4,12},{8,16},{12,20},{16,24},{20,28},{24,0},{28,4},{32,40},... | collective-permute-start | bytes 1572872 | tf_op jit(solution)/shard_map/ppermute | solution.py:21
  34.7 23.8 %collective-permute-start.10 = (f32[1,32,32,128]{3,2,1,0:T(8,128)S(1)}, f32[1,32,32,128]{3,2,1,0:T(8,128)S(1)}, u32[]{:S(2)}, u32[]{:S(2)}) collective-permute-start(f32[1,32,32,128]{3,2,1,0:T(8,128)S(1)} %fusion.28), channel_id=1, source_target_pairs={{0,24},{4,28},{8,0},{12,4},{16,8},{20,12},{24,16},{28,20},{32,56},... | collective-permute-start | bytes 1572872 | tf_op jit(solution)/shard_map/ppermute | solution.py:21
  48.4 25.1 %copy-start.1 = (f32[1,32,32,128]{3,2,1,0:T(8,128)}, f32[1,32,32,128]{3,2,1,0:T(8,128)S(1)}, u32[]{:S(2)}) copy-start(f32[1,32,32,128]{3,2,1,0:T(8,128)S(1)} %collective-permute-done.11) | copy-start | bytes 1572868
  49.2 12.6 %collective-permute-start.12 = (f32[1,32,16,128]{3,2,1,0:T(8,128)}, f32[1,32,16,128]{3,2,1,0:T(8,128)S(1)}, u32[]{:S(2)}, u32[]{:S(2)}) collective-permute-start(f32[1,32,16,128]{3,2,1,0:T(8,128)} %slice.305), channel_id=1, source_target_pairs={{0,8},{4,12},{8,16},{12,20},{16,24},{20,28},{24,0},{28,4},{32,40},... | collective-permute-start | bytes 786440 | tf_op jit(solution)/shard_map/ppermute | solution.py:21
  49.7 8.8 %collective-permute-start.4 = (f32[1,32]{1,0:T(1,128)S(1)}, f32[1,32]{1,0:T(1,128)S(1)}, u32[]{:S(2)}, u32[]{:S(2)}) collective-permute-start(f32[1,32]{1,0:T(1,128)S(1)} %get-tuple-element.59), channel_id=1, source_target_pairs={{0,8},{4,12},{8,16},{12,20},{16,24},{20,28},{24,0},{28,4},{32,40},... | collective-permute-start | bytes 392 | tf_op jit(solution)/shard_map/ppermute | solution.py:21
  51.3 10.4 %collective-permute-start.3 = (f32[1,32]{1,0:T(1,128)S(1)}, f32[1,32]{1,0:T(1,128)S(1)}, u32[]{:S(2)}, u32[]{:S(2)}) collective-permute-start(f32[1,32]{1,0:T(1,128)S(1)} %get-tuple-element.59), channel_id=1, source_target_pairs={{0,24},{4,28},{8,0},{12,4},{16,8},{20,12},{24,16},{28,20},{32,56},... | collective-permute-start | bytes 392 | tf_op jit(solution)/shard_map/ppermute | solution.py:21
  58.5 7.4 %collective-permute-start.5 = (f32[1,32]{1,0:T(1,128)S(1)}, f32[1,32]{1,0:T(1,128)S(1)}, u32[]{:S(2)}, u32[]{:S(2)}) collective-permute-start(f32[1,32]{1,0:T(1,128)S(1)} %collective-permute-done.4), channel_id=1, source_target_pairs={{0,8},{4,12},{8,16},{12,20},{16,24},{20,28},{24,0},{28,4},{32,40},... | collective-permute-start | bytes 392 | tf_op jit(solution)/shard_map/ppermute | solution.py:21
  58.5 15.0 %copy-start.2 = (f32[1,32,32,128]{3,2,1,0:T(8,128)}, f32[1,32,32,128]{3,2,1,0:T(8,128)S(1)}, u32[]{:S(2)}) copy-start(f32[1,32,32,128]{3,2,1,0:T(8,128)S(1)} %collective-permute-done.10) | copy-start | bytes 1572868
  58.5 7.4 %collective-permute-start.13 = (f32[1,32,16,128]{3,2,1,0:T(8,128)S(1)}, f32[1,32,16,128]{3,2,1,0:T(8,128)S(1)}, u32[]{:S(2)}, u32[]{:S(2)}) collective-permute-start(f32[1,32,16,128]{3,2,1,0:T(8,128)S(1)} %slice.306), channel_id=1, source_target_pairs={{0,24},{4,28},{8,0},{12,4},{16,8},{20,12},{24,16},{28,20},{32,56},... | collective-permute-start | bytes 786440 | tf_op jit(solution)/shard_map/ppermute | solution.py:21
  61.8 11.7 %copy-start.28 = (f32[32]{0:T(128)}, f32[32]{0:T(128)S(1)}, u32[]{:S(2)}) copy-start(f32[32]{0:T(128)S(1)} %broadcast_multiply_fusion.2) | copy-start | bytes 388
  65.9 7.6 %copy-start.3 = (f32[1,32,32,128]{3,2,1,0:T(8,128)}, f32[1,32,32,128]{3,2,1,0:T(8,128)S(1)}, u32[]{:S(2)}) copy-start(f32[1,32,32,128]{3,2,1,0:T(8,128)S(1)} %constant_dynamic-update-slice_fusion) | copy-start | bytes 1572868
  67.1 14.4 %collective-permute-start.15 = (f32[1,32,32,128]{3,2,1,0:T(8,128)}, f32[1,32,32,128]{3,2,1,0:T(8,128)}, u32[]{:S(2)}, u32[]{:S(2)}) collective-permute-start(f32[1,32,32,128]{3,2,1,0:T(8,128)} %add_select_fusion.2), channel_id=1, source_target_pairs={{0,32},{4,36},{8,40},{12,44},{16,48},{20,52},{24,56},{28,60},{32,6... | collective-permute-start | bytes 1572872 | tf_op jit(solution)/shard_map/ppermute | solution.py:21
  70.8 13.3 %collective-permute-start.14 = (f32[1,32,32,128]{3,2,1,0:T(8,128)}, f32[1,32,32,128]{3,2,1,0:T(8,128)}, u32[]{:S(2)}, u32[]{:S(2)}) collective-permute-start(f32[1,32,32,128]{3,2,1,0:T(8,128)} %add_select_fusion.2), channel_id=1, source_target_pairs={{0,96},{4,100},{8,104},{12,108},{16,112},{20,116},{24,120},{28,124... | collective-permute-start | bytes 1572872 | tf_op jit(solution)/shard_map/ppermute | solution.py:21
  73.5 7.6 %collective-permute-start.6 = (f32[1,32]{1,0:T(1,128)}, f32[1,32]{1,0:T(1,128)S(1)}, u32[]{:S(2)}, u32[]{:S(2)}) collective-permute-start(f32[1,32]{1,0:T(1,128)} %get-tuple-element.23), channel_id=1, source_target_pairs={{0,32},{4,36},{8,40},{12,44},{16,48},{20,52},{24,56},{28,60},{32,6... | collective-permute-start | bytes 392 | tf_op jit(solution)/shard_map/ppermute | solution.py:21
  77.2 7.0 %collective-permute-start.8 = (f32[1,32]{1,0:T(1,128)}, f32[1,32]{1,0:T(1,128)S(1)}, u32[]{:S(2)}, u32[]{:S(2)}) collective-permute-start(f32[1,32]{1,0:T(1,128)} %get-tuple-element.23), channel_id=1, source_target_pairs={{0,96},{4,100},{8,104},{12,108},{16,112},{20,116},{24,120},{28,124... | collective-permute-start | bytes 392 | tf_op jit(solution)/shard_map/ppermute | solution.py:21
  81.1 13.4 %copy-start.22 = (f32[1,32]{1,0:T(1,128)}, f32[1,32]{1,0:T(1,128)S(1)}, u32[]{:S(2)}) copy-start(f32[1,32]{1,0:T(1,128)S(1)} %collective-permute-done.6) | copy-start | bytes 388
  81.1 10.7 %collective-permute-start.7 = (f32[1,32]{1,0:T(1,128)S(1)}, f32[1,32]{1,0:T(1,128)S(1)}, u32[]{:S(2)}, u32[]{:S(2)}) collective-permute-start(f32[1,32]{1,0:T(1,128)S(1)} %collective-permute-done.6), channel_id=1, source_target_pairs={{0,32},{4,36},{8,40},{12,44},{16,48},{20,52},{24,56},{28,60},{32,6... | collective-permute-start | bytes 392 | tf_op jit(solution)/shard_map/ppermute | solution.py:21
  82.6 7.7 %collective-permute-start.16 = (f32[1,32,16,128]{3,2,1,0:T(8,128)S(1)}, f32[1,32,16,128]{3,2,1,0:T(8,128)S(1)}, u32[]{:S(2)}, u32[]{:S(2)}) collective-permute-start(f32[1,32,16,128]{3,2,1,0:T(8,128)S(1)} %slice.307), channel_id=1, source_target_pairs={{0,32},{4,36},{8,40},{12,44},{16,48},{20,52},{24,56},{28,60},{32,6... | collective-permute-start | bytes 786440 | tf_op jit(solution)/shard_map/ppermute | solution.py:21
  84.1 10.5 %copy-start.26 = (f32[32]{0:T(128)}, f32[32]{0:T(128)S(1)}, u32[]{:S(2)}) copy-start(f32[32]{0:T(128)S(1)} %multiply_bitcast_fusion.1) | copy-start | bytes 388
  85.1 6.6 %collective-permute-start.17 = (f32[1,32,16,128]{3,2,1,0:T(8,128)S(1)}, f32[1,32,16,128]{3,2,1,0:T(8,128)S(1)}, u32[]{:S(2)}, u32[]{:S(2)}) collective-permute-start(f32[1,32,16,128]{3,2,1,0:T(8,128)S(1)} %slice.308), channel_id=1, source_target_pairs={{0,96},{4,100},{8,104},{12,108},{16,112},{20,116},{24,120},{28,124... | collective-permute-start | bytes 786440 | tf_op jit(solution)/shard_map/ppermute | solution.py:21
  91.8 12.5 %copy-start.24 = (f32[1,32]{1,0:T(1,128)}, f32[1,32]{1,0:T(1,128)S(1)}, u32[]{:S(2)}) copy-start(f32[1,32]{1,0:T(1,128)S(1)} %collective-permute-done.7) | copy-start | bytes 388
  94.7 9.6 %collective-permute-start.18 = (f32[1,32,32,128]{3,2,1,0:T(8,128)S(1)}, f32[1,32,32,128]{3,2,1,0:T(8,128)S(1)}, u32[]{:S(2)}, u32[]{:S(2)}) collective-permute-start(f32[1,32,32,128]{3,2,1,0:T(8,128)S(1)} %fusion.29), channel_id=1, source_target_pairs={{0,4},{4,0},{8,12},{12,8},{16,20},{20,16},{24,28},{28,24},{32,36},... | collective-permute-start | bytes 1572872 | tf_op jit(solution)/shard_map/ppermute | solution.py:21
  94.8 9.5 %copy-start.21 = (f32[32]{0:T(128)S(1)}, f32[32]{0:T(128)}, u32[]{:S(2)}) copy-start(f32[32]{0:T(128)} %param.22) | copy-start | bytes 388
  106.6 10.6 %copy-start.31 = (f32[2048]{0:T(1024)S(1)}, f32[2048]{0:T(1024)}, u32[]{:S(2)}) copy-start(f32[2048]{0:T(1024)} %param.25) | copy-start | bytes 24580
  108.0 6.6 %collective-permute-start.19 = (f32[512,1]{0,1:T(1,128)S(1)}, f32[512,1]{0,1:T(1,128)S(1)}, u32[]{:S(2)}, u32[]{:S(2)}) collective-permute-start(f32[512,1]{0,1:T(1,128)S(1)} %bitcast.247), channel_id=1, source_target_pairs={{0,1},{1,2},{2,3},{3,0},{4,5},{5,6},{6,7},{7,4},{8,9},{9,10},{10,1... | collective-permute-start | bytes 6152 | tf_op jit(solution)/shard_map/ppermute | solution.py:21
  110.0 5.2 %collective-permute-start.20 = (f32[512,1]{0,1:T(1,128)S(1)}, f32[512,1]{0,1:T(1,128)S(1)}, u32[]{:S(2)}, u32[]{:S(2)}) collective-permute-start(f32[512,1]{0,1:T(1,128)S(1)} %bitcast.248), channel_id=1, source_target_pairs={{0,2},{1,3},{2,0},{3,1},{4,6},{5,7},{6,4},{7,5},{8,10},{9,11},{10,... | collective-permute-start | bytes 6152 | tf_op jit(solution)/shard_map/ppermute | solution.py:21
  113.6 3.6 %collective-permute-start.21 = (f32[512,1]{0,1:T(1,128)S(1)}, f32[512,1]{0,1:T(1,128)S(1)}, u32[]{:S(2)}, u32[]{:S(2)}) collective-permute-start(f32[512,1]{0,1:T(1,128)S(1)} %bitcast.249), channel_id=1, source_target_pairs={{0,3},{1,0},{2,1},{3,2},{4,7},{5,4},{6,5},{7,6},{8,11},{9,8},{10,9... | collective-permute-start | bytes 6152 | tf_op jit(solution)/shard_map/ppermute | solution.py:21
  131.8 51.1 %copy-start.33 = (s32[8]{0:T(128)S(1)}, s32[8]{0:T(128)}, u32[]{:S(2)}) copy-start(s32[8]{0:T(128)} %param.27) | copy-start | bytes 100
  131.8 51.2 %copy-start.13 = (bf16[4,8,2048]{2,1,0:T(8,128)(2,1)S(1)}, bf16[4,8,2048]{2,1,0:T(8,128)(2,1)}, u32[]{:S(2)}) copy-start(bf16[4,8,2048]{2,1,0:T(8,128)(2,1)} %param.28) | copy-start | bytes 393220
  131.8 51.6 %copy-start.17 = (bf16[4,8,256]{2,1,0:T(8,128)(2,1)S(1)}, bf16[4,8,256]{2,1,0:T(8,128)(2,1)}, u32[]{:S(2)}) copy-start(bf16[4,8,256]{2,1,0:T(8,128)(2,1)} %param.30) | copy-start | bytes 49156
  131.8 52.1 %copy-start.18 = (f32[4,8,32]{2,1,0:T(8,128)S(1)}, f32[4,8,32]{2,1,0:T(8,128)}, u32[]{:S(2)}) copy-start(f32[4,8,32]{2,1,0:T(8,128)} %param.31) | copy-start | bytes 12292
  131.8 52.4 %copy-start.5 = (f32[1,32,32,128]{3,2,1,0:T(8,128)S(1)}, f32[1,32,32,128]{3,2,1,0:T(8,128)}, u32[]{:S(2)}) copy-start(f32[1,32,32,128]{3,2,1,0:T(8,128)} %copy-done.4) | copy-start | bytes 1572868
  131.8 52.4 %copy-start.23 = (f32[1,32]{1,0:T(1,128)S(1)}, f32[1,32]{1,0:T(1,128)}, u32[]{:S(2)}) copy-start(f32[1,32]{1,0:T(1,128)} %copy-done.22) | copy-start | bytes 388
  131.8 52.4 %copy-start.25 = (f32[1,32]{1,0:T(1,128)S(1)}, f32[1,32]{1,0:T(1,128)}, u32[]{:S(2)}) copy-start(f32[1,32]{1,0:T(1,128)} %copy-done.24) | copy-start | bytes 388
  131.8 52.4 %copy-start.27 = (f32[32]{0:T(128)S(1)}, f32[32]{0:T(128)}, u32[]{:S(2)}) copy-start(f32[32]{0:T(128)} %copy-done.26) | copy-start | bytes 388
  131.8 52.4 %copy-start.30 = (f32[1,32]{1,0:T(1,128)S(1)}, f32[1,32]{1,0:T(1,128)}, u32[]{:S(2)}) copy-start(f32[1,32]{1,0:T(1,128)} %copy-done.29) | copy-start | bytes 388
  186.0 3.1 %collective-permute-start.22 = (f32[1,32,32,128]{3,2,1,0:T(8,128)S(1)}, f32[1,32,32,128]{3,2,1,0:T(8,128)S(1)}, u32[]{:S(2)}, u32[]{:S(2)}) collective-permute-start(f32[1,32,32,128]{3,2,1,0:T(8,128)S(1)} %add_select_fusion), channel_id=1, source_target_pairs={{0,4},{4,0},{8,12},{12,8},{16,20},{20,16},{24,28},{28,24},{32,36},... | collective-permute-start | bytes 1572872 | tf_op jit(solution)/shard_map/ppermute | solution.py:21
  (10 other events, 46.9 us)
Sparse Core Ops, SparseCore 0:
  132.0 47.7 reduce-scatter.1

commit v8 on v7

--- a/solution.py
+++ b/solution.py
@@ -109,10 +109,11 @@
     count = lax.axis_size("ctx")
     here = lax.axis_index("ctx")
     core = here % 2
-    tails = jax.tree.map(
-        lambda part: lax.all_gather(part, "ctx")[count - 1],
-        (x_in[block_len - conv_taps + 1 :], bc_in[block_len - conv_taps + 1 :]),
-    )
+    history = lax.all_gather(
+        jnp.concatenate([x_in[block_len - conv_taps + 1 :], bc_in[block_len - conv_taps + 1 :]], -1),
+        "ctx",
+    )[count - 1]
+    tails = (history[..., :inner_loc], history[..., inner_loc:])
     half = head_dim // 2
     keep = lax.dynamic_slice_in_dim(s_local, core * half, half, 2)
     give = lax.dynamic_slice_in_dim(s_local, (1 - core) * half, half, 2)

time: 201 us -> 188 us (0.935)
  blocking collectives: 49.6 us -> 25.3 us
  waiting for transfers between devices: 31.3 us -> 43.1 us
    all_gather x2 -> x1, blocking collectives: 49.6 us -> 25.3 us  [body(): lax.all_gather(jnp.concatenate([x_in[block_len - conv_taps + 1:], bc_in[b...]
    reduce_scatter x1, waiting for transfers between devices: 0.01 us -> 11.7 us  [body(): lax.psum_scatter(jnp.einsum('tpi,id->tpd', normed, w_out, preferred_eleme...]
  transfers between devices with their start and end apart: 24 -> 24, of which waited for: 9 -> 10; matrix products, arithmetic and copies ran while one was open for 15% -> 16% of each run, Pallas kernels for 0% -> 0%
where the time goes in v8:
time: 188 us; the launch traced here: 187 us
  waiting for transfers between devices  43.1 us (23%)
  starting transfers between devices  37.3 us (20%)
  matrix products  28.9 us (15%)
  blocking collectives  25.3 us (13%)
  other arithmetic  21 us (11%)
  local copies, waits for them, and re-layouts  15.8 us (8%)
  between operations  15.1 us (8%)
    ppermute x21, starting transfers between devices, group_shift(): return lax.ppermute(value, axis, pairs)  31.6 us
    ppermute x21, waiting for transfers between devices, group_shift(): return lax.ppermute(value, axis, pairs)  31.3 us
    all_gather x1, blocking collectives, body(): lax.all_gather(jnp.concatenate([x_in[block_len - conv_taps + 1:], bc_in[b...  25.3 us
    dot_general x1, matrix products, body(): jnp.einsum('tpi,id->tpd', normed, w_out, preferred_element_type=jnp.float32)  14.6 us
    reduce_scatter x1, waiting for transfers between devices, body(): lax.psum_scatter(jnp.einsum('tpi,id->tpd', normed, w_out, preferred_eleme...  11.7 us
    dot_general x1, matrix products, body(): jnp.einsum('phij,jphd->iphd', mixing, x_heads, preferred_element_type=jnp...  9.46 us
    unnamed x75, local copies, waits for them, and re-layouts  7.57 us
    convert_element_type x1, other arithmetic, body(): weighted_x = (x_heads * tail_weights[..., None]).astype(jnp.bfloat16)  7.34 us
  transfers between devices with their start and end apart: 24, of which 10 were waited for; matrix products, arithmetic and copies ran while one was open for 16% of the time, Pallas kernels for 0%

profile of v8, /device:TPU:0, one launch (start us, length us, event | category | flops | bytes accessed | tf_op | source)
XLA Modules:
  0.0 186.6 jit_solution(11065482750221579708)
XLA Ops:
  7.3 2.9 %copy.82 = bf16[512,1,2048]{0,2,1:T(8,128)(2,1)S(1)} copy(bf16[512,1,2048]{2,0,1:T(8,128)(2,1)} %param.16) | data formatting | bytes 4194304 | tf_op args[0]
  10.4 2.1 %collective-permute-start = (bf16[3,1,2048]{0,2,1:T(8,128)(2,1)S(1)}, bf16[3,1,2048]{0,2,1:T(8,128)(2,1)}, u32[]{:S(2)}, u32[]{:S(2)}) collective-permute-start(bf16[3,1,2048]{0,2,1:T(8,128)(2,1)S(1)} %slice.297), channel_id=1, source_target_pairs={{0,4},{4,8},{8,12},{12,16},{16,20},{20,24},{24,28},{28,32},{32,36}... | collective-permute-start | bytes 36872 | tf_op jit(solution)/shard_map/ppermute | solution.py:12
  12.5 3.5 %collective-permute-start.1 = (bf16[3,1,256]{2,0,1:T(4,128)(2,1)S(1)}, bf16[3,1,256]{2,0,1:T(4,128)(2,1)S(1)}, u32[]{:S(2)}, u32[]{:S(2)}) collective-permute-start(bf16[3,1,256]{2,0,1:T(4,128)(2,1)S(1)} %slice.236), channel_id=1, source_target_pairs={{0,4},{4,8},{8,12},{12,16},{16,20},{20,24},{24,28},{28,32},{32,36}... | collective-permute-start | bytes 4616 | tf_op jit(solution)/shard_map/ppermute | solution.py:12
  16.1 0.7 fusion.97
  16.9 1.2 reduce-window.6
  19.8 7.3 %fusion.9 = (bf16[512,1,2048]{0,2,1:T(8,128)(2,1)S(1)}, bf16[512,1,2048]{0,2,1:T(8,128)(2,1)}) fusion(f32[2048]{0:T(1024)S(1)} %bitcast.233, bf16[512,1,2048]{0,2,1:T(8,128)(2,1)S(1)} %copy.82, f32[2048]{0:T(1024)S(1)} %bitcast.235, bf16[3,1,2048]{0,2,1:T(8,128)(2,1)} %collective-permute-done, f32[2048]{0:T(1024)S(1)} %bitcast.231, f32[2048]{0:T(1024)S(1)} %bitcast.229, ...), kind=kLoop, calls=%fused_computation.15 | loop fusion | flops 29360128 | bytes 10530816 | tf_op jit(solution)/shard_map/convert_element_type | solution.py:105
  27.2 0.7 fusion.37
  27.9 1.4 collective-permute-start.9
  29.4 1.4 collective-permute-done.2
  30.9 0.8 copy-done.6
  31.8 2.9 %collective-permute-start.11 = (f32[1,32,32,128]{3,2,1,0:T(8,128)S(1)}, f32[1,32,32,128]{3,2,1,0:T(8,128)S(1)}, u32[]{:S(2)}, u32[]{:S(2)}) collective-permute-start(f32[1,32,32,128]{3,2,1,0:T(8,128)S(1)} %fusion.28), channel_id=1, source_target_pairs={{0,8},{4,12},{8,16},{12,20},{16,24},{20,28},{24,0},{28,4},{32,40},... | collective-permute-start | bytes 1572872 | tf_op jit(solution)/shard_map/ppermute | solution.py:21
  34.7 1.5 collective-permute-start.10
  36.2 12.1 %collective-permute-done.11 = f32[1,32,32,128]{3,2,1,0:T(8,128)S(1)} collective-permute-done((f32[1,32,32,128]{3,2,1,0:T(8,128)S(1)}, f32[1,32,32,128]{3,2,1,0:T(8,128)S(1)}, u32[]{:S(2)}, u32[]{:S(2)}) %collective-permute-start.11) | collective-permute-done | bytes 524320 | tf_op jit(solution)/shard_map/ppermute | solution.py:21
  48.4 0.8 slice.310
  49.7 1.6 collective-permute-start.4
  51.3 1.7 collective-permute-start.3
  53.0 5.5 %collective-permute-done.4 = f32[1,32]{1,0:T(1,128)S(1)} collective-permute-done((f32[1,32]{1,0:T(1,128)S(1)}, f32[1,32]{1,0:T(1,128)S(1)}, u32[]{:S(2)}, u32[]{:S(2)}) %collective-permute-start.4) | collective-permute-done | bytes 160 | tf_op jit(solution)/shard_map/ppermute | solution.py:21
  58.5 3.3 %collective-permute-start.13 = (f32[1,32,16,128]{3,2,1,0:T(8,128)S(1)}, f32[1,32,16,128]{3,2,1,0:T(8,128)S(1)}, u32[]{:S(2)}, u32[]{:S(2)}) collective-permute-start(f32[1,32,16,128]{3,2,1,0:T(8,128)S(1)} %slice.311), channel_id=1, source_target_pairs={{0,24},{4,28},{8,0},{12,4},{16,8},{20,12},{24,16},{28,20},{32,56},... | collective-permute-start | bytes 786440 | tf_op jit(solution)/shard_map/ppermute | solution.py:21
  61.8 4.0 %collective-permute-done.13 = f32[1,32,16,128]{3,2,1,0:T(8,128)S(1)} collective-permute-done((f32[1,32,16,128]{3,2,1,0:T(8,128)S(1)}, f32[1,32,16,128]{3,2,1,0:T(8,128)S(1)}, u32[]{:S(2)}, u32[]{:S(2)}) %collective-permute-start.13) | collective-permute-done | bytes 262176 | tf_op jit(solution)/shard_map/ppermute | solution.py:21
  65.9 1.2 add_select_fusion.2
  67.1 3.1 %collective-permute-start.15 = (f32[1,32,32,128]{3,2,1,0:T(8,128)}, f32[1,32,32,128]{3,2,1,0:T(8,128)}, u32[]{:S(2)}, u32[]{:S(2)}) collective-permute-start(f32[1,32,32,128]{3,2,1,0:T(8,128)} %add_select_fusion.2), channel_id=1, source_target_pairs={{0,32},{4,36},{8,40},{12,44},{16,48},{20,52},{24,56},{28,60},{32,6... | collective-permute-start | bytes 1572872 | tf_op jit(solution)/shard_map/ppermute | solution.py:21
  70.8 1.3 collective-permute-start.14
  72.1 0.8 iota_compare_fusion
  73.5 0.8 collective-permute-start.6
  74.3 2.9 %copy.91 = bf16[512,1,2048]{0,2,1:T(8,128)(2,1)S(1)} copy(bf16[512,1,2048]{2,0,1:T(8,128)(2,1)} %param.17) | data formatting | bytes 4194304 | tf_op args[1]
  77.2 2.5 %collective-permute-start.8 = (f32[1,32]{1,0:T(1,128)}, f32[1,32]{1,0:T(1,128)S(1)}, u32[]{:S(2)}, u32[]{:S(2)}) collective-permute-start(f32[1,32]{1,0:T(1,128)} %get-tuple-element.23), channel_id=1, source_target_pairs={{0,96},{4,100},{8,104},{12,108},{16,112},{20,116},{24,120},{28,124... | collective-permute-start | bytes 392 | tf_op jit(solution)/shard_map/ppermute | solution.py:21
  79.7 1.4 collective-permute-done.6
  81.6 1.0 slice.312
  82.6 1.6 collective-permute-start.16
  84.1 1.0 slice.313
  85.1 2.0 %collective-permute-start.17 = (f32[1,32,16,128]{3,2,1,0:T(8,128)S(1)}, f32[1,32,16,128]{3,2,1,0:T(8,128)S(1)}, u32[]{:S(2)}, u32[]{:S(2)}) collective-permute-start(f32[1,32,16,128]{3,2,1,0:T(8,128)S(1)} %slice.313), channel_id=1, source_target_pairs={{0,96},{4,100},{8,104},{12,108},{16,112},{20,116},{24,120},{28,124... | collective-permute-start | bytes 786440 | tf_op jit(solution)/shard_map/ppermute | solution.py:21
  87.5 2.8 %collective-permute-done.16 = f32[1,32,16,128]{3,2,1,0:T(8,128)S(1)} collective-permute-done((f32[1,32,16,128]{3,2,1,0:T(8,128)S(1)}, f32[1,32,16,128]{3,2,1,0:T(8,128)S(1)}, u32[]{:S(2)}, u32[]{:S(2)}) %collective-permute-start.16) | collective-permute-done | bytes 262176 | tf_op jit(solution)/shard_map/ppermute | solution.py:21
  90.2 1.5 collective-permute-done.17
  91.8 2.7 %select_bitcast_fusion = (f32[32,32,128]{2,1,0:T(8,128)S(1)}, f32[1,32,32,128]{3,2,1,0:T(8,128)S(1)}) fusion(f32[1,32,32,128]{3,2,1,0:T(8,128)} %copy-done.6, f32[32,64,128]{2,1,0:T(8,128)S(1)} %fusion.37, s32[]{:T(128)S(6)} %select_n.251, f32[32]{0:T(128)S(1)} %get-tuple-element.60, pred[]{:T(512)S(6)} %eq.9, f32[1,32,32,128]{3,2,1,0:T(8,128)} %copy-done.1, ...), kind=kLoop, calls=%fused_computation.52 | loop fusion | flops 2883584 | bytes 5243915 | tf_op jit(solution)/shard_map/concatenate | solution.py:142
  94.8 9.5 %fusion = f32[32,64,512]{2,1,0:T(8,128)S(1)} fusion(bf16[512,32,64]{0,2,1:T(8,128)(2,1)S(1)} %bitcast.217, f32[32,512]{1,0:T(8,128)S(1)} %copy-done.14, f32[32,512]{1,0:T(8,128)S(1)} %copy-done.15, f32[512,512]{1,0:T(8,128)S(1)} %fusion.39, pred[512,512]{1,0:T(8,128)(4,1)S(1)} %copy-done.11), kind=kOutput, calls=%fused_computation.1 | convolution fusion | flops 1115684864 | bytes 7733248 | tf_op jit(solution)/shard_map/phij,jphd->iphd/dot_general | solution.py:156
  104.3 2.3 %fusion.8 = f32[512,1,32,64]{0,3,2,1:T(8,128)S(1)} fusion(f32[32,64,512]{2,1,0:T(8,128)S(1)} %fusion, f32[32]{0:T(128)S(1)} %copy-done.21, f32[512,32]{0,1:T(8,128)S(1)} %bitcast.225, f32[32,32,128]{2,1,0:T(8,128)S(1)} %bitcast.223, f32[32,32,128]{2,1,0:T(8,128)S(1)} %get-tuple-element.21, pred[]{:T(512)S(6)} %eq.9, ...), kind=kOutput, calls=%fused_computation.13 | convolution fusion | flops 1616642048 | bytes 11731457 | tf_op jit(solution)/shard_map/ipn,phdn->iphd/dot_general | solution.py:158
  106.6 1.4 multiply_reduce_fusion
  108.0 2.0 %collective-permute-start.19 = (f32[512,1]{0,1:T(1,128)S(1)}, f32[512,1]{0,1:T(1,128)S(1)}, u32[]{:S(2)}, u32[]{:S(2)}) collective-permute-start(f32[512,1]{0,1:T(1,128)S(1)} %bitcast.247), channel_id=1, source_target_pairs={{0,1},{1,2},{2,3},{3,0},{4,5},{5,6},{6,7},{7,4},{8,9},{9,10},{10,1... | collective-permute-start | bytes 6152 | tf_op jit(solution)/shard_map/ppermute | solution.py:21
  110.0 3.6 %collective-permute-start.20 = (f32[512,1]{0,1:T(1,128)S(1)}, f32[512,1]{0,1:T(1,128)S(1)}, u32[]{:S(2)}, u32[]{:S(2)}) collective-permute-start(f32[512,1]{0,1:T(1,128)S(1)} %bitcast.248), channel_id=1, source_target_pairs={{0,2},{1,3},{2,0},{3,1},{4,6},{5,7},{6,4},{7,5},{8,10},{9,11},{10,... | collective-permute-start | bytes 6152 | tf_op jit(solution)/shard_map/ppermute | solution.py:21
  113.6 1.0 collective-permute-start.21
  115.2 2.0 %collective-permute-done.21 = f32[512,1]{0,1:T(1,128)S(1)} collective-permute-done((f32[512,1]{0,1:T(1,128)S(1)}, f32[512,1]{0,1:T(1,128)S(1)}, u32[]{:S(2)}, u32[]{:S(2)}) %collective-permute-start.21) | collective-permute-done | bytes 2080 | tf_op jit(solution)/shard_map/ppermute | solution.py:21
  117.2 14.6 %fusion.2 = bf16[512,1,4096]{2,0,1:T(8,128)(2,1)} fusion(bf16[2048,4096]{1,0:T(8,128)(2,1)} %param.26, f32[512,1,2048]{0,2,1:T(8,128)S(1)} %get-tuple-element.20, f32[2048]{0:T(1024)S(1)} %copy-done.31, f32[512]{0:T(512)S(1)} %bitcast.257), kind=kOutput, calls=%fused_computation.4 | convolution fusion | flops 8595177472 | bytes 25176064 | tf_op jit(solution)/shard_map/tpi,id->tpd/dot_general | solution.py:175
  132.0 0.8 copy-done.8
  133.3 25.3 %all-gather = bf16[96,1,2304]{2,1,0:T(2,128)(2,1)S(1)} all-gather(bf16[3,1,2304]{2,1,0:T(2,128)(2,1)S(1)} %copy.93), channel_id=2, replica_groups=mesh['ctx'=32,'head'=4] {'ctx'}, dimensions={0}, use_global_device_ids=true | all-gather | bytes 456192 | tf_op jit(solution)/shard_map/all_gather | solution.py:112
  160.1 1.8 add_select_fusion
  165.0 1.6 convolution_multiply_fusion
  167.3 0.7 pad_maximum_fusion.4
  168.0 11.7 %reduce-scatter.2.cloned.1.call-done = bf16[128,1,4096]{2,0,1:T(8,128)(2,1)} async-done(((bf16[512,1,4096]{2,0,1:T(8,128)(2,1)}), bf16[128,1,4096]{2,0,1:T(8,128)(2,1)}) %reduce-scatter.2.cloned.1.call-update) | async-done | bytes 1048592 | tf_op jit(solution)/shard_map/reduce_scatter | solution.py:174
  (184 shorter events, 11.4 us)
Async XLA Ops:
  7.2 8.9 %copy-start.32 = (f32[32]{0:T(128)S(1)}, f32[32]{0:T(128)}, u32[]{:S(2)}) copy-start(f32[32]{0:T(128)} %param.21) | copy-start | bytes 388
  7.2 8.9 %copy-start.10 = (f32[512,1,32]{0,2,1:T(8,128)S(1)}, f32[512,1,32]{0,2,1:T(8,128)}, u32[]{:S(2)}) copy-start(f32[512,1,32]{0,2,1:T(8,128)} %param.19) | copy-start | bytes 196612
  7.2 8.9 %copy-start.20 = (f32[32]{0:T(128)S(1)}, f32[32]{0:T(128)}, u32[]{:S(2)}) copy-start(f32[32]{0:T(128)} %param.20) | copy-start | bytes 388
  7.2 11.6 %copy-start.16 = (bf16[4,2048]{1,0:T(4,128)(2,1)S(1)}, bf16[4,2048]{1,0:T(4,128)(2,1)}, u32[]{:S(2)}) copy-start(bf16[4,2048]{1,0:T(4,128)(2,1)} %param.23) | copy-start | bytes 49156
  7.2 11.7 %copy-start.19 = (bf16[4,256]{1,0:T(4,128)(2,1)S(1)}, bf16[4,256]{1,0:T(4,128)(2,1)}, u32[]{:S(2)}) copy-start(bf16[4,256]{1,0:T(4,128)(2,1)} %param.24) | copy-start | bytes 6148
  7.2 172.5 %reduce-scatter.2.cloned.1.call-start = ((), (), s32[]{:S(2)}) async-start(), calls=%async_computation.1 | async-start | bytes 5242880 | tf_op jit(solution)/shard_map/reduce_scatter | solution.py:174
  10.4 16.8 %copy-start.7 = (bf16[3,1,2048]{0,2,1:T(8,128)(2,1)}, bf16[3,1,2048]{0,2,1:T(8,128)(2,1)S(1)}, u32[]{:S(2)}) copy-start(bf16[3,1,2048]{0,2,1:T(8,128)(2,1)S(1)} %slice.297) | copy-start | bytes 36868
  10.4 8.9 %collective-permute-start = (bf16[3,1,2048]{0,2,1:T(8,128)(2,1)S(1)}, bf16[3,1,2048]{0,2,1:T(8,128)(2,1)}, u32[]{:S(2)}, u32[]{:S(2)}) collective-permute-start(bf16[3,1,2048]{0,2,1:T(8,128)(2,1)S(1)} %slice.297), channel_id=1, source_target_pairs={{0,4},{4,8},{8,12},{12,16},{16,20},{20,24},{24,28},{28,32},{32,36}... | collective-permute-start | bytes 36872 | tf_op jit(solution)/shard_map/ppermute | solution.py:12
  12.5 6.4 %collective-permute-start.1 = (bf16[3,1,256]{2,0,1:T(4,128)(2,1)S(1)}, bf16[3,1,256]{2,0,1:T(4,128)(2,1)S(1)}, u32[]{:S(2)}, u32[]{:S(2)}) collective-permute-start(bf16[3,1,256]{2,0,1:T(4,128)(2,1)S(1)} %slice.236), channel_id=1, source_target_pairs={{0,4},{4,8},{8,12},{12,16},{16,20},{20,24},{24,28},{28,32},{32,36}... | collective-permute-start | bytes 4616 | tf_op jit(solution)/shard_map/ppermute | solution.py:12
  27.9 2.9 %collective-permute-start.9 = (f32[1,32,32,128]{3,2,1,0:T(8,128)S(1)}, f32[1,32,32,128]{3,2,1,0:T(8,128)S(1)}, u32[]{:S(2)}, u32[]{:S(2)}) collective-permute-start(f32[1,32,32,128]{3,2,1,0:T(8,128)S(1)} %dynamic-slice_bitcast_fusion), channel_id=1, source_target_pairs={{0,4},{4,0},{8,12},{12,8},{16,20},{20,16},{24,28},{28,24},{32,36},... | collective-permute-start | bytes 1572872 | tf_op jit(solution)/shard_map/ppermute | solution.py:21
  29.3 1.5 collective-permute-start.2
  31.8 16.6 %collective-permute-start.11 = (f32[1,32,32,128]{3,2,1,0:T(8,128)S(1)}, f32[1,32,32,128]{3,2,1,0:T(8,128)S(1)}, u32[]{:S(2)}, u32[]{:S(2)}) collective-permute-start(f32[1,32,32,128]{3,2,1,0:T(8,128)S(1)} %fusion.28), channel_id=1, source_target_pairs={{0,8},{4,12},{8,16},{12,20},{16,24},{20,28},{24,0},{28,4},{32,40},... | collective-permute-start | bytes 1572872 | tf_op jit(solution)/shard_map/ppermute | solution.py:21
  34.7 23.8 %collective-permute-start.10 = (f32[1,32,32,128]{3,2,1,0:T(8,128)S(1)}, f32[1,32,32,128]{3,2,1,0:T(8,128)S(1)}, u32[]{:S(2)}, u32[]{:S(2)}) collective-permute-start(f32[1,32,32,128]{3,2,1,0:T(8,128)S(1)} %fusion.28), channel_id=1, source_target_pairs={{0,24},{4,28},{8,0},{12,4},{16,8},{20,12},{24,16},{28,20},{32,56},... | collective-permute-start | bytes 1572872 | tf_op jit(solution)/shard_map/ppermute | solution.py:21
  48.4 25.1 %copy-start.1 = (f32[1,32,32,128]{3,2,1,0:T(8,128)}, f32[1,32,32,128]{3,2,1,0:T(8,128)S(1)}, u32[]{:S(2)}) copy-start(f32[1,32,32,128]{3,2,1,0:T(8,128)S(1)} %collective-permute-done.11) | copy-start | bytes 1572868
  49.2 12.6 %collective-permute-start.12 = (f32[1,32,16,128]{3,2,1,0:T(8,128)}, f32[1,32,16,128]{3,2,1,0:T(8,128)S(1)}, u32[]{:S(2)}, u32[]{:S(2)}) collective-permute-start(f32[1,32,16,128]{3,2,1,0:T(8,128)} %slice.310), channel_id=1, source_target_pairs={{0,8},{4,12},{8,16},{12,20},{16,24},{20,28},{24,0},{28,4},{32,40},... | collective-permute-start | bytes 786440 | tf_op jit(solution)/shard_map/ppermute | solution.py:21
  49.7 8.8 %collective-permute-start.4 = (f32[1,32]{1,0:T(1,128)S(1)}, f32[1,32]{1,0:T(1,128)S(1)}, u32[]{:S(2)}, u32[]{:S(2)}) collective-permute-start(f32[1,32]{1,0:T(1,128)S(1)} %get-tuple-element.59), channel_id=1, source_target_pairs={{0,8},{4,12},{8,16},{12,20},{16,24},{20,28},{24,0},{28,4},{32,40},... | collective-permute-start | bytes 392 | tf_op jit(solution)/shard_map/ppermute | solution.py:21
  51.3 10.4 %collective-permute-start.3 = (f32[1,32]{1,0:T(1,128)S(1)}, f32[1,32]{1,0:T(1,128)S(1)}, u32[]{:S(2)}, u32[]{:S(2)}) collective-permute-start(f32[1,32]{1,0:T(1,128)S(1)} %get-tuple-element.59), channel_id=1, source_target_pairs={{0,24},{4,28},{8,0},{12,4},{16,8},{20,12},{24,16},{28,20},{32,56},... | collective-permute-start | bytes 392 | tf_op jit(solution)/shard_map/ppermute | solution.py:21
  58.5 7.4 %collective-permute-start.5 = (f32[1,32]{1,0:T(1,128)S(1)}, f32[1,32]{1,0:T(1,128)S(1)}, u32[]{:S(2)}, u32[]{:S(2)}) collective-permute-start(f32[1,32]{1,0:T(1,128)S(1)} %collective-permute-done.4), channel_id=1, source_target_pairs={{0,8},{4,12},{8,16},{12,20},{16,24},{20,28},{24,0},{28,4},{32,40},... | collective-permute-start | bytes 392 | tf_op jit(solution)/shard_map/ppermute | solution.py:21
  58.5 15.0 %copy-start.2 = (f32[1,32,32,128]{3,2,1,0:T(8,128)}, f32[1,32,32,128]{3,2,1,0:T(8,128)S(1)}, u32[]{:S(2)}) copy-start(f32[1,32,32,128]{3,2,1,0:T(8,128)S(1)} %collective-permute-done.10) | copy-start | bytes 1572868
  58.5 7.4 %collective-permute-start.13 = (f32[1,32,16,128]{3,2,1,0:T(8,128)S(1)}, f32[1,32,16,128]{3,2,1,0:T(8,128)S(1)}, u32[]{:S(2)}, u32[]{:S(2)}) collective-permute-start(f32[1,32,16,128]{3,2,1,0:T(8,128)S(1)} %slice.311), channel_id=1, source_target_pairs={{0,24},{4,28},{8,0},{12,4},{16,8},{20,12},{24,16},{28,20},{32,56},... | collective-permute-start | bytes 786440 | tf_op jit(solution)/shard_map/ppermute | solution.py:21
  61.8 11.7 %copy-start.28 = (f32[32]{0:T(128)}, f32[32]{0:T(128)S(1)}, u32[]{:S(2)}) copy-start(f32[32]{0:T(128)S(1)} %broadcast_multiply_fusion.2) | copy-start | bytes 388
  65.9 7.6 %copy-start.3 = (f32[1,32,32,128]{3,2,1,0:T(8,128)}, f32[1,32,32,128]{3,2,1,0:T(8,128)S(1)}, u32[]{:S(2)}) copy-start(f32[1,32,32,128]{3,2,1,0:T(8,128)S(1)} %constant_dynamic-update-slice_fusion) | copy-start | bytes 1572868
  67.1 14.4 %collective-permute-start.15 = (f32[1,32,32,128]{3,2,1,0:T(8,128)}, f32[1,32,32,128]{3,2,1,0:T(8,128)}, u32[]{:S(2)}, u32[]{:S(2)}) collective-permute-start(f32[1,32,32,128]{3,2,1,0:T(8,128)} %add_select_fusion.2), channel_id=1, source_target_pairs={{0,32},{4,36},{8,40},{12,44},{16,48},{20,52},{24,56},{28,60},{32,6... | collective-permute-start | bytes 1572872 | tf_op jit(solution)/shard_map/ppermute | solution.py:21
  70.8 13.3 %collective-permute-start.14 = (f32[1,32,32,128]{3,2,1,0:T(8,128)}, f32[1,32,32,128]{3,2,1,0:T(8,128)}, u32[]{:S(2)}, u32[]{:S(2)}) collective-permute-start(f32[1,32,32,128]{3,2,1,0:T(8,128)} %add_select_fusion.2), channel_id=1, source_target_pairs={{0,96},{4,100},{8,104},{12,108},{16,112},{20,116},{24,120},{28,124... | collective-permute-start | bytes 1572872 | tf_op jit(solution)/shard_map/ppermute | solution.py:21
  73.5 7.6 %collective-permute-start.6 = (f32[1,32]{1,0:T(1,128)}, f32[1,32]{1,0:T(1,128)S(1)}, u32[]{:S(2)}, u32[]{:S(2)}) collective-permute-start(f32[1,32]{1,0:T(1,128)} %get-tuple-element.23), channel_id=1, source_target_pairs={{0,32},{4,36},{8,40},{12,44},{16,48},{20,52},{24,56},{28,60},{32,6... | collective-permute-start | bytes 392 | tf_op jit(solution)/shard_map/ppermute | solution.py:21
  77.2 7.0 %collective-permute-start.8 = (f32[1,32]{1,0:T(1,128)}, f32[1,32]{1,0:T(1,128)S(1)}, u32[]{:S(2)}, u32[]{:S(2)}) collective-permute-start(f32[1,32]{1,0:T(1,128)} %get-tuple-element.23), channel_id=1, source_target_pairs={{0,96},{4,100},{8,104},{12,108},{16,112},{20,116},{24,120},{28,124... | collective-permute-start | bytes 392 | tf_op jit(solution)/shard_map/ppermute | solution.py:21
  81.1 13.4 %copy-start.22 = (f32[1,32]{1,0:T(1,128)}, f32[1,32]{1,0:T(1,128)S(1)}, u32[]{:S(2)}) copy-start(f32[1,32]{1,0:T(1,128)S(1)} %collective-permute-done.6) | copy-start | bytes 388
  81.1 10.7 %collective-permute-start.7 = (f32[1,32]{1,0:T(1,128)S(1)}, f32[1,32]{1,0:T(1,128)S(1)}, u32[]{:S(2)}, u32[]{:S(2)}) collective-permute-start(f32[1,32]{1,0:T(1,128)S(1)} %collective-permute-done.6), channel_id=1, source_target_pairs={{0,32},{4,36},{8,40},{12,44},{16,48},{20,52},{24,56},{28,60},{32,6... | collective-permute-start | bytes 392 | tf_op jit(solution)/shard_map/ppermute | solution.py:21
  82.6 7.7 %collective-permute-start.16 = (f32[1,32,16,128]{3,2,1,0:T(8,128)S(1)}, f32[1,32,16,128]{3,2,1,0:T(8,128)S(1)}, u32[]{:S(2)}, u32[]{:S(2)}) collective-permute-start(f32[1,32,16,128]{3,2,1,0:T(8,128)S(1)} %slice.312), channel_id=1, source_target_pairs={{0,32},{4,36},{8,40},{12,44},{16,48},{20,52},{24,56},{28,60},{32,6... | collective-permute-start | bytes 786440 | tf_op jit(solution)/shard_map/ppermute | solution.py:21
  84.1 10.5 %copy-start.26 = (f32[32]{0:T(128)}, f32[32]{0:T(128)S(1)}, u32[]{:S(2)}) copy-start(f32[32]{0:T(128)S(1)} %multiply_bitcast_fusion.1) | copy-start | bytes 388
  85.1 6.6 %collective-permute-start.17 = (f32[1,32,16,128]{3,2,1,0:T(8,128)S(1)}, f32[1,32,16,128]{3,2,1,0:T(8,128)S(1)}, u32[]{:S(2)}, u32[]{:S(2)}) collective-permute-start(f32[1,32,16,128]{3,2,1,0:T(8,128)S(1)} %slice.313), channel_id=1, source_target_pairs={{0,96},{4,100},{8,104},{12,108},{16,112},{20,116},{24,120},{28,124... | collective-permute-start | bytes 786440 | tf_op jit(solution)/shard_map/ppermute | solution.py:21
  91.8 12.5 %copy-start.24 = (f32[1,32]{1,0:T(1,128)}, f32[1,32]{1,0:T(1,128)S(1)}, u32[]{:S(2)}) copy-start(f32[1,32]{1,0:T(1,128)S(1)} %collective-permute-done.7) | copy-start | bytes 388
  94.7 9.6 %collective-permute-start.18 = (f32[1,32,32,128]{3,2,1,0:T(8,128)S(1)}, f32[1,32,32,128]{3,2,1,0:T(8,128)S(1)}, u32[]{:S(2)}, u32[]{:S(2)}) collective-permute-start(f32[1,32,32,128]{3,2,1,0:T(8,128)S(1)} %fusion.29), channel_id=1, source_target_pairs={{0,4},{4,0},{8,12},{12,8},{16,20},{20,16},{24,28},{28,24},{32,36},... | collective-permute-start | bytes 1572872 | tf_op jit(solution)/shard_map/ppermute | solution.py:21
  94.8 9.5 %copy-start.21 = (f32[32]{0:T(128)S(1)}, f32[32]{0:T(128)}, u32[]{:S(2)}) copy-start(f32[32]{0:T(128)} %param.22) | copy-start | bytes 388
  106.6 10.6 %copy-start.31 = (f32[2048]{0:T(1024)S(1)}, f32[2048]{0:T(1024)}, u32[]{:S(2)}) copy-start(f32[2048]{0:T(1024)} %param.25) | copy-start | bytes 24580
  108.0 6.6 %collective-permute-start.19 = (f32[512,1]{0,1:T(1,128)S(1)}, f32[512,1]{0,1:T(1,128)S(1)}, u32[]{:S(2)}, u32[]{:S(2)}) collective-permute-start(f32[512,1]{0,1:T(1,128)S(1)} %bitcast.247), channel_id=1, source_target_pairs={{0,1},{1,2},{2,3},{3,0},{4,5},{5,6},{6,7},{7,4},{8,9},{9,10},{10,1... | collective-permute-start | bytes 6152 | tf_op jit(solution)/shard_map/ppermute | solution.py:21
  110.0 5.2 %collective-permute-start.20 = (f32[512,1]{0,1:T(1,128)S(1)}, f32[512,1]{0,1:T(1,128)S(1)}, u32[]{:S(2)}, u32[]{:S(2)}) collective-permute-start(f32[512,1]{0,1:T(1,128)S(1)} %bitcast.248), channel_id=1, source_target_pairs={{0,2},{1,3},{2,0},{3,1},{4,6},{5,7},{6,4},{7,5},{8,10},{9,11},{10,... | collective-permute-start | bytes 6152 | tf_op jit(solution)/shard_map/ppermute | solution.py:21
  113.6 3.6 %collective-permute-start.21 = (f32[512,1]{0,1:T(1,128)S(1)}, f32[512,1]{0,1:T(1,128)S(1)}, u32[]{:S(2)}, u32[]{:S(2)}) collective-permute-start(f32[512,1]{0,1:T(1,128)S(1)} %bitcast.249), channel_id=1, source_target_pairs={{0,3},{1,0},{2,1},{3,2},{4,7},{5,4},{6,5},{7,6},{8,11},{9,8},{10,9... | collective-permute-start | bytes 6152 | tf_op jit(solution)/shard_map/ppermute | solution.py:21
  131.8 27.0 %copy-start.33 = (s32[8]{0:T(128)S(1)}, s32[8]{0:T(128)}, u32[]{:S(2)}) copy-start(s32[8]{0:T(128)} %param.27) | copy-start | bytes 100
  131.8 27.1 %copy-start.13 = (bf16[4,8,2048]{2,1,0:T(8,128)(2,1)S(1)}, bf16[4,8,2048]{2,1,0:T(8,128)(2,1)}, u32[]{:S(2)}) copy-start(bf16[4,8,2048]{2,1,0:T(8,128)(2,1)} %param.28) | copy-start | bytes 393220
  131.8 27.5 %copy-start.17 = (bf16[4,8,256]{2,1,0:T(8,128)(2,1)S(1)}, bf16[4,8,256]{2,1,0:T(8,128)(2,1)}, u32[]{:S(2)}) copy-start(bf16[4,8,256]{2,1,0:T(8,128)(2,1)} %param.30) | copy-start | bytes 49156
  131.8 28.0 %copy-start.18 = (f32[4,8,32]{2,1,0:T(8,128)S(1)}, f32[4,8,32]{2,1,0:T(8,128)}, u32[]{:S(2)}) copy-start(f32[4,8,32]{2,1,0:T(8,128)} %param.31) | copy-start | bytes 12292
  131.8 28.2 %copy-start.5 = (f32[1,32,32,128]{3,2,1,0:T(8,128)S(1)}, f32[1,32,32,128]{3,2,1,0:T(8,128)}, u32[]{:S(2)}) copy-start(f32[1,32,32,128]{3,2,1,0:T(8,128)} %copy-done.4) | copy-start | bytes 1572868
  131.8 28.2 %copy-start.23 = (f32[1,32]{1,0:T(1,128)S(1)}, f32[1,32]{1,0:T(1,128)}, u32[]{:S(2)}) copy-start(f32[1,32]{1,0:T(1,128)} %copy-done.22) | copy-start | bytes 388
  131.8 28.2 %copy-start.25 = (f32[1,32]{1,0:T(1,128)S(1)}, f32[1,32]{1,0:T(1,128)}, u32[]{:S(2)}) copy-start(f32[1,32]{1,0:T(1,128)} %copy-done.24) | copy-start | bytes 388
  131.8 28.2 %copy-start.27 = (f32[32]{0:T(128)S(1)}, f32[32]{0:T(128)}, u32[]{:S(2)}) copy-start(f32[32]{0:T(128)} %copy-done.26) | copy-start | bytes 388
  131.8 28.2 %copy-start.30 = (f32[1,32]{1,0:T(1,128)S(1)}, f32[1,32]{1,0:T(1,128)}, u32[]{:S(2)}) copy-start(f32[1,32]{1,0:T(1,128)} %copy-done.29) | copy-start | bytes 388
  161.9 3.1 %collective-permute-start.22 = (f32[1,32,32,128]{3,2,1,0:T(8,128)S(1)}, f32[1,32,32,128]{3,2,1,0:T(8,128)S(1)}, u32[]{:S(2)}, u32[]{:S(2)}) collective-permute-start(f32[1,32,32,128]{3,2,1,0:T(8,128)S(1)} %add_select_fusion), channel_id=1, source_target_pairs={{0,4},{4,0},{8,12},{12,8},{16,20},{20,16},{24,28},{28,24},{32,36},... | collective-permute-start | bytes 1572872 | tf_op jit(solution)/shard_map/ppermute | solution.py:21
  (10 other events, 46.9 us)
Sparse Core Ops, SparseCore 0:
  131.9 47.7 reduce-scatter.1

commit v9 on v8

--- a/solution.py
+++ b/solution.py
@@ -171,6 +171,7 @@
     normed = (
         gated_out * lax.rsqrt(square_sums / inner_total + norm_eps)[..., None] * norm_gain
     ).astype(jnp.bfloat16)
+    normed = lax.optimization_barrier(normed)
     projected = lax.psum_scatter(
         jnp.einsum("tpi,id->tpd", normed, w_out, preferred_element_type=jnp.float32).astype(
             jnp.bfloat16

time: 188 us -> 186 us (0.989)
  matrix products: 28.9 us -> 25 us
    dot_general x1, matrix products: 14.6 us -> 10.6 us  [body(): jnp.einsum('tpi,id->tpd', normed, w_out, preferred_element_type=jnp.float32)]
    unnamed x75 -> x83, local copies, waits for them, and re-layouts: 7.57 us -> 7.6 us
where the time goes in v9:
time: 186 us; the launch traced here: 184 us
  waiting for transfers between devices  43 us (23%)
  starting transfers between devices  37.3 us (20%)
  blocking collectives  25.3 us (14%)
  matrix products  25 us (13%)
  other arithmetic  22.8 us (12%)
  local copies, waits for them, and re-layouts  15.8 us (8%)
  between operations  15.2 us (8%)
    ppermute x21, starting transfers between devices, group_shift(): return lax.ppermute(value, axis, pairs)  31.6 us
    ppermute x21, waiting for transfers between devices, group_shift(): return lax.ppermute(value, axis, pairs)  31.3 us
    all_gather x1, blocking collectives, body(): lax.all_gather(jnp.concatenate([x_in[block_len - conv_taps + 1:], bc_in[b...  25.3 us
    reduce_scatter x1, waiting for transfers between devices, body(): lax.psum_scatter(jnp.einsum('tpi,id->tpd', normed, w_out, preferred_eleme...  11.7 us
    dot_general x1, matrix products, body(): jnp.einsum('tpi,id->tpd', normed, w_out, preferred_element_type=jnp.float32)  10.6 us
    dot_general x1, matrix products, body(): jnp.einsum('phij,jphd->iphd', mixing, x_heads, preferred_element_type=jnp...  9.46 us
    unnamed x83, local copies, waits for them, and re-layouts  7.6 us
    convert_element_type x1, other arithmetic, body(): weighted_x = (x_heads * tail_weights[..., None]).astype(jnp.bfloat16)  7.33 us
  transfers between devices with their start and end apart: 24, of which 10 were waited for; matrix products, arithmetic and copies ran while one was open for 16% of the time, Pallas kernels for 0%

profile of v9, /device:TPU:0, one launch (start us, length us, event | category | flops | bytes accessed | tf_op | source)
XLA Modules:
  0.0 184.4 jit_solution(13051621871633239894)
XLA Ops:
  7.3 2.9 %copy.82 = bf16[512,1,2048]{0,2,1:T(8,128)(2,1)S(1)} copy(bf16[512,1,2048]{2,0,1:T(8,128)(2,1)} %param.16) | data formatting | bytes 4194304 | tf_op args[0]
  10.4 2.1 %collective-permute-start = (bf16[3,1,2048]{0,2,1:T(8,128)(2,1)S(1)}, bf16[3,1,2048]{0,2,1:T(8,128)(2,1)}, u32[]{:S(2)}, u32[]{:S(2)}) collective-permute-start(bf16[3,1,2048]{0,2,1:T(8,128)(2,1)S(1)} %slice.297), channel_id=1, source_target_pairs={{0,4},{4,8},{8,12},{12,16},{16,20},{20,24},{24,28},{28,32},{32,36}... | collective-permute-start | bytes 36872 | tf_op jit(solution)/shard_map/ppermute | solution.py:12
  12.5 3.5 %collective-permute-start.1 = (bf16[3,1,256]{2,0,1:T(4,128)(2,1)S(1)}, bf16[3,1,256]{2,0,1:T(4,128)(2,1)S(1)}, u32[]{:S(2)}, u32[]{:S(2)}) collective-permute-start(bf16[3,1,256]{2,0,1:T(4,128)(2,1)S(1)} %slice.236), channel_id=1, source_target_pairs={{0,4},{4,8},{8,12},{12,16},{16,20},{20,24},{24,28},{28,32},{32,36}... | collective-permute-start | bytes 4616 | tf_op jit(solution)/shard_map/ppermute | solution.py:12
  16.1 0.7 fusion.94
  16.9 1.2 reduce-window.6
  19.8 7.3 %fusion.9 = (bf16[512,1,2048]{0,2,1:T(8,128)(2,1)S(1)}, bf16[512,1,2048]{0,2,1:T(8,128)(2,1)}) fusion(f32[2048]{0:T(1024)S(1)} %bitcast.236, bf16[512,1,2048]{0,2,1:T(8,128)(2,1)S(1)} %copy.82, f32[2048]{0:T(1024)S(1)} %bitcast.238, bf16[3,1,2048]{0,2,1:T(8,128)(2,1)} %collective-permute-done, f32[2048]{0:T(1024)S(1)} %bitcast.234, f32[2048]{0:T(1024)S(1)} %bitcast.232, ...), kind=kLoop, calls=%fused_computation.15 | loop fusion | flops 29360128 | bytes 10530816 | tf_op jit(solution)/shard_map/convert_element_type | solution.py:105
  27.2 0.7 fusion.34
  27.9 1.4 collective-permute-start.9
  29.4 1.4 collective-permute-done.2
  30.9 0.8 copy-done.6
  31.8 2.9 %collective-permute-start.11 = (f32[1,32,32,128]{3,2,1,0:T(8,128)S(1)}, f32[1,32,32,128]{3,2,1,0:T(8,128)S(1)}, u32[]{:S(2)}, u32[]{:S(2)}) collective-permute-start(f32[1,32,32,128]{3,2,1,0:T(8,128)S(1)} %fusion.25), channel_id=1, source_target_pairs={{0,8},{4,12},{8,16},{12,20},{16,24},{20,28},{24,0},{28,4},{32,40},... | collective-permute-start | bytes 1572872 | tf_op jit(solution)/shard_map/ppermute | solution.py:21
  34.7 1.5 collective-permute-start.10
  36.2 12.1 %collective-permute-done.11 = f32[1,32,32,128]{3,2,1,0:T(8,128)S(1)} collective-permute-done((f32[1,32,32,128]{3,2,1,0:T(8,128)S(1)}, f32[1,32,32,128]{3,2,1,0:T(8,128)S(1)}, u32[]{:S(2)}, u32[]{:S(2)}) %collective-permute-start.11) | collective-permute-done | bytes 524320 | tf_op jit(solution)/shard_map/ppermute | solution.py:21
  48.4 0.7 slice.310
  49.6 1.6 collective-permute-start.4
  51.3 1.7 collective-permute-start.3
  53.0 5.5 %collective-permute-done.4 = f32[1,32]{1,0:T(1,128)S(1)} collective-permute-done((f32[1,32]{1,0:T(1,128)S(1)}, f32[1,32]{1,0:T(1,128)S(1)}, u32[]{:S(2)}, u32[]{:S(2)}) %collective-permute-start.4) | collective-permute-done | bytes 160 | tf_op jit(solution)/shard_map/ppermute | solution.py:21
  58.4 3.3 %collective-permute-start.13 = (f32[1,32,16,128]{3,2,1,0:T(8,128)S(1)}, f32[1,32,16,128]{3,2,1,0:T(8,128)S(1)}, u32[]{:S(2)}, u32[]{:S(2)}) collective-permute-start(f32[1,32,16,128]{3,2,1,0:T(8,128)S(1)} %slice.311), channel_id=1, source_target_pairs={{0,24},{4,28},{8,0},{12,4},{16,8},{20,12},{24,16},{28,20},{32,56},... | collective-permute-start | bytes 786440 | tf_op jit(solution)/shard_map/ppermute | solution.py:21
  61.8 4.0 %collective-permute-done.13 = f32[1,32,16,128]{3,2,1,0:T(8,128)S(1)} collective-permute-done((f32[1,32,16,128]{3,2,1,0:T(8,128)S(1)}, f32[1,32,16,128]{3,2,1,0:T(8,128)S(1)}, u32[]{:S(2)}, u32[]{:S(2)}) %collective-permute-start.13) | collective-permute-done | bytes 262176 | tf_op jit(solution)/shard_map/ppermute | solution.py:21
  65.9 1.2 add_select_fusion.2
  67.1 3.1 %collective-permute-start.15 = (f32[1,32,32,128]{3,2,1,0:T(8,128)}, f32[1,32,32,128]{3,2,1,0:T(8,128)}, u32[]{:S(2)}, u32[]{:S(2)}) collective-permute-start(f32[1,32,32,128]{3,2,1,0:T(8,128)} %add_select_fusion.2), channel_id=1, source_target_pairs={{0,32},{4,36},{8,40},{12,44},{16,48},{20,52},{24,56},{28,60},{32,6... | collective-permute-start | bytes 1572872 | tf_op jit(solution)/shard_map/ppermute | solution.py:21
  70.8 1.3 collective-permute-start.14
  72.1 0.8 iota_compare_fusion
  73.5 0.8 collective-permute-start.6
  74.3 2.9 %copy.91 = bf16[512,1,2048]{0,2,1:T(8,128)(2,1)S(1)} copy(bf16[512,1,2048]{2,0,1:T(8,128)(2,1)} %param.17) | data formatting | bytes 4194304 | tf_op args[1]
  77.2 2.6 %collective-permute-start.8 = (f32[1,32]{1,0:T(1,128)}, f32[1,32]{1,0:T(1,128)S(1)}, u32[]{:S(2)}, u32[]{:S(2)}) collective-permute-start(f32[1,32]{1,0:T(1,128)} %get-tuple-element.21), channel_id=1, source_target_pairs={{0,96},{4,100},{8,104},{12,108},{16,112},{20,116},{24,120},{28,124... | collective-permute-start | bytes 392 | tf_op jit(solution)/shard_map/ppermute | solution.py:21
  79.7 1.4 collective-permute-done.6
  81.5 1.0 slice.312
  82.5 1.6 collective-permute-start.16
  84.1 1.0 slice.313
  85.1 2.0 %collective-permute-start.17 = (f32[1,32,16,128]{3,2,1,0:T(8,128)S(1)}, f32[1,32,16,128]{3,2,1,0:T(8,128)S(1)}, u32[]{:S(2)}, u32[]{:S(2)}) collective-permute-start(f32[1,32,16,128]{3,2,1,0:T(8,128)S(1)} %slice.313), channel_id=1, source_target_pairs={{0,96},{4,100},{8,104},{12,108},{16,112},{20,116},{24,120},{28,124... | collective-permute-start | bytes 786440 | tf_op jit(solution)/shard_map/ppermute | solution.py:21
  87.4 2.8 %collective-permute-done.16 = f32[1,32,16,128]{3,2,1,0:T(8,128)S(1)} collective-permute-done((f32[1,32,16,128]{3,2,1,0:T(8,128)S(1)}, f32[1,32,16,128]{3,2,1,0:T(8,128)S(1)}, u32[]{:S(2)}, u32[]{:S(2)}) %collective-permute-start.16) | collective-permute-done | bytes 262176 | tf_op jit(solution)/shard_map/ppermute | solution.py:21
  90.2 1.5 collective-permute-done.17
  91.8 2.7 %select_bitcast_fusion = (f32[32,32,128]{2,1,0:T(8,128)S(1)}, f32[1,32,32,128]{3,2,1,0:T(8,128)S(1)}) fusion(f32[1,32,32,128]{3,2,1,0:T(8,128)} %copy-done.6, f32[32,64,128]{2,1,0:T(8,128)S(1)} %fusion.34, s32[]{:T(128)S(6)} %select_n.251, f32[32]{0:T(128)S(1)} %get-tuple-element.58, pred[]{:T(512)S(6)} %eq.9, f32[1,32,32,128]{3,2,1,0:T(8,128)} %copy-done.1, ...), kind=kLoop, calls=%fused_computation.50 | loop fusion | flops 2883584 | bytes 5243915 | tf_op jit(solution)/shard_map/concatenate | solution.py:142
  94.8 9.5 %fusion = f32[32,64,512]{2,1,0:T(8,128)S(1)} fusion(bf16[512,32,64]{0,2,1:T(8,128)(2,1)S(1)} %bitcast.220, f32[32,512]{1,0:T(8,128)S(1)} %copy-done.14, f32[32,512]{1,0:T(8,128)S(1)} %copy-done.15, f32[512,512]{1,0:T(8,128)S(1)} %fusion.36, pred[512,512]{1,0:T(8,128)(4,1)S(1)} %copy-done.11), kind=kOutput, calls=%fused_computation.1 | convolution fusion | flops 1115684864 | bytes 7733248 | tf_op jit(solution)/shard_map/phij,jphd->iphd/dot_general | solution.py:156
  104.3 2.3 %fusion.8 = f32[512,1,32,64]{0,3,2,1:T(8,128)S(1)} fusion(f32[32,64,512]{2,1,0:T(8,128)S(1)} %fusion, f32[32]{0:T(128)S(1)} %copy-done.22, f32[512,32]{0,1:T(8,128)S(1)} %bitcast.228, f32[32,32,128]{2,1,0:T(8,128)S(1)} %bitcast.226, f32[32,32,128]{2,1,0:T(8,128)S(1)} %get-tuple-element.19, pred[]{:T(512)S(6)} %eq.9, ...), kind=kOutput, calls=%fused_computation.13 | convolution fusion | flops 1616642048 | bytes 11731457 | tf_op jit(solution)/shard_map/ipn,phdn->iphd/dot_general | solution.py:158
  106.6 1.4 multiply_reduce_fusion
  108.0 2.0 %collective-permute-start.19 = (f32[512,1]{0,1:T(1,128)S(1)}, f32[512,1]{0,1:T(1,128)S(1)}, u32[]{:S(2)}, u32[]{:S(2)}) collective-permute-start(f32[512,1]{0,1:T(1,128)S(1)} %bitcast.249), channel_id=1, source_target_pairs={{0,1},{1,2},{2,3},{3,0},{4,5},{5,6},{6,7},{7,4},{8,9},{9,10},{10,1... | collective-permute-start | bytes 6152 | tf_op jit(solution)/shard_map/ppermute | solution.py:21
  110.0 3.6 %collective-permute-start.20 = (f32[512,1]{0,1:T(1,128)S(1)}, f32[512,1]{0,1:T(1,128)S(1)}, u32[]{:S(2)}, u32[]{:S(2)}) collective-permute-start(f32[512,1]{0,1:T(1,128)S(1)} %bitcast.250), channel_id=1, source_target_pairs={{0,2},{1,3},{2,0},{3,1},{4,6},{5,7},{6,4},{7,5},{8,10},{9,11},{10,... | collective-permute-start | bytes 6152 | tf_op jit(solution)/shard_map/ppermute | solution.py:21
  113.6 1.0 collective-permute-start.21
  115.2 2.0 %collective-permute-done.21 = f32[512,1]{0,1:T(1,128)S(1)} collective-permute-done((f32[512,1]{0,1:T(1,128)S(1)}, f32[512,1]{0,1:T(1,128)S(1)}, u32[]{:S(2)}, u32[]{:S(2)}) %collective-permute-start.21) | collective-permute-done | bytes 2080 | tf_op jit(solution)/shard_map/ppermute | solution.py:21
  117.2 1.8 multiply_convert_fusion.2
  119.0 10.6 %fusion.2 = bf16[512,1,4096]{2,0,1:T(8,128)(2,1)} fusion(bf16[2048,4096]{1,0:T(8,128)(2,1)S(1)} %bitcast.269, bf16[512,1,2048]{0,2,1:T(8,128)(2,1)S(1)} %multiply_convert_fusion.2), kind=kOutput, calls=%fused_computation.4 | convolution fusion | flops 8592031744 | bytes 23068672 | tf_op jit(solution)/shard_map/tpi,id->tpd/dot_general | solution.py:176
  129.9 0.8 copy-done.8
  131.2 25.3 %all-gather = bf16[96,1,2304]{2,1,0:T(2,128)(2,1)S(1)} all-gather(bf16[3,1,2304]{2,1,0:T(2,128)(2,1)S(1)} %copy.93), channel_id=2, replica_groups=mesh['ctx'=32,'head'=4] {'ctx'}, dimensions={0}, use_global_device_ids=true | all-gather | bytes 456192 | tf_op jit(solution)/shard_map/all_gather | solution.py:112
  157.9 1.8 add_select_fusion
  162.8 1.6 convolution_multiply_fusion
  165.8 11.7 %reduce-scatter.2.cloned.1.call-done = bf16[128,1,4096]{2,0,1:T(8,128)(2,1)} async-done(((bf16[512,1,4096]{2,0,1:T(8,128)(2,1)}), bf16[128,1,4096]{2,0,1:T(8,128)(2,1)}) %reduce-scatter.2.cloned.1.call-update) | async-done | bytes 1048592 | tf_op jit(solution)/shard_map/reduce_scatter | solution.py:175
  (194 shorter events, 12.1 us)
Async XLA Ops:
  7.2 11.6 %copy-start.16 = (bf16[4,2048]{1,0:T(4,128)(2,1)S(1)}, bf16[4,2048]{1,0:T(4,128)(2,1)}, u32[]{:S(2)}) copy-start(bf16[4,2048]{1,0:T(4,128)(2,1)} %param.23) | copy-start | bytes 49156
  7.2 11.7 %copy-start.19 = (bf16[4,256]{1,0:T(4,128)(2,1)S(1)}, bf16[4,256]{1,0:T(4,128)(2,1)}, u32[]{:S(2)}) copy-start(bf16[4,256]{1,0:T(4,128)(2,1)} %param.24) | copy-start | bytes 6148
  7.2 170.3 %reduce-scatter.2.cloned.1.call-start = ((), (), s32[]{:S(2)}) async-start(), calls=%async_computation.1 | async-start | bytes 5242880 | tf_op jit(solution)/shard_map/reduce_scatter | solution.py:175
  10.4 16.8 %copy-start.7 = (bf16[3,1,2048]{0,2,1:T(8,128)(2,1)}, bf16[3,1,2048]{0,2,1:T(8,128)(2,1)S(1)}, u32[]{:S(2)}) copy-start(bf16[3,1,2048]{0,2,1:T(8,128)(2,1)S(1)} %slice.297) | copy-start | bytes 36868
  10.4 8.9 %collective-permute-start = (bf16[3,1,2048]{0,2,1:T(8,128)(2,1)S(1)}, bf16[3,1,2048]{0,2,1:T(8,128)(2,1)}, u32[]{:S(2)}, u32[]{:S(2)}) collective-permute-start(bf16[3,1,2048]{0,2,1:T(8,128)(2,1)S(1)} %slice.297), channel_id=1, source_target_pairs={{0,4},{4,8},{8,12},{12,16},{16,20},{20,24},{24,28},{28,32},{32,36}... | collective-permute-start | bytes 36872 | tf_op jit(solution)/shard_map/ppermute | solution.py:12
  12.5 6.4 %collective-permute-start.1 = (bf16[3,1,256]{2,0,1:T(4,128)(2,1)S(1)}, bf16[3,1,256]{2,0,1:T(4,128)(2,1)S(1)}, u32[]{:S(2)}, u32[]{:S(2)}) collective-permute-start(bf16[3,1,256]{2,0,1:T(4,128)(2,1)S(1)} %slice.236), channel_id=1, source_target_pairs={{0,4},{4,8},{8,12},{12,16},{16,20},{20,24},{24,28},{28,32},{32,36}... | collective-permute-start | bytes 4616 | tf_op jit(solution)/shard_map/ppermute | solution.py:12
  27.9 2.9 %collective-permute-start.9 = (f32[1,32,32,128]{3,2,1,0:T(8,128)S(1)}, f32[1,32,32,128]{3,2,1,0:T(8,128)S(1)}, u32[]{:S(2)}, u32[]{:S(2)}) collective-permute-start(f32[1,32,32,128]{3,2,1,0:T(8,128)S(1)} %dynamic-slice_bitcast_fusion), channel_id=1, source_target_pairs={{0,4},{4,0},{8,12},{12,8},{16,20},{20,16},{24,28},{28,24},{32,36},... | collective-permute-start | bytes 1572872 | tf_op jit(solution)/shard_map/ppermute | solution.py:21
  29.3 1.5 collective-permute-start.2
  31.8 16.6 %collective-permute-start.11 = (f32[1,32,32,128]{3,2,1,0:T(8,128)S(1)}, f32[1,32,32,128]{3,2,1,0:T(8,128)S(1)}, u32[]{:S(2)}, u32[]{:S(2)}) collective-permute-start(f32[1,32,32,128]{3,2,1,0:T(8,128)S(1)} %fusion.25), channel_id=1, source_target_pairs={{0,8},{4,12},{8,16},{12,20},{16,24},{20,28},{24,0},{28,4},{32,40},... | collective-permute-start | bytes 1572872 | tf_op jit(solution)/shard_map/ppermute | solution.py:21
  34.7 23.7 %collective-permute-start.10 = (f32[1,32,32,128]{3,2,1,0:T(8,128)S(1)}, f32[1,32,32,128]{3,2,1,0:T(8,128)S(1)}, u32[]{:S(2)}, u32[]{:S(2)}) collective-permute-start(f32[1,32,32,128]{3,2,1,0:T(8,128)S(1)} %fusion.25), channel_id=1, source_target_pairs={{0,24},{4,28},{8,0},{12,4},{16,8},{20,12},{24,16},{28,20},{32,56},... | collective-permute-start | bytes 1572872 | tf_op jit(solution)/shard_map/ppermute | solution.py:21
  48.4 25.1 %copy-start.1 = (f32[1,32,32,128]{3,2,1,0:T(8,128)}, f32[1,32,32,128]{3,2,1,0:T(8,128)S(1)}, u32[]{:S(2)}) copy-start(f32[1,32,32,128]{3,2,1,0:T(8,128)S(1)} %collective-permute-done.11) | copy-start | bytes 1572868
  49.1 12.6 %collective-permute-start.12 = (f32[1,32,16,128]{3,2,1,0:T(8,128)}, f32[1,32,16,128]{3,2,1,0:T(8,128)S(1)}, u32[]{:S(2)}, u32[]{:S(2)}) collective-permute-start(f32[1,32,16,128]{3,2,1,0:T(8,128)} %slice.310), channel_id=1, source_target_pairs={{0,8},{4,12},{8,16},{12,20},{16,24},{20,28},{24,0},{28,4},{32,40},... | collective-permute-start | bytes 786440 | tf_op jit(solution)/shard_map/ppermute | solution.py:21
  49.6 8.8 %collective-permute-start.4 = (f32[1,32]{1,0:T(1,128)S(1)}, f32[1,32]{1,0:T(1,128)S(1)}, u32[]{:S(2)}, u32[]{:S(2)}) collective-permute-start(f32[1,32]{1,0:T(1,128)S(1)} %get-tuple-element.57), channel_id=1, source_target_pairs={{0,8},{4,12},{8,16},{12,20},{16,24},{20,28},{24,0},{28,4},{32,40},... | collective-permute-start | bytes 392 | tf_op jit(solution)/shard_map/ppermute | solution.py:21
  51.3 10.4 %collective-permute-start.3 = (f32[1,32]{1,0:T(1,128)S(1)}, f32[1,32]{1,0:T(1,128)S(1)}, u32[]{:S(2)}, u32[]{:S(2)}) collective-permute-start(f32[1,32]{1,0:T(1,128)S(1)} %get-tuple-element.57), channel_id=1, source_target_pairs={{0,24},{4,28},{8,0},{12,4},{16,8},{20,12},{24,16},{28,20},{32,56},... | collective-permute-start | bytes 392 | tf_op jit(solution)/shard_map/ppermute | solution.py:21
  58.4 7.4 %collective-permute-start.5 = (f32[1,32]{1,0:T(1,128)S(1)}, f32[1,32]{1,0:T(1,128)S(1)}, u32[]{:S(2)}, u32[]{:S(2)}) collective-permute-start(f32[1,32]{1,0:T(1,128)S(1)} %collective-permute-done.4), channel_id=1, source_target_pairs={{0,8},{4,12},{8,16},{12,20},{16,24},{20,28},{24,0},{28,4},{32,40},... | collective-permute-start | bytes 392 | tf_op jit(solution)/shard_map/ppermute | solution.py:21
  58.4 15.0 %copy-start.2 = (f32[1,32,32,128]{3,2,1,0:T(8,128)}, f32[1,32,32,128]{3,2,1,0:T(8,128)S(1)}, u32[]{:S(2)}) copy-start(f32[1,32,32,128]{3,2,1,0:T(8,128)S(1)} %collective-permute-done.10) | copy-start | bytes 1572868
  58.4 7.4 %collective-permute-start.13 = (f32[1,32,16,128]{3,2,1,0:T(8,128)S(1)}, f32[1,32,16,128]{3,2,1,0:T(8,128)S(1)}, u32[]{:S(2)}, u32[]{:S(2)}) collective-permute-start(f32[1,32,16,128]{3,2,1,0:T(8,128)S(1)} %slice.311), channel_id=1, source_target_pairs={{0,24},{4,28},{8,0},{12,4},{16,8},{20,12},{24,16},{28,20},{32,56},... | collective-permute-start | bytes 786440 | tf_op jit(solution)/shard_map/ppermute | solution.py:21
  61.7 11.7 %copy-start.29 = (f32[32]{0:T(128)}, f32[32]{0:T(128)S(1)}, u32[]{:S(2)}) copy-start(f32[32]{0:T(128)S(1)} %broadcast_multiply_fusion.2) | copy-start | bytes 388
  67.1 14.4 %collective-permute-start.15 = (f32[1,32,32,128]{3,2,1,0:T(8,128)}, f32[1,32,32,128]{3,2,1,0:T(8,128)}, u32[]{:S(2)}, u32[]{:S(2)}) collective-permute-start(f32[1,32,32,128]{3,2,1,0:T(8,128)} %add_select_fusion.2), channel_id=1, source_target_pairs={{0,32},{4,36},{8,40},{12,44},{16,48},{20,52},{24,56},{28,60},{32,6... | collective-permute-start | bytes 1572872 | tf_op jit(solution)/shard_map/ppermute | solution.py:21
  70.8 13.3 %collective-permute-start.14 = (f32[1,32,32,128]{3,2,1,0:T(8,128)}, f32[1,32,32,128]{3,2,1,0:T(8,128)}, u32[]{:S(2)}, u32[]{:S(2)}) collective-permute-start(f32[1,32,32,128]{3,2,1,0:T(8,128)} %add_select_fusion.2), channel_id=1, source_target_pairs={{0,96},{4,100},{8,104},{12,108},{16,112},{20,116},{24,120},{28,124... | collective-permute-start | bytes 1572872 | tf_op jit(solution)/shard_map/ppermute | solution.py:21
  73.5 7.6 %collective-permute-start.6 = (f32[1,32]{1,0:T(1,128)}, f32[1,32]{1,0:T(1,128)S(1)}, u32[]{:S(2)}, u32[]{:S(2)}) collective-permute-start(f32[1,32]{1,0:T(1,128)} %get-tuple-element.21), channel_id=1, source_target_pairs={{0,32},{4,36},{8,40},{12,44},{16,48},{20,52},{24,56},{28,60},{32,6... | collective-permute-start | bytes 392 | tf_op jit(solution)/shard_map/ppermute | solution.py:21
  77.2 6.9 %collective-permute-start.8 = (f32[1,32]{1,0:T(1,128)}, f32[1,32]{1,0:T(1,128)S(1)}, u32[]{:S(2)}, u32[]{:S(2)}) collective-permute-start(f32[1,32]{1,0:T(1,128)} %get-tuple-element.21), channel_id=1, source_target_pairs={{0,96},{4,100},{8,104},{12,108},{16,112},{20,116},{24,120},{28,124... | collective-permute-start | bytes 392 | tf_op jit(solution)/shard_map/ppermute | solution.py:21
  81.1 13.4 %copy-start.23 = (f32[1,32]{1,0:T(1,128)}, f32[1,32]{1,0:T(1,128)S(1)}, u32[]{:S(2)}) copy-start(f32[1,32]{1,0:T(1,128)S(1)} %collective-permute-done.6) | copy-start | bytes 388
  81.1 10.7 %collective-permute-start.7 = (f32[1,32]{1,0:T(1,128)S(1)}, f32[1,32]{1,0:T(1,128)S(1)}, u32[]{:S(2)}, u32[]{:S(2)}) collective-permute-start(f32[1,32]{1,0:T(1,128)S(1)} %collective-permute-done.6), channel_id=1, source_target_pairs={{0,32},{4,36},{8,40},{12,44},{16,48},{20,52},{24,56},{28,60},{32,6... | collective-permute-start | bytes 392 | tf_op jit(solution)/shard_map/ppermute | solution.py:21
  82.5 7.7 %collective-permute-start.16 = (f32[1,32,16,128]{3,2,1,0:T(8,128)S(1)}, f32[1,32,16,128]{3,2,1,0:T(8,128)S(1)}, u32[]{:S(2)}, u32[]{:S(2)}) collective-permute-start(f32[1,32,16,128]{3,2,1,0:T(8,128)S(1)} %slice.312), channel_id=1, source_target_pairs={{0,32},{4,36},{8,40},{12,44},{16,48},{20,52},{24,56},{28,60},{32,6... | collective-permute-start | bytes 786440 | tf_op jit(solution)/shard_map/ppermute | solution.py:21
  84.1 10.5 %copy-start.30 = (f32[1,32]{1,0:T(1,128)}, f32[1,32]{1,0:T(1,128)S(1)}, u32[]{:S(2)}) copy-start(f32[1,32]{1,0:T(1,128)S(1)} %collective-permute-done.8) | copy-start | bytes 388
  84.1 10.5 %copy-start.27 = (f32[32]{0:T(128)}, f32[32]{0:T(128)S(1)}, u32[]{:S(2)}) copy-start(f32[32]{0:T(128)S(1)} %multiply_bitcast_fusion.1) | copy-start | bytes 388
  85.1 6.6 %collective-permute-start.17 = (f32[1,32,16,128]{3,2,1,0:T(8,128)S(1)}, f32[1,32,16,128]{3,2,1,0:T(8,128)S(1)}, u32[]{:S(2)}, u32[]{:S(2)}) collective-permute-start(f32[1,32,16,128]{3,2,1,0:T(8,128)S(1)} %slice.313), channel_id=1, source_target_pairs={{0,96},{4,100},{8,104},{12,108},{16,112},{20,116},{24,120},{28,124... | collective-permute-start | bytes 786440 | tf_op jit(solution)/shard_map/ppermute | solution.py:21
  94.6 9.7 %collective-permute-start.18 = (f32[1,32,32,128]{3,2,1,0:T(8,128)S(1)}, f32[1,32,32,128]{3,2,1,0:T(8,128)S(1)}, u32[]{:S(2)}, u32[]{:S(2)}) collective-permute-start(f32[1,32,32,128]{3,2,1,0:T(8,128)S(1)} %fusion.26), channel_id=1, source_target_pairs={{0,4},{4,0},{8,12},{12,8},{16,20},{20,16},{24,28},{28,24},{32,36},... | collective-permute-start | bytes 1572872 | tf_op jit(solution)/shard_map/ppermute | solution.py:21
  94.8 9.5 %copy-start.22 = (f32[32]{0:T(128)S(1)}, f32[32]{0:T(128)}, u32[]{:S(2)}) copy-start(f32[32]{0:T(128)} %param.22) | copy-start | bytes 388
  94.8 24.1 %slice-start = ((s8[16777216]{0:T(1024)(128)(4,1)}), s8[4194304]{0:T(1024)(128)(4,1)S(1)}, s32[]{:S(2)}) async-start(s8[16777216]{0:T(1024)(128)(4,1)} %bitcast.268), calls=%async_computation.2 | async-start | bytes 8388608
  94.8 24.1 %slice-start.1 = ((s8[16777216]{0:T(1024)(128)(4,1)}), s8[4194304]{0:T(1024)(128)(4,1)S(1)}, s32[]{:S(2)}) async-start(s8[16777216]{0:T(1024)(128)(4,1)} %bitcast.268), calls=%async_computation.3 | async-start | bytes 8388608
  94.8 24.1 %slice-start.2 = ((s8[16777216]{0:T(1024)(128)(4,1)}), s8[4194304]{0:T(1024)(128)(4,1)S(1)}, s32[]{:S(2)}) async-start(s8[16777216]{0:T(1024)(128)(4,1)} %bitcast.268), calls=%async_computation.4 | async-start | bytes 8388608
  104.3 14.6 %slice-start.3 = ((s8[16777216]{0:T(1024)(128)(4,1)}), s8[4194304]{0:T(1024)(128)(4,1)S(1)}, s32[]{:S(2)}) async-start(s8[16777216]{0:T(1024)(128)(4,1)} %bitcast.268), calls=%async_computation.5 | async-start | bytes 8388608
  106.6 10.6 %copy-start.20 = (f32[2048]{0:T(1024)S(1)}, f32[2048]{0:T(1024)}, u32[]{:S(2)}) copy-start(f32[2048]{0:T(1024)} %param.25) | copy-start | bytes 24580
  108.0 6.6 %collective-permute-start.19 = (f32[512,1]{0,1:T(1,128)S(1)}, f32[512,1]{0,1:T(1,128)S(1)}, u32[]{:S(2)}, u32[]{:S(2)}) collective-permute-start(f32[512,1]{0,1:T(1,128)S(1)} %bitcast.249), channel_id=1, source_target_pairs={{0,1},{1,2},{2,3},{3,0},{4,5},{5,6},{6,7},{7,4},{8,9},{9,10},{10,1... | collective-permute-start | bytes 6152 | tf_op jit(solution)/shard_map/ppermute | solution.py:21
  110.0 5.2 %collective-permute-start.20 = (f32[512,1]{0,1:T(1,128)S(1)}, f32[512,1]{0,1:T(1,128)S(1)}, u32[]{:S(2)}, u32[]{:S(2)}) collective-permute-start(f32[512,1]{0,1:T(1,128)S(1)} %bitcast.250), channel_id=1, source_target_pairs={{0,2},{1,3},{2,0},{3,1},{4,6},{5,7},{6,4},{7,5},{8,10},{9,11},{10,... | collective-permute-start | bytes 6152 | tf_op jit(solution)/shard_map/ppermute | solution.py:21
  113.6 3.6 %collective-permute-start.21 = (f32[512,1]{0,1:T(1,128)S(1)}, f32[512,1]{0,1:T(1,128)S(1)}, u32[]{:S(2)}, u32[]{:S(2)}) collective-permute-start(f32[512,1]{0,1:T(1,128)S(1)} %bitcast.251), channel_id=1, source_target_pairs={{0,3},{1,0},{2,1},{3,2},{4,7},{5,4},{6,5},{7,6},{8,11},{9,8},{10,9... | collective-permute-start | bytes 6152 | tf_op jit(solution)/shard_map/ppermute | solution.py:21
  129.6 27.0 %copy-start.33 = (s32[8]{0:T(128)S(1)}, s32[8]{0:T(128)}, u32[]{:S(2)}) copy-start(s32[8]{0:T(128)} %param.27) | copy-start | bytes 100
  129.6 27.1 %copy-start.13 = (bf16[4,8,2048]{2,1,0:T(8,128)(2,1)S(1)}, bf16[4,8,2048]{2,1,0:T(8,128)(2,1)}, u32[]{:S(2)}) copy-start(bf16[4,8,2048]{2,1,0:T(8,128)(2,1)} %param.28) | copy-start | bytes 393220
  129.6 27.5 %copy-start.17 = (bf16[4,8,256]{2,1,0:T(8,128)(2,1)S(1)}, bf16[4,8,256]{2,1,0:T(8,128)(2,1)}, u32[]{:S(2)}) copy-start(bf16[4,8,256]{2,1,0:T(8,128)(2,1)} %param.30) | copy-start | bytes 49156
  129.6 28.0 %copy-start.18 = (f32[4,8,32]{2,1,0:T(8,128)S(1)}, f32[4,8,32]{2,1,0:T(8,128)}, u32[]{:S(2)}) copy-start(f32[4,8,32]{2,1,0:T(8,128)} %param.31) | copy-start | bytes 12292
  129.6 28.2 %copy-start.5 = (f32[1,32,32,128]{3,2,1,0:T(8,128)S(1)}, f32[1,32,32,128]{3,2,1,0:T(8,128)}, u32[]{:S(2)}) copy-start(f32[1,32,32,128]{3,2,1,0:T(8,128)} %copy-done.4) | copy-start | bytes 1572868
  129.7 28.2 %copy-start.24 = (f32[1,32]{1,0:T(1,128)S(1)}, f32[1,32]{1,0:T(1,128)}, u32[]{:S(2)}) copy-start(f32[1,32]{1,0:T(1,128)} %copy-done.23) | copy-start | bytes 388
  129.7 28.2 %copy-start.26 = (f32[1,32]{1,0:T(1,128)S(1)}, f32[1,32]{1,0:T(1,128)}, u32[]{:S(2)}) copy-start(f32[1,32]{1,0:T(1,128)} %copy-done.25) | copy-start | bytes 388
  129.7 28.2 %copy-start.28 = (f32[32]{0:T(128)S(1)}, f32[32]{0:T(128)}, u32[]{:S(2)}) copy-start(f32[32]{0:T(128)} %copy-done.27) | copy-start | bytes 388
  129.7 28.2 %copy-start.31 = (f32[1,32]{1,0:T(1,128)S(1)}, f32[1,32]{1,0:T(1,128)}, u32[]{:S(2)}) copy-start(f32[1,32]{1,0:T(1,128)} %copy-done.30) | copy-start | bytes 388
  159.7 3.1 %collective-permute-start.22 = (f32[1,32,32,128]{3,2,1,0:T(8,128)S(1)}, f32[1,32,32,128]{3,2,1,0:T(8,128)S(1)}, u32[]{:S(2)}, u32[]{:S(2)}) collective-permute-start(f32[1,32,32,128]{3,2,1,0:T(8,128)S(1)} %add_select_fusion), channel_id=1, source_target_pairs={{0,4},{4,0},{8,12},{12,8},{16,20},{20,16},{24,28},{28,24},{32,36},... | collective-permute-start | bytes 1572872 | tf_op jit(solution)/shard_map/ppermute | solution.py:21
  (14 other events, 81.3 us)
Sparse Core Ops, SparseCore 0:
  129.8 47.7 reduce-scatter.1
